TPU v7x, 32 devices: a whole 2x2x4 slice. The times are simulated.
32 devices in a mesh: req: 8 (over y, x, core), tp: 4 (over z).
Axes of the slice: x: 2, y: 2, z: 4, core: 2. Of those that a mesh axis runs over, the one named last changes fastest.
Arguments:
- queries: bfloat16 [1536, 2560], P('req', 'tp'), may hold values from -5 to 5
- new_keys: bfloat16 [1536, 512], P('req', 'tp'), may hold values from -5 to 5
- new_values: bfloat16 [1536, 512], P('req', 'tp'), may hold values from -5 to 5
- key_pages: bfloat16 [512, 64, 512], P('req', None, 'tp'), may hold values from -5 to 5
- value_pages: bfloat16 [512, 64, 512], P('req', None, 'tp'), may hold values from -5 to 5
- page_table: int32 [32, 16], P('req'), may hold values from 0 to 511, as said below
- cache_lengths: int32 [32], P('req'), may hold values from 2 to 1024, as said below
- parents: int32 [32, 48], P('req'), may hold values from -1 to 46, as said below
- residual: bfloat16 [1536, 2560], P('req'), may hold values from -6 to 6
- out_weight: bfloat16 [2560, 2560], P('tp'), may hold values from -0.125 to 0.125
- norm_gain: float32 [2560], replicated, may hold values from 0.1 to 1.9
- router_weight: float32 [2560, 16], replicated, may hold values from -0.125 to 0.125
- routes: int32 [1536, 6], P('req'), may hold values from 0 to 15, all different within a row; in each aligned block of 192 rows (0 to 191, 192 to 383, ...) at most 91 rows name the same one
- expert_gate_up: bfloat16 [16, 2560, 2, 1536], P('req', None, None, 'tp'), may hold values from -0.125 to 0.125
- expert_down: bfloat16 [16, 1536, 2560], P('req', 'tp'), may hold values from -0.15625 to 0.15625
- shared_gate_up: bfloat16 [2560, 2, 1536], P(None, None, 'tp'), may hold values from -0.125 to 0.125
- shared_down: bfloat16 [1536, 2560], P('tp'), may hold values from -0.15625 to 0.15625
Outputs:
- layer_out: bfloat16 [1536, 2560], P('req', 'tp')
Inputs may be any that keep to these rules, and one draw needn't show every extreme that they name: `page_table`: the pages of the 4 requests of the d-th block of 4 rows are the d-th block of 64 pages of the pool, each named once. `cache_lengths`: some request holds 1024 positions. parents[r, 0] = -1, and 0 <= parents[r, i] < i for i >= 1. `routes`: A token's 6 experts differ. In each aligned block of 192 rows no expert is named by more than 91 rows, and in some block one expert is named by exactly 91.
All inputs are finite; a program needn't handle non-finite values.
Results may differ from a plain program's by a relative error of at most 0.02.
Values may be sent and summed in bfloat16 or wider, within the bound.
No kernel may reach another device: no remote copies, remote signals or barrier semaphores. Data moves between devices by JAX's collectives and lax.ppermute only.
A program may use at most 128 MiB of HBM per device.

v0:
```python
import math

import jax
import jax.numpy as jnp
from jax import lax
from jax.sharding import PartitionSpec as P

QH = 20
KVH = 4
HD = 128


EPSILON = 1e-06
NEGATIVE = -1e30


def rounded(values):
    return lax.optimization_barrier(values.astype(jnp.bfloat16)).astype(jnp.float32)


def ancestors(parents):
    tree_size = parents.shape[-1]
    position = jnp.arange(tree_size, dtype=jnp.int32)
    adjacency = (parents[..., :, None] == position[None, :]) | (
        position[:, None] == position[None, :]
    )
    closure = adjacency.astype(jnp.float32)
    for doubling in range(max(1, (tree_size - 1).bit_length())):
        closure = jnp.minimum(
            jnp.einsum("...ij,...jk->...ik", closure, closure, precision=lax.Precision.HIGHEST), 1.0
        )
    return closure > 0.5


def tree_attention(queries, cache_keys, cache_values, new_keys, new_values, lengths, allowed):
    scaling = 1.0 / math.sqrt(queries.shape[-1])
    cache_scores = (
        jnp.einsum("rtkgd,rckd->rkgtc", queries, cache_keys, preferred_element_type=jnp.float32)
        * scaling
    )
    tree_scores = (
        jnp.einsum("rtkgd,rskd->rkgts", queries, new_keys, preferred_element_type=jnp.float32)
        * scaling
    )
    live = jnp.arange(cache_keys.shape[1], dtype=jnp.int32)[None, :] < lengths[:, None]
    cache_scores = jnp.where(live[:, None, None, None, :], cache_scores, NEGATIVE)
    tree_scores = jnp.where(allowed[:, None, None, :, :], tree_scores, NEGATIVE)
    highest = jnp.maximum(jnp.max(cache_scores, axis=-1), jnp.max(tree_scores, axis=-1))[..., None]
    cache_exp = jnp.exp(cache_scores - highest)
    tree_exp = jnp.exp(tree_scores - highest)
    denominator = (jnp.sum(cache_exp, axis=-1) + jnp.sum(tree_exp, axis=-1))[..., None]
    cache_probs = (cache_exp / denominator).astype(jnp.bfloat16)
    tree_probs = (tree_exp / denominator).astype(jnp.bfloat16)
    mixed = jnp.einsum(
        "rkgtc,rckd->rtkgd", cache_probs, cache_values, preferred_element_type=jnp.float32
    )
    mixed = mixed + jnp.einsum(
        "rkgts,rskd->rtkgd", tree_probs, new_values, preferred_element_type=jnp.float32
    )
    return mixed.astype(jnp.bfloat16).reshape(queries.shape[0], queries.shape[1], -1)


def place_rows(routes, experts_local, groups, capacity):
    flat_expert = routes.reshape(-1)
    expert_ids = jnp.arange(experts_local * groups, dtype=jnp.int32)
    onehot = (flat_expert[:, None] == expert_ids[None, :]).astype(jnp.int32)
    earlier = jnp.cumsum(onehot, axis=0) - onehot
    rank = jnp.sum(earlier * onehot, axis=1)
    owner = flat_expert // experts_local
    local_expert = flat_expert % experts_local
    return (local_expert * groups + owner) * capacity + rank


def fill_outbox(row_values, slot_index, top_count, lead_shape):
    repeated = jnp.repeat(row_values, top_count, axis=0)
    outbox = jnp.zeros(
        (lead_shape[0] * lead_shape[1] * lead_shape[2], row_values.shape[1]), row_values.dtype
    )
    outbox = outbox.at[slot_index].set(repeated)
    return outbox.reshape(lead_shape + (row_values.shape[1],))


def shards(
    queries,
    new_keys,
    new_values,
    key_pages,
    value_pages,
    page_table,
    cache_lengths,
    parents,
    residual,
    out_weight,
    norm_gain,
    router_weight,
    routes,
    expert_gate_up,
    expert_down,
    shared_gate_up,
    shared_down,
):
    groups = lax.axis_size("req")
    tp_count = lax.axis_size("tp")
    requests = parents.shape[0]
    tree_size = parents.shape[1]
    row_count = requests * tree_size
    kv_local = new_keys.shape[1] // HD
    head_ratio = QH // KVH
    model_width = residual.shape[1]
    part_width = model_width // tp_count
    pages_dev = key_pages.shape[0]
    local_pages = page_table - lax.axis_index("req") * pages_dev
    cache_keys = key_pages[local_pages].reshape(requests, -1, kv_local, HD)
    cache_values = value_pages[local_pages].reshape(requests, -1, kv_local, HD)
    head_outputs = tree_attention(
        queries.reshape(requests, tree_size, kv_local, head_ratio, HD),
        cache_keys,
        cache_values,
        new_keys.reshape(requests, tree_size, kv_local, HD),
        new_values.reshape(requests, tree_size, kv_local, HD),
        cache_lengths,
        ancestors(parents),
    )
    attn_terms = jnp.dot(
        head_outputs.reshape(row_count, -1), out_weight, preferred_element_type=jnp.float32
    )
    column = lax.axis_index("tp") * part_width
    experts_local = expert_gate_up.shape[0]
    top_count = routes.shape[1]
    expert_count = experts_local * groups
    capacity = max(10 * requests, row_count * top_count * 5 // (4 * expert_count) + 1)
    slot_index = place_rows(routes, experts_local, groups, capacity)
    lead_shape = (experts_local, groups, capacity)
    attn_out = lax.psum(attn_terms.astype(jnp.bfloat16), "tp").astype(jnp.float32)
    hidden = rounded(residual.astype(jnp.float32) + attn_out)
    rstd = lax.rsqrt(jnp.mean(hidden * hidden, axis=1, keepdims=True) + EPSILON)
    normed = hidden * rstd * norm_gain
    logits = jnp.dot(normed, router_weight, precision=lax.Precision.HIGHEST)
    normed_bf = normed.astype(jnp.bfloat16)
    hidden_part = lax.dynamic_slice_in_dim(hidden, column, part_width, 1)
    outbox = fill_outbox(normed_bf, slot_index, top_count, lead_shape)
    arrived = lax.all_to_all(outbox, "req", split_axis=1, concat_axis=1, tiled=True)
    arrived = arrived.reshape(experts_local, groups * capacity, model_width)
    gate_up = jnp.einsum(
        "emd,edcf->emcf", arrived, expert_gate_up, preferred_element_type=jnp.float32
    )
    act = (jax.nn.silu(gate_up[:, :, 0]) * gate_up[:, :, 1]).astype(jnp.bfloat16)
    partial_value = rounded(
        jnp.einsum("emf,efd->emd", act, expert_down, preferred_element_type=jnp.float32)
    )
    summed = lax.psum_scatter(
        partial_value.astype(jnp.bfloat16), "tp", scatter_dimension=2, tiled=True
    )
    outputs = summed.reshape(experts_local, groups, capacity, part_width)
    returned = lax.all_to_all(outputs, "req", split_axis=1, concat_axis=1, tiled=True).reshape(
        -1, part_width
    )
    picked = returned[slot_index].astype(jnp.float32).reshape(row_count, top_count, part_width)
    expert_ids = jnp.arange(expert_count, dtype=jnp.int32)
    chosen = jnp.sum(
        jnp.where(routes[:, :, None] == expert_ids[None, None, :], logits[:, None, :], 0.0), axis=-1
    )
    gate_values = jax.nn.sigmoid(chosen)
    gate_values = gate_values / jnp.sum(gate_values, axis=1, keepdims=True)
    routed = jnp.sum(picked * gate_values[:, :, None], axis=1)
    shared_gu = jnp.einsum(
        "td,dcf->tcf", normed_bf, shared_gate_up, preferred_element_type=jnp.float32
    )
    shared_act = (jax.nn.silu(shared_gu[:, 0]) * shared_gu[:, 1]).astype(jnp.bfloat16)
    shared_terms = jnp.dot(shared_act, shared_down, preferred_element_type=jnp.float32)
    shared_out = lax.psum_scatter(
        shared_terms.astype(jnp.bfloat16), "tp", scatter_dimension=1, tiled=True
    ).astype(jnp.float32)
    return (hidden_part + shared_out + routed).astype(jnp.bfloat16)


def solution(mesh):
    in_specs = (
        P("req", "tp"),
        P("req", "tp"),
        P("req", "tp"),
        P("req", None, "tp"),
        P("req", None, "tp"),
        P("req", None),
        P("req"),
        P("req", None),
        P("req", None),
        P("tp", None),
        P(),
        P(),
        P("req", None),
        P("req", None, None, "tp"),
        P("req", "tp", None),
        P(None, None, "tp"),
        P("tp", None),
    )
    out_specs = P("req", "tp")
    return jax.shard_map(shards, mesh=mesh, in_specs=in_specs, out_specs=out_specs, check_vma=False)
```

profile of v0, /device:TPU:0, one launch (start us, length us, event | category | flops | bytes accessed | tf_op | source)
XLA Modules:
  0.0 486.2 jit_solution(5703992235077245131)
XLA Ops:
  6.6 0.8 compare_select_fusion.4
  7.5 0.8 iota_compare_fusion.5
  8.3 2.0 reshape.306
  10.2 1.0 convolution_minimum_fusion.5
  12.5 2.9 gather_fusion.1
  15.4 2.1 bitcast_reduce_fusion
  17.6 0.4 fusion.55
  18.0 1.4 copy-done.2
  19.4 1.0 fusion.8
  20.5 2.9 gather_fusion
  23.4 3.5 fusion.11
  26.9 0.3 fusion.21
  27.4 1.9 convolution_convert_fusion.2
  30.1 4.5 reduce-window.6
  34.7 0.4 slice_reduce_fusion
  35.5 46.5 %all-reduce.2.cloned.1.call-done = bf16[192,2560]{1,0:T(8,128)(2,1)} async-done(((bf16[192,2560]{1,0:T(8,128)(2,1)}), bf16[192,2560]{1,0:T(8,128)(2,1)}) %all-reduce.2.cloned.1.call-update) | async-done | bytes 983056 | tf_op jit(solution)/shard_map/psum | solution.py:134
  82.0 1.7 add_convert_fusion
  84.0 0.3 fusion.15
  84.3 4.0 broadcast_in_dim.72
  88.3 10.2 %reshape.347 = bf16[1152,2560]{1,0:T(8,128)(2,1)} reshape(bf16[192,6,2560]{2,1,0:T(8,128)(2,1)} %broadcast_in_dim.72) | data formatting | bytes 11796480 | tf_op jit(solution)/shard_map/reshape | solution.py:75
  98.5 17.2 %scatter_custom_fusion = bf16[1456,2560]{1,0:T(8,128)(2,1)} fusion(s32[1152]{0:T(1024)S(1)} %fusion.48, bf16[1152,2560]{1,0:T(8,128)(2,1)} %reshape.347, bf16[]{:T(256)} %constant.73.clone.1), kind=kCustom, calls=%fused_computation.18 | custom fusion | bytes 7455232 | tf_op jit(solution)/shard_map/scatter | solution.py:79
  115.7 6.3 %reshape.314 = bf16[2,8,91,2560]{3,2,1,0:T(8,128)(2,1)} reshape(bf16[1456,2560]{1,0:T(8,128)(2,1)} %scatter_custom_fusion) | data formatting | bytes 14909440 | tf_op jit(solution)/shard_map/reshape | solution.py:80
  121.9 27.5 %copy.66 = bf16[2,8,91,2560]{3,0,2,1:T(2,128)(2,1)S(1)} copy(bf16[2,8,91,2560]{3,2,1,0:T(8,128)(2,1)} %reshape.314) | data formatting | bytes 14909440 | tf_op jit(solution)/shard_map/reshape | solution.py:80
  149.4 87.5 %all_to_all.10 = bf16[2,8,91,2560]{3,0,2,1:T(2,128)(2,1)S(1)} all-to-all(bf16[2,8,91,2560]{3,0,2,1:T(2,128)(2,1)S(1)} %copy.66), channel_id=1, replica_groups=mesh['req'=8,'tp'=4] {'req'}, dimensions={1} | all-to-all | bytes 14909440 | tf_op jit(solution)/shard_map/all_to_all | solution.py:142
  236.9 9.0 %fusion = f32[2,728,2,384]{3,1,2,0:T(8,128)S(1)} fusion(bf16[2,2560,2,384]{3,2,1,0:T(2,128)(2,1)} %param.30, bf16[2,728,2560,1]{2,0,1,3:T(2,128)(2,1)S(1)} %bitcast.150), kind=kOutput, calls=%fused_computation.4 | convolution fusion | flops 5725224960 | bytes 19791872 | tf_op jit(solution)/shard_map/emd,edcf->emcf/dot_general | solution.py:144
  245.9 6.1 %convolution_convert_fusion = bf16[2,728,2560]{2,1,0:T(8,128)(2,1)} fusion(bf16[2,384,2560]{2,1,0:T(8,128)(2,1)S(1)} %copy-done.9, f32[2,728,2,384]{3,1,2,0:T(8,128)S(1)} %fusion), kind=kOutput, calls=%fused_computation.7 | convolution fusion | flops 2869694464 | bytes 15859712 | tf_op jit(solution)/shard_map/emf,efd->emd/dot_general | solution.py:149
  252.0 20.1 %copy.85 = bf16[2,728,2560]{1,0,2:T(2,128)(2,1)} copy(bf16[2,728,2560]{2,1,0:T(8,128)(2,1)} %convolution_convert_fusion) | data formatting | bytes 14909440
  272.1 18.3 %reshape.365 = bf16[2560,1456]{1,0:T(8,128)(2,1)} reshape(bf16[2560,2,728]{2,1,0:T(2,128)(2,1)} %bitcast.148) | data formatting | bytes 14909440
  290.5 0.3 reduce-scatter.7.cloned.1.call-start
  290.8 3.2 fusion.4
  294.0 0.7 convolution_convert_fusion.1
  294.7 1.4 copy.83
  296.1 128.2 %reduce-scatter.9.cloned.1.call-done = bf16[640,1456]{1,0:T(8,128)(2,1)} async-done(((bf16[2560,1456]{1,0:T(8,128)(2,1)}), bf16[640,1456]{1,0:T(8,128)(2,1)}) %reduce-scatter.9.cloned.1.call-update) | async-done | bytes 1863696
  424.4 5.2 %reshape.366 = bf16[640,2,728]{2,1,0:T(2,128)(2,1)S(1)} reshape(bf16[640,1456]{1,0:T(8,128)(2,1)} %reduce-scatter.9.cloned.1.call-done) | data formatting | bytes 3727360
  429.5 5.0 %copy.82 = bf16[2,728,640]{2,0,1:T(2,128)(2,1)} copy(bf16[2,728,640]{1,0,2:T(2,128)(2,1)S(1)} %bitcast.149) | data formatting | bytes 3727360 | tf_op jit(solution)/shard_map/reshape | solution.py:154
  434.5 3.8 all-to-all-start.1
  438.3 1.5 convert_element_type.77
  439.8 1.8 fusion.14
  441.7 0.8 copy.72
  442.4 16.1 %reduce-scatter.7.cloned.1.call-done = bf16[640,192]{1,0:T(8,128)(2,1)} async-done(((bf16[2560,192]{1,0:T(8,128)(2,1)}), bf16[640,192]{1,0:T(8,128)(2,1)}) %reduce-scatter.7.cloned.1.call-update) | async-done | bytes 245776
  458.5 1.1 copy.84
  459.7 2.7 all-to-all-done.1
  462.4 1.5 copy.71
  463.9 1.8 reshape.317
  465.8 4.8 gather_fusion.2
  470.6 4.0 reshape.318
  474.5 3.4 multiply_reduce_fusion
  477.9 1.8 add_convert_fusion.1
  (58 shorter events, 3.2 us)
Async XLA Ops:
  6.5 20.8 %copy-start = (bf16[640,2560]{1,0:T(8,128)(2,1)S(1)}, bf16[640,2560]{1,0:T(8,128)(2,1)}, u32[]{:S(2)}) copy-start(bf16[640,2560]{1,0:T(8,128)(2,1)} %param.26) | copy-start | bytes 9830404
  6.5 75.4 %all-reduce.2.cloned.1.call-start = ((), (), s32[]{:S(2)}) async-start(), calls=%async_computation.4 | async-start | bytes 1966080 | tf_op jit(solution)/shard_map/psum | solution.py:134
  11.9 5.6 %copy-start.6 = (bf16[192,128]{1,0:T(8,128)(2,1)S(1)}, bf16[192,128]{1,0:T(8,128)(2,1)}, u32[]{:S(2)}) copy-start(bf16[192,128]{1,0:T(8,128)(2,1)} %param.18) | copy-start | bytes 147460
  15.4 2.2 copy-start.3
  17.6 1.9 copy-start.2
  18.0 2.4 copy-start.4
  23.4 3.5 copy-start.5
  23.4 3.5 copy-start.12
  26.9 2.6 copy-start.7
  29.3 54.7 %copy-start.8 = (f32[2560]{0:T(1024)S(1)}, f32[2560]{0:T(1024)}, u32[]{:S(2)}) copy-start(f32[2560]{0:T(1024)} %param.27) | copy-start | bytes 30724
  29.3 395.0 %reduce-scatter.9.cloned.1.call-start = ((), (), s32[]{:S(2)}) async-start(), calls=%async_computation.6 | async-start | bytes 9830400
  236.9 9.0 %copy-start.9 = (bf16[2,384,2560]{2,1,0:T(8,128)(2,1)S(1)}, bf16[2,384,2560]{2,1,0:T(8,128)(2,1)}, u32[]{:S(2)}) copy-start(bf16[2,384,2560]{2,1,0:T(8,128)(2,1)} %param.31) | copy-start | bytes 11796484
  290.5 168.1 %reduce-scatter.7.cloned.1.call-start = ((), (), s32[]{:S(2)}) async-start(), calls=%async_computation.5 | async-start | bytes 1638400
  290.8 3.2 copy-start.10
  434.5 5.3 %copy-start.11 = (f32[2560,16]{0,1:T(8,128)S(1)}, f32[2560,16]{0,1:T(8,128)}, u32[]{:S(2)}) copy-start(f32[2560,16]{0,1:T(8,128)} %param.28) | copy-start | bytes 491524
  434.5 27.9 %all-to-all-start.1 = ((bf16[2,8,91,640]{3,0,2,1:T(2,128)(2,1)}), bf16[2,8,91,640]{3,0,2,1:T(2,128)(2,1)S(1)}, u32[]{:S(2)}, u32[]{:S(2)}) async-start(bf16[2,8,91,640]{3,0,2,1:T(2,128)(2,1)} %bitcast.151), calls=%async_computation.1 | async-start | bytes 3727360 | tf_op jit(solution)/shard_map/all_to_all | solution.py:155
  470.6 9.1 %copy-start.1 = (bf16[640,2560]{1,0:T(8,128)(2,1)S(1)}, bf16[640,2560]{1,0:T(8,128)(2,1)}, u32[]{:S(2)}) copy-start(bf16[640,2560]{1,0:T(8,128)(2,1)} %param.26) | copy-start | bytes 9830404
Sparse Core Ops, SparseCore 0:
  29.4 52.4 all-reduce.1
  290.6 133.7 reduce-scatter.8
  426.8 31.7 reduce-scatter.6
where the time goes:
time: 488 us; the launch traced here: 486 us
  waiting for transfers between devices  194 us (40%)
  local copies, waits for them, and re-layouts  140 us (29%)
  blocking collectives  87.5 us (18%)
  matrix products  31.1 us (6%)
  other arithmetic  16.7 us (3%)
  between operations  13.5 us (3%)
    unnamed x5, waiting for transfers between devices  144 us
    all_to_all x1, blocking collectives, shards(): lax.all_to_all(outbox, 'req', split_axis=1, concat_axis=1, tiled=True)  87.5 us
    unnamed x32, local copies, waits for them, and re-layouts  47.7 us
    psum x1, waiting for transfers between devices, shards(): lax.psum(attn_terms.astype(jnp.bfloat16), 'tp').astype(jnp.float32)  46.5 us
    reshape x2, local copies, waits for them, and re-layouts, fill_outbox(): return outbox.reshape(lead_shape + (row_values.shape[1],))  33.8 us
    scatter x1, local copies, waits for them, and re-layouts, fill_outbox(): outbox = outbox.at[slot_index].set(repeated)  17.2 us
    reshape x1, local copies, waits for them, and re-layouts, fill_outbox(): repeated = jnp.repeat(row_values, top_count, axis=0)  10.2 us
  transfers between devices with their start and end apart: 4, of which 4 were waited for; matrix products, arithmetic and copies ran while one was open for 5% of the time, Pallas kernels for 0%

commit v1 on v0

--- a/solution.py
+++ b/solution.py
@@ -60,26 +60,6 @@
     return mixed.astype(jnp.bfloat16).reshape(queries.shape[0], queries.shape[1], -1)
 
 
-def place_rows(routes, experts_local, groups, capacity):
-    flat_expert = routes.reshape(-1)
-    expert_ids = jnp.arange(experts_local * groups, dtype=jnp.int32)
-    onehot = (flat_expert[:, None] == expert_ids[None, :]).astype(jnp.int32)
-    earlier = jnp.cumsum(onehot, axis=0) - onehot
-    rank = jnp.sum(earlier * onehot, axis=1)
-    owner = flat_expert // experts_local
-    local_expert = flat_expert % experts_local
-    return (local_expert * groups + owner) * capacity + rank
-
-
-def fill_outbox(row_values, slot_index, top_count, lead_shape):
-    repeated = jnp.repeat(row_values, top_count, axis=0)
-    outbox = jnp.zeros(
-        (lead_shape[0] * lead_shape[1] * lead_shape[2], row_values.shape[1]), row_values.dtype
-    )
-    outbox = outbox.at[slot_index].set(repeated)
-    return outbox.reshape(lead_shape + (row_values.shape[1],))
-
-
 def shards(
     queries,
     new_keys,
@@ -129,8 +109,18 @@
     top_count = routes.shape[1]
     expert_count = experts_local * groups
     capacity = max(10 * requests, row_count * top_count * 5 // (4 * expert_count) + 1)
-    slot_index = place_rows(routes, experts_local, groups, capacity)
-    lead_shape = (experts_local, groups, capacity)
+    capacity = -(-capacity // 16) * 16
+    slot_count = expert_count * capacity
+
+    flat_expert = routes.reshape(-1)
+    expert_ids = jnp.arange(expert_count, dtype=jnp.int32)
+    onehot = (flat_expert[:, None] == expert_ids[None, :]).astype(jnp.int32)
+    earlier = jnp.cumsum(onehot, axis=0) - onehot
+    rank = jnp.sum(earlier * onehot, axis=1)
+    slot = (flat_expert * capacity + rank).reshape(row_count, top_count)
+    slot_ids = jnp.arange(slot_count, dtype=jnp.int32)
+    hit = slot[:, :, None] == slot_ids[None, None, :]
+
     attn_out = lax.psum(attn_terms.astype(jnp.bfloat16), "tp").astype(jnp.float32)
     hidden = rounded(residual.astype(jnp.float32) + attn_out)
     rstd = lax.rsqrt(jnp.mean(hidden * hidden, axis=1, keepdims=True) + EPSILON)
@@ -138,40 +128,48 @@
     logits = jnp.dot(normed, router_weight, precision=lax.Precision.HIGHEST)
     normed_bf = normed.astype(jnp.bfloat16)
     hidden_part = lax.dynamic_slice_in_dim(hidden, column, part_width, 1)
-    outbox = fill_outbox(normed_bf, slot_index, top_count, lead_shape)
-    arrived = lax.all_to_all(outbox, "req", split_axis=1, concat_axis=1, tiled=True)
-    arrived = arrived.reshape(experts_local, groups * capacity, model_width)
-    gate_up = jnp.einsum(
-        "emd,edcf->emcf", arrived, expert_gate_up, preferred_element_type=jnp.float32
-    )
-    act = (jax.nn.silu(gate_up[:, :, 0]) * gate_up[:, :, 1]).astype(jnp.bfloat16)
-    partial_value = rounded(
-        jnp.einsum("emf,efd->emd", act, expert_down, preferred_element_type=jnp.float32)
-    )
-    summed = lax.psum_scatter(
-        partial_value.astype(jnp.bfloat16), "tp", scatter_dimension=2, tiled=True
-    )
-    outputs = summed.reshape(experts_local, groups, capacity, part_width)
-    returned = lax.all_to_all(outputs, "req", split_axis=1, concat_axis=1, tiled=True).reshape(
-        -1, part_width
-    )
-    picked = returned[slot_index].astype(jnp.float32).reshape(row_count, top_count, part_width)
-    expert_ids = jnp.arange(expert_count, dtype=jnp.int32)
+
+    dispatch = jnp.any(hit, axis=1).astype(jnp.bfloat16)
+    outbox = jnp.einsum(
+        "ts,td->sd", dispatch, normed_bf, preferred_element_type=jnp.float32
+    ).astype(jnp.bfloat16)
+    outbox = outbox.reshape(groups, experts_local * capacity, model_width)
+    arrived = lax.all_to_all(outbox, "req", split_axis=0, concat_axis=0, tiled=True)
+    arrived = arrived.reshape(groups, experts_local, capacity, model_width)
+    results = []
+    for expert in range(experts_local):
+        rows = arrived[:, expert].reshape(groups * capacity, model_width)
+        gate_up = jnp.einsum(
+            "md,dcf->mcf", rows, expert_gate_up[expert], preferred_element_type=jnp.float32
+        )
+        act = (jax.nn.silu(gate_up[:, 0]) * gate_up[:, 1]).astype(jnp.bfloat16)
+        partial_value = jnp.dot(act, expert_down[expert], preferred_element_type=jnp.float32)
+        results.append(partial_value.astype(jnp.bfloat16).reshape(groups, capacity, model_width))
+    outputs = jnp.stack(results, axis=1).reshape(groups, experts_local * capacity, model_width)
+    returned = lax.all_to_all(outputs, "req", split_axis=0, concat_axis=0, tiled=True)
+    returned = returned.reshape(slot_count, model_width)
+
     chosen = jnp.sum(
         jnp.where(routes[:, :, None] == expert_ids[None, None, :], logits[:, None, :], 0.0), axis=-1
     )
     gate_values = jax.nn.sigmoid(chosen)
     gate_values = gate_values / jnp.sum(gate_values, axis=1, keepdims=True)
-    routed = jnp.sum(picked * gate_values[:, :, None], axis=1)
+    weights = jnp.sum(jnp.where(hit, gate_values[:, :, None], 0.0), axis=1)
+    weights_hi = weights.astype(jnp.bfloat16)
+    weights_lo = (weights - weights_hi.astype(jnp.float32)).astype(jnp.bfloat16)
+    routed = jnp.dot(weights_hi, returned, preferred_element_type=jnp.float32) + jnp.dot(
+        weights_lo, returned, preferred_element_type=jnp.float32
+    )
+
     shared_gu = jnp.einsum(
         "td,dcf->tcf", normed_bf, shared_gate_up, preferred_element_type=jnp.float32
     )
     shared_act = (jax.nn.silu(shared_gu[:, 0]) * shared_gu[:, 1]).astype(jnp.bfloat16)
     shared_terms = jnp.dot(shared_act, shared_down, preferred_element_type=jnp.float32)
-    shared_out = lax.psum_scatter(
-        shared_terms.astype(jnp.bfloat16), "tp", scatter_dimension=1, tiled=True
+    summed = lax.psum_scatter(
+        (shared_terms + routed).astype(jnp.bfloat16), "tp", scatter_dimension=1, tiled=True
     ).astype(jnp.float32)
-    return (hidden_part + shared_out + routed).astype(jnp.bfloat16)
+    return (hidden_part + summed).astype(jnp.bfloat16)
 
 
 def solution(mesh):

time: 488 us -> 353 us (0.72)
  local copies, waits for them, and re-layouts: 140 us -> 26.6 us
  blocking collectives: 87.5 us -> 0 us
  waiting for transfers between devices: 194 us -> 233 us
  matrix products: 31.1 us -> 46.1 us
  starting transfers between devices: 4.32 us -> 10.5 us
  other arithmetic: 16.7 us -> 22.4 us
    all_to_all x1 -> x2, waiting for transfers between devices: 2.72 us -> 161 us  [the longest x1 81.1 us: shards(): lax.all_to_all(outputs, 'req', split_axis=0, concat_axis=0, tiled=True)]
    unnamed x5 -> x3, waiting for transfers between devices: 144 us -> 26.2 us
    all_to_all x1 -> x0, blocking collectives: 87.5 us -> none  [shards(): lax.all_to_all(outbox, 'req', split_axis=1, concat_axis=1, tiled=True)]
    reshape x6 -> x0, local copies, waits for them, and re-layouts: 50.9 us -> none  [the longest x2 33.8 us: fill_outbox(): return outbox.reshape(lead_shape + (row_values.shape[1],))]
    unnamed x32 -> x37, local copies, waits for them, and re-layouts: 47.7 us -> 5.75 us
    scatter x1 -> x0, local copies, waits for them, and re-layouts: 17.2 us -> none  [fill_outbox(): outbox = outbox.at[slot_index].set(repeated)]
    dot_general x2 -> x7, matrix products: 15.1 us -> 28.4 us  [the longest x2 6.44 us: shards(): jnp.dot(act, expert_down[expert], preferred_element_type=jnp.float32)]
    slice x1 -> x3, local copies, waits for them, and re-layouts: 0.43 us -> 12.4 us  [the longest x1 8.13 us: shards(): expert_gate_up[expert]]
  transfers between devices with their start and end apart: 4 -> 4, of which waited for: 4 -> 4; matrix products, arithmetic and copies ran while one was open for 5% -> 7% of each run, Pallas kernels for 0% -> 0%
where the time goes in v1:
time: 353 us
  waiting for transfers between devices  233 us (66%)
  matrix products  46.1 us (13%)
  local copies, waits for them, and re-layouts  26.6 us (8%)
  other arithmetic  22.4 us (6%)
  between operations  13.9 us (4%)
  starting transfers between devices  10.5 us (3%)
    all_to_all x1, waiting for transfers between devices, shards(): lax.all_to_all(outputs, 'req', split_axis=0, concat_axis=0, tiled=True)  81.1 us
    all_to_all x1, waiting for transfers between devices, shards(): lax.all_to_all(outbox, 'req', split_axis=0, concat_axis=0, tiled=True)  80.1 us
    psum x1, waiting for transfers between devices, shards(): lax.psum(attn_terms.astype(jnp.bfloat16), 'tp').astype(jnp.float32)  45.5 us
    unnamed x3, waiting for transfers between devices  26.2 us
    slice x1, local copies, waits for them, and re-layouts, shards(): expert_gate_up[expert]  8.13 us
  transfers between devices with their start and end apart: 4, of which 4 were waited for; matrix products, arithmetic and copies ran while one was open for 7% of the time, Pallas kernels for 0%

profile of v1, /device:TPU:0, one launch (start us, length us, event | category | flops | bytes accessed | tf_op | source)
XLA Modules:
  0.0 352.5 jit_solution(10721387964018037830)
XLA Ops:
  6.6 0.8 compare_select_fusion
  7.5 0.8 iota_compare_fusion.6
  8.3 2.0 reshape.185
  10.2 1.0 convolution_minimum_fusion.5
  11.5 0.2 convolution_minimum_fusion.3
  11.7 0.2 convolution_minimum_fusion.2
  11.9 0.2 convolution_minimum_fusion.1
  12.2 0.2 fusion.25
  12.5 2.9 gather_fusion.1
  15.4 2.1 bitcast_reduce_fusion
  17.6 0.4 fusion.65
  18.0 1.4 copy-done.2
  19.4 1.0 fusion.7
  20.5 2.9 gather_fusion
  23.4 3.5 fusion.10
  26.9 0.3 fusion.24
  27.4 1.9 convolution_convert_fusion.3
  29.7 4.5 %reduce-window.6 = s32[16,9,128]{2,1,0:T(8,128)S(1)} reduce-window(s32[16,9,128]{2,1,0:T(8,128)S(1)} %fusion.50, s32[]{:T(128)} %constant.20.clone.1), window={size=1x1x128 pad=0_0x0_0x127_0}, to_apply=%region_6.7 | reduce-window | flops 2340864 | bytes 147460 | tf_op jit(solution)/shard_map/reduce-window
  34.3 0.4 slice_reduce_fusion
  35.3 1.2 fusion
  36.4 45.5 %all-reduce.2.cloned.1.call-done = bf16[192,2560]{1,0:T(8,128)(2,1)} async-done(((bf16[192,2560]{1,0:T(8,128)(2,1)}), bf16[192,2560]{1,0:T(8,128)(2,1)}) %all-reduce.2.cloned.1.call-update) | async-done | bytes 983056 | tf_op jit(solution)/shard_map/psum | solution.py:124
  82.0 1.7 add_convert_fusion
  83.7 0.3 multiply_reduce_fusion
  84.0 5.5 %convolution_convert_fusion = bf16[1536,2560]{1,0:T(8,128)(2,1)} fusion(pred[192,1536]{1,0:T(8,128)(4,1)S(1)} %fusion, bf16[192,2560]{1,0:T(8,128)(2,1)S(1)} %add_convert_fusion, f32[2560]{0:T(1024)S(1)} %copy-done.13, f32[192]{0:T(256)S(1)} %add_rsqrt_fusion), kind=kOutput, calls=%fused_computation.2 | convolution fusion | flops 1515847680 | bytes 9153280 | tf_op jit(solution)/shard_map/ts,td->sd/dot_general | solution.py:133
  89.5 5.1 %all-to-all-start = ((bf16[8,192,2560]{2,1,0:T(8,128)(2,1)}), bf16[8,192,2560]{2,1,0:T(8,128)(2,1)}, u32[]{:S(2)}, u32[]{:S(2)}) async-start(bf16[8,192,2560]{2,1,0:T(8,128)(2,1)} %bitcast.170), calls=%async_computation | async-start | bytes 15728640 | tf_op jit(solution)/shard_map/all_to_all | solution.py:137
  94.6 8.1 %fusion.63 = (bf16[1,2560,2,384]{3,2,1,0:T(2,128)(2,1)}, bf16[1,2560,2,384]{3,2,1,0:T(2,128)(2,1)}) fusion(bf16[2,2560,2,384]{3,2,1,0:T(2,128)(2,1)} %param.30), kind=kLoop, calls=%fused_computation.110 | loop fusion | bytes 15728640 | tf_op jit(solution)/shard_map/slice | solution.py:143
  102.7 80.1 %all-to-all-done = bf16[8,192,2560]{2,1,0:T(8,128)(2,1)} async-done(((bf16[8,192,2560]{2,1,0:T(8,128)(2,1)}), bf16[8,192,2560]{2,1,0:T(8,128)(2,1)}, u32[]{:S(2)}, u32[]{:S(2)}) %all-to-all-start) | async-done | bytes 7864352 | tf_op jit(solution)/shard_map/all_to_all | solution.py:137
  182.9 3.8 %fusion.64 = (bf16[8,1,96,2560]{3,2,1,0:T(8,128)(2,1)S(1)}, bf16[8,1,96,2560]{3,2,1,0:T(8,128)(2,1)S(1)}) fusion(bf16[8,2,96,2560]{3,2,1,0:T(8,128)(2,1)} %bitcast.26), kind=kLoop, calls=%fused_computation.111 | loop fusion | bytes 15728640 | tf_op jit(solution)/shard_map/slice | solution.py:141
  186.7 0.6 copy-done.5
  187.3 3.2 fusion.2
  190.5 2.2 convolution_convert_fusion.2
  192.8 3.2 fusion.1
  196.0 4.2 %convolution_convert_fusion.1 = bf16[768,2560]{1,0:T(8,128)(2,1)} fusion(bf16[2,384,2560]{2,1,0:T(8,128)(2,1)S(1)} %copy-done.14, f32[768,2,384]{2,0,1:T(8,128)S(1)} %fusion.1), kind=kOutput, calls=%fused_computation.7 | convolution fusion | flops 1513684992 | bytes 8257536 | tf_op jit(solution)/shard_map/dot_general | solution.py:146
  200.2 5.9 %pad_maximum_fusion = bf16[8,2,96,2560]{3,2,1,0:T(8,128)(2,1)} fusion(bf16[8,1,96,2560]{3,2,1,0:T(8,128)(2,1)} %bitcast.177, bf16[8,1,96,2560]{3,2,1,0:T(8,128)(2,1)S(1)} %bitcast.175), kind=kLoop, calls=%fused_computation.3 | loop fusion | flops 3932160 | bytes 15728640 | tf_op jit(solution)/shard_map/stack | solution.py:148
  206.1 5.1 %all-to-all-start.1 = ((bf16[8,192,2560]{2,1,0:T(8,128)(2,1)}), bf16[8,192,2560]{2,1,0:T(8,128)(2,1)}, u32[]{:S(2)}, u32[]{:S(2)}) async-start(bf16[8,192,2560]{2,1,0:T(8,128)(2,1)} %bitcast.171), calls=%async_computation.1 | async-start | bytes 15728640 | tf_op jit(solution)/shard_map/all_to_all | solution.py:149
  211.3 0.3 reduce-scatter.4.cloned.1.call-start
  211.6 1.8 fusion.15
  213.4 1.2 select_reduce_fusion
  214.6 4.0 %fusion.4 = f32[192,2,384]{2,0,1:T(8,128)} fusion(bf16[2560,2,384]{2,1,0:T(2,128)(2,1)} %param.32, bf16[192,2560]{1,0:T(8,128)(2,1)S(1)} %add_convert_fusion, f32[2560]{0:T(1024)S(1)} %copy-done.13, f32[192]{0:T(256)S(1)} %add_rsqrt_fusion), kind=kOutput, calls=%fused_computation.18 | convolution fusion | flops 756940800 | bytes 5516032 | tf_op jit(solution)/shard_map/td,dcf->tcf/dot_general | solution.py:164
  218.6 81.1 %all-to-all-done.1 = bf16[8,192,2560]{2,1,0:T(8,128)(2,1)} async-done(((bf16[8,192,2560]{2,1,0:T(8,128)(2,1)}), bf16[8,192,2560]{2,1,0:T(8,128)(2,1)}, u32[]{:S(2)}, u32[]{:S(2)}) %all-to-all-start.1) | async-done | bytes 7864352 | tf_op jit(solution)/shard_map/all_to_all | solution.py:149
  299.7 4.9 %fusion.37 = f32[192,2560]{1,0:T(8,128)S(1)} fusion(bf16[1536,2560]{1,0:T(8,128)(2,1)} %bitcast.42, f32[192,1536]{1,0:T(8,128)S(1)} %select_reduce_fusion), kind=kOutput, calls=%fused_computation.71 | convolution fusion | flops 1510244352 | bytes 11010048 | tf_op jit(solution)/shard_map/dot_general | solution.py:160
  304.7 5.1 %convolution_add_fusion.1 = f32[192,2560]{1,0:T(8,128)S(1)} fusion(f32[192,2560]{1,0:T(8,128)S(1)} %fusion.37, bf16[1536,2560]{1,0:T(8,128)(2,1)} %bitcast.42, f32[192,1536]{1,0:T(8,128)S(1)} %select_reduce_fusion), kind=kOutput, calls=%fused_computation.21 | convolution fusion | flops 1511620608 | bytes 12976128 | tf_op jit(solution)/shard_map/dot_general | solution.py:160
  309.8 1.6 fusion.6
  311.4 2.4 copy.103
  313.8 2.7 convert_element_type.93
  316.5 26.2 %reduce-scatter.4.cloned.1.call-done = bf16[640,192]{1,0:T(8,128)(2,1)} async-done(((bf16[2560,192]{1,0:T(8,128)(2,1)}), bf16[640,192]{1,0:T(8,128)(2,1)}) %reduce-scatter.4.cloned.1.call-update) | async-done | bytes 245776
  342.7 1.1 copy.104
  343.9 1.8 add_convert_fusion.1
  (58 shorter events, 1.8 us)
Async XLA Ops:
  6.5 20.8 %copy-start = (bf16[640,2560]{1,0:T(8,128)(2,1)S(1)}, bf16[640,2560]{1,0:T(8,128)(2,1)}, u32[]{:S(2)}) copy-start(bf16[640,2560]{1,0:T(8,128)(2,1)} %param.26) | copy-start | bytes 9830404
  6.5 75.4 %all-reduce.2.cloned.1.call-start = ((), (), s32[]{:S(2)}) async-start(), calls=%async_computation.3 | async-start | bytes 1966080 | tf_op jit(solution)/shard_map/psum | solution.py:124
  11.9 5.6 %copy-start.12 = (bf16[192,128]{1,0:T(8,128)(2,1)S(1)}, bf16[192,128]{1,0:T(8,128)(2,1)}, u32[]{:S(2)}) copy-start(bf16[192,128]{1,0:T(8,128)(2,1)} %param.18) | copy-start | bytes 147460
  15.4 2.2 copy-start.6
  17.6 1.9 copy-start.2
  18.0 2.4 copy-start.7
  23.4 3.5 copy-start.8
  23.4 3.5 copy-start.16
  26.9 2.4 copy-start.11
  29.3 54.7 %copy-start.13 = (f32[2560]{0:T(1024)S(1)}, f32[2560]{0:T(1024)}, u32[]{:S(2)}) copy-start(f32[2560]{0:T(1024)} %param.27) | copy-start | bytes 30724
  83.7 130.9 %copy-start.3 = (bf16[192,2560]{1,0:T(8,128)(2,1)}, bf16[192,2560]{1,0:T(8,128)(2,1)S(1)}, u32[]{:S(2)}) copy-start(bf16[192,2560]{1,0:T(8,128)(2,1)S(1)} %add_convert_fusion) | copy-start | bytes 2949124
  89.5 93.4 %all-to-all-start = ((bf16[8,192,2560]{2,1,0:T(8,128)(2,1)}), bf16[8,192,2560]{2,1,0:T(8,128)(2,1)}, u32[]{:S(2)}, u32[]{:S(2)}) async-start(bf16[8,192,2560]{2,1,0:T(8,128)(2,1)} %bitcast.170), calls=%async_computation | async-start | bytes 15728640 | tf_op jit(solution)/shard_map/all_to_all | solution.py:137
  182.9 4.4 %copy-start.5 = (bf16[1,2560,2,384]{3,2,1,0:T(2,128)(2,1)S(1)}, bf16[1,2560,2,384]{3,2,1,0:T(2,128)(2,1)}, u32[]{:S(2)}) copy-start(bf16[1,2560,2,384]{3,2,1,0:T(2,128)(2,1)} %get-tuple-element.5) | copy-start | bytes 11796484
  187.3 3.2 copy-start.14
  190.5 2.2 copy-start.4
  206.1 5.4 %copy-start.15 = (f32[2560,16]{0,1:T(8,128)S(1)}, f32[2560,16]{0,1:T(8,128)}, u32[]{:S(2)}) copy-start(f32[2560,16]{0,1:T(8,128)} %param.28) | copy-start | bytes 491524
  206.1 93.6 %all-to-all-start.1 = ((bf16[8,192,2560]{2,1,0:T(8,128)(2,1)}), bf16[8,192,2560]{2,1,0:T(8,128)(2,1)}, u32[]{:S(2)}, u32[]{:S(2)}) async-start(bf16[8,192,2560]{2,1,0:T(8,128)(2,1)} %bitcast.171), calls=%async_computation.1 | async-start | bytes 15728640 | tf_op jit(solution)/shard_map/all_to_all | solution.py:149
  211.3 131.5 %reduce-scatter.4.cloned.1.call-start = ((), (), s32[]{:S(2)}) async-start(), calls=%async_computation.4 | async-start | bytes 1638400
  304.7 5.1 %copy-start.9 = (bf16[384,2560]{1,0:T(8,128)(2,1)S(1)}, bf16[384,2560]{1,0:T(8,128)(2,1)}, u32[]{:S(2)}) copy-start(bf16[384,2560]{1,0:T(8,128)(2,1)} %param.33) | copy-start | bytes 5898244
  304.7 5.1 %copy-start.10 = (f32[192,2,384]{2,0,1:T(8,128)S(1)}, f32[192,2,384]{2,0,1:T(8,128)}, u32[]{:S(2)}) copy-start(f32[192,2,384]{2,0,1:T(8,128)} %fusion.4) | copy-start | bytes 1769476
  309.8 35.9 %copy-start.1 = (bf16[640,2560]{1,0:T(8,128)(2,1)S(1)}, bf16[640,2560]{1,0:T(8,128)(2,1)}, u32[]{:S(2)}) copy-start(bf16[640,2560]{1,0:T(8,128)(2,1)} %param.26) | copy-start | bytes 9830404
Sparse Core Ops, SparseCore 0:
  29.4 52.4 all-reduce.1
  314.0 28.7 reduce-scatter.3

commit v2 on v1

--- a/solution.py
+++ b/solution.py
@@ -121,33 +121,37 @@
     slot_ids = jnp.arange(slot_count, dtype=jnp.int32)
     hit = slot[:, :, None] == slot_ids[None, None, :]
 
-    attn_out = lax.psum(attn_terms.astype(jnp.bfloat16), "tp").astype(jnp.float32)
-    hidden = rounded(residual.astype(jnp.float32) + attn_out)
+    attn_blocks = attn_terms.astype(jnp.bfloat16).reshape(row_count, tp_count, part_width)
+    attn_blocks = lax.all_to_all(
+        attn_blocks.transpose(1, 0, 2), "tp", split_axis=0, concat_axis=0, tiled=True
+    )
+    attn_part = jnp.sum(attn_blocks.astype(jnp.float32), axis=0)
+    residual_part = lax.dynamic_slice_in_dim(residual, column, part_width, 1)
+    hidden_part_bf = (residual_part.astype(jnp.float32) + attn_part).astype(jnp.bfloat16)
+    hidden_bf = lax.all_gather(hidden_part_bf[None], "tp", axis=0, tiled=True)
+    hidden = hidden_bf.transpose(1, 0, 2).reshape(row_count, model_width).astype(jnp.float32)
     rstd = lax.rsqrt(jnp.mean(hidden * hidden, axis=1, keepdims=True) + EPSILON)
     normed = hidden * rstd * norm_gain
     logits = jnp.dot(normed, router_weight, precision=lax.Precision.HIGHEST)
     normed_bf = normed.astype(jnp.bfloat16)
-    hidden_part = lax.dynamic_slice_in_dim(hidden, column, part_width, 1)
+    hidden_part = hidden_part_bf.astype(jnp.float32)
 
     dispatch = jnp.any(hit, axis=1).astype(jnp.bfloat16)
-    outbox = jnp.einsum(
-        "ts,td->sd", dispatch, normed_bf, preferred_element_type=jnp.float32
-    ).astype(jnp.bfloat16)
-    outbox = outbox.reshape(groups, experts_local * capacity, model_width)
-    arrived = lax.all_to_all(outbox, "req", split_axis=0, concat_axis=0, tiled=True)
-    arrived = arrived.reshape(groups, experts_local, capacity, model_width)
-    results = []
+    dispatch = dispatch.reshape(row_count, groups, experts_local, capacity)
+    returns = []
     for expert in range(experts_local):
-        rows = arrived[:, expert].reshape(groups * capacity, model_width)
+        outbox = jnp.einsum(
+            "tgc,td->gcd", dispatch[:, :, expert], normed_bf, preferred_element_type=jnp.float32
+        ).astype(jnp.bfloat16)
+        arrived = lax.all_to_all(outbox, "req", split_axis=0, concat_axis=0, tiled=True)
+        rows = arrived.reshape(groups * capacity, model_width)
         gate_up = jnp.einsum(
             "md,dcf->mcf", rows, expert_gate_up[expert], preferred_element_type=jnp.float32
         )
         act = (jax.nn.silu(gate_up[:, 0]) * gate_up[:, 1]).astype(jnp.bfloat16)
         partial_value = jnp.dot(act, expert_down[expert], preferred_element_type=jnp.float32)
-        results.append(partial_value.astype(jnp.bfloat16).reshape(groups, capacity, model_width))
-    outputs = jnp.stack(results, axis=1).reshape(groups, experts_local * capacity, model_width)
-    returned = lax.all_to_all(outputs, "req", split_axis=0, concat_axis=0, tiled=True)
-    returned = returned.reshape(slot_count, model_width)
+        outputs = partial_value.astype(jnp.bfloat16).reshape(groups, capacity, model_width)
+        returns.append(lax.all_to_all(outputs, "req", split_axis=0, concat_axis=0, tiled=True))
 
     chosen = jnp.sum(
         jnp.where(routes[:, :, None] == expert_ids[None, None, :], logits[:, None, :], 0.0), axis=-1
@@ -155,20 +159,25 @@
     gate_values = jax.nn.sigmoid(chosen)
     gate_values = gate_values / jnp.sum(gate_values, axis=1, keepdims=True)
     weights = jnp.sum(jnp.where(hit, gate_values[:, :, None], 0.0), axis=1)
+    weights = weights.reshape(row_count, groups, experts_local, capacity)
     weights_hi = weights.astype(jnp.bfloat16)
     weights_lo = (weights - weights_hi.astype(jnp.float32)).astype(jnp.bfloat16)
-    routed = jnp.dot(weights_hi, returned, preferred_element_type=jnp.float32) + jnp.dot(
-        weights_lo, returned, preferred_element_type=jnp.float32
-    )
+    routed = jnp.zeros((row_count, model_width), jnp.float32)
+    for expert in range(experts_local):
+        for split in (weights_hi, weights_lo):
+            routed = routed + jnp.einsum(
+                "tgc,gcd->td", split[:, :, expert], returns[expert],
+                preferred_element_type=jnp.float32,
+            )
 
     shared_gu = jnp.einsum(
         "td,dcf->tcf", normed_bf, shared_gate_up, preferred_element_type=jnp.float32
     )
     shared_act = (jax.nn.silu(shared_gu[:, 0]) * shared_gu[:, 1]).astype(jnp.bfloat16)
     shared_terms = jnp.dot(shared_act, shared_down, preferred_element_type=jnp.float32)
-    summed = lax.psum_scatter(
-        (shared_terms + routed).astype(jnp.bfloat16), "tp", scatter_dimension=1, tiled=True
-    ).astype(jnp.float32)
+    total = (shared_terms + routed).astype(jnp.bfloat16).reshape(row_count, tp_count, part_width)
+    total = lax.all_to_all(total.transpose(1, 0, 2), "tp", split_axis=0, concat_axis=0, tiled=True)
+    summed = jnp.sum(total.astype(jnp.float32), axis=0)
     return (hidden_part + summed).astype(jnp.bfloat16)
 
 

time: 353 us -> 314 us (0.89)
  waiting for transfers between devices: 233 us -> 150 us
  blocking collectives: 0 us -> 44.5 us
  starting transfers between devices: 10.5 us -> 24.9 us
  between operations: 13.9 us -> 0.6 us
  other arithmetic: 22.4 us -> 13.3 us
  matrix products: 46.1 us -> 55 us
    psum x1 -> x0, waiting for transfers between devices: 45.5 us -> none  [shards(): lax.psum(attn_terms.astype(jnp.bfloat16), 'tp').astype(jnp.float32)]
    unnamed x3 -> x0, waiting for transfers between devices: 26.2 us -> none
    all_to_all x0 -> x1, blocking collectives: none -> 24.9 us  [shards(): lax.all_to_all(total.transpose(1, 0, 2), 'tp', split_axis=0, concat_axis=...]
    all_gather x0 -> x1, blocking collectives: none -> 19.6 us  [shards(): hidden_bf = lax.all_gather(hidden_part_bf[None], 'tp', axis=0, tiled=True)]
    all_to_all x1 -> x2, waiting for transfers between devices: 81.1 us -> 61.8 us  [shards(): lax.all_to_all(outputs, 'req', split_axis=0, concat_axis=0, tiled=True)]
    all_to_all x0 -> x1, waiting for transfers between devices: none -> 15.9 us  [shards(): lax.all_to_all(attn_blocks.transpose(1, 0, 2), 'tp', split_axis=0, concat...]
    all_to_all x1 -> x2, waiting for transfers between devices: 80.1 us -> 72.1 us  [shards(): lax.all_to_all(outbox, 'req', split_axis=0, concat_axis=0, tiled=True)]
    all_to_all x0 -> x1, starting transfers between devices: none -> 6.32 us  [shards(): lax.all_to_all(attn_blocks.transpose(1, 0, 2), 'tp', split_axis=0, concat...]
  transfers between devices with their start and end apart: 4 -> 5, of which waited for: 4 -> 5; matrix products, arithmetic and copies ran while one was open for 7% -> 19% of each run, Pallas kernels for 0% -> 0%
where the time goes in v2:
time: 314 us; the launch traced here: 312 us
  waiting for transfers between devices  150 us (48%)
  matrix products  55 us (18%)
  blocking collectives  44.5 us (14%)
  starting transfers between devices  24.9 us (8%)
  local copies, waits for them, and re-layouts  23.5 us (7%)
  other arithmetic  13.3 us (4%)
    all_to_all x2, waiting for transfers between devices, shards(): lax.all_to_all(outbox, 'req', split_axis=0, concat_axis=0, tiled=True)  72.1 us
    all_to_all x2, waiting for transfers between devices, shards(): lax.all_to_all(outputs, 'req', split_axis=0, concat_axis=0, tiled=True)  61.8 us
    all_to_all x1, blocking collectives, shards(): lax.all_to_all(total.transpose(1, 0, 2), 'tp', split_axis=0, concat_axis=...  24.9 us
    all_gather x1, blocking collectives, shards(): hidden_bf = lax.all_gather(hidden_part_bf[None], 'tp', axis=0, tiled=True)  19.6 us
    all_to_all x1, waiting for transfers between devices, shards(): lax.all_to_all(attn_blocks.transpose(1, 0, 2), 'tp', split_axis=0, concat...  15.9 us
    dot_general x4, matrix products, shards(): jnp.einsum('tgc,gcd->td', split[:, :, expert], returns[expert], preferred...  14.4 us
    dot_general x2, matrix products, shards(): jnp.einsum('md,dcf->mcf', rows, expert_gate_up[expert], preferred_element...  12.1 us
    all_to_all x2, starting transfers between devices, shards(): lax.all_to_all(outbox, 'req', split_axis=0, concat_axis=0, tiled=True)  9.34 us
  transfers between devices with their start and end apart: 5, of which 5 were waited for; matrix products, arithmetic and copies ran while one was open for 19% of the time, Pallas kernels for 0%

profile of v2, /device:TPU:0, one launch (start us, length us, event | category | flops | bytes accessed | tf_op | source)
XLA Modules:
  0.0 311.7 jit_solution(16282208259055026572)
XLA Ops:
  0.0 0.8 compare_select_fusion
  1.0 0.9 iota_compare_fusion.6
  1.9 2.9 gather_fusion
  4.8 2.9 gather_fusion.1
  7.7 1.0 reshape.220
  10.3 2.1 bitcast_reduce_fusion
  12.9 1.0 fusion.10
  14.0 1.3 fusion.16
  15.7 0.9 convolution_convert_fusion.4
  16.6 1.0 copy.155
  17.7 6.3 %all-to-all-start = ((bf16[4,192,640]{2,1,0:T(8,128)(2,1)}), bf16[4,192,640]{2,1,0:T(8,128)(2,1)S(1)}, u32[]{:S(2)}, u32[]{:S(2)}) async-start(bf16[4,192,640]{2,1,0:T(8,128)(2,1)} %bitcast.216), calls=%async_computation | async-start | bytes 1966080 | tf_op jit(solution)/shard_map/all_to_all | solution.py:125
  24.5 4.5 %reduce-window.6 = s32[16,9,128]{2,1,0:T(8,128)S(1)} reduce-window(s32[16,9,128]{2,1,0:T(8,128)S(1)} %fusion.54, s32[]{:T(128)} %constant.17.clone.1), window={size=1x1x128 pad=0_0x0_0x127_0}, to_apply=%region_6.7 | reduce-window | flops 2340864 | bytes 147460 | tf_op jit(solution)/shard_map/reduce-window
  30.0 1.2 fusion
  31.2 1.2 copy.106
  32.4 15.9 %all-to-all-done = bf16[4,192,640]{2,1,0:T(8,128)(2,1)S(1)} async-done(((bf16[4,192,640]{2,1,0:T(8,128)(2,1)}), bf16[4,192,640]{2,1,0:T(8,128)(2,1)S(1)}, u32[]{:S(2)}, u32[]{:S(2)}) %all-to-all-start) | async-done | bytes 983072 | tf_op jit(solution)/shard_map/all_to_all | solution.py:125
  48.5 1.0 add_convert_fusion.1
  49.5 19.6 %all-gather = bf16[768,640]{1,0:T(8,128)(2,1)S(1)} all-gather(bf16[192,640]{1,0:T(8,128)(2,1)S(1)} %add_convert_fusion.1), channel_id=2, replica_groups=mesh['req'=8,'tp'=4] {'tp'}, dimensions={0}, use_global_device_ids=true | all-gather | bytes 1228800 | tf_op jit(solution)/shard_map/all_gather | solution.py:131
  69.6 0.8 copy.108
  70.8 4.0 %convolution_convert_fusion = bf16[8,96,2560]{2,1,0:T(8,128)(2,1)} fusion(bf16[192,2560,1]{1,0,2:T(8,128)(2,1)S(1)} %reshape.265, pred[192,8,2,96]{0,3,2,1:T(32,128)(4,1)} %bitcast.229), kind=kOutput, calls=%fused_computation.5 | convolution fusion | flops 756940800 | bytes 5111808 | tf_op jit(solution)/shard_map/tgc,td->gcd/dot_general | solution.py:143
  74.7 4.8 %all-to-all-start.3 = ((bf16[8,96,2560]{2,1,0:T(8,128)(2,1)}), bf16[8,96,2560]{2,1,0:T(8,128)(2,1)}, u32[]{:S(2)}, u32[]{:S(2)}) async-start(bf16[8,96,2560]{2,1,0:T(8,128)(2,1)} %convolution_convert_fusion), calls=%async_computation.3 | async-start | bytes 7864320 | tf_op jit(solution)/shard_map/all_to_all | solution.py:146
  79.6 3.1 convolution_convert_fusion.1
  82.7 43.0 %all-to-all-done.3 = bf16[8,96,2560]{2,1,0:T(8,128)(2,1)} async-done(((bf16[8,96,2560]{2,1,0:T(8,128)(2,1)}), bf16[8,96,2560]{2,1,0:T(8,128)(2,1)}, u32[]{:S(2)}, u32[]{:S(2)}) %all-to-all-start.3) | async-done | bytes 3932192 | tf_op jit(solution)/shard_map/all_to_all | solution.py:146
  125.7 4.5 %all-to-all-start.1 = ((bf16[8,96,2560]{2,1,0:T(8,128)(2,1)}), bf16[8,96,2560]{2,1,0:T(8,128)(2,1)}, u32[]{:S(2)}, u32[]{:S(2)}) async-start(bf16[8,96,2560]{2,1,0:T(8,128)(2,1)} %convolution_convert_fusion.1), calls=%async_computation.1 | async-start | bytes 7864320 | tf_op jit(solution)/shard_map/all_to_all | solution.py:146
  130.2 7.6 %fusion.67 = (bf16[1,2560,2,384]{3,2,1,0:T(2,128)(2,1)}, bf16[1,2560,2,384]{3,2,1,0:T(2,128)(2,1)S(1)}) fusion(bf16[2,2560,2,384]{3,2,1,0:T(2,128)(2,1)} %param.30), kind=kLoop, calls=%fused_computation.131 | loop fusion | bytes 15728640 | tf_op jit(solution)/shard_map/slice | solution.py:149
  137.8 5.5 %fusion.1 = f32[768,2,384]{2,0,1:T(8,128)S(1)} fusion(bf16[768,2560,1]{1,0,2:T(8,128)(2,1)} %bitcast.45, bf16[1,2560,2,384]{3,2,1,0:T(2,128)(2,1)S(1)} %get-tuple-element.6), kind=kOutput, calls=%fused_computation.11 | convolution fusion | flops 3019898880 | bytes 10223616 | tf_op jit(solution)/shard_map/md,dcf->mcf/dot_general | solution.py:148
  143.3 4.2 %convolution_convert_fusion.2 = bf16[768,2560]{1,0:T(8,128)(2,1)} fusion(bf16[2,384,2560]{2,1,0:T(8,128)(2,1)S(1)} %copy-done.16, f32[768,2,384]{2,0,1:T(8,128)S(1)} %fusion.1), kind=kOutput, calls=%fused_computation.7 | convolution fusion | flops 1513684992 | bytes 8257536 | tf_op jit(solution)/shard_map/dot_general | solution.py:152
  147.5 29.1 %all-to-all-done.1 = bf16[8,96,2560]{2,1,0:T(8,128)(2,1)} async-done(((bf16[8,96,2560]{2,1,0:T(8,128)(2,1)}), bf16[8,96,2560]{2,1,0:T(8,128)(2,1)}, u32[]{:S(2)}, u32[]{:S(2)}) %all-to-all-start.1) | async-done | bytes 3932192 | tf_op jit(solution)/shard_map/all_to_all | solution.py:146
  176.5 4.5 %all-to-all-start.4 = ((bf16[8,96,2560]{2,1,0:T(8,128)(2,1)}), bf16[8,96,2560]{2,1,0:T(8,128)(2,1)}, u32[]{:S(2)}, u32[]{:S(2)}) async-start(bf16[8,96,2560]{2,1,0:T(8,128)(2,1)} %bitcast.226), calls=%async_computation.4 | async-start | bytes 7864320 | tf_op jit(solution)/shard_map/all_to_all | solution.py:154
  181.1 6.7 %fusion.2 = f32[768,2,384]{2,0,1:T(8,128)S(1)} fusion(bf16[768,2560,1]{1,0,2:T(8,128)(2,1)} %bitcast.34, bf16[1,2560,2,384]{3,2,1,0:T(2,128)(2,1)} %get-tuple-element.5), kind=kOutput, calls=%fused_computation.13 | convolution fusion | flops 3019898880 | bytes 10223616 | tf_op jit(solution)/shard_map/md,dcf->mcf/dot_general | solution.py:148
  187.7 4.2 %convolution_convert_fusion.3 = bf16[768,2560]{1,0:T(8,128)(2,1)} fusion(bf16[2,384,2560]{2,1,0:T(8,128)(2,1)S(1)} %copy-done.17, f32[768,2,384]{2,0,1:T(8,128)S(1)} %fusion.2), kind=kOutput, calls=%fused_computation.8 | convolution fusion | flops 1513684992 | bytes 8257536 | tf_op jit(solution)/shard_map/dot_general | solution.py:152
  191.9 35.4 %all-to-all-done.4 = bf16[8,96,2560]{2,1,0:T(8,128)(2,1)} async-done(((bf16[8,96,2560]{2,1,0:T(8,128)(2,1)}), bf16[8,96,2560]{2,1,0:T(8,128)(2,1)}, u32[]{:S(2)}, u32[]{:S(2)}) %all-to-all-start.4) | async-done | bytes 3932192 | tf_op jit(solution)/shard_map/all_to_all | solution.py:154
  227.4 4.7 %all-to-all-start.2 = ((bf16[8,96,2560]{2,1,0:T(8,128)(2,1)}), bf16[8,96,2560]{2,1,0:T(8,128)(2,1)}, u32[]{:S(2)}, u32[]{:S(2)}) async-start(bf16[8,96,2560]{2,1,0:T(8,128)(2,1)} %bitcast.225), calls=%async_computation.2 | async-start | bytes 7864320 | tf_op jit(solution)/shard_map/all_to_all | solution.py:154
  232.5 0.5 copy-done.11
  233.0 1.7 fusion.21
  234.9 1.2 select_reduce_fusion
  236.0 2.4 reshape.227
  238.4 0.5 copy.149
  238.9 0.5 subtract_convert_fusion
  239.4 0.5 copy-done.3
  239.9 4.3 %fusion.4 = f32[192,2,384]{2,0,1:T(8,128)} fusion(bf16[2560,2,384]{2,1,0:T(2,128)(2,1)} %param.32, f32[192,2560]{1,0:T(8,128)S(1)} %bitcast.222, f32[2560]{0:T(1024)S(1)} %copy-done.14, f32[192]{0:T(256)S(1)} %add_rsqrt_fusion), kind=kOutput, calls=%fused_computation.18 | convolution fusion | flops 756449280 | bytes 6499072 | tf_op jit(solution)/shard_map/td,dcf->tcf/dot_general | solution.py:173
  244.2 3.1 convolution_bitcast_fusion
  247.3 4.5 %convolution_bitcast_fusion.1 = f32[192,2560]{1,0:T(8,128)} fusion(bf16[8,96,2560]{2,1,0:T(8,128)(2,1)} %all-to-all-done.4, bf16[192,8,2,96]{3,0,1,2:T(8,128)(2,1)S(1)} %copy.149), kind=kOutput, calls=%fused_computation.22 | convolution fusion | flops 754974720 | bytes 6291456 | tf_op jit(solution)/shard_map/tgc,gcd->td/dot_general | solution.py:168
  251.8 26.4 %all-to-all-done.2 = bf16[8,96,2560]{2,1,0:T(8,128)(2,1)} async-done(((bf16[8,96,2560]{2,1,0:T(8,128)(2,1)}), bf16[8,96,2560]{2,1,0:T(8,128)(2,1)}, u32[]{:S(2)}, u32[]{:S(2)}) %all-to-all-start.2) | async-done | bytes 3932192 | tf_op jit(solution)/shard_map/all_to_all | solution.py:154
  278.2 3.3 %convolution_bitcast_fusion.2 = f32[192,2560]{1,0:T(8,128)S(1)} fusion(bf16[8,96,2560]{2,1,0:T(8,128)(2,1)} %all-to-all-done.2, bf16[192,8,2,96]{3,0,1,2:T(8,128)(2,1)} %copy-done.9), kind=kOutput, calls=%fused_computation.23 | convolution fusion | flops 754974720 | bytes 6291456 | tf_op jit(solution)/shard_map/tgc,gcd->td/dot_general | solution.py:168
  281.6 3.5 %fusion.8 = f32[192,2560]{1,0:T(8,128)S(1)} fusion(f32[192,2560]{1,0:T(8,128)S(1)} %convolution_bitcast_fusion, f32[192,2560]{1,0:T(8,128)S(1)} %copy-done.4, f32[192,2560]{1,0:T(8,128)S(1)} %convolution_bitcast_fusion.2, bf16[8,96,2560]{2,1,0:T(8,128)(2,1)} %all-to-all-done.2, bf16[192,8,2,96]{3,0,1,2:T(8,128)(2,1)S(1)} %copy.149), kind=kOutput, calls=%fused_computation.27 | convolution fusion | flops 756449280 | bytes 12189696 | tf_op jit(solution)/shard_map/tgc,gcd->td/dot_general | solution.py:168
  285.1 0.7 fusion.9
  285.9 24.9 %all_to_all.30 = bf16[4,192,640]{2,1,0:T(8,128)(2,1)S(1)} all-to-all(bf16[4,192,640]{2,1,0:T(8,128)(2,1)S(1)} %bitcast.228), channel_id=1, replica_groups=mesh['req'=8,'tp'=4] {'tp'}, dimensions={0} | all-to-all | bytes 1966080 | tf_op jit(solution)/shard_map/all_to_all | solution.py:179
  310.9 0.7 add_convert_fusion
  (78 shorter events, 5.6 us)
Async XLA Ops:
  0.0 15.7 %copy-start = (bf16[640,2560]{1,0:T(8,128)(2,1)S(1)}, bf16[640,2560]{1,0:T(8,128)(2,1)}, u32[]{:S(2)}) copy-start(bf16[640,2560]{1,0:T(8,128)(2,1)} %param.26) | copy-start | bytes 9830404
  0.0 7.7 %copy-start.10 = (bf16[192,640]{1,0:T(8,128)(2,1)S(1)}, bf16[192,640]{1,0:T(8,128)(2,1)}, u32[]{:S(2)}) copy-start(bf16[192,640]{1,0:T(8,128)(2,1)} %param.17) | copy-start | bytes 737284
  0.0 8.7 %copy-start.19 = (s32[4,48]{1,0:T(4,128)S(1)}, s32[4,48]{1,0:T(4,128)}, u32[]{:S(2)}) copy-start(s32[4,48]{1,0:T(4,128)} %param.24) | copy-start | bytes 2308
  9.0 3.5 %copy-start.15 = (bf16[192,128]{1,0:T(8,128)(2,1)S(1)}, bf16[192,128]{1,0:T(8,128)(2,1)}, u32[]{:S(2)}) copy-start(bf16[192,128]{1,0:T(8,128)(2,1)} %param.18) | copy-start | bytes 147460
  10.3 2.2 copy-start.5
  12.4 1.5 copy-start.8
  14.0 1.3 copy-start.18
  15.7 8.3 %copy-start.13 = (s32[192,6]{0,1:T(8,128)S(1)}, s32[192,6]{0,1:T(8,128)}, u32[]{:S(2)}) copy-start(s32[192,6]{0,1:T(8,128)} %param.29) | copy-start | bytes 13828
  15.7 8.7 %copy-start.14 = (f32[2560]{0:T(1024)S(1)}, f32[2560]{0:T(1024)}, u32[]{:S(2)}) copy-start(f32[2560]{0:T(1024)} %param.27) | copy-start | bytes 30724
  17.7 30.6 %all-to-all-start = ((bf16[4,192,640]{2,1,0:T(8,128)(2,1)}), bf16[4,192,640]{2,1,0:T(8,128)(2,1)S(1)}, u32[]{:S(2)}, u32[]{:S(2)}) async-start(bf16[4,192,640]{2,1,0:T(8,128)(2,1)} %bitcast.216), calls=%async_computation | async-start | bytes 1966080 | tf_op jit(solution)/shard_map/all_to_all | solution.py:125
  74.7 4.8 %copy-start.7 = (pred[192,1536]{0,1:T(32,128)(4,1)S(1)}, pred[192,1536]{0,1:T(32,128)(4,1)}, u32[]{:S(2)}) copy-start(pred[192,1536]{0,1:T(32,128)(4,1)} %copy.106) | copy-start | bytes 884740
  74.7 51.0 %all-to-all-start.3 = ((bf16[8,96,2560]{2,1,0:T(8,128)(2,1)}), bf16[8,96,2560]{2,1,0:T(8,128)(2,1)}, u32[]{:S(2)}, u32[]{:S(2)}) async-start(bf16[8,96,2560]{2,1,0:T(8,128)(2,1)} %convolution_convert_fusion), calls=%async_computation.3 | async-start | bytes 7864320 | tf_op jit(solution)/shard_map/all_to_all | solution.py:146
  125.7 50.8 %all-to-all-start.1 = ((bf16[8,96,2560]{2,1,0:T(8,128)(2,1)}), bf16[8,96,2560]{2,1,0:T(8,128)(2,1)}, u32[]{:S(2)}, u32[]{:S(2)}) async-start(bf16[8,96,2560]{2,1,0:T(8,128)(2,1)} %convolution_convert_fusion.1), calls=%async_computation.1 | async-start | bytes 7864320 | tf_op jit(solution)/shard_map/all_to_all | solution.py:146
  137.8 5.5 %copy-start.16 = (bf16[2,384,2560]{2,1,0:T(8,128)(2,1)S(1)}, bf16[2,384,2560]{2,1,0:T(8,128)(2,1)}, u32[]{:S(2)}) copy-start(bf16[2,384,2560]{2,1,0:T(8,128)(2,1)} %param.31) | copy-start | bytes 11796484
  176.5 50.8 %all-to-all-start.4 = ((bf16[8,96,2560]{2,1,0:T(8,128)(2,1)}), bf16[8,96,2560]{2,1,0:T(8,128)(2,1)}, u32[]{:S(2)}, u32[]{:S(2)}) async-start(bf16[8,96,2560]{2,1,0:T(8,128)(2,1)} %bitcast.226), calls=%async_computation.4 | async-start | bytes 7864320 | tf_op jit(solution)/shard_map/all_to_all | solution.py:154
  181.1 6.7 %copy-start.17 = (bf16[2,384,2560]{2,1,0:T(8,128)(2,1)S(1)}, bf16[2,384,2560]{2,1,0:T(8,128)(2,1)}, u32[]{:S(2)}) copy-start(bf16[2,384,2560]{2,1,0:T(8,128)(2,1)} %param.31) | copy-start | bytes 11796484
  227.4 50.8 %all-to-all-start.2 = ((bf16[8,96,2560]{2,1,0:T(8,128)(2,1)}), bf16[8,96,2560]{2,1,0:T(8,128)(2,1)}, u32[]{:S(2)}, u32[]{:S(2)}) async-start(bf16[8,96,2560]{2,1,0:T(8,128)(2,1)} %bitcast.225), calls=%async_computation.2 | async-start | bytes 7864320 | tf_op jit(solution)/shard_map/all_to_all | solution.py:154
  232.1 0.9 copy-start.11
  232.5 2.4 copy-start.2
  238.4 1.5 copy-start.3
  239.9 4.3 %copy-start.9 = (bf16[192,8,2,96]{3,0,1,2:T(8,128)(2,1)}, bf16[192,8,2,96]{3,0,1,2:T(8,128)(2,1)S(1)}, u32[]{:S(2)}) copy-start(bf16[192,8,2,96]{3,0,1,2:T(8,128)(2,1)S(1)} %subtract_convert_fusion) | copy-start | bytes 1769476
  278.2 3.4 %copy-start.4 = (f32[192,2560]{1,0:T(8,128)S(1)}, f32[192,2560]{1,0:T(8,128)}, u32[]{:S(2)}) copy-start(f32[192,2560]{1,0:T(8,128)} %convolution_bitcast_fusion.1) | copy-start | bytes 5898244
  281.6 3.5 %copy-start.6 = (bf16[384,2560]{1,0:T(8,128)(2,1)S(1)}, bf16[384,2560]{1,0:T(8,128)(2,1)}, u32[]{:S(2)}) copy-start(bf16[384,2560]{1,0:T(8,128)(2,1)} %param.33) | copy-start | bytes 5898244
  281.6 3.5 %copy-start.12 = (f32[192,2,384]{2,0,1:T(8,128)S(1)}, f32[192,2,384]{2,0,1:T(8,128)}, u32[]{:S(2)}) copy-start(f32[192,2,384]{2,0,1:T(8,128)} %fusion.4) | copy-start | bytes 1769476
  285.1 26.6 %copy-start.1 = (bf16[640,2560]{1,0:T(8,128)(2,1)S(1)}, bf16[640,2560]{1,0:T(8,128)(2,1)}, u32[]{:S(2)}) copy-start(bf16[640,2560]{1,0:T(8,128)(2,1)} %param.26) | copy-start | bytes 9830404

commit v3 on v2

--- a/solution.py
+++ b/solution.py
@@ -136,21 +136,41 @@
     normed_bf = normed.astype(jnp.bfloat16)
     hidden_part = hidden_part_bf.astype(jnp.float32)
 
+    near_width = part_width // 2
+    far_width = part_width - near_width
+    normed_blocks = normed_bf.reshape(row_count, tp_count, part_width)
+    normed_near = normed_blocks[:, :, :near_width].reshape(row_count, tp_count * near_width)
+    normed_far = lax.dynamic_slice_in_dim(normed_bf, column + near_width, far_width, 1)
+    send_rows = jnp.concatenate([normed_near, normed_far], axis=1)
     dispatch = jnp.any(hit, axis=1).astype(jnp.bfloat16)
     dispatch = dispatch.reshape(row_count, groups, experts_local, capacity)
     returns = []
     for expert in range(experts_local):
         outbox = jnp.einsum(
-            "tgc,td->gcd", dispatch[:, :, expert], normed_bf, preferred_element_type=jnp.float32
+            "tgc,tk->gck", dispatch[:, :, expert], send_rows, preferred_element_type=jnp.float32
         ).astype(jnp.bfloat16)
         arrived = lax.all_to_all(outbox, "req", split_axis=0, concat_axis=0, tiled=True)
-        rows = arrived.reshape(groups * capacity, model_width)
+        arrived = arrived.reshape(groups * capacity, -1)
+        rows_near = arrived[:, : tp_count * near_width]
+        rows_far = lax.all_gather(
+            arrived[None, :, tp_count * near_width :], "tp", axis=0, tiled=True
+        )
+        weight_blocks = expert_gate_up[expert].reshape(tp_count, part_width, 2, -1)
+        weight_near = weight_blocks[:, :near_width].reshape(tp_count * near_width, 2, -1)
+        weight_far = weight_blocks[:, near_width:]
         gate_up = jnp.einsum(
-            "md,dcf->mcf", rows, expert_gate_up[expert], preferred_element_type=jnp.float32
-        )
+            "mk,kcf->mcf", rows_near, weight_near, preferred_element_type=jnp.float32
+        ) + jnp.einsum("zmk,zkcf->mcf", rows_far, weight_far, preferred_element_type=jnp.float32)
         act = (jax.nn.silu(gate_up[:, 0]) * gate_up[:, 1]).astype(jnp.bfloat16)
         partial_value = jnp.dot(act, expert_down[expert], preferred_element_type=jnp.float32)
-        outputs = partial_value.astype(jnp.bfloat16).reshape(groups, capacity, model_width)
+        partial_blocks = partial_value.astype(jnp.bfloat16).reshape(-1, tp_count, part_width)
+        back_near = partial_blocks[:, :, :near_width].reshape(-1, tp_count * near_width)
+        far_parts = lax.all_to_all(
+            partial_blocks[:, :, near_width:].transpose(1, 0, 2),
+            "tp", split_axis=0, concat_axis=0, tiled=True,
+        )
+        back_far = jnp.sum(far_parts.astype(jnp.float32), axis=0).astype(jnp.bfloat16)
+        outputs = jnp.concatenate([back_near, back_far], axis=1).reshape(groups, capacity, -1)
         returns.append(lax.all_to_all(outputs, "req", split_axis=0, concat_axis=0, tiled=True))
 
     chosen = jnp.sum(
@@ -162,22 +182,30 @@
     weights = weights.reshape(row_count, groups, experts_local, capacity)
     weights_hi = weights.astype(jnp.bfloat16)
     weights_lo = (weights - weights_hi.astype(jnp.float32)).astype(jnp.bfloat16)
-    routed = jnp.zeros((row_count, model_width), jnp.float32)
+    routed = jnp.zeros((row_count, tp_count * near_width + far_width), jnp.float32)
     for expert in range(experts_local):
         for split in (weights_hi, weights_lo):
             routed = routed + jnp.einsum(
-                "tgc,gcd->td", split[:, :, expert], returns[expert],
+                "tgc,gck->tk", split[:, :, expert], returns[expert],
                 preferred_element_type=jnp.float32,
             )
+    routed_near = routed[:, : tp_count * near_width].reshape(row_count, tp_count, near_width)
+    routed_far = routed[:, tp_count * near_width :]
 
     shared_gu = jnp.einsum(
         "td,dcf->tcf", normed_bf, shared_gate_up, preferred_element_type=jnp.float32
     )
     shared_act = (jax.nn.silu(shared_gu[:, 0]) * shared_gu[:, 1]).astype(jnp.bfloat16)
     shared_terms = jnp.dot(shared_act, shared_down, preferred_element_type=jnp.float32)
-    total = (shared_terms + routed).astype(jnp.bfloat16).reshape(row_count, tp_count, part_width)
+    shared_blocks = shared_terms.reshape(row_count, tp_count, part_width)
+    total = jnp.concatenate(
+        [shared_blocks[:, :, :near_width] + routed_near, shared_blocks[:, :, near_width:]], axis=2
+    ).astype(jnp.bfloat16)
     total = lax.all_to_all(total.transpose(1, 0, 2), "tp", split_axis=0, concat_axis=0, tiled=True)
     summed = jnp.sum(total.astype(jnp.float32), axis=0)
+    summed = summed + jnp.concatenate(
+        [jnp.zeros((row_count, near_width), jnp.float32), routed_far], axis=1
+    )
     return (hidden_part + summed).astype(jnp.bfloat16)
 
 

time: 314 us -> 456 us (1.45); the launches traced: 312 us -> 447 us
  local copies, waits for them, and re-layouts: 23.5 us -> 105 us
  other arithmetic: 13.3 us -> 28.9 us
  between operations: 0.6 us -> 14.5 us
  blocking collectives: 44.5 us -> 55.1 us
  waiting for transfers between devices: 150 us -> 159 us
  starting transfers between devices: 24.9 us -> 33.4 us
    all_to_all x0 -> x3, waiting for transfers between devices: none -> 54.9 us  [the longest x2 34.9 us: shards(): lax.all_to_all(partial_blocks[:, :, near_width:].transpose(1, 0, 2), 'tp'...]
    all_to_all x2 -> x1, waiting for transfers between devices: 72.1 us -> 19.8 us  [shards(): lax.all_to_all(outbox, 'req', split_axis=0, concat_axis=0, tiled=True)]
    all_gather x0 -> x2, waiting for transfers between devices: none -> 34.2 us  [shards(): lax.all_gather(arrived[None, :, tp_count * near_width:], 'tp', axis=0, ti...]
    slice x2 -> x14, local copies, waits for them, and re-layouts: 8.02 us -> 36 us  [the longest x2 14.6 us: shards(): partial_blocks[:, :, :near_width].reshape(-1, tp_count * near_width)]
    all_to_all x2, waiting for transfers between devices: 61.8 us -> 33.9 us  [shards(): lax.all_to_all(outputs, 'req', split_axis=0, concat_axis=0, tiled=True)]
    unnamed x41 -> x58, local copies, waits for them, and re-layouts: 1.24 us -> 21.6 us
    reshape x1 -> x4, local copies, waits for them, and re-layouts: 0.09 us -> 17.7 us  [the longest x2 15.3 us: shards(): partial_value.astype(jnp.bfloat16).reshape(-1, tp_count, part_width)]
    all_to_all x0 -> x3, starting transfers between devices: none -> 13.5 us  [the longest x2 9.08 us: shards(): lax.all_to_all(partial_blocks[:, :, near_width:].transpose(1, 0, 2), 'tp'...]
  transfers between devices with their start and end apart: 5 -> 9, of which waited for: 5 -> 8; matrix products, arithmetic and copies ran while one was open for 19% -> 29% of each run, Pallas kernels for 0% -> 0%
where the time goes in v3:
time: 456 us; the launch traced here: 447 us
  waiting for transfers between devices  159 us (35%)
  local copies, waits for them, and re-layouts  105 us (23%)
  blocking collectives  55.1 us (12%)
  matrix products  50.7 us (11%)
  starting transfers between devices  33.4 us (7%)
  other arithmetic  28.9 us (6%)
  between operations  14.5 us (3%)
    all_to_all x1, blocking collectives, shards(): lax.all_to_all(outbox, 'req', split_axis=0, concat_axis=0, tiled=True)  35 us
    all_to_all x2, waiting for transfers between devices, shards(): lax.all_to_all(partial_blocks[:, :, near_width:].transpose(1, 0, 2), 'tp'...  34.9 us
    all_gather x2, waiting for transfers between devices, shards(): lax.all_gather(arrived[None, :, tp_count * near_width:], 'tp', axis=0, ti...  34.2 us
    all_to_all x2, waiting for transfers between devices, shards(): lax.all_to_all(outputs, 'req', split_axis=0, concat_axis=0, tiled=True)  33.9 us
    unnamed x58, local copies, waits for them, and re-layouts  21.6 us
    all_gather x1, blocking collectives, shards(): hidden_bf = lax.all_gather(hidden_part_bf[None], 'tp', axis=0, tiled=True)  20 us
    all_to_all x1, waiting for transfers between devices, shards(): lax.all_to_all(total.transpose(1, 0, 2), 'tp', split_axis=0, concat_axis=...  20 us
    all_to_all x1, waiting for transfers between devices, shards(): lax.all_to_all(outbox, 'req', split_axis=0, concat_axis=0, tiled=True)  19.8 us
  transfers between devices with their start and end apart: 9, of which 8 were waited for; matrix products, arithmetic and copies ran while one was open for 29% of the time, Pallas kernels for 0%

profile of v3, /device:TPU:0, one launch (start us, length us, event | category | flops | bytes accessed | tf_op | source)
XLA Modules:
  0.0 446.7 jit_solution(14865229061335307913)
XLA Ops:
  12.5 2.9 gather_fusion.1
  15.4 2.1 bitcast_reduce_fusion
  19.7 2.9 gather_fusion
  22.6 3.5 fusion.16
  28.5 6.3 %all-to-all-start = ((bf16[4,192,640]{2,1,0:T(8,128)(2,1)}), bf16[4,192,640]{2,1,0:T(8,128)(2,1)S(1)}, u32[]{:S(2)}, u32[]{:S(2)}) async-start(bf16[4,192,640]{2,1,0:T(8,128)(2,1)} %bitcast.226), calls=%async_computation | async-start | bytes 1966080 | tf_op jit(solution)/shard_map/all_to_all | solution.py:125
  35.3 4.5 %reduce-window.6 = s32[16,9,128]{2,1,0:T(8,128)S(1)} reduce-window(s32[16,9,128]{2,1,0:T(8,128)S(1)} %fusion.52, s32[]{:T(128)} %constant.20.clone.1), window={size=1x1x128 pad=0_0x0_0x127_0}, to_apply=%region_6.7 | reduce-window | flops 2340864 | bytes 147460 | tf_op jit(solution)/shard_map/reduce-window
  43.2 15.9 %all-to-all-done = bf16[4,192,640]{2,1,0:T(8,128)(2,1)S(1)} async-done(((bf16[4,192,640]{2,1,0:T(8,128)(2,1)}), bf16[4,192,640]{2,1,0:T(8,128)(2,1)S(1)}, u32[]{:S(2)}, u32[]{:S(2)}) %all-to-all-start) | async-done | bytes 983072 | tf_op jit(solution)/shard_map/all_to_all | solution.py:125
  60.3 20.0 %all-gather = bf16[768,640]{1,0:T(8,128)(2,1)S(1)} all-gather(bf16[192,640]{1,0:T(8,128)(2,1)S(1)} %add_convert_fusion.1), channel_id=2, replica_groups=mesh['req'=8,'tp'=4] {'tp'}, dimensions={0}, use_global_device_ids=true | all-gather | bytes 1228800 | tf_op jit(solution)/shard_map/all_gather | solution.py:131
  88.5 35.0 %all_to_all.40 = bf16[8,96,1600]{2,1,0:T(8,128)(2,1)S(1)} all-to-all(bf16[8,96,1600]{2,1,0:T(8,128)(2,1)S(1)} %convolution_convert_fusion.4), channel_id=1, replica_groups=mesh['req'=8,'tp'=4] {'req'}, dimensions={0} | all-to-all | bytes 4915200 | tf_op jit(solution)/shard_map/all_to_all | solution.py:152
  126.0 2.4 convolution_convert_fusion.3
  128.4 4.4 all-to-all-start.4
  133.0 7.6 %fusion.67 = (bf16[1,2560,2,384]{3,2,1,0:T(2,128)(2,1)S(1)}, bf16[1,2560,2,384]{3,2,1,0:T(2,128)(2,1)}) fusion(bf16[2,2560,2,384]{3,2,1,0:T(2,128)(2,1)} %param.30), kind=kLoop, calls=%fused_computation.137 | loop fusion | bytes 15728640 | tf_op jit(solution)/shard_map/slice | solution.py:158
  144.6 19.8 %all-to-all-done.4 = bf16[8,96,1600]{2,1,0:T(8,128)(2,1)} async-done(((bf16[8,96,1600]{2,1,0:T(8,128)(2,1)}), bf16[8,96,1600]{2,1,0:T(8,128)(2,1)}, u32[]{:S(2)}, u32[]{:S(2)}) %all-to-all-start.4) | async-done | bytes 2457632 | tf_op jit(solution)/shard_map/all_to_all | solution.py:152
  166.4 8.6 %all-gather.6.cloned.1.call-done = bf16[3072,320]{1,0:T(8,128)(2,1)} async-done(((bf16[768,320]{1,0:T(8,128)(2,1)}), bf16[3072,320]{1,0:T(8,128)(2,1)}) %all-gather.6.cloned.1.call-update) | async-done | bytes 1966096 | tf_op jit(solution)/shard_map/all_gather | solution.py:155
  174.9 4.1 fusion.11
  181.2 4.2 convolution_convert_fusion.1
  185.4 7.6 %reshape.244 = bf16[768,4,640]{2,1,0:T(4,128)(2,1)} reshape(bf16[768,2560]{1,0:T(8,128)(2,1)} %convolution_convert_fusion.1) | data formatting | bytes 7864320 | tf_op jit(solution)/shard_map/reshape | solution.py:166
  193.1 7.4 %fusion.68 = (bf16[768,4,320]{2,1,0:T(4,128)(2,1)}, bf16[768,4,320]{2,1,0:T(4,128)(2,1)}) fusion(bf16[768,4,640]{2,1,0:T(4,128)(2,1)} %reshape.244), kind=kLoop, calls=%fused_computation.138 | loop fusion | bytes 7864320 | tf_op jit(solution)/shard_map/slice | solution.py:167
  200.4 5.4 %copy.182 = bf16[768,4,320]{0,2,1:T(8,128)(2,1)} copy(bf16[768,4,320]{2,1,0:T(4,128)(2,1)} %get-tuple-element.8) | data formatting | bytes 3932160
  205.8 4.6 %all-to-all-start.2 = ((bf16[4,768,320]{1,2,0:T(8,128)(2,1)}), bf16[4,768,320]{1,2,0:T(8,128)(2,1)}, u32[]{:S(2)}, u32[]{:S(2)}) async-start(bf16[4,768,320]{1,2,0:T(8,128)(2,1)} %bitcast.238), calls=%async_computation.2 | async-start | bytes 3932160 | tf_op jit(solution)/shard_map/all_to_all | solution.py:168
  210.4 2.7 copy.164
  216.5 25.7 %all-gather.8.cloned.1.call-done = bf16[3072,320]{1,0:T(8,128)(2,1)} async-done(((bf16[768,320]{1,0:T(8,128)(2,1)}), bf16[3072,320]{1,0:T(8,128)(2,1)}) %all-gather.8.cloned.1.call-update) | async-done | bytes 1966096 | tf_op jit(solution)/shard_map/all_gather | solution.py:155
  242.2 4.1 fusion.8
  246.3 3.4 bitcast_add_fusion
  249.8 4.1 convolution_convert_fusion
  253.9 7.6 %reshape.247 = bf16[768,4,640]{2,1,0:T(4,128)(2,1)} reshape(bf16[768,2560]{1,0:T(8,128)(2,1)} %convolution_convert_fusion) | data formatting | bytes 7864320 | tf_op jit(solution)/shard_map/reshape | solution.py:166
  261.5 7.3 %fusion.69 = (bf16[768,4,320]{2,1,0:T(4,128)(2,1)}, bf16[768,4,320]{2,1,0:T(4,128)(2,1)}) fusion(bf16[768,4,640]{2,1,0:T(4,128)(2,1)} %reshape.247), kind=kLoop, calls=%fused_computation.139 | loop fusion | bytes 7864320 | tf_op jit(solution)/shard_map/slice | solution.py:167
  268.8 5.3 %copy.184 = bf16[768,4,320]{0,2,1:T(8,128)(2,1)} copy(bf16[768,4,320]{2,1,0:T(4,128)(2,1)} %get-tuple-element.10) | data formatting | bytes 3932160
  274.1 4.4 all-to-all-start.5
  278.6 4.7 %concatenate.27 = bf16[8,96,1280]{2,1,0:T(8,128)(2,1)} reshape(bf16[768,4,320]{2,1,0:T(4,128)(2,1)} %get-tuple-element.7) | data formatting | bytes 3932160 | tf_op jit(solution)/shard_map/concatenate | solution.py:173
  283.3 2.1 reduce_sum.116
  285.7 3.2 pad_maximum_fusion
  288.9 34.9 %all-to-all-done.5 = bf16[4,768,320]{1,2,0:T(8,128)(2,1)} async-done(((bf16[4,768,320]{1,2,0:T(8,128)(2,1)}), bf16[4,768,320]{1,2,0:T(8,128)(2,1)}, u32[]{:S(2)}, u32[]{:S(2)}) %all-to-all-start.5) | async-done | bytes 1966112 | tf_op jit(solution)/shard_map/all_to_all | solution.py:168
  323.8 4.4 all-to-all-start.3
  328.2 4.1 copy.178
  332.3 4.7 %concatenate.30 = bf16[8,96,1280]{2,1,0:T(8,128)(2,1)} reshape(bf16[768,4,320]{2,1,0:T(4,128)(2,1)} %get-tuple-element.9) | data formatting | bytes 3932160 | tf_op jit(solution)/shard_map/concatenate | solution.py:173
  339.3 3.3 pad_maximum_fusion.1
  342.6 17.2 %all-to-all-done.3 = bf16[8,96,1600]{2,1,0:T(8,128)(2,1)} async-done(((bf16[8,96,1600]{2,1,0:T(8,128)(2,1)}), bf16[8,96,1600]{2,1,0:T(8,128)(2,1)}, u32[]{:S(2)}, u32[]{:S(2)}) %all-to-all-start.3) | async-done | bytes 2457632 | tf_op jit(solution)/shard_map/all_to_all | solution.py:174
  359.8 4.6 %all-to-all-start.6 = ((bf16[8,96,1600]{2,1,0:T(8,128)(2,1)}), bf16[8,96,1600]{2,1,0:T(8,128)(2,1)}, u32[]{:S(2)}, u32[]{:S(2)}) async-start(bf16[8,96,1600]{2,1,0:T(8,128)(2,1)} %pad_maximum_fusion.1), calls=%async_computation.6 | async-start | bytes 5111808 | tf_op jit(solution)/shard_map/all_to_all | solution.py:174
  367.4 2.4 reshape.239
  370.3 3.7 fusion.2
  376.8 2.5 convolution_bitcast_fusion.2
  379.3 16.7 %all-to-all-done.6 = bf16[8,96,1600]{2,1,0:T(8,128)(2,1)} async-done(((bf16[8,96,1600]{2,1,0:T(8,128)(2,1)}), bf16[8,96,1600]{2,1,0:T(8,128)(2,1)}, u32[]{:S(2)}, u32[]{:S(2)}) %all-to-all-start.6) | async-done | bytes 2457632 | tf_op jit(solution)/shard_map/all_to_all | solution.py:174
  396.0 2.5 convolution_bitcast_fusion
  398.5 2.5 convolution_bitcast_fusion.1
  401.0 2.7 fusion.7
  410.2 4.4 all-to-all-start.7
  416.3 20.0 %all-to-all-done.7 = bf16[4,192,640]{2,1,0:T(8,128)(2,1)} async-done(((bf16[4,192,640]{2,1,0:T(8,128)(2,1)}), bf16[4,192,640]{2,1,0:T(8,128)(2,1)}, u32[]{:S(2)}, u32[]{:S(2)}) %all-to-all-start.7) | async-done | bytes 983072 | tf_op jit(solution)/shard_map/all_to_all | solution.py:204
  (133 shorter events, 57.7 us)
Async XLA Ops:
  6.5 19.9 %copy-start = (bf16[640,2560]{1,0:T(8,128)(2,1)S(1)}, bf16[640,2560]{1,0:T(8,128)(2,1)}, u32[]{:S(2)}) copy-start(bf16[640,2560]{1,0:T(8,128)(2,1)} %param.26) | copy-start | bytes 9830404
  15.4 2.2 copy-start.12
  15.4 2.2 copy-start.23
  17.5 1.9 copy-start.2
  18.0 1.6 copy-start.13
  22.5 3.5 copy-start.14
  22.6 3.5 copy-start.26
  27.4 7.4 %copy-start.22 = (s32[192,6]{0,1:T(8,128)S(1)}, s32[192,6]{0,1:T(8,128)}, u32[]{:S(2)}) copy-start(s32[192,6]{0,1:T(8,128)} %param.29) | copy-start | bytes 13828
  27.4 7.8 %copy-start.21 = (f32[2560]{0:T(1024)S(1)}, f32[2560]{0:T(1024)}, u32[]{:S(2)}) copy-start(f32[2560]{0:T(1024)} %param.27) | copy-start | bytes 30724
  28.5 30.6 %all-to-all-start = ((bf16[4,192,640]{2,1,0:T(8,128)(2,1)}), bf16[4,192,640]{2,1,0:T(8,128)(2,1)S(1)}, u32[]{:S(2)}, u32[]{:S(2)}) async-start(bf16[4,192,640]{2,1,0:T(8,128)(2,1)} %bitcast.226), calls=%async_computation | async-start | bytes 1966080 | tf_op jit(solution)/shard_map/all_to_all | solution.py:125
  34.8 140.1 %all-gather.6.cloned.1.call-start = ((), (), s32[]{:S(2)}) async-start(), calls=%async_computation.8 | async-start | bytes 2949120 | tf_op jit(solution)/shard_map/all_gather | solution.py:155
  86.4 1.2 copy-start.18
  86.7 0.9 copy-start.19
  123.6 1.5 copy-start.9
  128.4 36.0 %all-to-all-start.4 = ((bf16[8,96,1600]{2,1,0:T(8,128)(2,1)}), bf16[8,96,1600]{2,1,0:T(8,128)(2,1)}, u32[]{:S(2)}, u32[]{:S(2)}) async-start(bf16[8,96,1600]{2,1,0:T(8,128)(2,1)} %convolution_convert_fusion.3), calls=%async_computation.4 | async-start | bytes 5111808 | tf_op jit(solution)/shard_map/all_to_all | solution.py:152
  132.8 109.3 %all-gather.8.cloned.1.call-start = ((), (), s32[]{:S(2)}) async-start(), calls=%async_computation.9 | async-start | bytes 2949120 | tf_op jit(solution)/shard_map/all_gather | solution.py:155
  141.2 1.9 copy-start.3
  174.9 4.2 copy-start.10
  174.9 4.2 copy-start.15
  179.1 2.1 copy-start.24
  205.8 68.3 %all-to-all-start.2 = ((bf16[4,768,320]{1,2,0:T(8,128)(2,1)}), bf16[4,768,320]{1,2,0:T(8,128)(2,1)}, u32[]{:S(2)}, u32[]{:S(2)}) async-start(bf16[4,768,320]{1,2,0:T(8,128)(2,1)} %bitcast.238), calls=%async_computation.2 | async-start | bytes 3932160 | tf_op jit(solution)/shard_map/all_to_all | solution.py:168
  213.1 1.9 copy-start.4
  242.1 4.1 copy-start.16
  246.3 3.5 copy-start.25
  274.1 49.7 %all-to-all-start.5 = ((bf16[4,768,320]{1,2,0:T(8,128)(2,1)}), bf16[4,768,320]{1,2,0:T(8,128)(2,1)}, u32[]{:S(2)}, u32[]{:S(2)}) async-start(bf16[4,768,320]{1,2,0:T(8,128)(2,1)} %bitcast.239), calls=%async_computation.5 | async-start | bytes 3932160 | tf_op jit(solution)/shard_map/all_to_all | solution.py:168
  323.8 36.0 %all-to-all-start.3 = ((bf16[8,96,1600]{2,1,0:T(8,128)(2,1)}), bf16[8,96,1600]{2,1,0:T(8,128)(2,1)}, u32[]{:S(2)}, u32[]{:S(2)}) async-start(bf16[8,96,1600]{2,1,0:T(8,128)(2,1)} %pad_maximum_fusion), calls=%async_computation.3 | async-start | bytes 5111808 | tf_op jit(solution)/shard_map/all_to_all | solution.py:174
  342.6 21.8 %copy-start.20 = (f32[2560,16]{0,1:T(8,128)S(1)}, f32[2560,16]{0,1:T(8,128)}, u32[]{:S(2)}) copy-start(f32[2560,16]{0,1:T(8,128)} %param.28) | copy-start | bytes 491524
  359.8 36.2 %all-to-all-start.6 = ((bf16[8,96,1600]{2,1,0:T(8,128)(2,1)}), bf16[8,96,1600]{2,1,0:T(8,128)(2,1)}, u32[]{:S(2)}, u32[]{:S(2)}) async-start(bf16[8,96,1600]{2,1,0:T(8,128)(2,1)} %pad_maximum_fusion.1), calls=%async_computation.6 | async-start | bytes 5111808 | tf_op jit(solution)/shard_map/all_to_all | solution.py:174
  370.3 28.2 %copy-start.17 = (bf16[192,8,2,96]{3,0,1,2:T(8,128)(2,1)}, bf16[192,8,2,96]{3,0,1,2:T(8,128)(2,1)S(1)}, u32[]{:S(2)}) copy-start(bf16[192,8,2,96]{3,0,1,2:T(8,128)(2,1)S(1)} %copy.207) | copy-start | bytes 1769476
  370.3 3.7 copy-start.5
  374.9 1.9 copy-start.6
  403.7 1.1 copy-start.8
  404.8 3.1 copy-start.7
  407.8 1.1 copy-start.11
  408.9 30.6 %copy-start.1 = (bf16[640,2560]{1,0:T(8,128)(2,1)S(1)}, bf16[640,2560]{1,0:T(8,128)(2,1)}, u32[]{:S(2)}) copy-start(bf16[640,2560]{1,0:T(8,128)(2,1)} %param.26) | copy-start | bytes 9830404
  410.2 26.1 %all-to-all-start.7 = ((bf16[4,192,640]{2,1,0:T(8,128)(2,1)}), bf16[4,192,640]{2,1,0:T(8,128)(2,1)}, u32[]{:S(2)}, u32[]{:S(2)}) async-start(bf16[4,192,640]{2,1,0:T(8,128)(2,1)} %maximum_bitcast_fusion), calls=%async_computation.7 | async-start | bytes 1966080 | tf_op jit(solution)/shard_map/all_to_all | solution.py:204
Sparse Core Ops, SparseCore 0:
  126.2 48.7 all-gather.5
  176.5 65.5 all-gather.7

commit v4 on v2

--- a/solution.py
+++ b/solution.py
@@ -137,21 +137,21 @@
     hidden_part = hidden_part_bf.astype(jnp.float32)
 
     dispatch = jnp.any(hit, axis=1).astype(jnp.bfloat16)
-    dispatch = dispatch.reshape(row_count, groups, experts_local, capacity)
-    returns = []
-    for expert in range(experts_local):
-        outbox = jnp.einsum(
-            "tgc,td->gcd", dispatch[:, :, expert], normed_bf, preferred_element_type=jnp.float32
-        ).astype(jnp.bfloat16)
-        arrived = lax.all_to_all(outbox, "req", split_axis=0, concat_axis=0, tiled=True)
-        rows = arrived.reshape(groups * capacity, model_width)
-        gate_up = jnp.einsum(
-            "md,dcf->mcf", rows, expert_gate_up[expert], preferred_element_type=jnp.float32
-        )
-        act = (jax.nn.silu(gate_up[:, 0]) * gate_up[:, 1]).astype(jnp.bfloat16)
-        partial_value = jnp.dot(act, expert_down[expert], preferred_element_type=jnp.float32)
-        outputs = partial_value.astype(jnp.bfloat16).reshape(groups, capacity, model_width)
-        returns.append(lax.all_to_all(outputs, "req", split_axis=0, concat_axis=0, tiled=True))
+    dispatch = dispatch.reshape(row_count, groups, experts_local * capacity)
+    outbox = jnp.einsum(
+        "tgc,td->gcd", dispatch, normed_bf, preferred_element_type=jnp.float32
+    ).astype(jnp.bfloat16)
+    arrived = lax.all_to_all(outbox, "req", split_axis=0, concat_axis=0, tiled=True)
+    arrived = arrived.reshape(groups, experts_local, capacity, model_width)
+    gate_up = jnp.einsum(
+        "gecd,edkf->egckf", arrived, expert_gate_up, preferred_element_type=jnp.float32
+    )
+    act = (jax.nn.silu(gate_up[:, :, :, 0]) * gate_up[:, :, :, 1]).astype(jnp.bfloat16)
+    partial_value = jnp.einsum(
+        "egcf,efd->gecd", act, expert_down, preferred_element_type=jnp.float32
+    ).astype(jnp.bfloat16)
+    outputs = partial_value.reshape(groups, experts_local * capacity, model_width)
+    returned = lax.all_to_all(outputs, "req", split_axis=0, concat_axis=0, tiled=True)
 
     chosen = jnp.sum(
         jnp.where(routes[:, :, None] == expert_ids[None, None, :], logits[:, None, :], 0.0), axis=-1
@@ -159,16 +159,12 @@
     gate_values = jax.nn.sigmoid(chosen)
     gate_values = gate_values / jnp.sum(gate_values, axis=1, keepdims=True)
     weights = jnp.sum(jnp.where(hit, gate_values[:, :, None], 0.0), axis=1)
-    weights = weights.reshape(row_count, groups, experts_local, capacity)
+    weights = weights.reshape(row_count, groups, experts_local * capacity)
     weights_hi = weights.astype(jnp.bfloat16)
     weights_lo = (weights - weights_hi.astype(jnp.float32)).astype(jnp.bfloat16)
-    routed = jnp.zeros((row_count, model_width), jnp.float32)
-    for expert in range(experts_local):
-        for split in (weights_hi, weights_lo):
-            routed = routed + jnp.einsum(
-                "tgc,gcd->td", split[:, :, expert], returns[expert],
-                preferred_element_type=jnp.float32,
-            )
+    routed = jnp.einsum(
+        "tgc,gcd->td", weights_hi, returned, preferred_element_type=jnp.float32
+    ) + jnp.einsum("tgc,gcd->td", weights_lo, returned, preferred_element_type=jnp.float32)
 
     shared_gu = jnp.einsum(
         "td,dcf->tcf", normed_bf, shared_gate_up, preferred_element_type=jnp.float32

time: 314 us -> 320 us (1.019)
  blocking collectives: 44.5 us -> 137 us
  waiting for transfers between devices: 150 us -> 91.9 us
  starting transfers between devices: 24.9 us -> 11.2 us
  matrix products: 55 us -> 41.8 us
    all_to_all x0 -> x1, blocking collectives: none -> 91.9 us  [shards(): lax.all_to_all(outbox, 'req', split_axis=0, concat_axis=0, tiled=True)]
    all_to_all x2 -> x0, waiting for transfers between devices: 72.1 us -> none  [shards(): lax.all_to_all(outbox, 'req', split_axis=0, concat_axis=0, tiled=True)]
    all_to_all x2 -> x1, waiting for transfers between devices: 61.8 us -> 75.9 us  [shards(): lax.all_to_all(outputs, 'req', split_axis=0, concat_axis=0, tiled=True)]
    dot_general x10 -> x5, matrix products: 41.9 us -> 29.1 us  [the longest x1 9.02 us: shards(): jnp.einsum('gecd,edkf->egckf', arrived, expert_gate_up, preferred_element...]
    all_to_all x2 -> x0, starting transfers between devices: 9.34 us -> none  [shards(): lax.all_to_all(outbox, 'req', split_axis=0, concat_axis=0, tiled=True)]
    slice x2 -> x1, local copies, waits for them, and re-layouts: 8.02 us -> 0.43 us  [the longest x1 7.58 us: shards(): expert_gate_up[expert]]
    convert_element_type x0 -> x1, local copies, waits for them, and re-layouts: none -> 7.09 us  [shards(): partial_value = jnp.einsum('egcf,efd->gecd', act, expert_down, preferred_...]
    all_to_all x2 -> x1, starting transfers between devices: 9.25 us -> 4.9 us  [shards(): lax.all_to_all(outputs, 'req', split_axis=0, concat_axis=0, tiled=True)]
  transfers between devices with their start and end apart: 5 -> 2, of which waited for: 5 -> 2; matrix products, arithmetic and copies ran while one was open for 19% -> 6% of each run, Pallas kernels for 0% -> 0%
where the time goes in v4:
time: 320 us; the launch traced here: 319 us
  blocking collectives  137 us (43%)
  waiting for transfers between devices  91.9 us (29%)
  matrix products  41.8 us (13%)
  local copies, waits for them, and re-layouts  21.2 us (7%)
  other arithmetic  15.9 us (5%)
  starting transfers between devices  11.2 us (4%)
    all_to_all x1, blocking collectives, shards(): lax.all_to_all(outbox, 'req', split_axis=0, concat_axis=0, tiled=True)  91.9 us
    all_to_all x1, waiting for transfers between devices, shards(): lax.all_to_all(outputs, 'req', split_axis=0, concat_axis=0, tiled=True)  75.9 us
    all_to_all x1, blocking collectives, shards(): lax.all_to_all(total.transpose(1, 0, 2), 'tp', split_axis=0, concat_axis=...  25.1 us
    all_gather x1, blocking collectives, shards(): hidden_bf = lax.all_gather(hidden_part_bf[None], 'tp', axis=0, tiled=True)  19.6 us
    all_to_all x1, waiting for transfers between devices, shards(): lax.all_to_all(attn_blocks.transpose(1, 0, 2), 'tp', split_axis=0, concat...  15.9 us
    dot_general x1, matrix products, shards(): jnp.einsum('gecd,edkf->egckf', arrived, expert_gate_up, preferred_element...  9.02 us
    convert_element_type x1, local copies, waits for them, and re-layouts, shards(): partial_value = jnp.einsum('egcf,efd->gecd', act, expert_down, preferred_...  7.09 us
  transfers between devices with their start and end apart: 2, of which 2 were waited for; matrix products, arithmetic and copies ran while one was open for 6% of the time, Pallas kernels for 0%

profile of v4, /device:TPU:0, one launch (start us, length us, event | category | flops | bytes accessed | tf_op | source)
XLA Modules:
  0.0 319.0 jit_solution(6616554751262019396)
XLA Ops:
  0.0 0.8 compare_select_fusion
  1.0 0.9 iota_compare_fusion.6
  1.9 2.9 gather_fusion
  4.8 2.9 gather_fusion.1
  7.7 1.0 reshape.202
  8.7 0.2 convolution_minimum_fusion.5
  9.0 0.2 convolution_minimum_fusion.4
  9.2 0.2 convolution_minimum_fusion.3
  9.4 0.2 convolution_minimum_fusion.2
  9.7 0.2 convolution_minimum_fusion.1
  9.9 0.2 fusion.28
  10.3 2.1 bitcast_reduce_fusion
  12.4 0.4 fusion.62
  12.8 1.0 fusion.10
  14.0 1.3 fusion.16
  15.2 0.3 fusion.27
  15.7 0.9 convolution_convert_fusion.1
  16.6 1.0 copy.160
  17.7 6.3 %all-to-all-start = ((bf16[4,192,640]{2,1,0:T(8,128)(2,1)}), bf16[4,192,640]{2,1,0:T(8,128)(2,1)S(1)}, u32[]{:S(2)}, u32[]{:S(2)}) async-start(bf16[4,192,640]{2,1,0:T(8,128)(2,1)} %bitcast.182), calls=%async_computation | async-start | bytes 1966080 | tf_op jit(solution)/shard_map/all_to_all | solution.py:125
  24.4 4.5 %reduce-window.6 = s32[16,9,128]{2,1,0:T(8,128)S(1)} reduce-window(s32[16,9,128]{2,1,0:T(8,128)S(1)} %fusion.50, s32[]{:T(128)} %constant.17.clone.1), window={size=1x1x128 pad=0_0x0_0x127_0}, to_apply=%region_6.7 | reduce-window | flops 2340864 | bytes 147460 | tf_op jit(solution)/shard_map/reduce-window
  29.0 0.4 slice_reduce_fusion
  29.9 1.2 fusion.3
  31.1 1.2 copy.123
  32.4 15.9 %all-to-all-done = bf16[4,192,640]{2,1,0:T(8,128)(2,1)S(1)} async-done(((bf16[4,192,640]{2,1,0:T(8,128)(2,1)}), bf16[4,192,640]{2,1,0:T(8,128)(2,1)S(1)}, u32[]{:S(2)}, u32[]{:S(2)}) %all-to-all-start) | async-done | bytes 983072 | tf_op jit(solution)/shard_map/all_to_all | solution.py:125
  48.4 1.0 add_convert_fusion.1
  49.4 19.6 %all-gather = bf16[768,640]{1,0:T(8,128)(2,1)S(1)} all-gather(bf16[192,640]{1,0:T(8,128)(2,1)S(1)} %add_convert_fusion.1), channel_id=2, replica_groups=mesh['req'=8,'tp'=4] {'tp'}, dimensions={0}, use_global_device_ids=true | all-gather | bytes 1228800 | tf_op jit(solution)/shard_map/all_gather | solution.py:131
  69.0 0.3 fusion.13
  69.3 0.3 fusion.31
  69.6 0.8 copy.106
  70.4 0.4 reshape.245
  70.8 3.2 convolution_convert_fusion
  74.0 91.9 %all_to_all.20 = bf16[8,192,2560]{2,1,0:T(8,128)(2,1)S(1)} all-to-all(bf16[8,192,2560]{2,1,0:T(8,128)(2,1)S(1)} %convolution_convert_fusion), channel_id=1, replica_groups=mesh['req'=8,'tp'=4] {'req'}, dimensions={0} | all-to-all | bytes 15728640 | tf_op jit(solution)/shard_map/all_to_all | solution.py:144
  165.9 9.0 %fusion = f32[2,8,96,2,384]{4,2,3,1,0:T(8,128)S(1)} fusion(bf16[2,2560,2,384,1]{3,2,1,0,4:T(2,128)(2,1)} %bitcast.201, bf16[8,2,96,2560,1]{3,2,1,0,4:T(8,128)(2,1)S(1)} %bitcast.188), kind=kOutput, calls=%fused_computation.2 | convolution fusion | flops 6039797760 | bytes 20447232 | tf_op jit(solution)/shard_map/gecd,edkf->egckf/dot_general | solution.py:146
  174.9 6.4 %convert_bitcast_fusion = bf16[8,2,96,2560]{3,2,0,1:T(8,128)(2,1)} fusion(bf16[2,384,2560]{2,1,0:T(8,128)(2,1)S(1)} %copy-done.11, f32[2,8,96,2,384]{4,2,3,1,0:T(8,128)S(1)} %fusion), kind=kOutput, calls=%fused_computation.5 | convolution fusion | flops 3027369984 | bytes 16515072 | tf_op jit(solution)/shard_map/egcf,efd->gecd/dot_general | solution.py:150
  181.3 7.1 %copy.111 = bf16[8,2,96,2560]{3,2,1,0:T(8,128)(2,1)} copy(bf16[8,2,96,2560]{3,2,0,1:T(8,128)(2,1)} %convert_bitcast_fusion) | data formatting | bytes 15728640 | tf_op jit(solution)/shard_map/convert_element_type | solution.py:152
  188.4 4.9 %all-to-all-start.2 = ((bf16[8,192,2560]{2,1,0:T(8,128)(2,1)}), bf16[8,192,2560]{2,1,0:T(8,128)(2,1)}, u32[]{:S(2)}, u32[]{:S(2)}) async-start(bf16[8,192,2560]{2,1,0:T(8,128)(2,1)} %bitcast.184), calls=%async_computation.2 | async-start | bytes 15728640 | tf_op jit(solution)/shard_map/all_to_all | solution.py:154
  193.7 0.5 copy-done.6
  194.2 1.7 fusion.19
  196.0 1.2 select_reduce_fusion
  197.2 1.6 reshape.209
  198.8 3.1 subtract_convert_fusion
  201.9 3.9 %fusion.6 = f32[192,2,384]{2,0,1:T(8,128)} fusion(bf16[2560,2,384]{2,1,0:T(2,128)(2,1)} %param.32, f32[192,2560]{1,0:T(8,128)S(1)} %bitcast.190, f32[2560]{0:T(1024)S(1)} %copy-done.9, f32[192]{0:T(256)S(1)} %add_rsqrt_fusion), kind=kOutput, calls=%fused_computation.16 | convolution fusion | flops 756449280 | bytes 6499072 | tf_op jit(solution)/shard_map/td,dcf->tcf/dot_general | solution.py:169
  205.8 75.9 %all-to-all-done.2 = bf16[8,192,2560]{2,1,0:T(8,128)(2,1)} async-done(((bf16[8,192,2560]{2,1,0:T(8,128)(2,1)}), bf16[8,192,2560]{2,1,0:T(8,128)(2,1)}, u32[]{:S(2)}, u32[]{:S(2)}) %all-to-all-start.2) | async-done | bytes 7864352 | tf_op jit(solution)/shard_map/all_to_all | solution.py:154
  281.7 5.3 %convolution_bitcast_fusion = f32[192,2560]{1,0:T(8,128)S(1)} fusion(bf16[8,192,2560]{2,1,0:T(8,128)(2,1)} %all-to-all-done.2, bf16[192,8,192]{2,1,0:T(8,128)(2,1)} %get-tuple-element.5), kind=kOutput, calls=%fused_computation.19 | convolution fusion | flops 1509949440 | bytes 10420224 | tf_op jit(solution)/shard_map/tgc,gcd->td/dot_general | solution.py:167
  287.1 5.2 %fusion.8 = f32[192,2560]{1,0:T(8,128)S(1)} fusion(f32[192,2560]{1,0:T(8,128)S(1)} %convolution_bitcast_fusion, bf16[8,192,2560]{2,1,0:T(8,128)(2,1)} %all-to-all-done.2, bf16[192,8,192]{2,1,0:T(8,128)(2,1)S(1)} %get-tuple-element.6), kind=kOutput, calls=%fused_computation.21 | convolution fusion | flops 1510440960 | bytes 12386304 | tf_op jit(solution)/shard_map/tgc,gcd->td/dot_general | solution.py:165
  292.3 0.7 fusion.9
  293.1 25.1 %all_to_all.21 = bf16[4,192,640]{2,1,0:T(8,128)(2,1)S(1)} all-to-all(bf16[4,192,640]{2,1,0:T(8,128)(2,1)S(1)} %bitcast.194), channel_id=1, replica_groups=mesh['req'=8,'tp'=4] {'tp'}, dimensions={0} | all-to-all | bytes 1966080 | tf_op jit(solution)/shard_map/all_to_all | solution.py:175
  318.3 0.7 add_convert_fusion
  (55 shorter events, 2.2 us)
Async XLA Ops:
  0.0 15.7 %copy-start = (bf16[640,2560]{1,0:T(8,128)(2,1)S(1)}, bf16[640,2560]{1,0:T(8,128)(2,1)}, u32[]{:S(2)}) copy-start(bf16[640,2560]{1,0:T(8,128)(2,1)} %param.26) | copy-start | bytes 9830404
  0.0 7.7 %copy-start.5 = (bf16[192,640]{1,0:T(8,128)(2,1)S(1)}, bf16[192,640]{1,0:T(8,128)(2,1)}, u32[]{:S(2)}) copy-start(bf16[192,640]{1,0:T(8,128)(2,1)} %param.17) | copy-start | bytes 737284
  0.0 8.7 %copy-start.13 = (s32[4,48]{1,0:T(4,128)S(1)}, s32[4,48]{1,0:T(4,128)}, u32[]{:S(2)}) copy-start(s32[4,48]{1,0:T(4,128)} %param.24) | copy-start | bytes 2308
  8.7 3.7 %copy-start.10 = (bf16[192,128]{1,0:T(8,128)(2,1)S(1)}, bf16[192,128]{1,0:T(8,128)(2,1)}, u32[]{:S(2)}) copy-start(bf16[192,128]{1,0:T(8,128)(2,1)} %param.18) | copy-start | bytes 147460
  10.3 2.2 copy-start.2
  12.4 1.5 copy-start.4
  14.0 1.3 copy-start.12
  15.7 8.3 %copy-start.8 = (s32[192,6]{0,1:T(8,128)S(1)}, s32[192,6]{0,1:T(8,128)}, u32[]{:S(2)}) copy-start(s32[192,6]{0,1:T(8,128)} %param.29) | copy-start | bytes 13828
  16.6 15.7 %copy-start.9 = (f32[2560]{0:T(1024)S(1)}, f32[2560]{0:T(1024)}, u32[]{:S(2)}) copy-start(f32[2560]{0:T(1024)} %param.27) | copy-start | bytes 30724
  17.7 30.6 %all-to-all-start = ((bf16[4,192,640]{2,1,0:T(8,128)(2,1)}), bf16[4,192,640]{2,1,0:T(8,128)(2,1)S(1)}, u32[]{:S(2)}, u32[]{:S(2)}) async-start(bf16[4,192,640]{2,1,0:T(8,128)(2,1)} %bitcast.182), calls=%async_computation | async-start | bytes 1966080 | tf_op jit(solution)/shard_map/all_to_all | solution.py:125
  165.9 9.0 %copy-start.11 = (bf16[2,384,2560]{2,1,0:T(8,128)(2,1)S(1)}, bf16[2,384,2560]{2,1,0:T(8,128)(2,1)}, u32[]{:S(2)}) copy-start(bf16[2,384,2560]{2,1,0:T(8,128)(2,1)} %param.31) | copy-start | bytes 11796484
  188.4 93.4 %all-to-all-start.2 = ((bf16[8,192,2560]{2,1,0:T(8,128)(2,1)}), bf16[8,192,2560]{2,1,0:T(8,128)(2,1)}, u32[]{:S(2)}, u32[]{:S(2)}) async-start(bf16[8,192,2560]{2,1,0:T(8,128)(2,1)} %bitcast.184), calls=%async_computation.2 | async-start | bytes 15728640 | tf_op jit(solution)/shard_map/all_to_all | solution.py:154
  193.3 0.9 copy-start.6
  287.0 5.2 %copy-start.3 = (bf16[384,2560]{1,0:T(8,128)(2,1)S(1)}, bf16[384,2560]{1,0:T(8,128)(2,1)}, u32[]{:S(2)}) copy-start(bf16[384,2560]{1,0:T(8,128)(2,1)} %param.33) | copy-start | bytes 5898244
  287.0 5.2 %copy-start.7 = (f32[192,2,384]{2,0,1:T(8,128)S(1)}, f32[192,2,384]{2,0,1:T(8,128)}, u32[]{:S(2)}) copy-start(f32[192,2,384]{2,0,1:T(8,128)} %fusion.6) | copy-start | bytes 1769476
  292.3 26.7 %copy-start.1 = (bf16[640,2560]{1,0:T(8,128)(2,1)S(1)}, bf16[640,2560]{1,0:T(8,128)(2,1)}, u32[]{:S(2)}) copy-start(bf16[640,2560]{1,0:T(8,128)(2,1)} %param.26) | copy-start | bytes 9830404

commit v5 on v2

--- a/solution.py
+++ b/solution.py
@@ -162,14 +162,14 @@
     weights = weights.reshape(row_count, groups, experts_local, capacity)
     weights_hi = weights.astype(jnp.bfloat16)
     weights_lo = (weights - weights_hi.astype(jnp.float32)).astype(jnp.bfloat16)
+    weights_split = jnp.stack([weights_hi, weights_lo])
     routed = jnp.zeros((row_count, model_width), jnp.float32)
     for expert in range(experts_local):
-        for split in (weights_hi, weights_lo):
-            routed = routed + jnp.einsum(
-                "tgc,gcd->td", split[:, :, expert], returns[expert],
-                preferred_element_type=jnp.float32,
-            )
-
+        both = jnp.einsum(
+            "stgc,gcd->std", weights_split[:, :, :, expert], returns[expert],
+            preferred_element_type=jnp.float32,
+        )
+        routed = routed + both[0] + both[1]
     shared_gu = jnp.einsum(
         "td,dcf->tcf", normed_bf, shared_gate_up, preferred_element_type=jnp.float32
     )

time: 314 us -> 316 us (level)
    dot_general x4 -> x2, matrix products: 14.4 us -> 9.96 us  [shards(): jnp.einsum('stgc,gcd->std', weights_split[:, :, :, expert], returns[exper...]
  transfers between devices with their start and end apart: 5 -> 5, of which waited for: 5 -> 5; matrix products, arithmetic and copies ran while one was open for 19% -> 18% of each run, Pallas kernels for 0% -> 0%
where the time goes in v5:
time: 316 us; the launch traced here: 314 us
  waiting for transfers between devices  152 us (48%)
  matrix products  53.3 us (17%)
  blocking collectives  44.5 us (14%)
  local copies, waits for them, and re-layouts  25.8 us (8%)
  starting transfers between devices  24.9 us (8%)
  other arithmetic  13.2 us (4%)
    all_to_all x2, waiting for transfers between devices, shards(): lax.all_to_all(outbox, 'req', split_axis=0, concat_axis=0, tiled=True)  72 us
    all_to_all x2, waiting for transfers between devices, shards(): lax.all_to_all(outputs, 'req', split_axis=0, concat_axis=0, tiled=True)  63.9 us
    all_to_all x1, blocking collectives, shards(): lax.all_to_all(total.transpose(1, 0, 2), 'tp', split_axis=0, concat_axis=...  24.9 us
    all_gather x1, blocking collectives, shards(): hidden_bf = lax.all_gather(hidden_part_bf[None], 'tp', axis=0, tiled=True)  19.6 us
    all_to_all x1, waiting for transfers between devices, shards(): lax.all_to_all(attn_blocks.transpose(1, 0, 2), 'tp', split_axis=0, concat...  15.9 us
    dot_general x2, matrix products, shards(): jnp.einsum('md,dcf->mcf', rows, expert_gate_up[expert], preferred_element...  12.1 us
    dot_general x2, matrix products, shards(): jnp.einsum('stgc,gcd->std', weights_split[:, :, :, expert], returns[exper...  9.96 us
    all_to_all x2, starting transfers between devices, shards(): lax.all_to_all(outbox, 'req', split_axis=0, concat_axis=0, tiled=True)  9.34 us
  transfers between devices with their start and end apart: 5, of which 5 were waited for; matrix products, arithmetic and copies ran while one was open for 18% of the time, Pallas kernels for 0%

profile of v5, /device:TPU:0, one launch (start us, length us, event | category | flops | bytes accessed | tf_op | source)
XLA Modules:
  0.0 314.1 jit_solution(3244755412794882768)
XLA Ops:
  0.0 0.8 compare_select_fusion
  1.0 0.8 iota_compare_fusion.6
  1.7 2.0 reshape.252
  3.7 1.0 convolution_minimum_fusion.5
  6.0 2.9 gather_fusion.1
  8.9 2.1 bitcast_reduce_fusion
  11.5 1.4 copy-done.2
  12.9 1.0 fusion.9
  14.0 2.9 gather_fusion
  16.9 3.5 %fusion.16 = f32[4,128,5,48]{1,3,2,0:T(8,128)S(1)} fusion(bf16[4,1024,128,1]{2,1,3,0:T(8,128)(2,1)} %bitcast.222, f32[4,1024,48,5]{1,2,3,0:T(8,128)} %copy-done.2, f32[4,5,48]{2,1,0:T(8,128)S(1)} %add.82, f32[4,5,48]{2,1,0:T(8,128)S(1)} %max.9, pred[4,1024]{1,0:T(4,128)(4,1)S(1)} %iota_compare_fusion.6), kind=kOutput, calls=%fused_computation.40 | convolution fusion | flops 256573440 | bytes 5484032 | tf_op jit(solution)/shard_map/rkgtc,rckd->rtkgd/dot_general | solution.py:54
  20.8 0.9 convolution_convert_fusion.4
  21.8 1.0 copy.157
  22.8 6.3 %all-to-all-start = ((bf16[4,192,640]{2,1,0:T(8,128)(2,1)}), bf16[4,192,640]{2,1,0:T(8,128)(2,1)S(1)}, u32[]{:S(2)}, u32[]{:S(2)}) async-start(bf16[4,192,640]{2,1,0:T(8,128)(2,1)} %bitcast.208), calls=%async_computation | async-start | bytes 1966080 | tf_op jit(solution)/shard_map/all_to_all | solution.py:125
  29.6 4.5 %reduce-window.6 = s32[16,9,128]{2,1,0:T(8,128)S(1)} reduce-window(s32[16,9,128]{2,1,0:T(8,128)S(1)} %fusion.60, s32[]{:T(128)} %constant.17.clone.1), window={size=1x1x128 pad=0_0x0_0x127_0}, to_apply=%region_6.7 | reduce-window | flops 2340864 | bytes 147460 | tf_op jit(solution)/shard_map/reduce-window
  35.1 1.2 fusion
  36.3 1.2 copy.107
  37.5 15.9 %all-to-all-done = bf16[4,192,640]{2,1,0:T(8,128)(2,1)S(1)} async-done(((bf16[4,192,640]{2,1,0:T(8,128)(2,1)}), bf16[4,192,640]{2,1,0:T(8,128)(2,1)S(1)}, u32[]{:S(2)}, u32[]{:S(2)}) %all-to-all-start) | async-done | bytes 983072 | tf_op jit(solution)/shard_map/all_to_all | solution.py:125
  53.6 1.0 add_convert_fusion.1
  54.6 19.6 %all-gather = bf16[768,640]{1,0:T(8,128)(2,1)S(1)} all-gather(bf16[192,640]{1,0:T(8,128)(2,1)S(1)} %add_convert_fusion.1), channel_id=2, replica_groups=mesh['req'=8,'tp'=4] {'tp'}, dimensions={0}, use_global_device_ids=true | all-gather | bytes 1228800 | tf_op jit(solution)/shard_map/all_gather | solution.py:131
  74.8 0.8 copy.109
  75.9 4.0 %convolution_convert_fusion.1 = bf16[8,96,2560]{2,1,0:T(8,128)(2,1)} fusion(bf16[192,2560,1]{1,0,2:T(8,128)(2,1)S(1)} %reshape.297, pred[192,8,2,96]{0,3,2,1:T(32,128)(4,1)} %bitcast.220), kind=kOutput, calls=%fused_computation.6 | convolution fusion | flops 756940800 | bytes 5111808 | tf_op jit(solution)/shard_map/tgc,td->gcd/dot_general | solution.py:143
  79.9 4.8 %all-to-all-start.1 = ((bf16[8,96,2560]{2,1,0:T(8,128)(2,1)}), bf16[8,96,2560]{2,1,0:T(8,128)(2,1)}, u32[]{:S(2)}, u32[]{:S(2)}) async-start(bf16[8,96,2560]{2,1,0:T(8,128)(2,1)} %convolution_convert_fusion.1), calls=%async_computation.1 | async-start | bytes 7864320 | tf_op jit(solution)/shard_map/all_to_all | solution.py:146
  84.7 3.2 %convolution_convert_fusion = bf16[8,96,2560]{2,1,0:T(8,128)(2,1)} fusion(bf16[192,2560,1]{1,0,2:T(8,128)(2,1)S(1)} %reshape.297, pred[192,8,2,96]{0,3,2,1:T(32,128)(4,1)S(1)} %bitcast.221), kind=kOutput, calls=%fused_computation.5 | convolution fusion | flops 756940800 | bytes 5111808 | tf_op jit(solution)/shard_map/tgc,td->gcd/dot_general | solution.py:143
  87.9 42.9 %all-to-all-done.1 = bf16[8,96,2560]{2,1,0:T(8,128)(2,1)} async-done(((bf16[8,96,2560]{2,1,0:T(8,128)(2,1)}), bf16[8,96,2560]{2,1,0:T(8,128)(2,1)}, u32[]{:S(2)}, u32[]{:S(2)}) %all-to-all-start.1) | async-done | bytes 3932192 | tf_op jit(solution)/shard_map/all_to_all | solution.py:146
  130.8 4.5 %all-to-all-start.3 = ((bf16[8,96,2560]{2,1,0:T(8,128)(2,1)}), bf16[8,96,2560]{2,1,0:T(8,128)(2,1)}, u32[]{:S(2)}, u32[]{:S(2)}) async-start(bf16[8,96,2560]{2,1,0:T(8,128)(2,1)} %convolution_convert_fusion), calls=%async_computation.3 | async-start | bytes 7864320 | tf_op jit(solution)/shard_map/all_to_all | solution.py:146
  135.4 7.6 %fusion.75 = (bf16[1,2560,2,384]{3,2,1,0:T(2,128)(2,1)S(1)}, bf16[1,2560,2,384]{3,2,1,0:T(2,128)(2,1)}) fusion(bf16[2,2560,2,384]{3,2,1,0:T(2,128)(2,1)} %param.30), kind=kLoop, calls=%fused_computation.137 | loop fusion | bytes 15728640 | tf_op jit(solution)/shard_map/slice | solution.py:149
  143.0 5.5 %fusion.2 = f32[768,2,384]{2,0,1:T(8,128)S(1)} fusion(bf16[768,2560,1]{1,0,2:T(8,128)(2,1)} %bitcast.34, bf16[1,2560,2,384]{3,2,1,0:T(2,128)(2,1)S(1)} %get-tuple-element.5), kind=kOutput, calls=%fused_computation.15 | convolution fusion | flops 3019898880 | bytes 10223616 | tf_op jit(solution)/shard_map/md,dcf->mcf/dot_general | solution.py:148
  148.5 4.1 %convolution_convert_fusion.3 = bf16[768,2560]{1,0:T(8,128)(2,1)} fusion(bf16[2,384,2560]{2,1,0:T(8,128)(2,1)S(1)} %copy-done.13, f32[768,2,384]{2,0,1:T(8,128)S(1)} %fusion.2), kind=kOutput, calls=%fused_computation.8 | convolution fusion | flops 1513684992 | bytes 8257536 | tf_op jit(solution)/shard_map/dot_general | solution.py:152
  152.6 29.1 %all-to-all-done.3 = bf16[8,96,2560]{2,1,0:T(8,128)(2,1)} async-done(((bf16[8,96,2560]{2,1,0:T(8,128)(2,1)}), bf16[8,96,2560]{2,1,0:T(8,128)(2,1)}, u32[]{:S(2)}, u32[]{:S(2)}) %all-to-all-start.3) | async-done | bytes 3932192 | tf_op jit(solution)/shard_map/all_to_all | solution.py:146
  181.7 4.5 %all-to-all-start.2 = ((bf16[8,96,2560]{2,1,0:T(8,128)(2,1)}), bf16[8,96,2560]{2,1,0:T(8,128)(2,1)}, u32[]{:S(2)}, u32[]{:S(2)}) async-start(bf16[8,96,2560]{2,1,0:T(8,128)(2,1)} %bitcast.217), calls=%async_computation.2 | async-start | bytes 7864320 | tf_op jit(solution)/shard_map/all_to_all | solution.py:154
  186.2 6.7 %fusion.1 = f32[768,2,384]{2,0,1:T(8,128)S(1)} fusion(bf16[768,2560,1]{1,0,2:T(8,128)(2,1)} %bitcast.45, bf16[1,2560,2,384]{3,2,1,0:T(2,128)(2,1)} %get-tuple-element.6), kind=kOutput, calls=%fused_computation.13 | convolution fusion | flops 3019898880 | bytes 10223616 | tf_op jit(solution)/shard_map/md,dcf->mcf/dot_general | solution.py:148
  192.9 4.1 %convolution_convert_fusion.2 = bf16[768,2560]{1,0:T(8,128)(2,1)} fusion(bf16[2,384,2560]{2,1,0:T(8,128)(2,1)S(1)} %copy-done.14, f32[768,2,384]{2,0,1:T(8,128)S(1)} %fusion.1), kind=kOutput, calls=%fused_computation.7 | convolution fusion | flops 1513684992 | bytes 8257536 | tf_op jit(solution)/shard_map/dot_general | solution.py:152
  197.0 35.5 %all-to-all-done.2 = bf16[8,96,2560]{2,1,0:T(8,128)(2,1)} async-done(((bf16[8,96,2560]{2,1,0:T(8,128)(2,1)}), bf16[8,96,2560]{2,1,0:T(8,128)(2,1)}, u32[]{:S(2)}, u32[]{:S(2)}) %all-to-all-start.2) | async-done | bytes 3932192 | tf_op jit(solution)/shard_map/all_to_all | solution.py:154
  232.5 4.8 %all-to-all-start.4 = ((bf16[8,96,2560]{2,1,0:T(8,128)(2,1)}), bf16[8,96,2560]{2,1,0:T(8,128)(2,1)}, u32[]{:S(2)}, u32[]{:S(2)}) async-start(bf16[8,96,2560]{2,1,0:T(8,128)(2,1)} %bitcast.216), calls=%async_computation.4 | async-start | bytes 7864320 | tf_op jit(solution)/shard_map/all_to_all | solution.py:154
  237.7 0.5 copy-done.9
  238.2 1.7 fusion.21
  240.0 1.2 select_reduce_fusion
  241.2 2.4 reshape.259
  243.6 0.5 copy.151
  244.1 0.5 subtract_convert_fusion
  244.6 0.5 copy-done.4
  245.1 4.0 %fusion.6 = f32[192,2,384]{2,0,1:T(8,128)} fusion(bf16[2560,2,384]{2,1,0:T(2,128)(2,1)} %param.32, f32[192,2560]{1,0:T(8,128)S(1)} %bitcast.214, f32[2560]{0:T(1024)S(1)} %copy-done.11, f32[192]{0:T(256)S(1)} %add_rsqrt_fusion), kind=kOutput, calls=%fused_computation.22 | convolution fusion | flops 756449280 | bytes 6499072 | tf_op jit(solution)/shard_map/td,dcf->tcf/dot_general | solution.py:173
  249.1 5.9 %convolution_bitcast_fusion.1 = f32[2,192,2560]{2,1,0:T(8,128)} fusion(bf16[8,96,2560]{2,1,0:T(8,128)(2,1)} %all-to-all-done.2, bf16[1,192,8,2,96]{4,1,2,0,3:T(8,128)(2,1)S(1)} %copy.151, bf16[1,192,8,2,96]{4,1,2,0,3:T(8,128)(2,1)S(1)} %subtract_convert_fusion), kind=kOutput, calls=%fused_computation.10 | convolution fusion | flops 1510244352 | bytes 9043968 | tf_op jit(solution)/shard_map/stgc,gcd->std/dot_general | solution.py:168
  255.0 28.4 %all-to-all-done.4 = bf16[8,96,2560]{2,1,0:T(8,128)(2,1)} async-done(((bf16[8,96,2560]{2,1,0:T(8,128)(2,1)}), bf16[8,96,2560]{2,1,0:T(8,128)(2,1)}, u32[]{:S(2)}, u32[]{:S(2)}) %all-to-all-start.4) | async-done | bytes 3932192 | tf_op jit(solution)/shard_map/all_to_all | solution.py:154
  283.4 4.1 %convolution_bitcast_fusion = f32[2,192,2560]{2,1,0:T(8,128)S(1)} fusion(bf16[8,96,2560]{2,1,0:T(8,128)(2,1)} %all-to-all-done.4, bf16[1,192,8,2,96]{4,1,2,0,3:T(8,128)(2,1)S(1)} %subtract_convert_fusion, bf16[1,192,8,2,96]{4,1,2,0,3:T(8,128)(2,1)S(1)} %copy.151), kind=kOutput, calls=%fused_computation.9 | convolution fusion | flops 1510244352 | bytes 9043968 | tf_op jit(solution)/shard_map/stgc,gcd->std/dot_general | solution.py:168
  287.5 0.8 fusion.8
  288.4 24.9 %all_to_all.30 = bf16[4,192,640]{2,1,0:T(8,128)(2,1)S(1)} all-to-all(bf16[4,192,640]{2,1,0:T(8,128)(2,1)S(1)} %bitcast.219), channel_id=1, replica_groups=mesh['req'=8,'tp'=4] {'tp'}, dimensions={0} | all-to-all | bytes 1966080 | tf_op jit(solution)/shard_map/all_to_all | solution.py:179
  313.4 0.7 add_convert_fusion
  (74 shorter events, 5.4 us)
Async XLA Ops:
  0.0 20.8 %copy-start = (bf16[640,2560]{1,0:T(8,128)(2,1)S(1)}, bf16[640,2560]{1,0:T(8,128)(2,1)}, u32[]{:S(2)}) copy-start(bf16[640,2560]{1,0:T(8,128)(2,1)} %param.26) | copy-start | bytes 9830404
  5.4 5.6 %copy-start.12 = (bf16[192,128]{1,0:T(8,128)(2,1)S(1)}, bf16[192,128]{1,0:T(8,128)(2,1)}, u32[]{:S(2)}) copy-start(bf16[192,128]{1,0:T(8,128)(2,1)} %param.18) | copy-start | bytes 147460
  8.9 2.2 copy-start.5
  11.0 1.9 copy-start.2
  11.4 2.4 copy-start.6
  16.9 3.5 %copy-start.7 = (f32[4,1,5,48,48]{3,4,2,0,1:T(8,128)S(1)}, f32[4,1,5,48,48]{3,4,2,0,1:T(8,128)}, u32[]{:S(2)}) copy-start(f32[4,1,5,48,48]{3,4,2,0,1:T(8,128)} %copy-done.6) | copy-start | bytes 552964
  16.9 3.5 %copy-start.16 = (bf16[192,128]{1,0:T(8,128)(2,1)S(1)}, bf16[192,128]{1,0:T(8,128)(2,1)}, u32[]{:S(2)}) copy-start(bf16[192,128]{1,0:T(8,128)(2,1)} %param.19) | copy-start | bytes 147460
  20.8 8.3 %copy-start.10 = (s32[192,6]{0,1:T(8,128)S(1)}, s32[192,6]{0,1:T(8,128)}, u32[]{:S(2)}) copy-start(s32[192,6]{0,1:T(8,128)} %param.29) | copy-start | bytes 13828
  20.8 14.3 %copy-start.11 = (f32[2560]{0:T(1024)S(1)}, f32[2560]{0:T(1024)}, u32[]{:S(2)}) copy-start(f32[2560]{0:T(1024)} %param.27) | copy-start | bytes 30724
  22.8 30.6 %all-to-all-start = ((bf16[4,192,640]{2,1,0:T(8,128)(2,1)}), bf16[4,192,640]{2,1,0:T(8,128)(2,1)S(1)}, u32[]{:S(2)}, u32[]{:S(2)}) async-start(bf16[4,192,640]{2,1,0:T(8,128)(2,1)} %bitcast.208), calls=%async_computation | async-start | bytes 1966080 | tf_op jit(solution)/shard_map/all_to_all | solution.py:125
  79.9 4.8 %copy-start.8 = (pred[192,1536]{0,1:T(32,128)(4,1)S(1)}, pred[192,1536]{0,1:T(32,128)(4,1)}, u32[]{:S(2)}) copy-start(pred[192,1536]{0,1:T(32,128)(4,1)} %copy.107) | copy-start | bytes 884740
  79.9 51.0 %all-to-all-start.1 = ((bf16[8,96,2560]{2,1,0:T(8,128)(2,1)}), bf16[8,96,2560]{2,1,0:T(8,128)(2,1)}, u32[]{:S(2)}, u32[]{:S(2)}) async-start(bf16[8,96,2560]{2,1,0:T(8,128)(2,1)} %convolution_convert_fusion.1), calls=%async_computation.1 | async-start | bytes 7864320 | tf_op jit(solution)/shard_map/all_to_all | solution.py:146
  130.8 50.8 %all-to-all-start.3 = ((bf16[8,96,2560]{2,1,0:T(8,128)(2,1)}), bf16[8,96,2560]{2,1,0:T(8,128)(2,1)}, u32[]{:S(2)}, u32[]{:S(2)}) async-start(bf16[8,96,2560]{2,1,0:T(8,128)(2,1)} %convolution_convert_fusion), calls=%async_computation.3 | async-start | bytes 7864320 | tf_op jit(solution)/shard_map/all_to_all | solution.py:146
  143.0 5.5 %copy-start.13 = (bf16[2,384,2560]{2,1,0:T(8,128)(2,1)S(1)}, bf16[2,384,2560]{2,1,0:T(8,128)(2,1)}, u32[]{:S(2)}) copy-start(bf16[2,384,2560]{2,1,0:T(8,128)(2,1)} %param.31) | copy-start | bytes 11796484
  181.7 50.8 %all-to-all-start.2 = ((bf16[8,96,2560]{2,1,0:T(8,128)(2,1)}), bf16[8,96,2560]{2,1,0:T(8,128)(2,1)}, u32[]{:S(2)}, u32[]{:S(2)}) async-start(bf16[8,96,2560]{2,1,0:T(8,128)(2,1)} %bitcast.217), calls=%async_computation.2 | async-start | bytes 7864320 | tf_op jit(solution)/shard_map/all_to_all | solution.py:154
  186.2 6.7 %copy-start.14 = (bf16[2,384,2560]{2,1,0:T(8,128)(2,1)S(1)}, bf16[2,384,2560]{2,1,0:T(8,128)(2,1)}, u32[]{:S(2)}) copy-start(bf16[2,384,2560]{2,1,0:T(8,128)(2,1)} %param.31) | copy-start | bytes 11796484
  232.5 50.9 %all-to-all-start.4 = ((bf16[8,96,2560]{2,1,0:T(8,128)(2,1)}), bf16[8,96,2560]{2,1,0:T(8,128)(2,1)}, u32[]{:S(2)}, u32[]{:S(2)}) async-start(bf16[8,96,2560]{2,1,0:T(8,128)(2,1)} %bitcast.216), calls=%async_computation.4 | async-start | bytes 7864320 | tf_op jit(solution)/shard_map/all_to_all | solution.py:154
  237.3 0.9 copy-start.9
  237.7 2.4 copy-start.3
  243.6 1.5 copy-start.4
  283.4 4.1 %copy-start.15 = (bf16[384,2560]{1,0:T(8,128)(2,1)S(1)}, bf16[384,2560]{1,0:T(8,128)(2,1)}, u32[]{:S(2)}) copy-start(bf16[384,2560]{1,0:T(8,128)(2,1)} %param.33) | copy-start | bytes 5898244
  283.4 4.1 %copy-start.17 = (f32[2,192,2560]{2,1,0:T(8,128)S(1)}, f32[2,192,2560]{2,1,0:T(8,128)}, u32[]{:S(2)}) copy-start(f32[2,192,2560]{2,1,0:T(8,128)} %convolution_bitcast_fusion.1) | copy-start | bytes 11796484
  283.4 4.1 %copy-start.18 = (f32[192,2,384]{2,0,1:T(8,128)S(1)}, f32[192,2,384]{2,0,1:T(8,128)}, u32[]{:S(2)}) copy-start(f32[192,2,384]{2,0,1:T(8,128)} %fusion.6) | copy-start | bytes 1769476
  287.5 26.6 %copy-start.1 = (bf16[640,2560]{1,0:T(8,128)(2,1)S(1)}, bf16[640,2560]{1,0:T(8,128)(2,1)}, u32[]{:S(2)}) copy-start(bf16[640,2560]{1,0:T(8,128)(2,1)} %param.26) | copy-start | bytes 9830404

commit v6 on v5

--- a/solution.py
+++ b/solution.py
@@ -137,14 +137,15 @@
     hidden_part = hidden_part_bf.astype(jnp.float32)
 
     dispatch = jnp.any(hit, axis=1).astype(jnp.bfloat16)
-    dispatch = dispatch.reshape(row_count, groups, experts_local, capacity)
+    dispatch = dispatch.reshape(row_count, groups, experts_local * capacity)
+    outbox = jnp.einsum(
+        "tgc,td->gcd", dispatch, normed_bf, preferred_element_type=jnp.float32
+    ).astype(jnp.bfloat16)
+    arrived = lax.all_to_all(outbox, "req", split_axis=0, concat_axis=0, tiled=True)
+    arrived = arrived.reshape(groups, experts_local, capacity, model_width)
     returns = []
     for expert in range(experts_local):
-        outbox = jnp.einsum(
-            "tgc,td->gcd", dispatch[:, :, expert], normed_bf, preferred_element_type=jnp.float32
-        ).astype(jnp.bfloat16)
-        arrived = lax.all_to_all(outbox, "req", split_axis=0, concat_axis=0, tiled=True)
-        rows = arrived.reshape(groups * capacity, model_width)
+        rows = arrived[:, expert].reshape(groups * capacity, model_width)
         gate_up = jnp.einsum(
             "md,dcf->mcf", rows, expert_gate_up[expert], preferred_element_type=jnp.float32
         )

time: 316 us -> 318 us (level)
  waiting for transfers between devices: 152 us -> 160 us
  matrix products: 53.3 us -> 47.3 us
  starting transfers between devices: 24.9 us -> 20.7 us
  local copies, waits for them, and re-layouts: 25.8 us -> 29.9 us
    all_to_all x2 -> x1, waiting for transfers between devices: 72 us -> 80.3 us  [shards(): lax.all_to_all(outbox, 'req', split_axis=0, concat_axis=0, tiled=True)]
    slice x1 -> x2, local copies, waits for them, and re-layouts: 0.43 us -> 5.42 us  [the longest x1 4.99 us: shards(): rows = arrived[:, expert].reshape(groups * capacity, model_width)]
    all_to_all x2 -> x1, starting transfers between devices: 9.34 us -> 5.08 us  [shards(): lax.all_to_all(outbox, 'req', split_axis=0, concat_axis=0, tiled=True)]
    dot_general x2 -> x1, matrix products: 7.13 us -> 6.35 us  [shards(): jnp.einsum('tgc,td->gcd', dispatch, normed_bf, preferred_element_type=jnp...]
  transfers between devices with their start and end apart: 5 -> 4, of which waited for: 5 -> 4; matrix products, arithmetic and copies ran while one was open for 18% -> 14% of each run, Pallas kernels for 0% -> 0%
where the time goes in v6:
time: 318 us; the launch traced here: 316 us
  waiting for transfers between devices  160 us (50%)
  matrix products  47.3 us (15%)
  blocking collectives  44.5 us (14%)
  local copies, waits for them, and re-layouts  29.9 us (9%)
  starting transfers between devices  20.7 us (7%)
  other arithmetic  13.3 us (4%)
    all_to_all x1, waiting for transfers between devices, shards(): lax.all_to_all(outbox, 'req', split_axis=0, concat_axis=0, tiled=True)  80.3 us
    all_to_all x2, waiting for transfers between devices, shards(): lax.all_to_all(outputs, 'req', split_axis=0, concat_axis=0, tiled=True)  63.9 us
    all_to_all x1, blocking collectives, shards(): lax.all_to_all(total.transpose(1, 0, 2), 'tp', split_axis=0, concat_axis=...  24.9 us
    all_gather x1, blocking collectives, shards(): hidden_bf = lax.all_gather(hidden_part_bf[None], 'tp', axis=0, tiled=True)  19.6 us
    all_to_all x1, waiting for transfers between devices, shards(): lax.all_to_all(attn_blocks.transpose(1, 0, 2), 'tp', split_axis=0, concat...  15.9 us
    dot_general x2, matrix products, shards(): jnp.einsum('stgc,gcd->std', weights_split[:, :, :, expert], returns[exper...  9.96 us
    dot_general x2, matrix products, shards(): jnp.einsum('md,dcf->mcf', rows, expert_gate_up[expert], preferred_element...  9.86 us
    all_to_all x2, starting transfers between devices, shards(): lax.all_to_all(outputs, 'req', split_axis=0, concat_axis=0, tiled=True)  9.26 us
  transfers between devices with their start and end apart: 4, of which 4 were waited for; matrix products, arithmetic and copies ran while one was open for 14% of the time, Pallas kernels for 0%

profile of v6, /device:TPU:0, one launch (start us, length us, event | category | flops | bytes accessed | tf_op | source)
XLA Modules:
  0.0 316.4 jit_solution(1201947144800542310)
XLA Ops:
  0.0 0.8 compare_select_fusion
  1.0 0.9 iota_compare_fusion.6
  1.9 2.9 gather_fusion
  4.8 2.9 gather_fusion.1
  7.7 1.0 reshape.239
  10.3 2.1 bitcast_reduce_fusion
  12.4 0.4 fusion.77
  12.8 1.0 fusion.9
  14.0 1.3 fusion.16
  15.7 0.9 convolution_convert_fusion.3
  16.6 1.0 copy.148
  17.7 6.3 %all-to-all-start = ((bf16[4,192,640]{2,1,0:T(8,128)(2,1)}), bf16[4,192,640]{2,1,0:T(8,128)(2,1)S(1)}, u32[]{:S(2)}, u32[]{:S(2)}) async-start(bf16[4,192,640]{2,1,0:T(8,128)(2,1)} %bitcast.199), calls=%async_computation | async-start | bytes 1966080 | tf_op jit(solution)/shard_map/all_to_all | solution.py:125
  24.4 4.5 %reduce-window.6 = s32[16,9,128]{2,1,0:T(8,128)S(1)} reduce-window(s32[16,9,128]{2,1,0:T(8,128)S(1)} %fusion.60, s32[]{:T(128)} %constant.17.clone.1), window={size=1x1x128 pad=0_0x0_0x127_0}, to_apply=%region_6.7 | reduce-window | flops 2340864 | bytes 147460 | tf_op jit(solution)/shard_map/reduce-window
  29.0 0.4 slice_reduce_fusion
  29.9 1.2 fusion
  31.1 1.2 copy.113
  32.4 15.9 %all-to-all-done = bf16[4,192,640]{2,1,0:T(8,128)(2,1)S(1)} async-done(((bf16[4,192,640]{2,1,0:T(8,128)(2,1)}), bf16[4,192,640]{2,1,0:T(8,128)(2,1)S(1)}, u32[]{:S(2)}, u32[]{:S(2)}) %all-to-all-start) | async-done | bytes 983072 | tf_op jit(solution)/shard_map/all_to_all | solution.py:125
  48.4 1.0 add_convert_fusion.1
  49.4 19.6 %all-gather = bf16[768,640]{1,0:T(8,128)(2,1)S(1)} all-gather(bf16[192,640]{1,0:T(8,128)(2,1)S(1)} %add_convert_fusion.1), channel_id=2, replica_groups=mesh['req'=8,'tp'=4] {'tp'}, dimensions={0}, use_global_device_ids=true | all-gather | bytes 1228800 | tf_op jit(solution)/shard_map/all_gather | solution.py:131
  69.6 0.8 copy.101
  70.4 0.4 reshape.283
  70.8 6.3 %convolution_convert_fusion = bf16[8,192,2560]{2,1,0:T(8,128)(2,1)} fusion(pred[192,8,192]{0,2,1:T(32,128)(4,1)} %bitcast.213, bf16[192,2560,1]{1,0,2:T(8,128)(2,1)S(1)} %reshape.283), kind=kOutput, calls=%fused_computation.5 | convolution fusion | flops 1513881600 | bytes 9142272 | tf_op jit(solution)/shard_map/tgc,td->gcd/dot_general | solution.py:141
  77.1 5.1 %all-to-all-start.1 = ((bf16[8,192,2560]{2,1,0:T(8,128)(2,1)}), bf16[8,192,2560]{2,1,0:T(8,128)(2,1)}, u32[]{:S(2)}, u32[]{:S(2)}) async-start(bf16[8,192,2560]{2,1,0:T(8,128)(2,1)} %convolution_convert_fusion), calls=%async_computation.1 | async-start | bytes 15728640 | tf_op jit(solution)/shard_map/all_to_all | solution.py:144
  82.2 8.1 %fusion.75 = (bf16[1,2560,2,384]{3,2,1,0:T(2,128)(2,1)}, bf16[1,2560,2,384]{3,2,1,0:T(2,128)(2,1)}) fusion(bf16[2,2560,2,384]{3,2,1,0:T(2,128)(2,1)} %param.30), kind=kLoop, calls=%fused_computation.134 | loop fusion | bytes 15728640 | tf_op jit(solution)/shard_map/slice | solution.py:150
  90.3 80.3 %all-to-all-done.1 = bf16[8,192,2560]{2,1,0:T(8,128)(2,1)} async-done(((bf16[8,192,2560]{2,1,0:T(8,128)(2,1)}), bf16[8,192,2560]{2,1,0:T(8,128)(2,1)}, u32[]{:S(2)}, u32[]{:S(2)}) %all-to-all-start.1) | async-done | bytes 7864352 | tf_op jit(solution)/shard_map/all_to_all | solution.py:144
  170.6 5.0 %fusion.76 = (bf16[8,1,96,2560]{3,2,1,0:T(8,128)(2,1)}, bf16[8,1,96,2560]{3,2,1,0:T(8,128)(2,1)S(1)}) fusion(bf16[8,2,96,2560]{3,2,1,0:T(8,128)(2,1)} %bitcast.32), kind=kLoop, calls=%fused_computation.135 | loop fusion | bytes 15728640 | tf_op jit(solution)/shard_map/slice | solution.py:148
  175.6 0.9 copy-done.4
  176.5 3.2 %fusion.1 = f32[768,2,384]{2,0,1:T(8,128)S(1)} fusion(bf16[768,2560,1]{1,0,2:T(8,128)(2,1)S(1)} %bitcast.212, bf16[1,2560,2,384]{3,2,1,0:T(2,128)(2,1)S(1)} %copy-done.4), kind=kOutput, calls=%fused_computation.12 | convolution fusion | flops 3019898880 | bytes 10223616 | tf_op jit(solution)/shard_map/md,dcf->mcf/dot_general | solution.py:149
  179.7 4.2 %convolution_convert_fusion.1 = bf16[768,2560]{1,0:T(8,128)(2,1)} fusion(bf16[2,384,2560]{2,1,0:T(8,128)(2,1)S(1)} %copy-done.12, f32[768,2,384]{2,0,1:T(8,128)S(1)} %fusion.1), kind=kOutput, calls=%fused_computation.6 | convolution fusion | flops 1513684992 | bytes 8257536 | tf_op jit(solution)/shard_map/dot_general | solution.py:153
  183.9 4.5 %all-to-all-start.3 = ((bf16[8,96,2560]{2,1,0:T(8,128)(2,1)}), bf16[8,96,2560]{2,1,0:T(8,128)(2,1)}, u32[]{:S(2)}, u32[]{:S(2)}) async-start(bf16[8,96,2560]{2,1,0:T(8,128)(2,1)} %bitcast.208), calls=%async_computation.3 | async-start | bytes 7864320 | tf_op jit(solution)/shard_map/all_to_all | solution.py:155
  188.4 6.7 %fusion.2 = f32[768,2,384]{2,0,1:T(8,128)S(1)} fusion(bf16[768,2560,1]{1,0,2:T(8,128)(2,1)} %bitcast.211, bf16[1,2560,2,384]{3,2,1,0:T(2,128)(2,1)} %get-tuple-element.5), kind=kOutput, calls=%fused_computation.14 | convolution fusion | flops 3019898880 | bytes 10223616 | tf_op jit(solution)/shard_map/md,dcf->mcf/dot_general | solution.py:149
  195.1 4.1 %convolution_convert_fusion.2 = bf16[768,2560]{1,0:T(8,128)(2,1)} fusion(bf16[2,384,2560]{2,1,0:T(8,128)(2,1)S(1)} %copy-done.13, f32[768,2,384]{2,0,1:T(8,128)S(1)} %fusion.2), kind=kOutput, calls=%fused_computation.7 | convolution fusion | flops 1513684992 | bytes 8257536 | tf_op jit(solution)/shard_map/dot_general | solution.py:153
  199.2 35.5 %all-to-all-done.3 = bf16[8,96,2560]{2,1,0:T(8,128)(2,1)} async-done(((bf16[8,96,2560]{2,1,0:T(8,128)(2,1)}), bf16[8,96,2560]{2,1,0:T(8,128)(2,1)}, u32[]{:S(2)}, u32[]{:S(2)}) %all-to-all-start.3) | async-done | bytes 3932192 | tf_op jit(solution)/shard_map/all_to_all | solution.py:155
  234.8 4.8 %all-to-all-start.2 = ((bf16[8,96,2560]{2,1,0:T(8,128)(2,1)}), bf16[8,96,2560]{2,1,0:T(8,128)(2,1)}, u32[]{:S(2)}, u32[]{:S(2)}) async-start(bf16[8,96,2560]{2,1,0:T(8,128)(2,1)} %bitcast.207), calls=%async_computation.2 | async-start | bytes 7864320 | tf_op jit(solution)/shard_map/all_to_all | solution.py:155
  239.9 0.5 copy-done.8
  240.4 1.7 fusion.21
  242.3 1.2 select_reduce_fusion
  243.4 2.4 reshape.246
  245.8 0.5 copy.142
  246.3 0.5 subtract_convert_fusion
  246.8 0.5 copy-done.3
  247.3 4.0 %fusion.6 = f32[192,2,384]{2,0,1:T(8,128)} fusion(bf16[2560,2,384]{2,1,0:T(2,128)(2,1)} %param.32, f32[192,2560]{1,0:T(8,128)S(1)} %bitcast.205, f32[2560]{0:T(1024)S(1)} %copy-done.10, f32[192]{0:T(256)S(1)} %add_rsqrt_fusion), kind=kOutput, calls=%fused_computation.21 | convolution fusion | flops 756449280 | bytes 6499072 | tf_op jit(solution)/shard_map/td,dcf->tcf/dot_general | solution.py:174
  251.3 5.9 %convolution_bitcast_fusion = f32[2,192,2560]{2,1,0:T(8,128)} fusion(bf16[8,96,2560]{2,1,0:T(8,128)(2,1)} %all-to-all-done.3, bf16[1,192,8,2,96]{4,1,2,0,3:T(8,128)(2,1)S(1)} %subtract_convert_fusion, bf16[1,192,8,2,96]{4,1,2,0,3:T(8,128)(2,1)S(1)} %copy.142), kind=kOutput, calls=%fused_computation.8 | convolution fusion | flops 1510244352 | bytes 9043968 | tf_op jit(solution)/shard_map/stgc,gcd->std/dot_general | solution.py:169
  257.2 28.4 %all-to-all-done.2 = bf16[8,96,2560]{2,1,0:T(8,128)(2,1)} async-done(((bf16[8,96,2560]{2,1,0:T(8,128)(2,1)}), bf16[8,96,2560]{2,1,0:T(8,128)(2,1)}, u32[]{:S(2)}, u32[]{:S(2)}) %all-to-all-start.2) | async-done | bytes 3932192 | tf_op jit(solution)/shard_map/all_to_all | solution.py:155
  285.6 4.1 %convolution_bitcast_fusion.1 = f32[2,192,2560]{2,1,0:T(8,128)S(1)} fusion(bf16[8,96,2560]{2,1,0:T(8,128)(2,1)} %all-to-all-done.2, bf16[1,192,8,2,96]{4,1,2,0,3:T(8,128)(2,1)S(1)} %copy.142, bf16[1,192,8,2,96]{4,1,2,0,3:T(8,128)(2,1)S(1)} %subtract_convert_fusion), kind=kOutput, calls=%fused_computation.9 | convolution fusion | flops 1510244352 | bytes 9043968 | tf_op jit(solution)/shard_map/stgc,gcd->std/dot_general | solution.py:169
  289.7 0.8 fusion.8
  290.6 24.9 %all_to_all.25 = bf16[4,192,640]{2,1,0:T(8,128)(2,1)S(1)} all-to-all(bf16[4,192,640]{2,1,0:T(8,128)(2,1)S(1)} %bitcast.210), channel_id=1, replica_groups=mesh['req'=8,'tp'=4] {'tp'}, dimensions={0} | all-to-all | bytes 1966080 | tf_op jit(solution)/shard_map/all_to_all | solution.py:180
  315.6 0.7 add_convert_fusion
  (72 shorter events, 4.4 us)
Async XLA Ops:
  0.0 15.7 %copy-start = (bf16[640,2560]{1,0:T(8,128)(2,1)S(1)}, bf16[640,2560]{1,0:T(8,128)(2,1)}, u32[]{:S(2)}) copy-start(bf16[640,2560]{1,0:T(8,128)(2,1)} %param.26) | copy-start | bytes 9830404
  0.0 7.7 %copy-start.7 = (bf16[192,640]{1,0:T(8,128)(2,1)S(1)}, bf16[192,640]{1,0:T(8,128)(2,1)}, u32[]{:S(2)}) copy-start(bf16[192,640]{1,0:T(8,128)(2,1)} %param.17) | copy-start | bytes 737284
  0.0 8.7 %copy-start.16 = (s32[4,48]{1,0:T(4,128)S(1)}, s32[4,48]{1,0:T(4,128)}, u32[]{:S(2)}) copy-start(s32[4,48]{1,0:T(4,128)} %param.24) | copy-start | bytes 2308
  8.7 3.7 %copy-start.11 = (bf16[192,128]{1,0:T(8,128)(2,1)S(1)}, bf16[192,128]{1,0:T(8,128)(2,1)}, u32[]{:S(2)}) copy-start(bf16[192,128]{1,0:T(8,128)(2,1)} %param.18) | copy-start | bytes 147460
  10.3 2.2 copy-start.5
  12.4 1.5 copy-start.6
  14.0 1.3 copy-start.15
  15.7 8.3 %copy-start.9 = (s32[192,6]{0,1:T(8,128)S(1)}, s32[192,6]{0,1:T(8,128)}, u32[]{:S(2)}) copy-start(s32[192,6]{0,1:T(8,128)} %param.29) | copy-start | bytes 13828
  16.6 15.7 %copy-start.10 = (f32[2560]{0:T(1024)S(1)}, f32[2560]{0:T(1024)}, u32[]{:S(2)}) copy-start(f32[2560]{0:T(1024)} %param.27) | copy-start | bytes 30724
  17.7 30.6 %all-to-all-start = ((bf16[4,192,640]{2,1,0:T(8,128)(2,1)}), bf16[4,192,640]{2,1,0:T(8,128)(2,1)S(1)}, u32[]{:S(2)}, u32[]{:S(2)}) async-start(bf16[4,192,640]{2,1,0:T(8,128)(2,1)} %bitcast.199), calls=%async_computation | async-start | bytes 1966080 | tf_op jit(solution)/shard_map/all_to_all | solution.py:125
  77.1 93.5 %all-to-all-start.1 = ((bf16[8,192,2560]{2,1,0:T(8,128)(2,1)}), bf16[8,192,2560]{2,1,0:T(8,128)(2,1)}, u32[]{:S(2)}, u32[]{:S(2)}) async-start(bf16[8,192,2560]{2,1,0:T(8,128)(2,1)} %convolution_convert_fusion), calls=%async_computation.1 | async-start | bytes 15728640 | tf_op jit(solution)/shard_map/all_to_all | solution.py:144
  170.6 5.8 %copy-start.4 = (bf16[1,2560,2,384]{3,2,1,0:T(2,128)(2,1)S(1)}, bf16[1,2560,2,384]{3,2,1,0:T(2,128)(2,1)}, u32[]{:S(2)}) copy-start(bf16[1,2560,2,384]{3,2,1,0:T(2,128)(2,1)} %get-tuple-element.6) | copy-start | bytes 11796484
  176.5 3.2 %copy-start.12 = (bf16[2,384,2560]{2,1,0:T(8,128)(2,1)S(1)}, bf16[2,384,2560]{2,1,0:T(8,128)(2,1)}, u32[]{:S(2)}) copy-start(bf16[2,384,2560]{2,1,0:T(8,128)(2,1)} %param.31) | copy-start | bytes 11796484
  183.9 50.8 %all-to-all-start.3 = ((bf16[8,96,2560]{2,1,0:T(8,128)(2,1)}), bf16[8,96,2560]{2,1,0:T(8,128)(2,1)}, u32[]{:S(2)}, u32[]{:S(2)}) async-start(bf16[8,96,2560]{2,1,0:T(8,128)(2,1)} %bitcast.208), calls=%async_computation.3 | async-start | bytes 7864320 | tf_op jit(solution)/shard_map/all_to_all | solution.py:155
  188.4 6.7 %copy-start.13 = (bf16[2,384,2560]{2,1,0:T(8,128)(2,1)S(1)}, bf16[2,384,2560]{2,1,0:T(8,128)(2,1)}, u32[]{:S(2)}) copy-start(bf16[2,384,2560]{2,1,0:T(8,128)(2,1)} %param.31) | copy-start | bytes 11796484
  234.8 50.9 %all-to-all-start.2 = ((bf16[8,96,2560]{2,1,0:T(8,128)(2,1)}), bf16[8,96,2560]{2,1,0:T(8,128)(2,1)}, u32[]{:S(2)}, u32[]{:S(2)}) async-start(bf16[8,96,2560]{2,1,0:T(8,128)(2,1)} %bitcast.207), calls=%async_computation.2 | async-start | bytes 7864320 | tf_op jit(solution)/shard_map/all_to_all | solution.py:155
  239.5 0.9 copy-start.8
  239.9 2.4 copy-start.2
  245.8 1.5 copy-start.3
  285.6 4.1 %copy-start.14 = (bf16[384,2560]{1,0:T(8,128)(2,1)S(1)}, bf16[384,2560]{1,0:T(8,128)(2,1)}, u32[]{:S(2)}) copy-start(bf16[384,2560]{1,0:T(8,128)(2,1)} %param.33) | copy-start | bytes 5898244
  285.6 4.1 %copy-start.17 = (f32[2,192,2560]{2,1,0:T(8,128)S(1)}, f32[2,192,2560]{2,1,0:T(8,128)}, u32[]{:S(2)}) copy-start(f32[2,192,2560]{2,1,0:T(8,128)} %convolution_bitcast_fusion) | copy-start | bytes 11796484
  285.6 4.1 %copy-start.18 = (f32[192,2,384]{2,0,1:T(8,128)S(1)}, f32[192,2,384]{2,0,1:T(8,128)}, u32[]{:S(2)}) copy-start(f32[192,2,384]{2,0,1:T(8,128)} %fusion.6) | copy-start | bytes 1769476
  289.7 26.6 %copy-start.1 = (bf16[640,2560]{1,0:T(8,128)(2,1)S(1)}, bf16[640,2560]{1,0:T(8,128)(2,1)}, u32[]{:S(2)}) copy-start(bf16[640,2560]{1,0:T(8,128)(2,1)} %param.26) | copy-start | bytes 9830404

commit v7 on v5

--- a/solution.py
+++ b/solution.py
@@ -150,7 +150,14 @@
         )
         act = (jax.nn.silu(gate_up[:, 0]) * gate_up[:, 1]).astype(jnp.bfloat16)
         partial_value = jnp.dot(act, expert_down[expert], preferred_element_type=jnp.float32)
-        outputs = partial_value.astype(jnp.bfloat16).reshape(groups, capacity, model_width)
+        partial_bf = partial_value.astype(jnp.bfloat16)
+        if expert < experts_local - 1:
+            outputs = partial_bf.reshape(groups, capacity, model_width)
+        else:
+            outputs = lax.psum_scatter(
+                partial_bf.reshape(-1, tp_count, part_width).transpose(1, 0, 2),
+                "tp", scatter_dimension=0, tiled=True,
+            ).reshape(groups, capacity, part_width)
         returns.append(lax.all_to_all(outputs, "req", split_axis=0, concat_axis=0, tiled=True))
 
     chosen = jnp.sum(
@@ -169,7 +176,11 @@
             "stgc,gcd->std", weights_split[:, :, :, expert], returns[expert],
             preferred_element_type=jnp.float32,
         )
-        routed = routed + both[0] + both[1]
+        if expert < experts_local - 1:
+            routed = routed + both[0] + both[1]
+        else:
+            routed_last = both[0] + both[1]
+
     shared_gu = jnp.einsum(
         "td,dcf->tcf", normed_bf, shared_gate_up, preferred_element_type=jnp.float32
     )
@@ -177,7 +188,7 @@
     shared_terms = jnp.dot(shared_act, shared_down, preferred_element_type=jnp.float32)
     total = (shared_terms + routed).astype(jnp.bfloat16).reshape(row_count, tp_count, part_width)
     total = lax.all_to_all(total.transpose(1, 0, 2), "tp", split_axis=0, concat_axis=0, tiled=True)
-    summed = jnp.sum(total.astype(jnp.float32), axis=0)
+    summed = jnp.sum(total.astype(jnp.float32), axis=0) + routed_last
     return (hidden_part + summed).astype(jnp.bfloat16)
 
 

time: 316 us -> 306 us (0.968)
  waiting for transfers between devices: 152 us -> 135 us
  between operations: 0.56 us -> 14 us
  matrix products: 53.3 us -> 44.2 us
  other arithmetic: 13.2 us -> 16.6 us
    all_to_all x2, waiting for transfers between devices: 63.9 us -> 47.2 us  [shards(): lax.all_to_all(outputs, 'req', split_axis=0, concat_axis=0, tiled=True)]
    dot_general x2, matrix products: 9.96 us -> 6.27 us  [shards(): jnp.einsum('stgc,gcd->std', weights_split[:, :, :, expert], returns[exper...]
  transfers between devices with their start and end apart: 5 -> 6, of which waited for: 5 -> 5; matrix products, arithmetic and copies ran while one was open for 18% -> 19% of each run, Pallas kernels for 0% -> 0%
where the time goes in v7:
time: 306 us; the launch traced here: 305 us
  waiting for transfers between devices  135 us (44%)
  blocking collectives  44.5 us (15%)
  matrix products  44.2 us (14%)
  local copies, waits for them, and re-layouts  25.8 us (8%)
  starting transfers between devices  25.6 us (8%)
  other arithmetic  16.6 us (5%)
  between operations  14 us (5%)
    all_to_all x2, waiting for transfers between devices, shards(): lax.all_to_all(outbox, 'req', split_axis=0, concat_axis=0, tiled=True)  71.7 us
    all_to_all x2, waiting for transfers between devices, shards(): lax.all_to_all(outputs, 'req', split_axis=0, concat_axis=0, tiled=True)  47.2 us
    all_to_all x1, blocking collectives, shards(): lax.all_to_all(total.transpose(1, 0, 2), 'tp', split_axis=0, concat_axis=...  24.9 us
    all_gather x1, blocking collectives, shards(): hidden_bf = lax.all_gather(hidden_part_bf[None], 'tp', axis=0, tiled=True)  19.6 us
    all_to_all x1, waiting for transfers between devices, shards(): lax.all_to_all(attn_blocks.transpose(1, 0, 2), 'tp', split_axis=0, concat...  15.9 us
    dot_general x2, matrix products, shards(): jnp.einsum('md,dcf->mcf', rows, expert_gate_up[expert], preferred_element...  12.1 us
    all_to_all x2, starting transfers between devices, shards(): lax.all_to_all(outputs, 'req', split_axis=0, concat_axis=0, tiled=True)  9.86 us
    all_to_all x2, starting transfers between devices, shards(): lax.all_to_all(outbox, 'req', split_axis=0, concat_axis=0, tiled=True)  9.35 us
  transfers between devices with their start and end apart: 6, of which 5 were waited for; matrix products, arithmetic and copies ran while one was open for 19% of the time, Pallas kernels for 0%

profile of v7, /device:TPU:0, one launch (start us, length us, event | category | flops | bytes accessed | tf_op | source)
XLA Modules:
  0.0 305.5 jit_solution(14694922301764383667)
XLA Ops:
  6.6 0.8 compare_select_fusion
  7.5 0.9 iota_compare_fusion.6
  8.4 2.9 gather_fusion
  11.3 2.9 gather_fusion.1
  14.2 1.0 reshape.254
  16.8 2.1 bitcast_reduce_fusion
  19.4 1.0 fusion.8
  20.5 1.3 fusion.15
  22.2 0.9 convolution_convert_fusion.4
  23.2 1.0 copy.164
  24.2 6.3 %all-to-all-start = ((bf16[4,192,640]{2,1,0:T(8,128)(2,1)}), bf16[4,192,640]{2,1,0:T(8,128)(2,1)S(1)}, u32[]{:S(2)}, u32[]{:S(2)}) async-start(bf16[4,192,640]{2,1,0:T(8,128)(2,1)} %bitcast.223), calls=%async_computation | async-start | bytes 1966080 | tf_op jit(solution)/shard_map/all_to_all | solution.py:125
  31.0 4.5 %reduce-window.6 = s32[16,9,128]{2,1,0:T(8,128)S(1)} reduce-window(s32[16,9,128]{2,1,0:T(8,128)S(1)} %fusion.64, s32[]{:T(128)} %constant.17.clone.1), window={size=1x1x128 pad=0_0x0_0x127_0}, to_apply=%region_6.7 | reduce-window | flops 2340864 | bytes 147460 | tf_op jit(solution)/shard_map/reduce-window
  36.5 1.2 fusion
  37.7 1.2 copy.110
  38.9 15.9 %all-to-all-done = bf16[4,192,640]{2,1,0:T(8,128)(2,1)S(1)} async-done(((bf16[4,192,640]{2,1,0:T(8,128)(2,1)}), bf16[4,192,640]{2,1,0:T(8,128)(2,1)S(1)}, u32[]{:S(2)}, u32[]{:S(2)}) %all-to-all-start) | async-done | bytes 983072 | tf_op jit(solution)/shard_map/all_to_all | solution.py:125
  55.0 1.0 add_convert_fusion
  56.0 19.6 %all-gather = bf16[768,640]{1,0:T(8,128)(2,1)S(1)} all-gather(bf16[192,640]{1,0:T(8,128)(2,1)S(1)} %add_convert_fusion), channel_id=2, replica_groups=mesh['req'=8,'tp'=4] {'tp'}, dimensions={0}, use_global_device_ids=true | all-gather | bytes 1228800 | tf_op jit(solution)/shard_map/all_gather | solution.py:131
  76.1 0.8 copy.112
  77.3 4.0 %convolution_convert_fusion = bf16[8,96,2560]{2,1,0:T(8,128)(2,1)} fusion(bf16[192,2560,1]{1,0,2:T(8,128)(2,1)S(1)} %reshape.300, pred[192,8,2,96]{0,3,2,1:T(32,128)(4,1)} %bitcast.236), kind=kOutput, calls=%fused_computation.5 | convolution fusion | flops 756940800 | bytes 5111808 | tf_op jit(solution)/shard_map/tgc,td->gcd/dot_general | solution.py:143
  81.3 4.8 %all-to-all-start.4 = ((bf16[8,96,2560]{2,1,0:T(8,128)(2,1)}), bf16[8,96,2560]{2,1,0:T(8,128)(2,1)}, u32[]{:S(2)}, u32[]{:S(2)}) async-start(bf16[8,96,2560]{2,1,0:T(8,128)(2,1)} %convolution_convert_fusion), calls=%async_computation.4 | async-start | bytes 7864320 | tf_op jit(solution)/shard_map/all_to_all | solution.py:146
  86.2 3.1 %convolution_convert_fusion.1 = bf16[8,96,2560]{2,1,0:T(8,128)(2,1)} fusion(bf16[192,2560,1]{1,0,2:T(8,128)(2,1)S(1)} %reshape.300, pred[192,8,2,96]{0,3,2,1:T(32,128)(4,1)S(1)} %bitcast.237), kind=kOutput, calls=%fused_computation.6 | convolution fusion | flops 756940800 | bytes 5111808 | tf_op jit(solution)/shard_map/tgc,td->gcd/dot_general | solution.py:143
  89.3 43.0 %all-to-all-done.4 = bf16[8,96,2560]{2,1,0:T(8,128)(2,1)} async-done(((bf16[8,96,2560]{2,1,0:T(8,128)(2,1)}), bf16[8,96,2560]{2,1,0:T(8,128)(2,1)}, u32[]{:S(2)}, u32[]{:S(2)}) %all-to-all-start.4) | async-done | bytes 3932192 | tf_op jit(solution)/shard_map/all_to_all | solution.py:146
  132.3 4.5 %all-to-all-start.1 = ((bf16[8,96,2560]{2,1,0:T(8,128)(2,1)}), bf16[8,96,2560]{2,1,0:T(8,128)(2,1)}, u32[]{:S(2)}, u32[]{:S(2)}) async-start(bf16[8,96,2560]{2,1,0:T(8,128)(2,1)} %convolution_convert_fusion.1), calls=%async_computation.1 | async-start | bytes 7864320 | tf_op jit(solution)/shard_map/all_to_all | solution.py:146
  136.9 7.6 %fusion.79 = (bf16[1,2560,2,384]{3,2,1,0:T(2,128)(2,1)S(1)}, bf16[1,2560,2,384]{3,2,1,0:T(2,128)(2,1)}) fusion(bf16[2,2560,2,384]{3,2,1,0:T(2,128)(2,1)} %param.30), kind=kLoop, calls=%fused_computation.140 | loop fusion | bytes 15728640 | tf_op jit(solution)/shard_map/slice | solution.py:149
  144.5 5.5 %fusion.1 = f32[768,2,384]{2,0,1:T(8,128)S(1)} fusion(bf16[768,2560,1]{1,0,2:T(8,128)(2,1)} %bitcast.47, bf16[1,2560,2,384]{3,2,1,0:T(2,128)(2,1)S(1)} %get-tuple-element.5), kind=kOutput, calls=%fused_computation.13 | convolution fusion | flops 3019898880 | bytes 10223616 | tf_op jit(solution)/shard_map/md,dcf->mcf/dot_general | solution.py:148
  150.0 2.2 convolution_convert_fusion.2
  152.2 2.2 copy.162
  154.5 28.7 %all-to-all-done.1 = bf16[8,96,2560]{2,1,0:T(8,128)(2,1)} async-done(((bf16[8,96,2560]{2,1,0:T(8,128)(2,1)}), bf16[8,96,2560]{2,1,0:T(8,128)(2,1)}, u32[]{:S(2)}, u32[]{:S(2)}) %all-to-all-start.1) | async-done | bytes 3932192 | tf_op jit(solution)/shard_map/all_to_all | solution.py:146
  183.2 6.7 %fusion.2 = f32[768,2,384]{2,0,1:T(8,128)S(1)} fusion(bf16[768,2560,1]{1,0,2:T(8,128)(2,1)} %bitcast.34, bf16[1,2560,2,384]{3,2,1,0:T(2,128)(2,1)} %get-tuple-element.6), kind=kOutput, calls=%fused_computation.15 | convolution fusion | flops 3019898880 | bytes 10223616 | tf_op jit(solution)/shard_map/md,dcf->mcf/dot_general | solution.py:148
  189.8 4.2 %convolution_convert_fusion.3 = bf16[768,2560]{1,0:T(8,128)(2,1)} fusion(bf16[2,384,2560]{2,1,0:T(8,128)(2,1)S(1)} %copy-done.15, f32[768,2,384]{2,0,1:T(8,128)S(1)} %fusion.2), kind=kOutput, calls=%fused_computation.8 | convolution fusion | flops 1513684992 | bytes 8257536 | tf_op jit(solution)/shard_map/dot_general | solution.py:152
  194.0 4.7 %all-to-all-start.2 = ((bf16[8,96,2560]{2,1,0:T(8,128)(2,1)}), bf16[8,96,2560]{2,1,0:T(8,128)(2,1)}, u32[]{:S(2)}, u32[]{:S(2)}) async-start(bf16[8,96,2560]{2,1,0:T(8,128)(2,1)} %bitcast.232), calls=%async_computation.2 | async-start | bytes 7864320 | tf_op jit(solution)/shard_map/all_to_all | solution.py:161
  199.2 0.5 copy-done.10
  199.7 1.7 fusion.20
  201.5 1.2 select_reduce_fusion
  202.7 2.4 reshape.261
  205.1 0.5 copy.157
  205.6 0.5 subtract_convert_fusion
  206.1 0.6 copy-done.3
  206.7 3.4 %fusion.5 = f32[192,2,384]{2,0,1:T(8,128)S(1)} fusion(bf16[2560,2,384]{2,1,0:T(2,128)(2,1)} %param.32, f32[192,2560]{1,0:T(8,128)S(1)} %bitcast.230, f32[2560]{0:T(1024)S(1)} %copy-done.12, f32[192]{0:T(256)S(1)} %add_rsqrt_fusion), kind=kOutput, calls=%fused_computation.21 | convolution fusion | flops 756449280 | bytes 6499072 | tf_op jit(solution)/shard_map/td,dcf->tcf/dot_general | solution.py:184
  210.2 34.7 %all-to-all-done.2 = bf16[8,96,2560]{2,1,0:T(8,128)(2,1)} async-done(((bf16[8,96,2560]{2,1,0:T(8,128)(2,1)}), bf16[8,96,2560]{2,1,0:T(8,128)(2,1)}, u32[]{:S(2)}, u32[]{:S(2)}) %all-to-all-start.2) | async-done | bytes 3932192 | tf_op jit(solution)/shard_map/all_to_all | solution.py:161
  244.9 4.1 %convolution_bitcast_fusion = f32[2,192,2560]{2,1,0:T(8,128)S(1)} fusion(bf16[8,96,2560]{2,1,0:T(8,128)(2,1)} %all-to-all-done.2, bf16[1,192,8,2,96]{4,1,2,0,3:T(8,128)(2,1)S(1)} %copy.157, bf16[1,192,8,2,96]{4,1,2,0,3:T(8,128)(2,1)S(1)} %subtract_convert_fusion), kind=kOutput, calls=%fused_computation.9 | convolution fusion | flops 1510244352 | bytes 9043968 | tf_op jit(solution)/shard_map/stgc,gcd->std/dot_general | solution.py:175
  249.0 0.7 fusion.7
  249.8 24.9 %all_to_all.30 = bf16[4,192,640]{2,1,0:T(8,128)(2,1)} all-to-all(bf16[4,192,640]{2,1,0:T(8,128)(2,1)S(1)} %bitcast.235), channel_id=1, replica_groups=mesh['req'=8,'tp'=4] {'tp'}, dimensions={0} | all-to-all | bytes 1966080 | tf_op jit(solution)/shard_map/all_to_all | solution.py:190
  274.7 5.1 %all-to-all-start.5 = ((bf16[8,96,640]{2,1,0:T(8,128)(2,1)}), bf16[8,96,640]{2,1,0:T(8,128)(2,1)}, u32[]{:S(2)}, u32[]{:S(2)}) async-start(bf16[8,96,640]{2,1,0:T(8,128)(2,1)} %bitcast.240), calls=%async_computation.6 | async-start | bytes 1966080 | tf_op jit(solution)/shard_map/all_to_all | solution.py:161
  279.8 2.3 convert_reduce_fusion
  282.1 12.5 %all-to-all-done.5 = bf16[8,96,640]{2,1,0:T(8,128)(2,1)} async-done(((bf16[8,96,640]{2,1,0:T(8,128)(2,1)}), bf16[8,96,640]{2,1,0:T(8,128)(2,1)}, u32[]{:S(2)}, u32[]{:S(2)}) %all-to-all-start.5) | async-done | bytes 983072 | tf_op jit(solution)/shard_map/all_to_all | solution.py:161
  294.6 2.2 convolution_bitcast_fusion.1
  296.8 1.8 fusion.51
  (78 shorter events, 5.6 us)
Async XLA Ops:
  6.5 15.7 %copy-start = (bf16[640,2560]{1,0:T(8,128)(2,1)S(1)}, bf16[640,2560]{1,0:T(8,128)(2,1)}, u32[]{:S(2)}) copy-start(bf16[640,2560]{1,0:T(8,128)(2,1)} %param.26) | copy-start | bytes 9830404
  6.5 7.7 %copy-start.9 = (bf16[192,640]{1,0:T(8,128)(2,1)S(1)}, bf16[192,640]{1,0:T(8,128)(2,1)}, u32[]{:S(2)}) copy-start(bf16[192,640]{1,0:T(8,128)(2,1)} %param.17) | copy-start | bytes 737284
  6.5 8.7 %copy-start.18 = (s32[4,48]{1,0:T(4,128)S(1)}, s32[4,48]{1,0:T(4,128)}, u32[]{:S(2)}) copy-start(s32[4,48]{1,0:T(4,128)} %param.24) | copy-start | bytes 2308
  15.3 3.7 %copy-start.13 = (bf16[192,128]{1,0:T(8,128)(2,1)S(1)}, bf16[192,128]{1,0:T(8,128)(2,1)}, u32[]{:S(2)}) copy-start(bf16[192,128]{1,0:T(8,128)(2,1)} %param.18) | copy-start | bytes 147460
  16.8 2.2 copy-start.6
  18.9 1.5 copy-start.8
  20.5 1.3 copy-start.17
  22.2 8.3 %copy-start.11 = (s32[192,6]{0,1:T(8,128)S(1)}, s32[192,6]{0,1:T(8,128)}, u32[]{:S(2)}) copy-start(s32[192,6]{0,1:T(8,128)} %param.29) | copy-start | bytes 13828
  22.2 8.7 %copy-start.12 = (f32[2560]{0:T(1024)S(1)}, f32[2560]{0:T(1024)}, u32[]{:S(2)}) copy-start(f32[2560]{0:T(1024)} %param.27) | copy-start | bytes 30724
  24.2 30.6 %all-to-all-start = ((bf16[4,192,640]{2,1,0:T(8,128)(2,1)}), bf16[4,192,640]{2,1,0:T(8,128)(2,1)S(1)}, u32[]{:S(2)}, u32[]{:S(2)}) async-start(bf16[4,192,640]{2,1,0:T(8,128)(2,1)} %bitcast.223), calls=%async_computation | async-start | bytes 1966080 | tf_op jit(solution)/shard_map/all_to_all | solution.py:125
  81.3 4.8 %copy-start.7 = (pred[192,1536]{0,1:T(32,128)(4,1)S(1)}, pred[192,1536]{0,1:T(32,128)(4,1)}, u32[]{:S(2)}) copy-start(pred[192,1536]{0,1:T(32,128)(4,1)} %copy.110) | copy-start | bytes 884740
  81.3 51.0 %all-to-all-start.4 = ((bf16[8,96,2560]{2,1,0:T(8,128)(2,1)}), bf16[8,96,2560]{2,1,0:T(8,128)(2,1)}, u32[]{:S(2)}, u32[]{:S(2)}) async-start(bf16[8,96,2560]{2,1,0:T(8,128)(2,1)} %convolution_convert_fusion), calls=%async_computation.4 | async-start | bytes 7864320 | tf_op jit(solution)/shard_map/all_to_all | solution.py:146
  132.3 50.9 %all-to-all-start.1 = ((bf16[8,96,2560]{2,1,0:T(8,128)(2,1)}), bf16[8,96,2560]{2,1,0:T(8,128)(2,1)}, u32[]{:S(2)}, u32[]{:S(2)}) async-start(bf16[8,96,2560]{2,1,0:T(8,128)(2,1)} %convolution_convert_fusion.1), calls=%async_computation.1 | async-start | bytes 7864320 | tf_op jit(solution)/shard_map/all_to_all | solution.py:146
  136.8 137.8 %reduce-scatter.2.cloned.1.call-start = ((), (), s32[]{:S(2)}) async-start(), calls=%async_computation.7 | async-start | bytes 4915200 | tf_op jit(solution)/shard_map/reduce_scatter | solution.py:157
  144.5 5.5 %copy-start.14 = (bf16[2,384,2560]{2,1,0:T(8,128)(2,1)S(1)}, bf16[2,384,2560]{2,1,0:T(8,128)(2,1)}, u32[]{:S(2)}) copy-start(bf16[2,384,2560]{2,1,0:T(8,128)(2,1)} %param.31) | copy-start | bytes 11796484
  183.2 6.7 %copy-start.15 = (bf16[2,384,2560]{2,1,0:T(8,128)(2,1)S(1)}, bf16[2,384,2560]{2,1,0:T(8,128)(2,1)}, u32[]{:S(2)}) copy-start(bf16[2,384,2560]{2,1,0:T(8,128)(2,1)} %param.31) | copy-start | bytes 11796484
  194.0 50.8 %all-to-all-start.2 = ((bf16[8,96,2560]{2,1,0:T(8,128)(2,1)}), bf16[8,96,2560]{2,1,0:T(8,128)(2,1)}, u32[]{:S(2)}, u32[]{:S(2)}) async-start(bf16[8,96,2560]{2,1,0:T(8,128)(2,1)} %bitcast.232), calls=%async_computation.2 | async-start | bytes 7864320 | tf_op jit(solution)/shard_map/all_to_all | solution.py:161
  198.8 0.9 copy-start.10
  199.2 2.4 copy-start.2
  205.1 1.7 copy-start.3
  205.6 39.3 %copy-start.4 = (bf16[1,192,8,2,96]{4,1,2,0,3:T(8,128)(2,1)}, bf16[1,192,8,2,96]{4,1,2,0,3:T(8,128)(2,1)S(1)}, u32[]{:S(2)}) copy-start(bf16[1,192,8,2,96]{4,1,2,0,3:T(8,128)(2,1)S(1)} %copy.157) | copy-start | bytes 1769476
  206.7 42.2 %copy-start.5 = (bf16[1,192,8,2,96]{4,1,2,0,3:T(8,128)(2,1)}, bf16[1,192,8,2,96]{4,1,2,0,3:T(8,128)(2,1)S(1)}, u32[]{:S(2)}) copy-start(bf16[1,192,8,2,96]{4,1,2,0,3:T(8,128)(2,1)S(1)} %subtract_convert_fusion) | copy-start | bytes 1769476
  244.9 4.1 %copy-start.16 = (bf16[384,2560]{1,0:T(8,128)(2,1)S(1)}, bf16[384,2560]{1,0:T(8,128)(2,1)}, u32[]{:S(2)}) copy-start(bf16[384,2560]{1,0:T(8,128)(2,1)} %param.33) | copy-start | bytes 5898244
  274.7 19.9 %all-to-all-start.5 = ((bf16[8,96,640]{2,1,0:T(8,128)(2,1)}), bf16[8,96,640]{2,1,0:T(8,128)(2,1)}, u32[]{:S(2)}, u32[]{:S(2)}) async-start(bf16[8,96,640]{2,1,0:T(8,128)(2,1)} %bitcast.240), calls=%async_computation.6 | async-start | bytes 1966080 | tf_op jit(solution)/shard_map/all_to_all | solution.py:161
  279.8 18.8 %copy-start.1 = (bf16[640,2560]{1,0:T(8,128)(2,1)S(1)}, bf16[640,2560]{1,0:T(8,128)(2,1)}, u32[]{:S(2)}) copy-start(bf16[640,2560]{1,0:T(8,128)(2,1)} %param.26) | copy-start | bytes 9830404
Sparse Core Ops, SparseCore 0:
  154.6 73.1 reduce-scatter.1

commit v8 on v7

--- a/solution.py
+++ b/solution.py
@@ -187,8 +187,8 @@
     shared_act = (jax.nn.silu(shared_gu[:, 0]) * shared_gu[:, 1]).astype(jnp.bfloat16)
     shared_terms = jnp.dot(shared_act, shared_down, preferred_element_type=jnp.float32)
     total = (shared_terms + routed).astype(jnp.bfloat16).reshape(row_count, tp_count, part_width)
-    total = lax.all_to_all(total.transpose(1, 0, 2), "tp", split_axis=0, concat_axis=0, tiled=True)
-    summed = jnp.sum(total.astype(jnp.float32), axis=0) + routed_last
+    summed = lax.psum_scatter(total.transpose(1, 0, 2), "tp", scatter_dimension=0, tiled=True)
+    summed = summed[0].astype(jnp.float32) + routed_last
     return (hidden_part + summed).astype(jnp.bfloat16)
 
 

time: 306 us -> 285 us (0.931)
  waiting for transfers between devices: 135 us -> 124 us
  blocking collectives: 44.5 us -> 38 us
  starting transfers between devices: 25.6 us -> 20.4 us
    all_to_all x2 -> x1, waiting for transfers between devices: 47.2 us -> 34.7 us  [shards(): lax.all_to_all(outputs, 'req', split_axis=0, concat_axis=0, tiled=True)]
    all_to_all x1, blocking collectives: 24.9 us -> 18.4 us  [shards(): lax.all_to_all(outputs, 'req', split_axis=0, concat_axis=0, tiled=True)]
    all_to_all x2 -> x1, starting transfers between devices: 9.86 us -> 4.52 us  [shards(): lax.all_to_all(outputs, 'req', split_axis=0, concat_axis=0, tiled=True)]
    reduce_scatter x0 -> x1, waiting for transfers between devices: none -> 3.3 us  [shards(): lax.psum_scatter(total.transpose(1, 0, 2), 'tp', scatter_dimension=0, til...]
  transfers between devices with their start and end apart: 6 -> 6, of which waited for: 5 -> 5; matrix products, arithmetic and copies ran while one was open for 19% -> 21% of each run, Pallas kernels for 0% -> 0%
where the time goes in v8:
time: 285 us; the launch traced here: 284 us
  waiting for transfers between devices  124 us (44%)
  matrix products  46 us (16%)
  blocking collectives  38 us (13%)
  local copies, waits for them, and re-layouts  27.3 us (10%)
  starting transfers between devices  20.4 us (7%)
  other arithmetic  14.5 us (5%)
  between operations  14 us (5%)
    all_to_all x2, waiting for transfers between devices, shards(): lax.all_to_all(outbox, 'req', split_axis=0, concat_axis=0, tiled=True)  70 us
    all_to_all x1, waiting for transfers between devices, shards(): lax.all_to_all(outputs, 'req', split_axis=0, concat_axis=0, tiled=True)  34.7 us
    all_gather x1, blocking collectives, shards(): hidden_bf = lax.all_gather(hidden_part_bf[None], 'tp', axis=0, tiled=True)  19.6 us
    all_to_all x1, blocking collectives, shards(): lax.all_to_all(outputs, 'req', split_axis=0, concat_axis=0, tiled=True)  18.4 us
    all_to_all x1, waiting for transfers between devices, shards(): lax.all_to_all(attn_blocks.transpose(1, 0, 2), 'tp', split_axis=0, concat...  15.9 us
    dot_general x2, matrix products, shards(): jnp.einsum('md,dcf->mcf', rows, expert_gate_up[expert], preferred_element...  13.3 us
    all_to_all x2, starting transfers between devices, shards(): lax.all_to_all(outbox, 'req', split_axis=0, concat_axis=0, tiled=True)  9.22 us
    slice x1, local copies, waits for them, and re-layouts, shards(): expert_gate_up[expert]  8.16 us
  transfers between devices with their start and end apart: 6, of which 5 were waited for; matrix products, arithmetic and copies ran while one was open for 21% of the time, Pallas kernels for 0%

profile of v8, /device:TPU:0, one launch (start us, length us, event | category | flops | bytes accessed | tf_op | source)
XLA Modules:
  0.0 284.1 jit_solution(17743703355676766620)
XLA Ops:
  6.6 0.8 compare_select_fusion
  7.5 0.9 iota_compare_fusion.6
  8.4 2.9 %gather_fusion = bf16[64,64,128]{2,1,0:T(8,128)(2,1)} fusion(bf16[64,64,128]{2,1,0:T(8,128)(2,1)} %param.21, s32[1024]{0:T(1024)S(1)} %pad_clamp_fusion), kind=kCustom, calls=%fused_computation | custom fusion | bytes 2097408 | tf_op jit(solution)/shard_map/gather | solution.py:94
  11.3 2.9 %gather_fusion.1 = bf16[64,64,128]{2,1,0:T(8,128)(2,1)} fusion(bf16[64,64,128]{2,1,0:T(8,128)(2,1)} %param.20, s32[1024]{0:T(1024)S(1)} %pad_clamp_fusion), kind=kCustom, calls=%fused_computation.1 | custom fusion | bytes 2097408 | tf_op jit(solution)/shard_map/gather | solution.py:93
  14.2 1.0 reshape.258
  16.8 2.1 bitcast_reduce_fusion
  19.0 0.4 fusion.80
  19.4 1.0 fusion.8
  20.5 1.3 fusion.15
  22.2 0.9 convolution_convert_fusion.4
  23.2 1.0 copy.166
  24.2 6.3 %all-to-all-start = ((bf16[4,192,640]{2,1,0:T(8,128)(2,1)}), bf16[4,192,640]{2,1,0:T(8,128)(2,1)S(1)}, u32[]{:S(2)}, u32[]{:S(2)}) async-start(bf16[4,192,640]{2,1,0:T(8,128)(2,1)} %bitcast.221), calls=%async_computation | async-start | bytes 1966080 | tf_op jit(solution)/shard_map/all_to_all | solution.py:125
  31.0 4.5 %reduce-window.6 = s32[16,9,128]{2,1,0:T(8,128)S(1)} reduce-window(s32[16,9,128]{2,1,0:T(8,128)S(1)} %fusion.64, s32[]{:T(128)} %constant.17.clone.1), window={size=1x1x128 pad=0_0x0_0x127_0}, to_apply=%region_6.7 | reduce-window | flops 2340864 | bytes 147460 | tf_op jit(solution)/shard_map/reduce-window
  35.5 0.4 slice_reduce_fusion
  36.5 1.2 fusion
  37.7 1.2 copy.112
  38.9 15.9 %all-to-all-done = bf16[4,192,640]{2,1,0:T(8,128)(2,1)S(1)} async-done(((bf16[4,192,640]{2,1,0:T(8,128)(2,1)}), bf16[4,192,640]{2,1,0:T(8,128)(2,1)S(1)}, u32[]{:S(2)}, u32[]{:S(2)}) %all-to-all-start) | async-done | bytes 983072 | tf_op jit(solution)/shard_map/all_to_all | solution.py:125
  55.0 1.0 add_convert_fusion
  56.0 19.6 %all-gather = bf16[768,640]{1,0:T(8,128)(2,1)S(1)} all-gather(bf16[192,640]{1,0:T(8,128)(2,1)S(1)} %add_convert_fusion), channel_id=2, replica_groups=mesh['req'=8,'tp'=4] {'tp'}, dimensions={0}, use_global_device_ids=true | all-gather | bytes 1228800 | tf_op jit(solution)/shard_map/all_gather | solution.py:131
  76.1 0.8 copy.114
  77.3 4.0 %convolution_convert_fusion = bf16[8,96,2560]{2,1,0:T(8,128)(2,1)} fusion(bf16[192,2560,1]{1,0,2:T(8,128)(2,1)S(1)} %reshape.304, pred[192,8,2,96]{0,3,2,1:T(32,128)(4,1)} %bitcast.234), kind=kOutput, calls=%fused_computation.5 | convolution fusion | flops 756940800 | bytes 5111808 | tf_op jit(solution)/shard_map/tgc,td->gcd/dot_general | solution.py:143
  81.3 4.7 %all-to-all-start.3 = ((bf16[8,96,2560]{2,1,0:T(8,128)(2,1)}), bf16[8,96,2560]{2,1,0:T(8,128)(2,1)}, u32[]{:S(2)}, u32[]{:S(2)}) async-start(bf16[8,96,2560]{2,1,0:T(8,128)(2,1)} %convolution_convert_fusion), calls=%async_computation.4 | async-start | bytes 7864320 | tf_op jit(solution)/shard_map/all_to_all | solution.py:146
  86.0 8.2 %fusion.79 = (bf16[1,2560,2,384]{3,2,1,0:T(2,128)(2,1)}, bf16[1,2560,2,384]{3,2,1,0:T(2,128)(2,1)}) fusion(bf16[2,2560,2,384]{3,2,1,0:T(2,128)(2,1)} %param.30), kind=kLoop, calls=%fused_computation.139 | loop fusion | bytes 15728640 | tf_op jit(solution)/shard_map/slice | solution.py:149
  94.2 3.1 %convolution_convert_fusion.1 = bf16[8,96,2560]{2,1,0:T(8,128)(2,1)} fusion(bf16[192,2560,1]{1,0,2:T(8,128)(2,1)S(1)} %reshape.304, pred[192,8,2,96]{0,3,2,1:T(32,128)(4,1)S(1)} %bitcast.235), kind=kOutput, calls=%fused_computation.6 | convolution fusion | flops 756940800 | bytes 5111808 | tf_op jit(solution)/shard_map/tgc,td->gcd/dot_general | solution.py:143
  97.3 34.9 %all-to-all-done.3 = bf16[8,96,2560]{2,1,0:T(8,128)(2,1)} async-done(((bf16[8,96,2560]{2,1,0:T(8,128)(2,1)}), bf16[8,96,2560]{2,1,0:T(8,128)(2,1)}, u32[]{:S(2)}, u32[]{:S(2)}) %all-to-all-start.3) | async-done | bytes 3932192 | tf_op jit(solution)/shard_map/all_to_all | solution.py:146
  132.2 4.5 %all-to-all-start.1 = ((bf16[8,96,2560]{2,1,0:T(8,128)(2,1)}), bf16[8,96,2560]{2,1,0:T(8,128)(2,1)}, u32[]{:S(2)}, u32[]{:S(2)}) async-start(bf16[8,96,2560]{2,1,0:T(8,128)(2,1)} %convolution_convert_fusion.1), calls=%async_computation.1 | async-start | bytes 7864320 | tf_op jit(solution)/shard_map/all_to_all | solution.py:146
  136.8 6.7 %fusion.1 = f32[768,2,384]{2,0,1:T(8,128)S(1)} fusion(bf16[768,2560,1]{1,0,2:T(8,128)(2,1)} %bitcast.47, bf16[1,2560,2,384]{3,2,1,0:T(2,128)(2,1)} %get-tuple-element.6), kind=kOutput, calls=%fused_computation.13 | convolution fusion | flops 3019898880 | bytes 10223616 | tf_op jit(solution)/shard_map/md,dcf->mcf/dot_general | solution.py:148
  143.4 2.2 convolution_convert_fusion.2
  145.7 2.2 copy.164
  147.9 35.1 %all-to-all-done.1 = bf16[8,96,2560]{2,1,0:T(8,128)(2,1)} async-done(((bf16[8,96,2560]{2,1,0:T(8,128)(2,1)}), bf16[8,96,2560]{2,1,0:T(8,128)(2,1)}, u32[]{:S(2)}, u32[]{:S(2)}) %all-to-all-start.1) | async-done | bytes 3932192 | tf_op jit(solution)/shard_map/all_to_all | solution.py:146
  183.0 6.7 %fusion.2 = f32[768,2,384]{2,0,1:T(8,128)S(1)} fusion(bf16[768,2560,1]{1,0,2:T(8,128)(2,1)} %bitcast.34, bf16[1,2560,2,384]{3,2,1,0:T(2,128)(2,1)} %get-tuple-element.5), kind=kOutput, calls=%fused_computation.15 | convolution fusion | flops 3019898880 | bytes 10223616 | tf_op jit(solution)/shard_map/md,dcf->mcf/dot_general | solution.py:148
  189.7 4.2 %convolution_convert_fusion.3 = bf16[768,2560]{1,0:T(8,128)(2,1)} fusion(bf16[2,384,2560]{2,1,0:T(8,128)(2,1)S(1)} %copy-done.15, f32[768,2,384]{2,0,1:T(8,128)S(1)} %fusion.2), kind=kOutput, calls=%fused_computation.8 | convolution fusion | flops 1513684992 | bytes 8257536 | tf_op jit(solution)/shard_map/dot_general | solution.py:152
  193.9 4.5 %all-to-all-start.2 = ((bf16[8,96,2560]{2,1,0:T(8,128)(2,1)}), bf16[8,96,2560]{2,1,0:T(8,128)(2,1)}, u32[]{:S(2)}, u32[]{:S(2)}) async-start(bf16[8,96,2560]{2,1,0:T(8,128)(2,1)} %bitcast.230), calls=%async_computation.2 | async-start | bytes 7864320 | tf_op jit(solution)/shard_map/all_to_all | solution.py:161
  199.4 1.7 fusion.20
  201.2 1.2 select_reduce_fusion
  202.3 2.4 reshape.265
  204.7 0.5 copy.159
  205.3 0.5 subtract_convert_fusion
  205.8 0.8 copy-done.3
  206.6 3.4 %fusion.5 = f32[192,2,384]{2,0,1:T(8,128)S(1)} fusion(bf16[2560,2,384]{2,1,0:T(2,128)(2,1)} %param.32, f32[192,2560]{1,0:T(8,128)S(1)} %bitcast.228, f32[2560]{0:T(1024)S(1)} %copy-done.12, f32[192]{0:T(256)S(1)} %add_rsqrt_fusion), kind=kOutput, calls=%fused_computation.21 | convolution fusion | flops 756449280 | bytes 6499072 | tf_op jit(solution)/shard_map/td,dcf->tcf/dot_general | solution.py:184
  210.0 34.7 %all-to-all-done.2 = bf16[8,96,2560]{2,1,0:T(8,128)(2,1)} async-done(((bf16[8,96,2560]{2,1,0:T(8,128)(2,1)}), bf16[8,96,2560]{2,1,0:T(8,128)(2,1)}, u32[]{:S(2)}, u32[]{:S(2)}) %all-to-all-start.2) | async-done | bytes 3932192 | tf_op jit(solution)/shard_map/all_to_all | solution.py:161
  244.8 4.1 %convolution_bitcast_fusion = f32[2,192,2560]{2,1,0:T(8,128)S(1)} fusion(bf16[8,96,2560]{2,1,0:T(8,128)(2,1)} %all-to-all-done.2, bf16[1,192,8,2,96]{4,1,2,0,3:T(8,128)(2,1)S(1)} %copy.159, bf16[1,192,8,2,96]{4,1,2,0,3:T(8,128)(2,1)S(1)} %subtract_convert_fusion), kind=kOutput, calls=%fused_computation.9 | convolution fusion | flops 1510244352 | bytes 9043968 | tf_op jit(solution)/shard_map/stgc,gcd->std/dot_general | solution.py:175
  248.8 0.7 fusion.7
  249.6 1.0 copy.165
  250.7 18.4 %all_to_all.25 = bf16[8,96,640]{2,1,0:T(8,128)(2,1)S(1)} all-to-all(bf16[8,96,640]{2,1,0:T(8,128)(2,1)} %bitcast.238), channel_id=1, replica_groups=mesh['req'=8,'tp'=4] {'req'}, dimensions={0} | all-to-all | bytes 1966080 | tf_op jit(solution)/shard_map/all_to_all | solution.py:161
  269.1 2.8 convolution_bitcast_fusion.1
  271.9 3.3 %reduce-scatter.3.cloned.1.call-done = bf16[1,192,640]{2,1,0:T(8,128)(2,1)} async-done(((bf16[4,192,640]{2,1,0:T(8,128)(2,1)}), bf16[1,192,640]{2,1,0:T(8,128)(2,1)}) %reduce-scatter.3.cloned.1.call-update) | async-done | bytes 245776 | tf_op jit(solution)/shard_map/reduce_scatter | solution.py:190
  275.2 2.0 fusion.51
  (78 shorter events, 5.2 us)
Async XLA Ops:
  6.5 15.7 %copy-start = (bf16[640,2560]{1,0:T(8,128)(2,1)S(1)}, bf16[640,2560]{1,0:T(8,128)(2,1)}, u32[]{:S(2)}) copy-start(bf16[640,2560]{1,0:T(8,128)(2,1)} %param.26) | copy-start | bytes 9830404
  6.5 7.7 %copy-start.9 = (bf16[192,640]{1,0:T(8,128)(2,1)S(1)}, bf16[192,640]{1,0:T(8,128)(2,1)}, u32[]{:S(2)}) copy-start(bf16[192,640]{1,0:T(8,128)(2,1)} %param.17) | copy-start | bytes 737284
  6.5 8.7 %copy-start.18 = (s32[4,48]{1,0:T(4,128)S(1)}, s32[4,48]{1,0:T(4,128)}, u32[]{:S(2)}) copy-start(s32[4,48]{1,0:T(4,128)} %param.24) | copy-start | bytes 2308
  15.3 3.7 %copy-start.13 = (bf16[192,128]{1,0:T(8,128)(2,1)S(1)}, bf16[192,128]{1,0:T(8,128)(2,1)}, u32[]{:S(2)}) copy-start(bf16[192,128]{1,0:T(8,128)(2,1)} %param.18) | copy-start | bytes 147460
  16.8 2.2 copy-start.6
  18.9 1.5 copy-start.8
  20.5 1.3 copy-start.17
  22.2 8.3 %copy-start.11 = (s32[192,6]{0,1:T(8,128)S(1)}, s32[192,6]{0,1:T(8,128)}, u32[]{:S(2)}) copy-start(s32[192,6]{0,1:T(8,128)} %param.29) | copy-start | bytes 13828
  22.2 8.7 %copy-start.12 = (f32[2560]{0:T(1024)S(1)}, f32[2560]{0:T(1024)}, u32[]{:S(2)}) copy-start(f32[2560]{0:T(1024)} %param.27) | copy-start | bytes 30724
  24.2 30.6 %all-to-all-start = ((bf16[4,192,640]{2,1,0:T(8,128)(2,1)}), bf16[4,192,640]{2,1,0:T(8,128)(2,1)S(1)}, u32[]{:S(2)}, u32[]{:S(2)}) async-start(bf16[4,192,640]{2,1,0:T(8,128)(2,1)} %bitcast.221), calls=%async_computation | async-start | bytes 1966080 | tf_op jit(solution)/shard_map/all_to_all | solution.py:125
  81.3 50.8 %all-to-all-start.3 = ((bf16[8,96,2560]{2,1,0:T(8,128)(2,1)}), bf16[8,96,2560]{2,1,0:T(8,128)(2,1)}, u32[]{:S(2)}, u32[]{:S(2)}) async-start(bf16[8,96,2560]{2,1,0:T(8,128)(2,1)} %convolution_convert_fusion), calls=%async_computation.4 | async-start | bytes 7864320 | tf_op jit(solution)/shard_map/all_to_all | solution.py:146
  86.0 8.2 %copy-start.7 = (pred[192,1536]{0,1:T(32,128)(4,1)S(1)}, pred[192,1536]{0,1:T(32,128)(4,1)}, u32[]{:S(2)}) copy-start(pred[192,1536]{0,1:T(32,128)(4,1)} %copy.112) | copy-start | bytes 884740
  132.2 50.9 %all-to-all-start.1 = ((bf16[8,96,2560]{2,1,0:T(8,128)(2,1)}), bf16[8,96,2560]{2,1,0:T(8,128)(2,1)}, u32[]{:S(2)}, u32[]{:S(2)}) async-start(bf16[8,96,2560]{2,1,0:T(8,128)(2,1)} %convolution_convert_fusion.1), calls=%async_computation.1 | async-start | bytes 7864320 | tf_op jit(solution)/shard_map/all_to_all | solution.py:146
  136.7 113.9 %reduce-scatter.5.cloned.1.call-start = ((), (), s32[]{:S(2)}) async-start(), calls=%async_computation.8 | async-start | bytes 4915200 | tf_op jit(solution)/shard_map/reduce_scatter | solution.py:157
  136.8 6.7 %copy-start.14 = (bf16[2,384,2560]{2,1,0:T(8,128)(2,1)S(1)}, bf16[2,384,2560]{2,1,0:T(8,128)(2,1)}, u32[]{:S(2)}) copy-start(bf16[2,384,2560]{2,1,0:T(8,128)(2,1)} %param.31) | copy-start | bytes 11796484
  183.0 6.7 %copy-start.15 = (bf16[2,384,2560]{2,1,0:T(8,128)(2,1)S(1)}, bf16[2,384,2560]{2,1,0:T(8,128)(2,1)}, u32[]{:S(2)}) copy-start(bf16[2,384,2560]{2,1,0:T(8,128)(2,1)} %param.31) | copy-start | bytes 11796484
  193.9 50.8 %all-to-all-start.2 = ((bf16[8,96,2560]{2,1,0:T(8,128)(2,1)}), bf16[8,96,2560]{2,1,0:T(8,128)(2,1)}, u32[]{:S(2)}, u32[]{:S(2)}) async-start(bf16[8,96,2560]{2,1,0:T(8,128)(2,1)} %bitcast.230), calls=%async_computation.2 | async-start | bytes 7864320 | tf_op jit(solution)/shard_map/all_to_all | solution.py:161
  198.4 0.9 copy-start.10
  198.4 76.7 %reduce-scatter.3.cloned.1.call-start = ((), (), s32[]{:S(2)}) async-start(), calls=%async_computation.7 | async-start | bytes 1228800 | tf_op jit(solution)/shard_map/reduce_scatter | solution.py:190
  199.1 2.1 copy-start.2
  204.7 1.9 copy-start.3
  205.2 39.5 %copy-start.4 = (bf16[1,192,8,2,96]{4,1,2,0,3:T(8,128)(2,1)}, bf16[1,192,8,2,96]{4,1,2,0,3:T(8,128)(2,1)S(1)}, u32[]{:S(2)}) copy-start(bf16[1,192,8,2,96]{4,1,2,0,3:T(8,128)(2,1)S(1)} %copy.159) | copy-start | bytes 1769476
  206.6 42.2 %copy-start.5 = (bf16[1,192,8,2,96]{4,1,2,0,3:T(8,128)(2,1)}, bf16[1,192,8,2,96]{4,1,2,0,3:T(8,128)(2,1)S(1)}, u32[]{:S(2)}) copy-start(bf16[1,192,8,2,96]{4,1,2,0,3:T(8,128)(2,1)S(1)} %subtract_convert_fusion) | copy-start | bytes 1769476
  244.8 4.1 %copy-start.16 = (bf16[384,2560]{1,0:T(8,128)(2,1)S(1)}, bf16[384,2560]{1,0:T(8,128)(2,1)}, u32[]{:S(2)}) copy-start(bf16[384,2560]{1,0:T(8,128)(2,1)} %param.33) | copy-start | bytes 5898244
  250.6 26.6 %copy-start.1 = (bf16[640,2560]{1,0:T(8,128)(2,1)S(1)}, bf16[640,2560]{1,0:T(8,128)(2,1)}, u32[]{:S(2)}) copy-start(bf16[640,2560]{1,0:T(8,128)(2,1)} %param.26) | copy-start | bytes 9830404
Sparse Core Ops, SparseCore 0:
  148.0 73.1 reduce-scatter.4
  250.7 24.3 reduce-scatter.2

commit v9 on v8

--- a/solution.py
+++ b/solution.py
@@ -90,20 +90,35 @@
     part_width = model_width // tp_count
     pages_dev = key_pages.shape[0]
     local_pages = page_table - lax.axis_index("req") * pages_dev
-    cache_keys = key_pages[local_pages].reshape(requests, -1, kv_local, HD)
-    cache_values = value_pages[local_pages].reshape(requests, -1, kv_local, HD)
-    head_outputs = tree_attention(
-        queries.reshape(requests, tree_size, kv_local, head_ratio, HD),
-        cache_keys,
-        cache_values,
-        new_keys.reshape(requests, tree_size, kv_local, HD),
-        new_values.reshape(requests, tree_size, kv_local, HD),
-        cache_lengths,
-        ancestors(parents),
-    )
-    attn_terms = jnp.dot(
-        head_outputs.reshape(row_count, -1), out_weight, preferred_element_type=jnp.float32
-    )
+    allowed = ancestors(parents)
+    column = lax.axis_index("tp") * part_width
+    half = requests // 2
+    attn_parts = []
+    for first, count in ((0, half), (half, requests - half)):
+        rows = slice(first * tree_size, (first + count) * tree_size)
+        pages = local_pages[first : first + count]
+        head_outputs = tree_attention(
+            queries[rows].reshape(count, tree_size, kv_local, head_ratio, HD),
+            key_pages[pages].reshape(count, -1, kv_local, HD),
+            value_pages[pages].reshape(count, -1, kv_local, HD),
+            new_keys[rows].reshape(count, tree_size, kv_local, HD),
+            new_values[rows].reshape(count, tree_size, kv_local, HD),
+            cache_lengths[first : first + count],
+            allowed[first : first + count],
+        )
+        attn_terms = jnp.dot(
+            head_outputs.reshape(count * tree_size, -1), out_weight,
+            preferred_element_type=jnp.float32,
+        )
+        attn_blocks = attn_terms.astype(jnp.bfloat16).reshape(-1, tp_count, part_width)
+        attn_blocks = attn_blocks.transpose(1, 0, 2)
+        if first == 0:
+            attn_sum = lax.psum_scatter(attn_blocks, "tp", scatter_dimension=0, tiled=True)[0]
+            attn_parts.append(attn_sum.astype(jnp.float32))
+        else:
+            attn_blocks = lax.all_to_all(attn_blocks, "tp", split_axis=0, concat_axis=0, tiled=True)
+            attn_parts.append(jnp.sum(attn_blocks.astype(jnp.float32), axis=0))
+    attn_part = jnp.concatenate(attn_parts, axis=0)
     column = lax.axis_index("tp") * part_width
     experts_local = expert_gate_up.shape[0]
     top_count = routes.shape[1]
@@ -121,15 +136,9 @@
     slot_ids = jnp.arange(slot_count, dtype=jnp.int32)
     hit = slot[:, :, None] == slot_ids[None, None, :]
 
-    attn_blocks = attn_terms.astype(jnp.bfloat16).reshape(row_count, tp_count, part_width)
-    attn_blocks = lax.all_to_all(
-        attn_blocks.transpose(1, 0, 2), "tp", split_axis=0, concat_axis=0, tiled=True
-    )
-    attn_part = jnp.sum(attn_blocks.astype(jnp.float32), axis=0)
     residual_part = lax.dynamic_slice_in_dim(residual, column, part_width, 1)
     hidden_part_bf = (residual_part.astype(jnp.float32) + attn_part).astype(jnp.bfloat16)
-    hidden_bf = lax.all_gather(hidden_part_bf[None], "tp", axis=0, tiled=True)
-    hidden = hidden_bf.transpose(1, 0, 2).reshape(row_count, model_width).astype(jnp.float32)
+    hidden = lax.all_gather(hidden_part_bf, "tp", axis=1, tiled=True).astype(jnp.float32)
     rstd = lax.rsqrt(jnp.mean(hidden * hidden, axis=1, keepdims=True) + EPSILON)
     normed = hidden * rstd * norm_gain
     logits = jnp.dot(normed, router_weight, precision=lax.Precision.HIGHEST)

time: 285 us -> 293 us (1.028)
  local copies, waits for them, and re-layouts: 27.3 us -> 38.3 us
  waiting for transfers between devices: 124 us -> 114 us
  other arithmetic: 14.5 us -> 17.8 us
    all_to_all x1, waiting for transfers between devices: 15.9 us -> 6.95 us  [shards(): lax.all_to_all(attn_blocks, 'tp', split_axis=0, concat_axis=0, tiled=True)]
    gather x2 -> x4, local copies, waits for them, and re-layouts: 5.83 us -> 10.8 us  [the longest x2 5.4 us: shards(): key_pages[pages].reshape(count, -1, kv_local, HD)]
    slice x1 -> x8, local copies, waits for them, and re-layouts: 0.43 us -> 5.13 us  [the longest x1 1.67 us: shards(): queries[rows].reshape(count, tree_size, kv_local, head_ratio, HD)]
  transfers between devices with their start and end apart: 6 -> 7, of which waited for: 5 -> 5; matrix products, arithmetic and copies ran while one was open for 21% -> 25% of each run, Pallas kernels for 0% -> 0%
where the time goes in v9:
time: 293 us; the launch traced here: 291 us
  waiting for transfers between devices  114 us (39%)
  matrix products  48.2 us (16%)
  blocking collectives  38.6 us (13%)
  local copies, waits for them, and re-layouts  38.3 us (13%)
  starting transfers between devices  20.5 us (7%)
  other arithmetic  17.8 us (6%)
  between operations  13.7 us (5%)
    all_to_all x2, waiting for transfers between devices, shards(): lax.all_to_all(outbox, 'req', split_axis=0, concat_axis=0, tiled=True)  69.9 us
    all_to_all x1, waiting for transfers between devices, shards(): lax.all_to_all(outputs, 'req', split_axis=0, concat_axis=0, tiled=True)  34.6 us
    all_gather x1, blocking collectives, shards(): lax.all_gather(hidden_part_bf, 'tp', axis=1, tiled=True).astype(jnp.float32)  20.2 us
    all_to_all x1, blocking collectives, shards(): lax.all_to_all(outputs, 'req', split_axis=0, concat_axis=0, tiled=True)  18.4 us
    dot_general x2, matrix products, shards(): jnp.einsum('md,dcf->mcf', rows, expert_gate_up[expert], preferred_element...  13.3 us
    all_to_all x2, starting transfers between devices, shards(): lax.all_to_all(outbox, 'req', split_axis=0, concat_axis=0, tiled=True)  9.22 us
    slice x1, local copies, waits for them, and re-layouts, shards(): expert_gate_up[expert]  8.13 us
    all_to_all x1, waiting for transfers between devices, shards(): lax.all_to_all(attn_blocks, 'tp', split_axis=0, concat_axis=0, tiled=True)  6.95 us
  transfers between devices with their start and end apart: 7, of which 5 were waited for; matrix products, arithmetic and copies ran while one was open for 25% of the time, Pallas kernels for 0%

profile of v9, /device:TPU:0, one launch (start us, length us, event | category | flops | bytes accessed | tf_op | source)
XLA Modules:
  0.0 291.4 jit_solution(364469494923805931)
XLA Ops:
  6.6 1.5 fusion.100
  10.0 1.7 fusion.96
  11.6 1.1 reshape.339
  12.7 1.0 convolution_minimum_fusion.5
  16.5 2.8 gather_fusion.1
  19.2 1.5 bitcast_reduce_fusion.1
  21.1 1.0 copy-done.2
  23.3 2.8 gather_fusion
  26.1 1.2 convolution_bitcast_fusion.3
  27.3 2.3 fusion.30
  30.4 0.8 copy.201
  31.3 2.6 gather_fusion.3
  34.0 2.6 gather_fusion.2
  36.6 1.1 reshape.347
  37.8 1.5 bitcast_reduce_fusion
  42.7 6.4 %all-to-all-start = ((bf16[4,96,640]{2,1,0:T(8,128)(2,1)}), bf16[4,96,640]{2,1,0:T(8,128)(2,1)S(1)}, u32[]{:S(2)}, u32[]{:S(2)}) async-start(bf16[4,96,640]{2,1,0:T(8,128)(2,1)} %bitcast.289), calls=%async_computation.1 | async-start | bytes 983040 | tf_op jit(solution)/shard_map/all_to_all | solution.py:119
  49.5 4.5 %reduce-window.6 = s32[16,9,128]{2,1,0:T(8,128)S(1)} reduce-window(s32[16,9,128]{2,1,0:T(8,128)S(1)} %fusion.61, s32[]{:T(128)} %constant.17.clone.1), window={size=1x1x128 pad=0_0x0_0x127_0}, to_apply=%region_11.12 | reduce-window | flops 2340864 | bytes 147460 | tf_op jit(solution)/shard_map/reduce-window
  55.0 1.2 fusion
  56.7 6.9 %all-to-all-done = bf16[4,96,640]{2,1,0:T(8,128)(2,1)S(1)} async-done(((bf16[4,96,640]{2,1,0:T(8,128)(2,1)}), bf16[4,96,640]{2,1,0:T(8,128)(2,1)S(1)}, u32[]{:S(2)}, u32[]{:S(2)}) %all-to-all-start) | async-done | bytes 491552 | tf_op jit(solution)/shard_map/all_to_all | solution.py:119
  63.7 0.9 bitcast_convert_fusion
  64.7 1.0 fusion.54
  65.7 20.2 %all_gather.3 = bf16[192,2560]{1,0:T(8,128)(2,1)S(1)} all-gather(bf16[192,640]{1,0:T(8,128)(2,1)S(1)} %fusion.54), channel_id=1, replica_groups=mesh['req'=8,'tp'=4] {'tp'}, dimensions={1}, use_global_device_ids=true | all-gather | bytes 1228800 | tf_op jit(solution)/shard_map/all_gather | solution.py:141
  86.1 3.3 %convolution_convert_fusion = bf16[8,96,2560]{2,1,0:T(8,128)(2,1)} fusion(pred[192,8,2,96]{0,3,2,1:T(32,128)(4,1)S(1)} %bitcast.302, bf16[192,2560]{1,0:T(8,128)(2,1)S(1)} %all_gather.3, f32[2560]{0:T(1024)S(1)} %copy-done.8, f32[192]{0:T(256)S(1)} %add_rsqrt_fusion), kind=kOutput, calls=%fused_computation.7 | convolution fusion | flops 758906880 | bytes 5125120 | tf_op jit(solution)/shard_map/tgc,td->gcd/dot_general | solution.py:152
  89.4 4.7 %all-to-all-start.3 = ((bf16[8,96,2560]{2,1,0:T(8,128)(2,1)}), bf16[8,96,2560]{2,1,0:T(8,128)(2,1)}, u32[]{:S(2)}, u32[]{:S(2)}) async-start(bf16[8,96,2560]{2,1,0:T(8,128)(2,1)} %convolution_convert_fusion), calls=%async_computation.5 | async-start | bytes 7864320 | tf_op jit(solution)/shard_map/all_to_all | solution.py:155
  94.1 8.1 %fusion.95 = (bf16[1,2560,2,384]{3,2,1,0:T(2,128)(2,1)}, bf16[1,2560,2,384]{3,2,1,0:T(2,128)(2,1)}) fusion(bf16[2,2560,2,384]{3,2,1,0:T(2,128)(2,1)} %param.30), kind=kLoop, calls=%fused_computation.169 | loop fusion | bytes 15728640 | tf_op jit(solution)/shard_map/slice | solution.py:158
  102.2 3.2 %convolution_convert_fusion.1 = bf16[8,96,2560]{2,1,0:T(8,128)(2,1)} fusion(pred[192,8,2,96]{0,3,2,1:T(32,128)(4,1)S(1)} %bitcast.303, bf16[192,2560]{1,0:T(8,128)(2,1)S(1)} %all_gather.3, f32[2560]{0:T(1024)S(1)} %copy-done.8, f32[192]{0:T(256)S(1)} %add_rsqrt_fusion), kind=kOutput, calls=%fused_computation.8 | convolution fusion | flops 758906880 | bytes 5125120 | tf_op jit(solution)/shard_map/tgc,td->gcd/dot_general | solution.py:152
  105.5 34.8 %all-to-all-done.3 = bf16[8,96,2560]{2,1,0:T(8,128)(2,1)} async-done(((bf16[8,96,2560]{2,1,0:T(8,128)(2,1)}), bf16[8,96,2560]{2,1,0:T(8,128)(2,1)}, u32[]{:S(2)}, u32[]{:S(2)}) %all-to-all-start.3) | async-done | bytes 3932192 | tf_op jit(solution)/shard_map/all_to_all | solution.py:155
  140.2 4.5 %all-to-all-start.1 = ((bf16[8,96,2560]{2,1,0:T(8,128)(2,1)}), bf16[8,96,2560]{2,1,0:T(8,128)(2,1)}, u32[]{:S(2)}, u32[]{:S(2)}) async-start(bf16[8,96,2560]{2,1,0:T(8,128)(2,1)} %convolution_convert_fusion.1), calls=%async_computation.2 | async-start | bytes 7864320 | tf_op jit(solution)/shard_map/all_to_all | solution.py:155
  144.8 6.7 %fusion.1 = f32[768,2,384]{2,0,1:T(8,128)S(1)} fusion(bf16[768,2560,1]{1,0,2:T(8,128)(2,1)} %bitcast.66, bf16[1,2560,2,384]{3,2,1,0:T(2,128)(2,1)} %get-tuple-element.6), kind=kOutput, calls=%fused_computation.15 | convolution fusion | flops 3019898880 | bytes 10223616 | tf_op jit(solution)/shard_map/md,dcf->mcf/dot_general | solution.py:157
  151.5 2.2 convolution_convert_fusion.2
  153.7 2.2 copy.198
  156.0 35.1 %all-to-all-done.1 = bf16[8,96,2560]{2,1,0:T(8,128)(2,1)} async-done(((bf16[8,96,2560]{2,1,0:T(8,128)(2,1)}), bf16[8,96,2560]{2,1,0:T(8,128)(2,1)}, u32[]{:S(2)}, u32[]{:S(2)}) %all-to-all-start.1) | async-done | bytes 3932192 | tf_op jit(solution)/shard_map/all_to_all | solution.py:155
  191.1 6.7 %fusion.2 = f32[768,2,384]{2,0,1:T(8,128)S(1)} fusion(bf16[768,2560,1]{1,0,2:T(8,128)(2,1)} %bitcast.53, bf16[1,2560,2,384]{3,2,1,0:T(2,128)(2,1)} %get-tuple-element.5), kind=kOutput, calls=%fused_computation.17 | convolution fusion | flops 3019898880 | bytes 10223616 | tf_op jit(solution)/shard_map/md,dcf->mcf/dot_general | solution.py:157
  197.8 4.2 %convolution_convert_fusion.3 = bf16[768,2560]{1,0:T(8,128)(2,1)} fusion(bf16[2,384,2560]{2,1,0:T(8,128)(2,1)S(1)} %copy-done.13, f32[768,2,384]{2,0,1:T(8,128)S(1)} %fusion.2), kind=kOutput, calls=%fused_computation.10 | convolution fusion | flops 1513684992 | bytes 8257536 | tf_op jit(solution)/shard_map/dot_general | solution.py:161
  202.0 4.6 %all-to-all-start.2 = ((bf16[8,96,2560]{2,1,0:T(8,128)(2,1)}), bf16[8,96,2560]{2,1,0:T(8,128)(2,1)}, u32[]{:S(2)}, u32[]{:S(2)}) async-start(bf16[8,96,2560]{2,1,0:T(8,128)(2,1)} %bitcast.294), calls=%async_computation.3 | async-start | bytes 7864320 | tf_op jit(solution)/shard_map/all_to_all | solution.py:170
  206.9 1.8 fusion.9
  208.8 2.2 select_reduce_fusion
  211.0 3.3 %reshape.354 = f32[1,192,8,2,96]{4,3,2,1,0:T(2,128)S(1)} reshape(f32[192,1536]{1,0:T(8,128)} %select_reduce_fusion) | data formatting | bytes 2359296 | tf_op jit(solution)/shard_map/reshape | solution.py:178
  214.3 1.4 copy.189
  215.8 1.4 subtract_convert_fusion
  217.2 1.1 fusion.4
  218.3 34.6 %all-to-all-done.2 = bf16[8,96,2560]{2,1,0:T(8,128)(2,1)} async-done(((bf16[8,96,2560]{2,1,0:T(8,128)(2,1)}), bf16[8,96,2560]{2,1,0:T(8,128)(2,1)}, u32[]{:S(2)}, u32[]{:S(2)}) %all-to-all-start.2) | async-done | bytes 3932192 | tf_op jit(solution)/shard_map/all_to_all | solution.py:170
  252.9 4.1 %convolution_bitcast_fusion = f32[2,192,2560]{2,1,0:T(8,128)S(1)} fusion(bf16[8,96,2560]{2,1,0:T(8,128)(2,1)} %all-to-all-done.2, bf16[1,192,8,2,96]{4,1,2,0,3:T(8,128)(2,1)S(1)} %copy-done.3, bf16[1,192,8,2,96]{4,1,2,0,3:T(8,128)(2,1)S(1)} %copy-done.4), kind=kOutput, calls=%fused_computation.11 | convolution fusion | flops 1510244352 | bytes 9043968 | tf_op jit(solution)/shard_map/stgc,gcd->std/dot_general | solution.py:184
  257.7 1.0 copy.199
  258.8 18.4 %all_to_all.25 = bf16[8,96,640]{2,1,0:T(8,128)(2,1)S(1)} all-to-all(bf16[8,96,640]{2,1,0:T(8,128)(2,1)} %bitcast.304), channel_id=1, replica_groups=mesh['req'=8,'tp'=4] {'req'}, dimensions={0} | all-to-all | bytes 1966080 | tf_op jit(solution)/shard_map/all_to_all | solution.py:170
  277.2 2.8 convolution_bitcast_fusion.1
  280.1 2.7 reduce-scatter.6.cloned.1.call-done
  282.8 2.0 fusion.53
  (95 shorter events, 13.8 us)
Async XLA Ops:
  6.5 23.1 %copy-start = (bf16[640,2560]{1,0:T(8,128)(2,1)S(1)}, bf16[640,2560]{1,0:T(8,128)(2,1)}, u32[]{:S(2)}) copy-start(bf16[640,2560]{1,0:T(8,128)(2,1)} %param.26) | copy-start | bytes 9830404
  6.5 57.2 %reduce-scatter.4.cloned.1.call-start = ((), (), s32[]{:S(2)}) async-start(), calls=%async_computation.8 | async-start | bytes 614400 | tf_op jit(solution)/shard_map/reduce_scatter | solution.py:116
  20.8 1.3 copy-start.2
  20.8 1.9 copy-start.9
  21.1 1.5 copy-start.5
  29.7 1.6 copy-start.11
  39.3 0.9 copy-start.10
  39.3 1.2 copy-start.6
  41.2 7.9 %copy-start.7 = (s32[192,6]{0,1:T(8,128)S(1)}, s32[192,6]{0,1:T(8,128)}, u32[]{:S(2)}) copy-start(s32[192,6]{0,1:T(8,128)} %param.29) | copy-start | bytes 13828
  42.7 20.9 %all-to-all-start = ((bf16[4,96,640]{2,1,0:T(8,128)(2,1)}), bf16[4,96,640]{2,1,0:T(8,128)(2,1)S(1)}, u32[]{:S(2)}, u32[]{:S(2)}) async-start(bf16[4,96,640]{2,1,0:T(8,128)(2,1)} %bitcast.289), calls=%async_computation.1 | async-start | bytes 983040 | tf_op jit(solution)/shard_map/all_to_all | solution.py:119
  63.7 22.4 %copy-start.8 = (f32[2560]{0:T(1024)S(1)}, f32[2560]{0:T(1024)}, u32[]{:S(2)}) copy-start(f32[2560]{0:T(1024)} %param.27) | copy-start | bytes 30724
  89.4 50.8 %all-to-all-start.3 = ((bf16[8,96,2560]{2,1,0:T(8,128)(2,1)}), bf16[8,96,2560]{2,1,0:T(8,128)(2,1)}, u32[]{:S(2)}, u32[]{:S(2)}) async-start(bf16[8,96,2560]{2,1,0:T(8,128)(2,1)} %convolution_convert_fusion), calls=%async_computation.5 | async-start | bytes 7864320 | tf_op jit(solution)/shard_map/all_to_all | solution.py:155
  140.2 50.9 %all-to-all-start.1 = ((bf16[8,96,2560]{2,1,0:T(8,128)(2,1)}), bf16[8,96,2560]{2,1,0:T(8,128)(2,1)}, u32[]{:S(2)}, u32[]{:S(2)}) async-start(bf16[8,96,2560]{2,1,0:T(8,128)(2,1)} %convolution_convert_fusion.1), calls=%async_computation.2 | async-start | bytes 7864320 | tf_op jit(solution)/shard_map/all_to_all | solution.py:155
  144.8 114.1 %reduce-scatter.8.cloned.1.call-start = ((), (), s32[]{:S(2)}) async-start(), calls=%async_computation.10 | async-start | bytes 4915200 | tf_op jit(solution)/shard_map/reduce_scatter | solution.py:166
  144.8 6.7 %copy-start.12 = (bf16[2,384,2560]{2,1,0:T(8,128)(2,1)S(1)}, bf16[2,384,2560]{2,1,0:T(8,128)(2,1)}, u32[]{:S(2)}) copy-start(bf16[2,384,2560]{2,1,0:T(8,128)(2,1)} %param.31) | copy-start | bytes 11796484
  191.1 6.7 %copy-start.13 = (bf16[2,384,2560]{2,1,0:T(8,128)(2,1)S(1)}, bf16[2,384,2560]{2,1,0:T(8,128)(2,1)}, u32[]{:S(2)}) copy-start(bf16[2,384,2560]{2,1,0:T(8,128)(2,1)} %param.31) | copy-start | bytes 11796484
  202.0 4.9 %copy-start.16 = (f32[2560,16]{0,1:T(8,128)S(1)}, f32[2560,16]{0,1:T(8,128)}, u32[]{:S(2)}) copy-start(f32[2560,16]{0,1:T(8,128)} %param.28) | copy-start | bytes 491524
  202.0 51.0 %all-to-all-start.2 = ((bf16[8,96,2560]{2,1,0:T(8,128)(2,1)}), bf16[8,96,2560]{2,1,0:T(8,128)(2,1)}, u32[]{:S(2)}, u32[]{:S(2)}) async-start(bf16[8,96,2560]{2,1,0:T(8,128)(2,1)} %bitcast.294), calls=%async_computation.3 | async-start | bytes 7864320 | tf_op jit(solution)/shard_map/all_to_all | solution.py:170
  206.6 76.2 %reduce-scatter.6.cloned.1.call-start = ((), (), s32[]{:S(2)}) async-start(), calls=%async_computation.9 | async-start | bytes 1228800 | tf_op jit(solution)/shard_map/reduce_scatter | solution.py:199
  214.3 2.8 copy-start.14
  217.2 35.8 %copy-start.3 = (bf16[1,192,8,2,96]{4,1,2,0,3:T(8,128)(2,1)S(1)}, bf16[1,192,8,2,96]{4,1,2,0,3:T(8,128)(2,1)}, u32[]{:S(2)}) copy-start(bf16[1,192,8,2,96]{4,1,2,0,3:T(8,128)(2,1)} %copy.189) | copy-start | bytes 1769476
  217.2 35.8 %copy-start.4 = (bf16[1,192,8,2,96]{4,1,2,0,3:T(8,128)(2,1)S(1)}, bf16[1,192,8,2,96]{4,1,2,0,3:T(8,128)(2,1)}, u32[]{:S(2)}) copy-start(bf16[1,192,8,2,96]{4,1,2,0,3:T(8,128)(2,1)} %subtract_convert_fusion) | copy-start | bytes 1769476
  252.9 4.1 %copy-start.15 = (bf16[384,2560]{1,0:T(8,128)(2,1)S(1)}, bf16[384,2560]{1,0:T(8,128)(2,1)}, u32[]{:S(2)}) copy-start(bf16[384,2560]{1,0:T(8,128)(2,1)} %param.33) | copy-start | bytes 5898244
  258.8 26.0 %copy-start.1 = (bf16[640,2560]{1,0:T(8,128)(2,1)S(1)}, bf16[640,2560]{1,0:T(8,128)(2,1)}, u32[]{:S(2)}) copy-start(bf16[640,2560]{1,0:T(8,128)(2,1)} %param.26) | copy-start | bytes 9830404
Sparse Core Ops, SparseCore 0:
  31.3 24.4 reduce-scatter.3
  156.1 72.5 reduce-scatter.7
  258.9 23.8 reduce-scatter.5

commit v10 on v8

--- a/solution.py
+++ b/solution.py
@@ -25,10 +25,13 @@
         position[:, None] == position[None, :]
     )
     closure = adjacency.astype(jnp.float32)
-    for doubling in range(max(1, (tree_size - 1).bit_length())):
-        closure = jnp.minimum(
+
+    def doubling(step, closure):
+        return jnp.minimum(
             jnp.einsum("...ij,...jk->...ik", closure, closure, precision=lax.Precision.HIGHEST), 1.0
         )
+
+    closure = lax.fori_loop(0, max(1, (tree_size - 1).bit_length()), doubling, closure)
     return closure > 0.5
 
 
@@ -128,8 +131,7 @@
     attn_part = jnp.sum(attn_blocks.astype(jnp.float32), axis=0)
     residual_part = lax.dynamic_slice_in_dim(residual, column, part_width, 1)
     hidden_part_bf = (residual_part.astype(jnp.float32) + attn_part).astype(jnp.bfloat16)
-    hidden_bf = lax.all_gather(hidden_part_bf[None], "tp", axis=0, tiled=True)
-    hidden = hidden_bf.transpose(1, 0, 2).reshape(row_count, model_width).astype(jnp.float32)
+    hidden = lax.all_gather(hidden_part_bf, "tp", axis=1, tiled=True).astype(jnp.float32)
     rstd = lax.rsqrt(jnp.mean(hidden * hidden, axis=1, keepdims=True) + EPSILON)
     normed = hidden * rstd * norm_gain
     logits = jnp.dot(normed, router_weight, precision=lax.Precision.HIGHEST)

time: 285 us -> 288 us (1.011)
  no operation moved by 1% of the time
where the time goes in v10:
time: 288 us
  waiting for transfers between devices  125 us (43%)
  matrix products  45.3 us (16%)
  blocking collectives  38.1 us (13%)
  local copies, waits for them, and re-layouts  28.3 us (10%)
  starting transfers between devices  20.5 us (7%)
  other arithmetic  16.7 us (6%)
  between operations  13.8 us (5%)
    all_to_all x2, waiting for transfers between devices, shards(): lax.all_to_all(outbox, 'req', split_axis=0, concat_axis=0, tiled=True)  70.1 us
    all_to_all x1, waiting for transfers between devices, shards(): lax.all_to_all(outputs, 'req', split_axis=0, concat_axis=0, tiled=True)  34.6 us
    all_gather x1, blocking collectives, shards(): lax.all_gather(hidden_part_bf, 'tp', axis=1, tiled=True).astype(jnp.float32)  19.7 us
    all_to_all x1, blocking collectives, shards(): lax.all_to_all(outputs, 'req', split_axis=0, concat_axis=0, tiled=True)  18.4 us
    all_to_all x1, waiting for transfers between devices, shards(): lax.all_to_all(attn_blocks.transpose(1, 0, 2), 'tp', split_axis=0, concat...  16.7 us
    dot_general x2, matrix products, shards(): jnp.einsum('md,dcf->mcf', rows, expert_gate_up[expert], preferred_element...  13.3 us
    all_to_all x2, starting transfers between devices, shards(): lax.all_to_all(outbox, 'req', split_axis=0, concat_axis=0, tiled=True)  9.22 us
    slice x1, local copies, waits for them, and re-layouts, shards(): expert_gate_up[expert]  8.13 us
  transfers between devices with their start and end apart: 6, of which 5 were waited for; matrix products, arithmetic and copies ran while one was open for 21% of the time, Pallas kernels for 0%

profile of v10, /device:TPU:0, one launch (start us, length us, event | category | flops | bytes accessed | tf_op | source)
XLA Modules:
  0.0 287.6 jit_solution(12714422827853273076)
XLA Ops:
  6.6 0.8 compare_select_fusion
  7.5 0.8 iota_compare_fusion.6
  8.3 2.0 reshape.235
  10.2 0.8 fusion.61
  11.0 1.6 while.10
  12.7 2.9 %gather_fusion.1 = bf16[64,64,128]{2,1,0:T(8,128)(2,1)} fusion(bf16[64,64,128]{2,1,0:T(8,128)(2,1)} %param.22, s32[1024]{0:T(1024)S(1)} %pad_clamp_fusion), kind=kCustom, calls=%fused_computation.1 | custom fusion | bytes 2097408 | tf_op jit(solution)/shard_map/gather | solution.py:96
  15.6 2.1 bitcast_reduce_fusion
  18.2 1.4 copy-done.2
  19.7 1.0 fusion.8
  20.8 2.9 %gather_fusion = bf16[64,64,128]{2,1,0:T(8,128)(2,1)} fusion(bf16[64,64,128]{2,1,0:T(8,128)(2,1)} %param.23, s32[1024]{0:T(1024)S(1)} %pad_clamp_fusion), kind=kCustom, calls=%fused_computation | custom fusion | bytes 2097408 | tf_op jit(solution)/shard_map/gather | solution.py:97
  23.7 3.5 %fusion.17 = f32[4,128,5,48]{1,3,2,0:T(8,128)S(1)} fusion(bf16[4,1024,128,1]{2,1,3,0:T(8,128)(2,1)} %bitcast.219, f32[4,1024,48,5]{1,2,3,0:T(8,128)} %copy-done.2, f32[4,5,48]{2,1,0:T(8,128)S(1)} %add.91, f32[4,5,48]{2,1,0:T(8,128)S(1)} %max.9, pred[4,1024]{1,0:T(4,128)(4,1)S(1)} %iota_compare_fusion.6), kind=kOutput, calls=%fused_computation.38 | convolution fusion | flops 256573440 | bytes 5484032 | tf_op jit(solution)/shard_map/rkgtc,rckd->rtkgd/dot_general | solution.py:57
  27.6 0.9 convolution_convert_fusion.4
  28.5 1.0 copy.155
  29.6 6.3 %all-to-all-start = ((bf16[4,192,640]{2,1,0:T(8,128)(2,1)}), bf16[4,192,640]{2,1,0:T(8,128)(2,1)S(1)}, u32[]{:S(2)}, u32[]{:S(2)}) async-start(bf16[4,192,640]{2,1,0:T(8,128)(2,1)} %bitcast.205), calls=%async_computation | async-start | bytes 1966080 | tf_op jit(solution)/shard_map/all_to_all | solution.py:128
  36.3 4.5 %reduce-window.6 = s32[16,9,128]{2,1,0:T(8,128)S(1)} reduce-window(s32[16,9,128]{2,1,0:T(8,128)S(1)} %fusion.59, s32[]{:T(128)} %constant.10.clone.1), window={size=1x1x128 pad=0_0x0_0x127_0}, to_apply=%region_8.9 | reduce-window | flops 2340864 | bytes 147460 | tf_op jit(solution)/shard_map/reduce-window
  40.9 0.4 slice_reduce_fusion
  41.8 1.2 fusion
  43.0 0.5 copy.103
  43.5 16.7 %all-to-all-done = bf16[4,192,640]{2,1,0:T(8,128)(2,1)S(1)} async-done(((bf16[4,192,640]{2,1,0:T(8,128)(2,1)}), bf16[4,192,640]{2,1,0:T(8,128)(2,1)S(1)}, u32[]{:S(2)}, u32[]{:S(2)}) %all-to-all-start) | async-done | bytes 983072 | tf_op jit(solution)/shard_map/all_to_all | solution.py:128
  60.3 1.0 add_convert_fusion
  61.3 19.7 %all_gather.3 = bf16[192,2560]{1,0:T(8,128)(2,1)S(1)} all-gather(bf16[192,640]{1,0:T(8,128)(2,1)S(1)} %add_convert_fusion), channel_id=1, replica_groups=mesh['req'=8,'tp'=4] {'tp'}, dimensions={1}, use_global_device_ids=true | all-gather | bytes 1228800 | tf_op jit(solution)/shard_map/all_gather | solution.py:134
  81.3 3.3 %convolution_convert_fusion = bf16[8,96,2560]{2,1,0:T(8,128)(2,1)} fusion(pred[192,8,2,96]{0,3,2,1:T(32,128)(4,1)S(1)} %bitcast.217, bf16[192,2560]{1,0:T(8,128)(2,1)S(1)} %all_gather.3, f32[2560]{0:T(1024)S(1)} %copy-done.9, f32[192]{0:T(256)S(1)} %add_rsqrt_fusion), kind=kOutput, calls=%fused_computation.6 | convolution fusion | flops 758906880 | bytes 5125120 | tf_op jit(solution)/shard_map/tgc,td->gcd/dot_general | solution.py:145
  84.6 4.5 %all-to-all-start.3 = ((bf16[8,96,2560]{2,1,0:T(8,128)(2,1)}), bf16[8,96,2560]{2,1,0:T(8,128)(2,1)}, u32[]{:S(2)}, u32[]{:S(2)}) async-start(bf16[8,96,2560]{2,1,0:T(8,128)(2,1)} %convolution_convert_fusion), calls=%async_computation.4 | async-start | bytes 7864320 | tf_op jit(solution)/shard_map/all_to_all | solution.py:148
  89.1 8.1 %fusion.75 = (bf16[1,2560,2,384]{3,2,1,0:T(2,128)(2,1)}, bf16[1,2560,2,384]{3,2,1,0:T(2,128)(2,1)}) fusion(bf16[2,2560,2,384]{3,2,1,0:T(2,128)(2,1)} %param.32), kind=kLoop, calls=%fused_computation.127 | loop fusion | bytes 15728640 | tf_op jit(solution)/shard_map/slice | solution.py:151
  97.3 3.2 %convolution_convert_fusion.1 = bf16[8,96,2560]{2,1,0:T(8,128)(2,1)} fusion(pred[192,8,2,96]{0,3,2,1:T(32,128)(4,1)S(1)} %bitcast.218, bf16[192,2560]{1,0:T(8,128)(2,1)S(1)} %all_gather.3, f32[2560]{0:T(1024)S(1)} %copy-done.9, f32[192]{0:T(256)S(1)} %add_rsqrt_fusion), kind=kOutput, calls=%fused_computation.7 | convolution fusion | flops 758906880 | bytes 5125120 | tf_op jit(solution)/shard_map/tgc,td->gcd/dot_general | solution.py:145
  100.5 34.9 %all-to-all-done.3 = bf16[8,96,2560]{2,1,0:T(8,128)(2,1)} async-done(((bf16[8,96,2560]{2,1,0:T(8,128)(2,1)}), bf16[8,96,2560]{2,1,0:T(8,128)(2,1)}, u32[]{:S(2)}, u32[]{:S(2)}) %all-to-all-start.3) | async-done | bytes 3932192 | tf_op jit(solution)/shard_map/all_to_all | solution.py:148
  135.4 4.7 %all-to-all-start.1 = ((bf16[8,96,2560]{2,1,0:T(8,128)(2,1)}), bf16[8,96,2560]{2,1,0:T(8,128)(2,1)}, u32[]{:S(2)}, u32[]{:S(2)}) async-start(bf16[8,96,2560]{2,1,0:T(8,128)(2,1)} %convolution_convert_fusion.1), calls=%async_computation.1 | async-start | bytes 7864320 | tf_op jit(solution)/shard_map/all_to_all | solution.py:148
  140.2 6.7 %fusion.1 = f32[768,2,384]{2,0,1:T(8,128)S(1)} fusion(bf16[768,2560,1]{1,0,2:T(8,128)(2,1)} %bitcast.43, bf16[1,2560,2,384]{3,2,1,0:T(2,128)(2,1)} %get-tuple-element.23), kind=kOutput, calls=%fused_computation.14 | convolution fusion | flops 3019898880 | bytes 10223616 | tf_op jit(solution)/shard_map/md,dcf->mcf/dot_general | solution.py:150
  146.9 2.2 convolution_convert_fusion.2
  149.1 2.2 copy.153
  151.4 35.1 %all-to-all-done.1 = bf16[8,96,2560]{2,1,0:T(8,128)(2,1)} async-done(((bf16[8,96,2560]{2,1,0:T(8,128)(2,1)}), bf16[8,96,2560]{2,1,0:T(8,128)(2,1)}, u32[]{:S(2)}, u32[]{:S(2)}) %all-to-all-start.1) | async-done | bytes 3932192 | tf_op jit(solution)/shard_map/all_to_all | solution.py:148
  186.5 6.7 %fusion.2 = f32[768,2,384]{2,0,1:T(8,128)S(1)} fusion(bf16[768,2560,1]{1,0,2:T(8,128)(2,1)} %bitcast.30, bf16[1,2560,2,384]{3,2,1,0:T(2,128)(2,1)} %get-tuple-element.22), kind=kOutput, calls=%fused_computation.16 | convolution fusion | flops 3019898880 | bytes 10223616 | tf_op jit(solution)/shard_map/md,dcf->mcf/dot_general | solution.py:150
  193.2 4.2 %convolution_convert_fusion.3 = bf16[768,2560]{1,0:T(8,128)(2,1)} fusion(bf16[2,384,2560]{2,1,0:T(8,128)(2,1)S(1)} %copy-done.12, f32[768,2,384]{2,0,1:T(8,128)S(1)} %fusion.2), kind=kOutput, calls=%fused_computation.9 | convolution fusion | flops 1513684992 | bytes 8257536 | tf_op jit(solution)/shard_map/dot_general | solution.py:154
  197.4 4.6 %all-to-all-start.2 = ((bf16[8,96,2560]{2,1,0:T(8,128)(2,1)}), bf16[8,96,2560]{2,1,0:T(8,128)(2,1)}, u32[]{:S(2)}, u32[]{:S(2)}) async-start(bf16[8,96,2560]{2,1,0:T(8,128)(2,1)} %bitcast.213), calls=%async_computation.2 | async-start | bytes 7864320 | tf_op jit(solution)/shard_map/all_to_all | solution.py:163
  202.3 1.8 fusion.11
  204.2 2.2 select_reduce_fusion
  206.4 3.3 %reshape.242 = f32[1,192,8,2,96]{4,3,2,1,0:T(2,128)S(1)} reshape(f32[192,1536]{1,0:T(8,128)} %select_reduce_fusion) | data formatting | bytes 2359296 | tf_op jit(solution)/shard_map/reshape | solution.py:171
  209.7 1.4 copy.148
  211.2 1.4 subtract_convert_fusion
  212.6 1.1 fusion.5
  213.7 34.6 %all-to-all-done.2 = bf16[8,96,2560]{2,1,0:T(8,128)(2,1)} async-done(((bf16[8,96,2560]{2,1,0:T(8,128)(2,1)}), bf16[8,96,2560]{2,1,0:T(8,128)(2,1)}, u32[]{:S(2)}, u32[]{:S(2)}) %all-to-all-start.2) | async-done | bytes 3932192 | tf_op jit(solution)/shard_map/all_to_all | solution.py:163
  248.3 4.1 %convolution_bitcast_fusion = f32[2,192,2560]{2,1,0:T(8,128)S(1)} fusion(bf16[8,96,2560]{2,1,0:T(8,128)(2,1)} %all-to-all-done.2, bf16[1,192,8,2,96]{4,1,2,0,3:T(8,128)(2,1)S(1)} %copy-done.3, bf16[1,192,8,2,96]{4,1,2,0,3:T(8,128)(2,1)S(1)} %copy-done.4), kind=kOutput, calls=%fused_computation.10 | convolution fusion | flops 1510244352 | bytes 9043968 | tf_op jit(solution)/shard_map/stgc,gcd->std/dot_general | solution.py:177
  252.4 0.7 fusion.7
  253.1 1.0 copy.154
  254.2 18.4 %all_to_all.25 = bf16[8,96,640]{2,1,0:T(8,128)(2,1)S(1)} all-to-all(bf16[8,96,640]{2,1,0:T(8,128)(2,1)} %bitcast.221), channel_id=1, replica_groups=mesh['req'=8,'tp'=4] {'req'}, dimensions={0} | all-to-all | bytes 1966080 | tf_op jit(solution)/shard_map/all_to_all | solution.py:163
  272.6 2.8 convolution_bitcast_fusion.1
  275.5 3.3 %reduce-scatter.3.cloned.1.call-done = bf16[1,192,640]{2,1,0:T(8,128)(2,1)} async-done(((bf16[4,192,640]{2,1,0:T(8,128)(2,1)}), bf16[1,192,640]{2,1,0:T(8,128)(2,1)}) %reduce-scatter.3.cloned.1.call-update) | async-done | bytes 245776 | tf_op jit(solution)/shard_map/reduce_scatter | solution.py:192
  278.8 2.0 fusion.46
  (77 shorter events, 4.3 us)
Async XLA Ops:
  6.5 21.0 %copy-start = (bf16[640,2560]{1,0:T(8,128)(2,1)S(1)}, bf16[640,2560]{1,0:T(8,128)(2,1)}, u32[]{:S(2)}) copy-start(bf16[640,2560]{1,0:T(8,128)(2,1)} %param.28) | copy-start | bytes 9830404
  12.6 5.2 %copy-start.10 = (bf16[192,128]{1,0:T(8,128)(2,1)S(1)}, bf16[192,128]{1,0:T(8,128)(2,1)}, u32[]{:S(2)}) copy-start(bf16[192,128]{1,0:T(8,128)(2,1)} %param.20) | copy-start | bytes 147460
  15.6 2.2 copy-start.5
  17.8 1.9 copy-start.2
  18.2 2.4 copy-start.6
  23.6 3.5 %copy-start.7 = (f32[4,1,5,48,48]{3,4,2,0,1:T(8,128)S(1)}, f32[4,1,5,48,48]{3,4,2,0,1:T(8,128)}, u32[]{:S(2)}) copy-start(f32[4,1,5,48,48]{3,4,2,0,1:T(8,128)} %copy-done.6) | copy-start | bytes 552964
  23.7 3.5 %copy-start.16 = (bf16[192,128]{1,0:T(8,128)(2,1)S(1)}, bf16[192,128]{1,0:T(8,128)(2,1)}, u32[]{:S(2)}) copy-start(bf16[192,128]{1,0:T(8,128)(2,1)} %param.21) | copy-start | bytes 147460
  27.6 8.3 %copy-start.8 = (s32[192,6]{0,1:T(8,128)S(1)}, s32[192,6]{0,1:T(8,128)}, u32[]{:S(2)}) copy-start(s32[192,6]{0,1:T(8,128)} %param.31) | copy-start | bytes 13828
  29.6 30.6 %all-to-all-start = ((bf16[4,192,640]{2,1,0:T(8,128)(2,1)}), bf16[4,192,640]{2,1,0:T(8,128)(2,1)S(1)}, u32[]{:S(2)}, u32[]{:S(2)}) async-start(bf16[4,192,640]{2,1,0:T(8,128)(2,1)} %bitcast.205), calls=%async_computation | async-start | bytes 1966080 | tf_op jit(solution)/shard_map/all_to_all | solution.py:128
  35.9 45.4 %copy-start.9 = (f32[2560]{0:T(1024)S(1)}, f32[2560]{0:T(1024)}, u32[]{:S(2)}) copy-start(f32[2560]{0:T(1024)} %param.29) | copy-start | bytes 30724
  84.6 50.8 %all-to-all-start.3 = ((bf16[8,96,2560]{2,1,0:T(8,128)(2,1)}), bf16[8,96,2560]{2,1,0:T(8,128)(2,1)}, u32[]{:S(2)}, u32[]{:S(2)}) async-start(bf16[8,96,2560]{2,1,0:T(8,128)(2,1)} %convolution_convert_fusion), calls=%async_computation.4 | async-start | bytes 7864320 | tf_op jit(solution)/shard_map/all_to_all | solution.py:148
  135.4 51.0 %all-to-all-start.1 = ((bf16[8,96,2560]{2,1,0:T(8,128)(2,1)}), bf16[8,96,2560]{2,1,0:T(8,128)(2,1)}, u32[]{:S(2)}, u32[]{:S(2)}) async-start(bf16[8,96,2560]{2,1,0:T(8,128)(2,1)} %convolution_convert_fusion.1), calls=%async_computation.1 | async-start | bytes 7864320 | tf_op jit(solution)/shard_map/all_to_all | solution.py:148
  140.2 114.1 %reduce-scatter.5.cloned.1.call-start = ((), (), s32[]{:S(2)}) async-start(), calls=%async_computation.8 | async-start | bytes 4915200 | tf_op jit(solution)/shard_map/reduce_scatter | solution.py:159
  140.2 6.7 %copy-start.11 = (bf16[2,384,2560]{2,1,0:T(8,128)(2,1)S(1)}, bf16[2,384,2560]{2,1,0:T(8,128)(2,1)}, u32[]{:S(2)}) copy-start(bf16[2,384,2560]{2,1,0:T(8,128)(2,1)} %param.33) | copy-start | bytes 11796484
  186.5 6.7 %copy-start.12 = (bf16[2,384,2560]{2,1,0:T(8,128)(2,1)S(1)}, bf16[2,384,2560]{2,1,0:T(8,128)(2,1)}, u32[]{:S(2)}) copy-start(bf16[2,384,2560]{2,1,0:T(8,128)(2,1)} %param.33) | copy-start | bytes 11796484
  197.4 4.9 %copy-start.15 = (f32[2560,16]{0,1:T(8,128)S(1)}, f32[2560,16]{0,1:T(8,128)}, u32[]{:S(2)}) copy-start(f32[2560,16]{0,1:T(8,128)} %param.30) | copy-start | bytes 491524
  197.4 51.0 %all-to-all-start.2 = ((bf16[8,96,2560]{2,1,0:T(8,128)(2,1)}), bf16[8,96,2560]{2,1,0:T(8,128)(2,1)}, u32[]{:S(2)}, u32[]{:S(2)}) async-start(bf16[8,96,2560]{2,1,0:T(8,128)(2,1)} %bitcast.213), calls=%async_computation.2 | async-start | bytes 7864320 | tf_op jit(solution)/shard_map/all_to_all | solution.py:163
  202.0 76.7 %reduce-scatter.3.cloned.1.call-start = ((), (), s32[]{:S(2)}) async-start(), calls=%async_computation.7 | async-start | bytes 1228800 | tf_op jit(solution)/shard_map/reduce_scatter | solution.py:192
  209.7 2.8 copy-start.13
  212.6 35.8 %copy-start.3 = (bf16[1,192,8,2,96]{4,1,2,0,3:T(8,128)(2,1)S(1)}, bf16[1,192,8,2,96]{4,1,2,0,3:T(8,128)(2,1)}, u32[]{:S(2)}) copy-start(bf16[1,192,8,2,96]{4,1,2,0,3:T(8,128)(2,1)} %copy.148) | copy-start | bytes 1769476
  212.6 35.8 %copy-start.4 = (bf16[1,192,8,2,96]{4,1,2,0,3:T(8,128)(2,1)S(1)}, bf16[1,192,8,2,96]{4,1,2,0,3:T(8,128)(2,1)}, u32[]{:S(2)}) copy-start(bf16[1,192,8,2,96]{4,1,2,0,3:T(8,128)(2,1)} %subtract_convert_fusion) | copy-start | bytes 1769476
  248.3 4.1 %copy-start.14 = (bf16[384,2560]{1,0:T(8,128)(2,1)S(1)}, bf16[384,2560]{1,0:T(8,128)(2,1)}, u32[]{:S(2)}) copy-start(bf16[384,2560]{1,0:T(8,128)(2,1)} %param.35) | copy-start | bytes 5898244
  254.2 26.6 %copy-start.1 = (bf16[640,2560]{1,0:T(8,128)(2,1)S(1)}, bf16[640,2560]{1,0:T(8,128)(2,1)}, u32[]{:S(2)}) copy-start(bf16[640,2560]{1,0:T(8,128)(2,1)} %param.28) | copy-start | bytes 9830404
Sparse Core Ops, SparseCore 0:
  151.5 73.1 reduce-scatter.4
  254.3 24.3 reduce-scatter.2

commit v11 on v8

--- a/solution.py
+++ b/solution.py
@@ -90,8 +90,15 @@
     part_width = model_width // tp_count
     pages_dev = key_pages.shape[0]
     local_pages = page_table - lax.axis_index("req") * pages_dev
-    cache_keys = key_pages[local_pages].reshape(requests, -1, kv_local, HD)
-    cache_values = value_pages[local_pages].reshape(requests, -1, kv_local, HD)
+    page_pick = (
+        local_pages.reshape(-1)[:, None] == jnp.arange(pages_dev, dtype=jnp.int32)[None, :]
+    ).astype(key_pages.dtype)
+    cache_keys = jnp.dot(
+        page_pick, key_pages.reshape(pages_dev, -1), preferred_element_type=jnp.float32
+    ).astype(key_pages.dtype).reshape(requests, -1, kv_local, HD)
+    cache_values = jnp.dot(
+        page_pick, value_pages.reshape(pages_dev, -1), preferred_element_type=jnp.float32
+    ).astype(value_pages.dtype).reshape(requests, -1, kv_local, HD)
     head_outputs = tree_attention(
         queries.reshape(requests, tree_size, kv_local, head_ratio, HD),
         cache_keys,
@@ -128,8 +135,7 @@
     attn_part = jnp.sum(attn_blocks.astype(jnp.float32), axis=0)
     residual_part = lax.dynamic_slice_in_dim(residual, column, part_width, 1)
     hidden_part_bf = (residual_part.astype(jnp.float32) + attn_part).astype(jnp.bfloat16)
-    hidden_bf = lax.all_gather(hidden_part_bf[None], "tp", axis=0, tiled=True)
-    hidden = hidden_bf.transpose(1, 0, 2).reshape(row_count, model_width).astype(jnp.float32)
+    hidden = lax.all_gather(hidden_part_bf, "tp", axis=1, tiled=True).astype(jnp.float32)
     rstd = lax.rsqrt(jnp.mean(hidden * hidden, axis=1, keepdims=True) + EPSILON)
     normed = hidden * rstd * norm_gain
     logits = jnp.dot(normed, router_weight, precision=lax.Precision.HIGHEST)

time: 285 us -> 290 us (1.018)
  matrix products: 46 us -> 50.5 us
    gather x2 -> x0, local copies, waits for them, and re-layouts: 5.83 us -> none  [the longest x1 2.94 us: shards(): cache_keys = key_pages[local_pages].reshape(requests, -1, kv_local, HD)]
    dot_general x0 -> x2, matrix products: none -> 5.19 us  [the longest x1 3.3 us: shards(): jnp.dot(page_pick, key_pages.reshape(pages_dev, -1), preferred_element_ty...]
    another operation x1 -> x3, local copies, waits for them, and re-layouts: 1.05 us -> 5.7 us
where the time goes in v11:
time: 290 us; the launch traced here: 289 us
  waiting for transfers between devices  125 us (43%)
  matrix products  50.5 us (17%)
  blocking collectives  38.3 us (13%)
  local copies, waits for them, and re-layouts  26.2 us (9%)
  starting transfers between devices  20.3 us (7%)
  other arithmetic  15.2 us (5%)
  between operations  13.9 us (5%)
    all_to_all x2, waiting for transfers between devices, shards(): lax.all_to_all(outbox, 'req', split_axis=0, concat_axis=0, tiled=True)  70 us
    all_to_all x1, waiting for transfers between devices, shards(): lax.all_to_all(outputs, 'req', split_axis=0, concat_axis=0, tiled=True)  34.6 us
    all_gather x1, blocking collectives, shards(): lax.all_gather(hidden_part_bf, 'tp', axis=1, tiled=True).astype(jnp.float32)  19.9 us
    all_to_all x1, blocking collectives, shards(): lax.all_to_all(outputs, 'req', split_axis=0, concat_axis=0, tiled=True)  18.4 us
    all_to_all x1, waiting for transfers between devices, shards(): lax.all_to_all(attn_blocks.transpose(1, 0, 2), 'tp', split_axis=0, concat...  16.7 us
    dot_general x2, matrix products, shards(): jnp.einsum('md,dcf->mcf', rows, expert_gate_up[expert], preferred_element...  13.3 us
    all_to_all x2, starting transfers between devices, shards(): lax.all_to_all(outbox, 'req', split_axis=0, concat_axis=0, tiled=True)  9.04 us
    slice x1, local copies, waits for them, and re-layouts, shards(): expert_gate_up[expert]  8.13 us
  transfers between devices with their start and end apart: 6, of which 5 were waited for; matrix products, arithmetic and copies ran while one was open for 21% of the time, Pallas kernels for 0%

profile of v11, /device:TPU:0, one launch (start us, length us, event | category | flops | bytes accessed | tf_op | source)
XLA Modules:
  0.0 289.1 jit_solution(2502633517825118963)
XLA Ops:
  6.6 0.8 broadcast_subtract_fusion
  7.5 3.3 %convolution_convert_fusion = bf16[64,8192]{1,0:T(8,128)(2,1)} fusion(bf16[8,8,64,128]{3,2,1,0:T(8,128)(2,1)} %bitcast.226, s32[64]{0:T(128)S(1)} %eq.96), kind=kOutput, calls=%fused_computation | convolution fusion | flops 67637248 | bytes 2097408 | tf_op jit(solution)/shard_map/dot_general | solution.py:96
  10.8 2.3 reshape.259
  13.2 1.0 reshape.244
  15.8 2.1 bitcast_reduce_fusion
  18.0 0.4 fusion.87
  18.4 1.4 copy-done.2
  19.8 1.0 fusion.8
  20.9 1.9 convolution_convert_fusion.1
  22.8 2.3 reshape.261
  25.1 3.5 %fusion.17 = f32[4,128,5,48]{1,3,2,0:T(8,128)S(1)} fusion(f32[4,1024,48,5]{1,2,3,0:T(8,128)} %copy-done.2, f32[4,5,48]{2,1,0:T(8,128)S(1)} %add.83, f32[4,5,48]{2,1,0:T(8,128)S(1)} %max.9, pred[4,1024]{1,0:T(4,128)(4,1)S(1)} %iota_compare_fusion.9, bf16[4,1024,128,1]{2,1,0,3:T(8,128)(2,1)} %reshape.261), kind=kOutput, calls=%fused_computation.37 | convolution fusion | flops 256573440 | bytes 5484032 | tf_op jit(solution)/shard_map/rkgtc,rckd->rtkgd/dot_general | solution.py:54
  29.1 0.9 convolution_convert_fusion.6
  30.0 1.0 copy.165
  31.0 6.3 %all-to-all-start = ((bf16[4,192,640]{2,1,0:T(8,128)(2,1)}), bf16[4,192,640]{2,1,0:T(8,128)(2,1)S(1)}, u32[]{:S(2)}, u32[]{:S(2)}) async-start(bf16[4,192,640]{2,1,0:T(8,128)(2,1)} %bitcast.217), calls=%async_computation | async-start | bytes 1966080 | tf_op jit(solution)/shard_map/all_to_all | solution.py:132
  37.8 4.5 %reduce-window.6 = s32[16,9,128]{2,1,0:T(8,128)S(1)} reduce-window(s32[16,9,128]{2,1,0:T(8,128)S(1)} %fusion.66, s32[]{:T(128)} %constant.17.clone.1), window={size=1x1x128 pad=0_0x0_0x127_0}, to_apply=%region_6.7 | reduce-window | flops 2340864 | bytes 147460 | tf_op jit(solution)/shard_map/reduce-window
  42.3 0.4 slice_reduce_fusion
  43.3 1.2 fusion
  44.5 0.5 copy.103
  45.0 16.7 %all-to-all-done = bf16[4,192,640]{2,1,0:T(8,128)(2,1)S(1)} async-done(((bf16[4,192,640]{2,1,0:T(8,128)(2,1)}), bf16[4,192,640]{2,1,0:T(8,128)(2,1)S(1)}, u32[]{:S(2)}, u32[]{:S(2)}) %all-to-all-start) | async-done | bytes 983072 | tf_op jit(solution)/shard_map/all_to_all | solution.py:132
  61.8 1.0 add_convert_fusion
  62.8 19.9 %all_gather.3 = bf16[192,2560]{1,0:T(8,128)(2,1)S(1)} all-gather(bf16[192,640]{1,0:T(8,128)(2,1)S(1)} %add_convert_fusion), channel_id=1, replica_groups=mesh['req'=8,'tp'=4] {'tp'}, dimensions={1}, use_global_device_ids=true | all-gather | bytes 1228800 | tf_op jit(solution)/shard_map/all_gather | solution.py:138
  83.0 3.3 %convolution_convert_fusion.2 = bf16[8,96,2560]{2,1,0:T(8,128)(2,1)} fusion(pred[192,8,2,96]{0,3,2,1:T(32,128)(4,1)S(1)} %bitcast.224, bf16[192,2560]{1,0:T(8,128)(2,1)S(1)} %all_gather.3, f32[2560]{0:T(1024)S(1)} %copy-done.11, f32[192]{0:T(256)S(1)} %add_rsqrt_fusion), kind=kOutput, calls=%fused_computation.5 | convolution fusion | flops 758906880 | bytes 5125120 | tf_op jit(solution)/shard_map/tgc,td->gcd/dot_general | solution.py:149
  86.3 4.5 %all-to-all-start.3 = ((bf16[8,96,2560]{2,1,0:T(8,128)(2,1)}), bf16[8,96,2560]{2,1,0:T(8,128)(2,1)}, u32[]{:S(2)}, u32[]{:S(2)}) async-start(bf16[8,96,2560]{2,1,0:T(8,128)(2,1)} %convolution_convert_fusion.2), calls=%async_computation.4 | async-start | bytes 7864320 | tf_op jit(solution)/shard_map/all_to_all | solution.py:152
  90.8 8.1 %fusion.86 = (bf16[1,2560,2,384]{3,2,1,0:T(2,128)(2,1)}, bf16[1,2560,2,384]{3,2,1,0:T(2,128)(2,1)}) fusion(bf16[2,2560,2,384]{3,2,1,0:T(2,128)(2,1)} %param.30), kind=kLoop, calls=%fused_computation.141 | loop fusion | bytes 15728640 | tf_op jit(solution)/shard_map/slice | solution.py:155
  98.9 3.2 %convolution_convert_fusion.3 = bf16[8,96,2560]{2,1,0:T(8,128)(2,1)} fusion(pred[192,8,2,96]{0,3,2,1:T(32,128)(4,1)S(1)} %bitcast.225, bf16[192,2560]{1,0:T(8,128)(2,1)S(1)} %all_gather.3, f32[2560]{0:T(1024)S(1)} %copy-done.11, f32[192]{0:T(256)S(1)} %add_rsqrt_fusion), kind=kOutput, calls=%fused_computation.6 | convolution fusion | flops 758906880 | bytes 5125120 | tf_op jit(solution)/shard_map/tgc,td->gcd/dot_general | solution.py:149
  102.2 34.9 %all-to-all-done.3 = bf16[8,96,2560]{2,1,0:T(8,128)(2,1)} async-done(((bf16[8,96,2560]{2,1,0:T(8,128)(2,1)}), bf16[8,96,2560]{2,1,0:T(8,128)(2,1)}, u32[]{:S(2)}, u32[]{:S(2)}) %all-to-all-start.3) | async-done | bytes 3932192 | tf_op jit(solution)/shard_map/all_to_all | solution.py:152
  137.1 4.5 %all-to-all-start.1 = ((bf16[8,96,2560]{2,1,0:T(8,128)(2,1)}), bf16[8,96,2560]{2,1,0:T(8,128)(2,1)}, u32[]{:S(2)}, u32[]{:S(2)}) async-start(bf16[8,96,2560]{2,1,0:T(8,128)(2,1)} %convolution_convert_fusion.3), calls=%async_computation.1 | async-start | bytes 7864320 | tf_op jit(solution)/shard_map/all_to_all | solution.py:152
  141.7 6.7 %fusion.1 = f32[768,2,384]{2,0,1:T(8,128)S(1)} fusion(bf16[768,2560,1]{1,0,2:T(8,128)(2,1)} %bitcast.39, bf16[1,2560,2,384]{3,2,1,0:T(2,128)(2,1)} %get-tuple-element.6), kind=kOutput, calls=%fused_computation.13 | convolution fusion | flops 3019898880 | bytes 10223616 | tf_op jit(solution)/shard_map/md,dcf->mcf/dot_general | solution.py:154
  148.4 2.2 convolution_convert_fusion.4
  150.6 2.2 copy.163
  152.8 35.1 %all-to-all-done.1 = bf16[8,96,2560]{2,1,0:T(8,128)(2,1)} async-done(((bf16[8,96,2560]{2,1,0:T(8,128)(2,1)}), bf16[8,96,2560]{2,1,0:T(8,128)(2,1)}, u32[]{:S(2)}, u32[]{:S(2)}) %all-to-all-start.1) | async-done | bytes 3932192 | tf_op jit(solution)/shard_map/all_to_all | solution.py:152
  188.0 6.7 %fusion.2 = f32[768,2,384]{2,0,1:T(8,128)S(1)} fusion(bf16[768,2560,1]{1,0,2:T(8,128)(2,1)} %bitcast.26, bf16[1,2560,2,384]{3,2,1,0:T(2,128)(2,1)} %get-tuple-element.5), kind=kOutput, calls=%fused_computation.15 | convolution fusion | flops 3019898880 | bytes 10223616 | tf_op jit(solution)/shard_map/md,dcf->mcf/dot_general | solution.py:154
  194.6 4.2 %convolution_convert_fusion.5 = bf16[768,2560]{1,0:T(8,128)(2,1)} fusion(bf16[2,384,2560]{2,1,0:T(8,128)(2,1)S(1)} %copy-done.15, f32[768,2,384]{2,0,1:T(8,128)S(1)} %fusion.2), kind=kOutput, calls=%fused_computation.8 | convolution fusion | flops 1513684992 | bytes 8257536 | tf_op jit(solution)/shard_map/dot_general | solution.py:158
  198.8 4.6 %all-to-all-start.2 = ((bf16[8,96,2560]{2,1,0:T(8,128)(2,1)}), bf16[8,96,2560]{2,1,0:T(8,128)(2,1)}, u32[]{:S(2)}, u32[]{:S(2)}) async-start(bf16[8,96,2560]{2,1,0:T(8,128)(2,1)} %bitcast.220), calls=%async_computation.2 | async-start | bytes 7864320 | tf_op jit(solution)/shard_map/all_to_all | solution.py:167
  203.8 1.8 fusion.11
  205.7 2.2 select_reduce_fusion
  207.9 3.3 %reshape.251 = f32[1,192,8,2,96]{4,3,2,1,0:T(2,128)S(1)} reshape(f32[192,1536]{1,0:T(8,128)} %select_reduce_fusion) | data formatting | bytes 2359296 | tf_op jit(solution)/shard_map/reshape | solution.py:175
  211.2 1.4 copy.158
  212.7 1.4 subtract_convert_fusion
  214.1 1.1 fusion.5
  215.2 34.6 %all-to-all-done.2 = bf16[8,96,2560]{2,1,0:T(8,128)(2,1)} async-done(((bf16[8,96,2560]{2,1,0:T(8,128)(2,1)}), bf16[8,96,2560]{2,1,0:T(8,128)(2,1)}, u32[]{:S(2)}, u32[]{:S(2)}) %all-to-all-start.2) | async-done | bytes 3932192 | tf_op jit(solution)/shard_map/all_to_all | solution.py:167
  249.8 4.1 %convolution_bitcast_fusion = f32[2,192,2560]{2,1,0:T(8,128)S(1)} fusion(bf16[8,96,2560]{2,1,0:T(8,128)(2,1)} %all-to-all-done.2, bf16[1,192,8,2,96]{4,1,2,0,3:T(8,128)(2,1)S(1)} %copy-done.3, bf16[1,192,8,2,96]{4,1,2,0,3:T(8,128)(2,1)S(1)} %copy-done.4), kind=kOutput, calls=%fused_computation.9 | convolution fusion | flops 1510244352 | bytes 9043968 | tf_op jit(solution)/shard_map/stgc,gcd->std/dot_general | solution.py:181
  253.9 0.7 fusion.7
  254.6 1.0 copy.164
  255.7 18.4 %all_to_all.25 = bf16[8,96,640]{2,1,0:T(8,128)(2,1)S(1)} all-to-all(bf16[8,96,640]{2,1,0:T(8,128)(2,1)} %bitcast.229), channel_id=1, replica_groups=mesh['req'=8,'tp'=4] {'req'}, dimensions={0} | all-to-all | bytes 1966080 | tf_op jit(solution)/shard_map/all_to_all | solution.py:167
  274.1 2.8 convolution_bitcast_fusion.1
  276.9 3.3 %reduce-scatter.3.cloned.1.call-done = bf16[1,192,640]{2,1,0:T(8,128)(2,1)} async-done(((bf16[4,192,640]{2,1,0:T(8,128)(2,1)}), bf16[1,192,640]{2,1,0:T(8,128)(2,1)}) %reduce-scatter.3.cloned.1.call-update) | async-done | bytes 245776 | tf_op jit(solution)/shard_map/reduce_scatter | solution.py:196
  280.2 2.0 fusion.54
  (77 shorter events, 4.0 us)
Async XLA Ops:
  6.5 22.5 %copy-start = (bf16[640,2560]{1,0:T(8,128)(2,1)S(1)}, bf16[640,2560]{1,0:T(8,128)(2,1)}, u32[]{:S(2)}) copy-start(bf16[640,2560]{1,0:T(8,128)(2,1)} %param.26) | copy-start | bytes 9830404
  6.5 6.6 %copy-start.13 = (s32[4]{0:T(128)S(1)}, s32[4]{0:T(128)}, u32[]{:S(2)}) copy-start(s32[4]{0:T(128)} %param.23) | copy-start | bytes 52
  6.5 6.7 %copy-start.9 = (bf16[192,640]{1,0:T(8,128)(2,1)S(1)}, bf16[192,640]{1,0:T(8,128)(2,1)}, u32[]{:S(2)}) copy-start(bf16[192,640]{1,0:T(8,128)(2,1)} %param.17) | copy-start | bytes 737284
  6.5 7.7 %copy-start.20 = (s32[4,48]{1,0:T(4,128)S(1)}, s32[4,48]{1,0:T(4,128)}, u32[]{:S(2)}) copy-start(s32[4,48]{1,0:T(4,128)} %param.24) | copy-start | bytes 2308
  14.2 3.7 %copy-start.12 = (bf16[192,128]{1,0:T(8,128)(2,1)S(1)}, bf16[192,128]{1,0:T(8,128)(2,1)}, u32[]{:S(2)}) copy-start(bf16[192,128]{1,0:T(8,128)(2,1)} %param.18) | copy-start | bytes 147460
  15.8 2.2 copy-start.5
  17.9 1.9 copy-start.2
  17.9 3.0 %copy-start.8 = (bf16[64,64,128]{2,1,0:T(8,128)(2,1)S(1)}, bf16[64,64,128]{2,1,0:T(8,128)(2,1)}, u32[]{:S(2)}) copy-start(bf16[64,64,128]{2,1,0:T(8,128)(2,1)} %param.21) | copy-start | bytes 3145732
  18.3 2.4 copy-start.6
  25.1 3.5 %copy-start.7 = (f32[4,1,5,48,48]{3,4,2,0,1:T(8,128)S(1)}, f32[4,1,5,48,48]{3,4,2,0,1:T(8,128)}, u32[]{:S(2)}) copy-start(f32[4,1,5,48,48]{3,4,2,0,1:T(8,128)} %copy-done.6) | copy-start | bytes 552964
  25.1 3.5 %copy-start.19 = (bf16[192,128]{1,0:T(8,128)(2,1)S(1)}, bf16[192,128]{1,0:T(8,128)(2,1)}, u32[]{:S(2)}) copy-start(bf16[192,128]{1,0:T(8,128)(2,1)} %param.19) | copy-start | bytes 147460
  29.1 8.3 %copy-start.10 = (s32[192,6]{0,1:T(8,128)S(1)}, s32[192,6]{0,1:T(8,128)}, u32[]{:S(2)}) copy-start(s32[192,6]{0,1:T(8,128)} %param.29) | copy-start | bytes 13828
  31.0 30.6 %all-to-all-start = ((bf16[4,192,640]{2,1,0:T(8,128)(2,1)}), bf16[4,192,640]{2,1,0:T(8,128)(2,1)S(1)}, u32[]{:S(2)}, u32[]{:S(2)}) async-start(bf16[4,192,640]{2,1,0:T(8,128)(2,1)} %bitcast.217), calls=%async_computation | async-start | bytes 1966080 | tf_op jit(solution)/shard_map/all_to_all | solution.py:132
  37.4 45.6 %copy-start.11 = (f32[2560]{0:T(1024)S(1)}, f32[2560]{0:T(1024)}, u32[]{:S(2)}) copy-start(f32[2560]{0:T(1024)} %param.27) | copy-start | bytes 30724
  86.3 50.8 %all-to-all-start.3 = ((bf16[8,96,2560]{2,1,0:T(8,128)(2,1)}), bf16[8,96,2560]{2,1,0:T(8,128)(2,1)}, u32[]{:S(2)}, u32[]{:S(2)}) async-start(bf16[8,96,2560]{2,1,0:T(8,128)(2,1)} %convolution_convert_fusion.2), calls=%async_computation.4 | async-start | bytes 7864320 | tf_op jit(solution)/shard_map/all_to_all | solution.py:152
  137.1 50.9 %all-to-all-start.1 = ((bf16[8,96,2560]{2,1,0:T(8,128)(2,1)}), bf16[8,96,2560]{2,1,0:T(8,128)(2,1)}, u32[]{:S(2)}, u32[]{:S(2)}) async-start(bf16[8,96,2560]{2,1,0:T(8,128)(2,1)} %convolution_convert_fusion.3), calls=%async_computation.1 | async-start | bytes 7864320 | tf_op jit(solution)/shard_map/all_to_all | solution.py:152
  141.6 114.1 %reduce-scatter.5.cloned.1.call-start = ((), (), s32[]{:S(2)}) async-start(), calls=%async_computation.8 | async-start | bytes 4915200 | tf_op jit(solution)/shard_map/reduce_scatter | solution.py:163
  141.7 6.7 %copy-start.14 = (bf16[2,384,2560]{2,1,0:T(8,128)(2,1)S(1)}, bf16[2,384,2560]{2,1,0:T(8,128)(2,1)}, u32[]{:S(2)}) copy-start(bf16[2,384,2560]{2,1,0:T(8,128)(2,1)} %param.31) | copy-start | bytes 11796484
  188.0 6.7 %copy-start.15 = (bf16[2,384,2560]{2,1,0:T(8,128)(2,1)S(1)}, bf16[2,384,2560]{2,1,0:T(8,128)(2,1)}, u32[]{:S(2)}) copy-start(bf16[2,384,2560]{2,1,0:T(8,128)(2,1)} %param.31) | copy-start | bytes 11796484
  198.8 4.9 %copy-start.18 = (f32[2560,16]{0,1:T(8,128)S(1)}, f32[2560,16]{0,1:T(8,128)}, u32[]{:S(2)}) copy-start(f32[2560,16]{0,1:T(8,128)} %param.28) | copy-start | bytes 491524
  198.8 51.0 %all-to-all-start.2 = ((bf16[8,96,2560]{2,1,0:T(8,128)(2,1)}), bf16[8,96,2560]{2,1,0:T(8,128)(2,1)}, u32[]{:S(2)}, u32[]{:S(2)}) async-start(bf16[8,96,2560]{2,1,0:T(8,128)(2,1)} %bitcast.220), calls=%async_computation.2 | async-start | bytes 7864320 | tf_op jit(solution)/shard_map/all_to_all | solution.py:167
  203.5 76.7 %reduce-scatter.3.cloned.1.call-start = ((), (), s32[]{:S(2)}) async-start(), calls=%async_computation.7 | async-start | bytes 1228800 | tf_op jit(solution)/shard_map/reduce_scatter | solution.py:196
  211.2 2.8 copy-start.16
  214.1 35.8 %copy-start.3 = (bf16[1,192,8,2,96]{4,1,2,0,3:T(8,128)(2,1)S(1)}, bf16[1,192,8,2,96]{4,1,2,0,3:T(8,128)(2,1)}, u32[]{:S(2)}) copy-start(bf16[1,192,8,2,96]{4,1,2,0,3:T(8,128)(2,1)} %copy.158) | copy-start | bytes 1769476
  214.1 35.8 %copy-start.4 = (bf16[1,192,8,2,96]{4,1,2,0,3:T(8,128)(2,1)S(1)}, bf16[1,192,8,2,96]{4,1,2,0,3:T(8,128)(2,1)}, u32[]{:S(2)}) copy-start(bf16[1,192,8,2,96]{4,1,2,0,3:T(8,128)(2,1)} %subtract_convert_fusion) | copy-start | bytes 1769476
  249.8 4.1 %copy-start.17 = (bf16[384,2560]{1,0:T(8,128)(2,1)S(1)}, bf16[384,2560]{1,0:T(8,128)(2,1)}, u32[]{:S(2)}) copy-start(bf16[384,2560]{1,0:T(8,128)(2,1)} %param.33) | copy-start | bytes 5898244
  255.7 26.6 %copy-start.1 = (bf16[640,2560]{1,0:T(8,128)(2,1)S(1)}, bf16[640,2560]{1,0:T(8,128)(2,1)}, u32[]{:S(2)}) copy-start(bf16[640,2560]{1,0:T(8,128)(2,1)} %param.26) | copy-start | bytes 9830404
Sparse Core Ops, SparseCore 0:
  153.0 73.1 reduce-scatter.4
  255.8 24.3 reduce-scatter.2

commit v12 on v8

--- a/solution.py
+++ b/solution.py
@@ -145,10 +145,14 @@
         ).astype(jnp.bfloat16)
         arrived = lax.all_to_all(outbox, "req", split_axis=0, concat_axis=0, tiled=True)
         rows = arrived.reshape(groups * capacity, model_width)
-        gate_up = jnp.einsum(
-            "md,dcf->mcf", rows, expert_gate_up[expert], preferred_element_type=jnp.float32
+        hidden_units = expert_gate_up.shape[-1]
+        gate_up = jnp.dot(
+            rows, expert_gate_up[expert].reshape(model_width, 2 * hidden_units),
+            preferred_element_type=jnp.float32,
         )
-        act = (jax.nn.silu(gate_up[:, 0]) * gate_up[:, 1]).astype(jnp.bfloat16)
+        act = (
+            jax.nn.silu(gate_up[:, :hidden_units]) * gate_up[:, hidden_units:]
+        ).astype(jnp.bfloat16)
         partial_value = jnp.dot(act, expert_down[expert], preferred_element_type=jnp.float32)
         partial_bf = partial_value.astype(jnp.bfloat16)
         if expert < experts_local - 1:
@@ -181,10 +185,14 @@
         else:
             routed_last = both[0] + both[1]
 
-    shared_gu = jnp.einsum(
-        "td,dcf->tcf", normed_bf, shared_gate_up, preferred_element_type=jnp.float32
-    )
-    shared_act = (jax.nn.silu(shared_gu[:, 0]) * shared_gu[:, 1]).astype(jnp.bfloat16)
+    shared_units = shared_gate_up.shape[-1]
+    shared_gu = jnp.dot(
+        normed_bf, shared_gate_up.reshape(model_width, 2 * shared_units),
+        preferred_element_type=jnp.float32,
+    )
+    shared_act = (
+        jax.nn.silu(shared_gu[:, :shared_units]) * shared_gu[:, shared_units:]
+    ).astype(jnp.bfloat16)
     shared_terms = jnp.dot(shared_act, shared_down, preferred_element_type=jnp.float32)
     total = (shared_terms + routed).astype(jnp.bfloat16).reshape(row_count, tp_count, part_width)
     summed = lax.psum_scatter(total.transpose(1, 0, 2), "tp", scatter_dimension=0, tiled=True)

time: 285 us -> 286 us (level)
  local copies, waits for them, and re-layouts: 27.3 us -> 40.6 us
  waiting for transfers between devices: 124 us -> 112 us
    unnamed x39 -> x41, local copies, waits for them, and re-layouts: 1.27 us -> 12.4 us
    all_to_all x2, waiting for transfers between devices: 70 us -> 63.2 us  [shards(): lax.all_to_all(outbox, 'req', split_axis=0, concat_axis=0, tiled=True)]
    all_to_all x1, waiting for transfers between devices: 34.7 us -> 29.8 us  [shards(): lax.all_to_all(outputs, 'req', split_axis=0, concat_axis=0, tiled=True)]
  transfers between devices with their start and end apart: 6 -> 6, of which waited for: 5 -> 5; matrix products, arithmetic and copies ran while one was open for 21% -> 26% of each run, Pallas kernels for 0% -> 0%
where the time goes in v12:
time: 286 us; the launch traced here: 285 us
  waiting for transfers between devices  112 us (39%)
  matrix products  43.5 us (15%)
  local copies, waits for them, and re-layouts  40.6 us (14%)
  blocking collectives  38 us (13%)
  starting transfers between devices  20.4 us (7%)
  other arithmetic  16.3 us (6%)
  between operations  13.9 us (5%)
    all_to_all x2, waiting for transfers between devices, shards(): lax.all_to_all(outbox, 'req', split_axis=0, concat_axis=0, tiled=True)  63.2 us
    all_to_all x1, waiting for transfers between devices, shards(): lax.all_to_all(outputs, 'req', split_axis=0, concat_axis=0, tiled=True)  29.8 us
    all_gather x1, blocking collectives, shards(): hidden_bf = lax.all_gather(hidden_part_bf[None], 'tp', axis=0, tiled=True)  19.6 us
    all_to_all x1, blocking collectives, shards(): lax.all_to_all(outputs, 'req', split_axis=0, concat_axis=0, tiled=True)  18.4 us
    all_to_all x1, waiting for transfers between devices, shards(): lax.all_to_all(attn_blocks.transpose(1, 0, 2), 'tp', split_axis=0, concat...  15.9 us
    dot_general x2, matrix products, shards(): jnp.dot(rows, expert_gate_up[expert].reshape(model_width, 2 * hidden_unit...  13.3 us
    unnamed x41, local copies, waits for them, and re-layouts  12.4 us
    all_to_all x2, starting transfers between devices, shards(): lax.all_to_all(outbox, 'req', split_axis=0, concat_axis=0, tiled=True)  9.23 us
  transfers between devices with their start and end apart: 6, of which 5 were waited for; matrix products, arithmetic and copies ran while one was open for 26% of the time, Pallas kernels for 0%

profile of v12, /device:TPU:0, one launch (start us, length us, event | category | flops | bytes accessed | tf_op | source)
XLA Modules:
  0.0 285.0 jit_solution(3502796219513417447)
XLA Ops:
  6.6 0.8 compare_select_fusion
  7.5 0.9 iota_compare_fusion.6
  8.4 2.9 %gather_fusion = bf16[64,64,128]{2,1,0:T(8,128)(2,1)} fusion(bf16[64,64,128]{2,1,0:T(8,128)(2,1)} %param.21, s32[1024]{0:T(1024)S(1)} %pad_clamp_fusion), kind=kCustom, calls=%fused_computation | custom fusion | bytes 2097408 | tf_op jit(solution)/shard_map/gather | solution.py:94
  11.3 2.9 %gather_fusion.1 = bf16[64,64,128]{2,1,0:T(8,128)(2,1)} fusion(bf16[64,64,128]{2,1,0:T(8,128)(2,1)} %param.20, s32[1024]{0:T(1024)S(1)} %pad_clamp_fusion), kind=kCustom, calls=%fused_computation.1 | custom fusion | bytes 2097408 | tf_op jit(solution)/shard_map/gather | solution.py:93
  14.2 1.0 reshape.270
  16.8 2.1 bitcast_reduce_fusion
  19.4 1.0 fusion.4
  20.5 1.3 fusion.8
  22.2 0.9 convolution_convert_fusion.4
  23.2 1.0 copy.146
  24.2 6.3 %all-to-all-start = ((bf16[4,192,640]{2,1,0:T(8,128)(2,1)}), bf16[4,192,640]{2,1,0:T(8,128)(2,1)S(1)}, u32[]{:S(2)}, u32[]{:S(2)}) async-start(bf16[4,192,640]{2,1,0:T(8,128)(2,1)} %bitcast.204), calls=%async_computation | async-start | bytes 1966080 | tf_op jit(solution)/shard_map/all_to_all | solution.py:125
  31.0 4.5 %reduce-window.6 = s32[16,9,128]{2,1,0:T(8,128)S(1)} reduce-window(s32[16,9,128]{2,1,0:T(8,128)S(1)} %fusion.54, s32[]{:T(128)} %constant.17.clone.1), window={size=1x1x128 pad=0_0x0_0x127_0}, to_apply=%region_6.7 | reduce-window | flops 2340864 | bytes 147460 | tf_op jit(solution)/shard_map/reduce-window
  36.5 1.2 fusion
  37.7 1.2 copy.99
  38.9 15.9 %all-to-all-done = bf16[4,192,640]{2,1,0:T(8,128)(2,1)S(1)} async-done(((bf16[4,192,640]{2,1,0:T(8,128)(2,1)}), bf16[4,192,640]{2,1,0:T(8,128)(2,1)S(1)}, u32[]{:S(2)}, u32[]{:S(2)}) %all-to-all-start) | async-done | bytes 983072 | tf_op jit(solution)/shard_map/all_to_all | solution.py:125
  55.0 1.0 add_convert_fusion
  56.0 19.6 %all-gather = bf16[768,640]{1,0:T(8,128)(2,1)S(1)} all-gather(bf16[192,640]{1,0:T(8,128)(2,1)S(1)} %add_convert_fusion), channel_id=2, replica_groups=mesh['req'=8,'tp'=4] {'tp'}, dimensions={0}, use_global_device_ids=true | all-gather | bytes 1228800 | tf_op jit(solution)/shard_map/all_gather | solution.py:131
  75.8 1.3 fusion.43
  78.3 4.0 %convolution_convert_fusion = bf16[8,96,2560]{2,1,0:T(8,128)(2,1)} fusion(bf16[192,2560,1]{1,0,2:T(8,128)(2,1)S(1)} %reshape.316, pred[192,8,2,96]{0,3,2,1:T(32,128)(4,1)} %bitcast.224), kind=kOutput, calls=%fused_computation.5 | convolution fusion | flops 756940800 | bytes 5111808 | tf_op jit(solution)/shard_map/tgc,td->gcd/dot_general | solution.py:143
  82.3 4.7 %all-to-all-start.3 = ((bf16[8,96,2560]{2,1,0:T(8,128)(2,1)}), bf16[8,96,2560]{2,1,0:T(8,128)(2,1)}, u32[]{:S(2)}, u32[]{:S(2)}) async-start(bf16[8,96,2560]{2,1,0:T(8,128)(2,1)} %convolution_convert_fusion), calls=%async_computation.4 | async-start | bytes 7864320 | tf_op jit(solution)/shard_map/all_to_all | solution.py:146
  87.0 7.6 %fusion.69 = (bf16[1,2560,2,384]{3,2,1,0:T(2,128)(2,1)}, bf16[1,2560,2,384]{3,2,1,0:T(2,128)(2,1)S(1)}) fusion(bf16[2,2560,2,384]{3,2,1,0:T(2,128)(2,1)} %param.30), kind=kLoop, calls=%fused_computation.125 | loop fusion | bytes 15728640 | tf_op jit(solution)/shard_map/slice | solution.py:150
  94.6 2.6 copy.122
  97.2 3.2 %convolution_convert_fusion.1 = bf16[8,96,2560]{2,1,0:T(8,128)(2,1)} fusion(bf16[192,2560,1]{1,0,2:T(8,128)(2,1)S(1)} %reshape.316, pred[192,8,2,96]{0,3,2,1:T(32,128)(4,1)S(1)} %bitcast.225), kind=kOutput, calls=%fused_computation.6 | convolution fusion | flops 756940800 | bytes 5111808 | tf_op jit(solution)/shard_map/tgc,td->gcd/dot_general | solution.py:143
  100.4 32.8 %all-to-all-done.3 = bf16[8,96,2560]{2,1,0:T(8,128)(2,1)} async-done(((bf16[8,96,2560]{2,1,0:T(8,128)(2,1)}), bf16[8,96,2560]{2,1,0:T(8,128)(2,1)}, u32[]{:S(2)}, u32[]{:S(2)}) %all-to-all-start.3) | async-done | bytes 3932192 | tf_op jit(solution)/shard_map/all_to_all | solution.py:146
  133.1 4.5 %all-to-all-start.1 = ((bf16[8,96,2560]{2,1,0:T(8,128)(2,1)}), bf16[8,96,2560]{2,1,0:T(8,128)(2,1)}, u32[]{:S(2)}, u32[]{:S(2)}) async-start(bf16[8,96,2560]{2,1,0:T(8,128)(2,1)} %convolution_convert_fusion.1), calls=%async_computation.1 | async-start | bytes 7864320 | tf_op jit(solution)/shard_map/all_to_all | solution.py:146
  137.7 6.6 %fusion.73 = f32[768,768]{1,0:T(8,128)S(1)} fusion(bf16[768,2560]{1,0:T(8,128)(2,1)} %bitcast.40, bf16[2560,768]{1,0:T(8,128)(2,1)} %bitcast.218), kind=kOutput, calls=%fused_computation.129 | convolution fusion | flops 3019898880 | bytes 10223616 | tf_op jit(solution)/shard_map/dot_general | solution.py:149
  144.4 2.2 convolution_convert_fusion.2
  146.6 2.2 copy.144
  148.8 4.7 %copy.121 = bf16[320,8,2,384]{3,1,2,0:T(8,128)(2,1)} copy(bf16[320,8,2,384]{3,2,1,0:T(2,128)(2,1)} %bitcast.211) | data formatting | bytes 7864320
  153.5 30.5 %all-to-all-done.1 = bf16[8,96,2560]{2,1,0:T(8,128)(2,1)} async-done(((bf16[8,96,2560]{2,1,0:T(8,128)(2,1)}), bf16[8,96,2560]{2,1,0:T(8,128)(2,1)}, u32[]{:S(2)}, u32[]{:S(2)}) %all-to-all-start.1) | async-done | bytes 3932192 | tf_op jit(solution)/shard_map/all_to_all | solution.py:146
  184.0 6.6 %fusion.72 = f32[768,768]{1,0:T(8,128)S(1)} fusion(bf16[768,2560]{1,0:T(8,128)(2,1)} %bitcast.30, bf16[2560,768]{1,0:T(8,128)(2,1)} %bitcast.219), kind=kOutput, calls=%fused_computation.128 | convolution fusion | flops 3019898880 | bytes 10223616 | tf_op jit(solution)/shard_map/dot_general | solution.py:149
  190.6 4.2 %convolution_convert_fusion.3 = bf16[768,2560]{1,0:T(8,128)(2,1)} fusion(bf16[2,384,2560]{2,1,0:T(8,128)(2,1)S(1)} %copy-done.14, f32[768,768]{1,0:T(8,128)S(1)} %fusion.72), kind=kOutput, calls=%fused_computation.8 | convolution fusion | flops 1513684992 | bytes 8257536 | tf_op jit(solution)/shard_map/dot_general | solution.py:156
  194.8 4.5 %all-to-all-start.2 = ((bf16[8,96,2560]{2,1,0:T(8,128)(2,1)}), bf16[8,96,2560]{2,1,0:T(8,128)(2,1)}, u32[]{:S(2)}, u32[]{:S(2)}) async-start(bf16[8,96,2560]{2,1,0:T(8,128)(2,1)} %bitcast.217), calls=%async_computation.2 | async-start | bytes 7864320 | tf_op jit(solution)/shard_map/all_to_all | solution.py:165
  199.6 4.8 %copy.118 = bf16[320,8,2,384]{3,1,2,0:T(8,128)(2,1)} copy(bf16[320,8,2,384]{3,2,1,0:T(2,128)(2,1)} %bitcast.216) | data formatting | bytes 7864320
  205.3 1.7 fusion.12
  207.1 1.2 select_reduce_fusion
  208.3 2.4 reshape.278
  210.7 1.4 copy.139
  212.1 1.4 copy.116
  213.5 1.4 subtract_convert_fusion
  214.9 0.9 fusion.71
  215.8 29.8 %all-to-all-done.2 = bf16[8,96,2560]{2,1,0:T(8,128)(2,1)} async-done(((bf16[8,96,2560]{2,1,0:T(8,128)(2,1)}), bf16[8,96,2560]{2,1,0:T(8,128)(2,1)}, u32[]{:S(2)}, u32[]{:S(2)}) %all-to-all-start.2) | async-done | bytes 3932192 | tf_op jit(solution)/shard_map/all_to_all | solution.py:165
  245.7 4.1 %convolution_bitcast_fusion = f32[2,192,2560]{2,1,0:T(8,128)S(1)} fusion(bf16[8,96,2560]{2,1,0:T(8,128)(2,1)} %all-to-all-done.2, bf16[1,192,8,2,96]{4,1,2,0,3:T(8,128)(2,1)S(1)} %copy-done.3, bf16[1,192,8,2,96]{4,1,2,0,3:T(8,128)(2,1)S(1)} %copy-done.4), kind=kOutput, calls=%fused_computation.9 | convolution fusion | flops 1510244352 | bytes 9043968 | tf_op jit(solution)/shard_map/stgc,gcd->std/dot_general | solution.py:179
  250.5 1.0 copy.145
  251.6 18.4 %all_to_all.25 = bf16[8,96,640]{2,1,0:T(8,128)(2,1)S(1)} all-to-all(bf16[8,96,640]{2,1,0:T(8,128)(2,1)} %bitcast.228), channel_id=1, replica_groups=mesh['req'=8,'tp'=4] {'req'}, dimensions={0} | all-to-all | bytes 1966080 | tf_op jit(solution)/shard_map/all_to_all | solution.py:165
  270.0 2.8 convolution_bitcast_fusion.1
  272.8 3.3 %reduce-scatter.3.cloned.1.call-done = bf16[1,192,640]{2,1,0:T(8,128)(2,1)} async-done(((bf16[4,192,640]{2,1,0:T(8,128)(2,1)}), bf16[1,192,640]{2,1,0:T(8,128)(2,1)}) %reduce-scatter.3.cloned.1.call-update) | async-done | bytes 245776 | tf_op jit(solution)/shard_map/reduce_scatter | solution.py:198
  276.1 2.0 fusion.40
  (80 shorter events, 7.5 us)
Async XLA Ops:
  6.5 15.7 %copy-start = (bf16[640,2560]{1,0:T(8,128)(2,1)S(1)}, bf16[640,2560]{1,0:T(8,128)(2,1)}, u32[]{:S(2)}) copy-start(bf16[640,2560]{1,0:T(8,128)(2,1)} %param.26) | copy-start | bytes 9830404
  6.5 7.7 %copy-start.8 = (bf16[192,640]{1,0:T(8,128)(2,1)S(1)}, bf16[192,640]{1,0:T(8,128)(2,1)}, u32[]{:S(2)}) copy-start(bf16[192,640]{1,0:T(8,128)(2,1)} %param.17) | copy-start | bytes 737284
  6.5 8.7 %copy-start.17 = (s32[4,48]{1,0:T(4,128)S(1)}, s32[4,48]{1,0:T(4,128)}, u32[]{:S(2)}) copy-start(s32[4,48]{1,0:T(4,128)} %param.24) | copy-start | bytes 2308
  15.3 3.7 %copy-start.12 = (bf16[192,128]{1,0:T(8,128)(2,1)S(1)}, bf16[192,128]{1,0:T(8,128)(2,1)}, u32[]{:S(2)}) copy-start(bf16[192,128]{1,0:T(8,128)(2,1)} %param.18) | copy-start | bytes 147460
  16.8 2.2 copy-start.5
  18.9 1.5 copy-start.7
  20.5 1.3 copy-start.16
  22.2 8.3 %copy-start.10 = (s32[192,6]{0,1:T(8,128)S(1)}, s32[192,6]{0,1:T(8,128)}, u32[]{:S(2)}) copy-start(s32[192,6]{0,1:T(8,128)} %param.29) | copy-start | bytes 13828
  22.2 8.7 %copy-start.11 = (f32[2560]{0:T(1024)S(1)}, f32[2560]{0:T(1024)}, u32[]{:S(2)}) copy-start(f32[2560]{0:T(1024)} %param.27) | copy-start | bytes 30724
  24.2 30.6 %all-to-all-start = ((bf16[4,192,640]{2,1,0:T(8,128)(2,1)}), bf16[4,192,640]{2,1,0:T(8,128)(2,1)S(1)}, u32[]{:S(2)}, u32[]{:S(2)}) async-start(bf16[4,192,640]{2,1,0:T(8,128)(2,1)} %bitcast.204), calls=%async_computation | async-start | bytes 1966080 | tf_op jit(solution)/shard_map/all_to_all | solution.py:125
  82.3 50.8 %all-to-all-start.3 = ((bf16[8,96,2560]{2,1,0:T(8,128)(2,1)}), bf16[8,96,2560]{2,1,0:T(8,128)(2,1)}, u32[]{:S(2)}, u32[]{:S(2)}) async-start(bf16[8,96,2560]{2,1,0:T(8,128)(2,1)} %convolution_convert_fusion), calls=%async_computation.4 | async-start | bytes 7864320 | tf_op jit(solution)/shard_map/all_to_all | solution.py:146
  94.6 2.6 copy-start.6
  133.1 50.9 %all-to-all-start.1 = ((bf16[8,96,2560]{2,1,0:T(8,128)(2,1)}), bf16[8,96,2560]{2,1,0:T(8,128)(2,1)}, u32[]{:S(2)}, u32[]{:S(2)}) async-start(bf16[8,96,2560]{2,1,0:T(8,128)(2,1)} %convolution_convert_fusion.1), calls=%async_computation.1 | async-start | bytes 7864320 | tf_op jit(solution)/shard_map/all_to_all | solution.py:146
  137.7 113.9 %reduce-scatter.5.cloned.1.call-start = ((), (), s32[]{:S(2)}) async-start(), calls=%async_computation.8 | async-start | bytes 4915200 | tf_op jit(solution)/shard_map/reduce_scatter | solution.py:161
  137.7 6.7 %copy-start.13 = (bf16[2,384,2560]{2,1,0:T(8,128)(2,1)S(1)}, bf16[2,384,2560]{2,1,0:T(8,128)(2,1)}, u32[]{:S(2)}) copy-start(bf16[2,384,2560]{2,1,0:T(8,128)(2,1)} %param.31) | copy-start | bytes 11796484
  184.0 6.7 %copy-start.14 = (bf16[2,384,2560]{2,1,0:T(8,128)(2,1)S(1)}, bf16[2,384,2560]{2,1,0:T(8,128)(2,1)}, u32[]{:S(2)}) copy-start(bf16[2,384,2560]{2,1,0:T(8,128)(2,1)} %param.31) | copy-start | bytes 11796484
  194.8 50.8 %all-to-all-start.2 = ((bf16[8,96,2560]{2,1,0:T(8,128)(2,1)}), bf16[8,96,2560]{2,1,0:T(8,128)(2,1)}, u32[]{:S(2)}, u32[]{:S(2)}) async-start(bf16[8,96,2560]{2,1,0:T(8,128)(2,1)} %bitcast.217), calls=%async_computation.2 | async-start | bytes 7864320 | tf_op jit(solution)/shard_map/all_to_all | solution.py:165
  199.4 76.7 %reduce-scatter.3.cloned.1.call-start = ((), (), s32[]{:S(2)}) async-start(), calls=%async_computation.7 | async-start | bytes 1228800 | tf_op jit(solution)/shard_map/reduce_scatter | solution.py:198
  204.4 0.9 copy-start.9
  210.7 4.2 %copy-start.2 = (bf16[320,8,2,384]{3,1,2,0:T(8,128)(2,1)S(1)}, bf16[320,8,2,384]{3,1,2,0:T(8,128)(2,1)}, u32[]{:S(2)}) copy-start(bf16[320,8,2,384]{3,1,2,0:T(8,128)(2,1)} %copy.118) | copy-start | bytes 11796484
  214.9 30.8 %copy-start.3 = (bf16[1,192,8,2,96]{4,1,2,0,3:T(8,128)(2,1)S(1)}, bf16[1,192,8,2,96]{4,1,2,0,3:T(8,128)(2,1)}, u32[]{:S(2)}) copy-start(bf16[1,192,8,2,96]{4,1,2,0,3:T(8,128)(2,1)} %copy.139) | copy-start | bytes 1769476
  214.9 30.8 %copy-start.4 = (bf16[1,192,8,2,96]{4,1,2,0,3:T(8,128)(2,1)S(1)}, bf16[1,192,8,2,96]{4,1,2,0,3:T(8,128)(2,1)}, u32[]{:S(2)}) copy-start(bf16[1,192,8,2,96]{4,1,2,0,3:T(8,128)(2,1)} %subtract_convert_fusion) | copy-start | bytes 1769476
  245.7 4.1 %copy-start.15 = (bf16[384,2560]{1,0:T(8,128)(2,1)S(1)}, bf16[384,2560]{1,0:T(8,128)(2,1)}, u32[]{:S(2)}) copy-start(bf16[384,2560]{1,0:T(8,128)(2,1)} %param.33) | copy-start | bytes 5898244
  251.5 26.6 %copy-start.1 = (bf16[640,2560]{1,0:T(8,128)(2,1)S(1)}, bf16[640,2560]{1,0:T(8,128)(2,1)}, u32[]{:S(2)}) copy-start(bf16[640,2560]{1,0:T(8,128)(2,1)} %param.26) | copy-start | bytes 9830404
Sparse Core Ops, SparseCore 0:
  149.0 73.1 reduce-scatter.4
  251.7 24.3 reduce-scatter.2

commit v13 on v8

--- a/solution.py
+++ b/solution.py
@@ -145,10 +145,9 @@
         ).astype(jnp.bfloat16)
         arrived = lax.all_to_all(outbox, "req", split_axis=0, concat_axis=0, tiled=True)
         rows = arrived.reshape(groups * capacity, model_width)
-        gate_up = jnp.einsum(
-            "md,dcf->mcf", rows, expert_gate_up[expert], preferred_element_type=jnp.float32
-        )
-        act = (jax.nn.silu(gate_up[:, 0]) * gate_up[:, 1]).astype(jnp.bfloat16)
+        gate = jnp.dot(rows, expert_gate_up[expert, :, 0], preferred_element_type=jnp.float32)
+        up = jnp.dot(rows, expert_gate_up[expert, :, 1], preferred_element_type=jnp.float32)
+        act = (jax.nn.silu(gate) * up).astype(jnp.bfloat16)
         partial_value = jnp.dot(act, expert_down[expert], preferred_element_type=jnp.float32)
         partial_bf = partial_value.astype(jnp.bfloat16)
         if expert < experts_local - 1:

time: 285 us -> 295 us (1.035)
  waiting for transfers between devices: 124 us -> 105 us
  local copies, waits for them, and re-layouts: 27.3 us -> 41.8 us
  matrix products: 46 us -> 60.4 us
    all_to_all x2, waiting for transfers between devices: 70 us -> 50.9 us  [shards(): lax.all_to_all(outbox, 'req', split_axis=0, concat_axis=0, tiled=True)]
    dot_general x2, matrix products: 6.44 us -> 20.2 us  [shards(): jnp.dot(act, expert_down[expert], preferred_element_type=jnp.float32)]
    slice x2, local copies, waits for them, and re-layouts: 8.59 us -> 18.9 us  [the longest x1 18.5 us: shards(): expert_gate_up[expert, :, 0]]
  transfers between devices with their start and end apart: 6 -> 6, of which waited for: 5 -> 5; matrix products, arithmetic and copies ran while one was open for 21% -> 29% of each run, Pallas kernels for 0% -> 0%
where the time goes in v13:
time: 295 us; the launch traced here: 294 us
  waiting for transfers between devices  105 us (36%)
  matrix products  60.4 us (20%)
  local copies, waits for them, and re-layouts  41.8 us (14%)
  blocking collectives  38 us (13%)
  starting transfers between devices  20.4 us (7%)
  other arithmetic  14.4 us (5%)
  between operations  13.9 us (5%)
    all_to_all x2, waiting for transfers between devices, shards(): lax.all_to_all(outbox, 'req', split_axis=0, concat_axis=0, tiled=True)  50.9 us
    all_to_all x1, waiting for transfers between devices, shards(): lax.all_to_all(outputs, 'req', split_axis=0, concat_axis=0, tiled=True)  34.9 us
    dot_general x2, matrix products, shards(): jnp.dot(act, expert_down[expert], preferred_element_type=jnp.float32)  20.2 us
    all_gather x1, blocking collectives, shards(): hidden_bf = lax.all_gather(hidden_part_bf[None], 'tp', axis=0, tiled=True)  19.6 us
    slice x1, local copies, waits for them, and re-layouts, shards(): expert_gate_up[expert, :, 0]  18.5 us
    all_to_all x1, blocking collectives, shards(): lax.all_to_all(outputs, 'req', split_axis=0, concat_axis=0, tiled=True)  18.4 us
    all_to_all x1, waiting for transfers between devices, shards(): lax.all_to_all(attn_blocks.transpose(1, 0, 2), 'tp', split_axis=0, concat...  15.9 us
    dot_general x2, matrix products, shards(): jnp.dot(rows, expert_gate_up[expert, :, 0], preferred_element_type=jnp.fl...  11 us
  transfers between devices with their start and end apart: 6, of which 5 were waited for; matrix products, arithmetic and copies ran while one was open for 29% of the time, Pallas kernels for 0%

profile of v13, /device:TPU:0, one launch (start us, length us, event | category | flops | bytes accessed | tf_op | source)
XLA Modules:
  0.0 293.9 jit_solution(7594717473642783759)
XLA Ops:
  6.6 0.8 compare_select_fusion
  7.5 0.8 iota_compare_fusion.6
  8.3 2.0 reshape.256
  10.2 1.0 convolution_minimum_fusion.5
  12.5 2.9 gather_fusion.1
  15.4 2.1 bitcast_reduce_fusion
  18.0 1.4 copy-done.2
  19.4 1.0 fusion.6
  20.5 2.9 gather_fusion
  23.4 3.5 %fusion.17 = f32[4,128,5,48]{1,3,2,0:T(8,128)S(1)} fusion(bf16[4,1024,128,1]{2,1,3,0:T(8,128)(2,1)} %bitcast.246, f32[4,1024,48,5]{1,2,3,0:T(8,128)} %copy-done.2, f32[4,5,48]{2,1,0:T(8,128)S(1)} %add.86, f32[4,5,48]{2,1,0:T(8,128)S(1)} %max.9, pred[4,1024]{1,0:T(4,128)(4,1)S(1)} %iota_compare_fusion.6), kind=kOutput, calls=%fused_computation.41 | convolution fusion | flops 256573440 | bytes 5484032 | tf_op jit(solution)/shard_map/rkgtc,rckd->rtkgd/dot_general | solution.py:54
  27.4 0.9 convolution_convert_fusion.4
  28.3 1.0 copy.190
  29.4 6.3 %all-to-all-start = ((bf16[4,192,640]{2,1,0:T(8,128)(2,1)}), bf16[4,192,640]{2,1,0:T(8,128)(2,1)S(1)}, u32[]{:S(2)}, u32[]{:S(2)}) async-start(bf16[4,192,640]{2,1,0:T(8,128)(2,1)} %bitcast.231), calls=%async_computation | async-start | bytes 1966080 | tf_op jit(solution)/shard_map/all_to_all | solution.py:125
  36.1 4.5 %reduce-window.6 = s32[16,9,128]{2,1,0:T(8,128)S(1)} reduce-window(s32[16,9,128]{2,1,0:T(8,128)S(1)} %fusion.66, s32[]{:T(128)} %constant.17.clone.1), window={size=1x1x128 pad=0_0x0_0x127_0}, to_apply=%region_6.7 | reduce-window | flops 2340864 | bytes 147460 | tf_op jit(solution)/shard_map/reduce-window
  41.7 1.2 fusion
  42.8 1.2 copy.116
  44.1 15.9 %all-to-all-done = bf16[4,192,640]{2,1,0:T(8,128)(2,1)S(1)} async-done(((bf16[4,192,640]{2,1,0:T(8,128)(2,1)}), bf16[4,192,640]{2,1,0:T(8,128)(2,1)S(1)}, u32[]{:S(2)}, u32[]{:S(2)}) %all-to-all-start) | async-done | bytes 983072 | tf_op jit(solution)/shard_map/all_to_all | solution.py:125
  60.1 1.0 add_convert_fusion
  61.1 19.6 %all-gather = bf16[768,640]{1,0:T(8,128)(2,1)S(1)} all-gather(bf16[192,640]{1,0:T(8,128)(2,1)S(1)} %add_convert_fusion), channel_id=2, replica_groups=mesh['req'=8,'tp'=4] {'tp'}, dimensions={0}, use_global_device_ids=true | all-gather | bytes 1228800 | tf_op jit(solution)/shard_map/all_gather | solution.py:131
  81.3 0.8 copy.118
  82.4 4.0 %convolution_convert_fusion = bf16[8,96,2560]{2,1,0:T(8,128)(2,1)} fusion(bf16[192,2560,1]{1,0,2:T(8,128)(2,1)S(1)} %reshape.302, pred[192,8,2,96]{0,3,2,1:T(32,128)(4,1)} %bitcast.244), kind=kOutput, calls=%fused_computation.5 | convolution fusion | flops 756940800 | bytes 5111808 | tf_op jit(solution)/shard_map/tgc,td->gcd/dot_general | solution.py:143
  86.5 4.7 %all-to-all-start.3 = ((bf16[8,96,2560]{2,1,0:T(8,128)(2,1)}), bf16[8,96,2560]{2,1,0:T(8,128)(2,1)}, u32[]{:S(2)}, u32[]{:S(2)}) async-start(bf16[8,96,2560]{2,1,0:T(8,128)(2,1)} %convolution_convert_fusion), calls=%async_computation.4 | async-start | bytes 7864320 | tf_op jit(solution)/shard_map/all_to_all | solution.py:146
  91.2 18.5 %fusion.81 = (bf16[1,2560,1,384]{3,2,1,0:T(2,128)(2,1)}, bf16[1,2560,1,384]{3,2,1,0:T(2,128)(2,1)}, bf16[1,2560,1,384]{3,2,1,0:T(2,128)(2,1)}, bf16[1,2560,1,384]{3,2,1,0:T(2,128)(2,1)}) fusion(bf16[2,2560,2,384]{3,2,1,0:T(2,128)(2,1)} %param.30), kind=kLoop, calls=%fused_computation.143 | loop fusion | bytes 15728640 | tf_op jit(solution)/shard_map/slice | solution.py:148
  109.6 3.1 %convolution_convert_fusion.1 = bf16[8,96,2560]{2,1,0:T(8,128)(2,1)} fusion(bf16[192,2560,1]{1,0,2:T(8,128)(2,1)S(1)} %reshape.302, pred[192,8,2,96]{0,3,2,1:T(32,128)(4,1)S(1)} %bitcast.245), kind=kOutput, calls=%fused_computation.6 | convolution fusion | flops 756940800 | bytes 5111808 | tf_op jit(solution)/shard_map/tgc,td->gcd/dot_general | solution.py:143
  112.8 24.5 %all-to-all-done.3 = bf16[8,96,2560]{2,1,0:T(8,128)(2,1)} async-done(((bf16[8,96,2560]{2,1,0:T(8,128)(2,1)}), bf16[8,96,2560]{2,1,0:T(8,128)(2,1)}, u32[]{:S(2)}, u32[]{:S(2)}) %all-to-all-start.3) | async-done | bytes 3932192 | tf_op jit(solution)/shard_map/all_to_all | solution.py:146
  137.3 4.5 %all-to-all-start.1 = ((bf16[8,96,2560]{2,1,0:T(8,128)(2,1)}), bf16[8,96,2560]{2,1,0:T(8,128)(2,1)}, u32[]{:S(2)}, u32[]{:S(2)}) async-start(bf16[8,96,2560]{2,1,0:T(8,128)(2,1)} %convolution_convert_fusion.1), calls=%async_computation.1 | async-start | bytes 7864320 | tf_op jit(solution)/shard_map/all_to_all | solution.py:146
  141.9 5.5 %fusion.12 = f32[768,384]{1,0:T(8,128)S(1)} fusion(bf16[768,2560]{1,0:T(8,128)(2,1)} %bitcast.45, bf16[1,2560,1,384]{3,2,1,0:T(2,128)(2,1)} %get-tuple-element.6), kind=kOutput, calls=%fused_computation.34 | convolution fusion | flops 1509949440 | bytes 7077888 | tf_op jit(solution)/shard_map/dot_general | solution.py:148
  147.4 10.0 %convolution_convert_fusion.2 = bf16[768,2560]{1,0:T(8,128)(2,1)} fusion(bf16[2,384,2560]{2,1,0:T(8,128)(2,1)} %param.31, bf16[768,2560]{1,0:T(8,128)(2,1)} %bitcast.45, bf16[1,2560,1,384]{3,2,1,0:T(2,128)(2,1)} %get-tuple-element.8, f32[768,384]{1,0:T(8,128)S(1)} %fusion.12), kind=kOutput, calls=%fused_computation.7 | convolution fusion | flops 3023634432 | bytes 14942208 | tf_op jit(solution)/shard_map/dot_general | solution.py:151
  157.4 4.3 %copy.188 = bf16[96,4,8,640]{3,2,0,1:T(8,128)(2,1)} copy(bf16[96,4,8,640]{3,2,1,0:T(8,128)(2,1)} %bitcast.241) | data formatting | bytes 7864320 | tf_op jit(solution)/shard_map/reshape | solution.py:157
  161.8 26.4 %all-to-all-done.1 = bf16[8,96,2560]{2,1,0:T(8,128)(2,1)} async-done(((bf16[8,96,2560]{2,1,0:T(8,128)(2,1)}), bf16[8,96,2560]{2,1,0:T(8,128)(2,1)}, u32[]{:S(2)}, u32[]{:S(2)}) %all-to-all-start.1) | async-done | bytes 3932192 | tf_op jit(solution)/shard_map/all_to_all | solution.py:146
  188.2 5.5 %fusion.14 = f32[768,384]{1,0:T(8,128)S(1)} fusion(bf16[768,2560]{1,0:T(8,128)(2,1)} %bitcast.33, bf16[1,2560,1,384]{3,2,1,0:T(2,128)(2,1)} %get-tuple-element.5), kind=kOutput, calls=%fused_computation.38 | convolution fusion | flops 1509949440 | bytes 7077888 | tf_op jit(solution)/shard_map/dot_general | solution.py:148
  193.7 10.2 %convolution_convert_fusion.3 = bf16[768,2560]{1,0:T(8,128)(2,1)} fusion(bf16[2,384,2560]{2,1,0:T(8,128)(2,1)} %param.31, bf16[768,2560]{1,0:T(8,128)(2,1)} %bitcast.33, bf16[1,2560,1,384]{3,2,1,0:T(2,128)(2,1)} %get-tuple-element.7, f32[768,384]{1,0:T(8,128)S(1)} %fusion.14), kind=kOutput, calls=%fused_computation.8 | convolution fusion | flops 3023634432 | bytes 14942208 | tf_op jit(solution)/shard_map/dot_general | solution.py:151
  203.8 4.5 %all-to-all-start.2 = ((bf16[8,96,2560]{2,1,0:T(8,128)(2,1)}), bf16[8,96,2560]{2,1,0:T(8,128)(2,1)}, u32[]{:S(2)}, u32[]{:S(2)}) async-start(bf16[8,96,2560]{2,1,0:T(8,128)(2,1)} %bitcast.240), calls=%async_computation.2 | async-start | bytes 7864320 | tf_op jit(solution)/shard_map/all_to_all | solution.py:160
  209.3 1.7 fusion.22
  211.1 1.2 select_reduce_fusion
  212.3 2.4 reshape.263
  214.7 0.5 copy.183
  215.2 0.5 subtract_convert_fusion
  215.7 0.6 copy-done.4
  216.3 3.4 %fusion.3 = f32[192,2,384]{2,0,1:T(8,128)S(1)} fusion(bf16[2560,2,384]{2,1,0:T(2,128)(2,1)} %param.32, f32[192,2560]{1,0:T(8,128)S(1)} %bitcast.238, f32[2560]{0:T(1024)S(1)} %copy-done.13, f32[192]{0:T(256)S(1)} %add_rsqrt_fusion), kind=kOutput, calls=%fused_computation.17 | convolution fusion | flops 756449280 | bytes 6499072 | tf_op jit(solution)/shard_map/td,dcf->tcf/dot_general | solution.py:183
  219.8 34.9 %all-to-all-done.2 = bf16[8,96,2560]{2,1,0:T(8,128)(2,1)} async-done(((bf16[8,96,2560]{2,1,0:T(8,128)(2,1)}), bf16[8,96,2560]{2,1,0:T(8,128)(2,1)}, u32[]{:S(2)}, u32[]{:S(2)}) %all-to-all-start.2) | async-done | bytes 3932192 | tf_op jit(solution)/shard_map/all_to_all | solution.py:160
  254.7 4.1 %convolution_bitcast_fusion = f32[2,192,2560]{2,1,0:T(8,128)S(1)} fusion(bf16[8,96,2560]{2,1,0:T(8,128)(2,1)} %all-to-all-done.2, bf16[1,192,8,2,96]{4,1,2,0,3:T(8,128)(2,1)S(1)} %copy.183, bf16[1,192,8,2,96]{4,1,2,0,3:T(8,128)(2,1)S(1)} %subtract_convert_fusion), kind=kOutput, calls=%fused_computation.9 | convolution fusion | flops 1510244352 | bytes 9043968 | tf_op jit(solution)/shard_map/stgc,gcd->std/dot_general | solution.py:174
  258.8 0.7 fusion.5
  259.5 1.0 copy.189
  260.6 18.4 %all_to_all.25 = bf16[8,96,640]{2,1,0:T(8,128)(2,1)S(1)} all-to-all(bf16[8,96,640]{2,1,0:T(8,128)(2,1)} %bitcast.248), channel_id=1, replica_groups=mesh['req'=8,'tp'=4] {'req'}, dimensions={0} | all-to-all | bytes 1966080 | tf_op jit(solution)/shard_map/all_to_all | solution.py:160
  279.0 2.8 convolution_bitcast_fusion.1
  281.8 3.2 %reduce-scatter.3.cloned.1.call-done = bf16[1,192,640]{2,1,0:T(8,128)(2,1)} async-done(((bf16[4,192,640]{2,1,0:T(8,128)(2,1)}), bf16[1,192,640]{2,1,0:T(8,128)(2,1)}) %reduce-scatter.3.cloned.1.call-update) | async-done | bytes 245776 | tf_op jit(solution)/shard_map/reduce_scatter | solution.py:189
  285.1 2.0 fusion.53
  (74 shorter events, 5.8 us)
Async XLA Ops:
  6.5 20.8 %copy-start = (bf16[640,2560]{1,0:T(8,128)(2,1)S(1)}, bf16[640,2560]{1,0:T(8,128)(2,1)}, u32[]{:S(2)}) copy-start(bf16[640,2560]{1,0:T(8,128)(2,1)} %param.26) | copy-start | bytes 9830404
  11.9 5.6 %copy-start.14 = (bf16[192,128]{1,0:T(8,128)(2,1)S(1)}, bf16[192,128]{1,0:T(8,128)(2,1)}, u32[]{:S(2)}) copy-start(bf16[192,128]{1,0:T(8,128)(2,1)} %param.18) | copy-start | bytes 147460
  15.4 2.2 copy-start.7
  17.6 1.9 copy-start.2
  18.0 2.4 copy-start.8
  23.4 3.5 %copy-start.9 = (f32[4,1,5,48,48]{3,4,2,0,1:T(8,128)S(1)}, f32[4,1,5,48,48]{3,4,2,0,1:T(8,128)}, u32[]{:S(2)}) copy-start(f32[4,1,5,48,48]{3,4,2,0,1:T(8,128)} %copy-done.8) | copy-start | bytes 552964
  23.4 3.5 %copy-start.16 = (bf16[192,128]{1,0:T(8,128)(2,1)S(1)}, bf16[192,128]{1,0:T(8,128)(2,1)}, u32[]{:S(2)}) copy-start(bf16[192,128]{1,0:T(8,128)(2,1)} %param.19) | copy-start | bytes 147460
  27.3 8.3 %copy-start.12 = (s32[192,6]{0,1:T(8,128)S(1)}, s32[192,6]{0,1:T(8,128)}, u32[]{:S(2)}) copy-start(s32[192,6]{0,1:T(8,128)} %param.29) | copy-start | bytes 13828
  27.4 8.7 %copy-start.13 = (f32[2560]{0:T(1024)S(1)}, f32[2560]{0:T(1024)}, u32[]{:S(2)}) copy-start(f32[2560]{0:T(1024)} %param.27) | copy-start | bytes 30724
  29.4 30.6 %all-to-all-start = ((bf16[4,192,640]{2,1,0:T(8,128)(2,1)}), bf16[4,192,640]{2,1,0:T(8,128)(2,1)S(1)}, u32[]{:S(2)}, u32[]{:S(2)}) async-start(bf16[4,192,640]{2,1,0:T(8,128)(2,1)} %bitcast.231), calls=%async_computation | async-start | bytes 1966080 | tf_op jit(solution)/shard_map/all_to_all | solution.py:125
  86.5 50.8 %all-to-all-start.3 = ((bf16[8,96,2560]{2,1,0:T(8,128)(2,1)}), bf16[8,96,2560]{2,1,0:T(8,128)(2,1)}, u32[]{:S(2)}, u32[]{:S(2)}) async-start(bf16[8,96,2560]{2,1,0:T(8,128)(2,1)} %convolution_convert_fusion), calls=%async_computation.4 | async-start | bytes 7864320 | tf_op jit(solution)/shard_map/all_to_all | solution.py:146
  91.2 18.5 %copy-start.10 = (pred[192,1536]{0,1:T(32,128)(4,1)S(1)}, pred[192,1536]{0,1:T(32,128)(4,1)}, u32[]{:S(2)}) copy-start(pred[192,1536]{0,1:T(32,128)(4,1)} %copy.116) | copy-start | bytes 884740
  137.3 50.9 %all-to-all-start.1 = ((bf16[8,96,2560]{2,1,0:T(8,128)(2,1)}), bf16[8,96,2560]{2,1,0:T(8,128)(2,1)}, u32[]{:S(2)}, u32[]{:S(2)}) async-start(bf16[8,96,2560]{2,1,0:T(8,128)(2,1)} %convolution_convert_fusion.1), calls=%async_computation.1 | async-start | bytes 7864320 | tf_op jit(solution)/shard_map/all_to_all | solution.py:146
  141.8 118.7 %reduce-scatter.5.cloned.1.call-start = ((), (), s32[]{:S(2)}) async-start(), calls=%async_computation.8 | async-start | bytes 4915200 | tf_op jit(solution)/shard_map/reduce_scatter | solution.py:156
  203.8 50.9 %all-to-all-start.2 = ((bf16[8,96,2560]{2,1,0:T(8,128)(2,1)}), bf16[8,96,2560]{2,1,0:T(8,128)(2,1)}, u32[]{:S(2)}, u32[]{:S(2)}) async-start(bf16[8,96,2560]{2,1,0:T(8,128)(2,1)} %bitcast.240), calls=%async_computation.2 | async-start | bytes 7864320 | tf_op jit(solution)/shard_map/all_to_all | solution.py:160
  208.4 0.9 copy-start.11
  208.4 76.7 %reduce-scatter.3.cloned.1.call-start = ((), (), s32[]{:S(2)}) async-start(), calls=%async_computation.7 | async-start | bytes 1228800 | tf_op jit(solution)/shard_map/reduce_scatter | solution.py:189
  209.0 2.1 copy-start.3
  214.7 1.7 copy-start.4
  215.2 39.5 %copy-start.5 = (bf16[1,192,8,2,96]{4,1,2,0,3:T(8,128)(2,1)}, bf16[1,192,8,2,96]{4,1,2,0,3:T(8,128)(2,1)S(1)}, u32[]{:S(2)}) copy-start(bf16[1,192,8,2,96]{4,1,2,0,3:T(8,128)(2,1)S(1)} %copy.183) | copy-start | bytes 1769476
  216.3 42.4 %copy-start.6 = (bf16[1,192,8,2,96]{4,1,2,0,3:T(8,128)(2,1)}, bf16[1,192,8,2,96]{4,1,2,0,3:T(8,128)(2,1)S(1)}, u32[]{:S(2)}) copy-start(bf16[1,192,8,2,96]{4,1,2,0,3:T(8,128)(2,1)S(1)} %subtract_convert_fusion) | copy-start | bytes 1769476
  254.7 4.1 %copy-start.15 = (bf16[384,2560]{1,0:T(8,128)(2,1)S(1)}, bf16[384,2560]{1,0:T(8,128)(2,1)}, u32[]{:S(2)}) copy-start(bf16[384,2560]{1,0:T(8,128)(2,1)} %param.33) | copy-start | bytes 5898244
  260.5 26.6 %copy-start.1 = (bf16[640,2560]{1,0:T(8,128)(2,1)S(1)}, bf16[640,2560]{1,0:T(8,128)(2,1)}, u32[]{:S(2)}) copy-start(bf16[640,2560]{1,0:T(8,128)(2,1)} %param.26) | copy-start | bytes 9830404
Sparse Core Ops, SparseCore 0:
  161.9 73.1 reduce-scatter.4
  260.7 24.3 reduce-scatter.2

commit v14 on v8

--- a/solution.py
+++ b/solution.py
@@ -167,19 +167,17 @@
     gate_values = gate_values / jnp.sum(gate_values, axis=1, keepdims=True)
     weights = jnp.sum(jnp.where(hit, gate_values[:, :, None], 0.0), axis=1)
     weights = weights.reshape(row_count, groups, experts_local, capacity)
-    weights_hi = weights.astype(jnp.bfloat16)
-    weights_lo = (weights - weights_hi.astype(jnp.float32)).astype(jnp.bfloat16)
-    weights_split = jnp.stack([weights_hi, weights_lo])
+    weights_bf = weights.astype(jnp.bfloat16)
     routed = jnp.zeros((row_count, model_width), jnp.float32)
     for expert in range(experts_local):
         both = jnp.einsum(
-            "stgc,gcd->std", weights_split[:, :, :, expert], returns[expert],
+            "tgc,gcd->td", weights_bf[:, :, expert], returns[expert],
             preferred_element_type=jnp.float32,
         )
         if expert < experts_local - 1:
-            routed = routed + both[0] + both[1]
+            routed = routed + both
         else:
-            routed_last = both[0] + both[1]
+            routed_last = both
 
     shared_gu = jnp.einsum(
         "td,dcf->tcf", normed_bf, shared_gate_up, preferred_element_type=jnp.float32

time: 285 us -> 285 us (level)
  blocking collectives: 38 us -> 19.6 us
  waiting for transfers between devices: 124 us -> 138 us
  starting transfers between devices: 20.4 us -> 24.6 us
    all_to_all x1 -> x0, blocking collectives: 18.4 us -> none  [shards(): lax.all_to_all(outputs, 'req', split_axis=0, concat_axis=0, tiled=True)]
    reduce_scatter x1, waiting for transfers between devices: 3.3 us -> 20.3 us  [shards(): lax.psum_scatter(total.transpose(1, 0, 2), 'tp', scatter_dimension=0, til...]
    all_to_all x1 -> x2, starting transfers between devices: 4.52 us -> 8.75 us  [shards(): lax.all_to_all(outputs, 'req', split_axis=0, concat_axis=0, tiled=True)]
    convert_element_type x0 -> x1, local copies, waits for them, and re-layouts: none -> 3.25 us  [shards(): weights_bf = weights.astype(jnp.bfloat16)]
    reshape x2 -> x0, local copies, waits for them, and re-layouts: 2.88 us -> none  [shards(): weights = weights.reshape(row_count, groups, experts_local, capacity)]
    all_to_all x1 -> x2, waiting for transfers between devices: 34.7 us -> 31.9 us  [shards(): lax.all_to_all(outputs, 'req', split_axis=0, concat_axis=0, tiled=True)]
  transfers between devices with their start and end apart: 6 -> 7, of which waited for: 5 -> 5; matrix products, arithmetic and copies ran while one was open for 21% -> 21% of each run, Pallas kernels for 0% -> 0%
where the time goes in v14:
time: 285 us; the launch traced here: 284 us
  waiting for transfers between devices  138 us (48%)
  matrix products  45.6 us (16%)
  local copies, waits for them, and re-layouts  29.1 us (10%)
  starting transfers between devices  24.6 us (9%)
  blocking collectives  19.6 us (7%)
  between operations  13.9 us (5%)
  other arithmetic  12.9 us (5%)
    all_to_all x2, waiting for transfers between devices, shards(): lax.all_to_all(outbox, 'req', split_axis=0, concat_axis=0, tiled=True)  70 us
    all_to_all x2, waiting for transfers between devices, shards(): lax.all_to_all(outputs, 'req', split_axis=0, concat_axis=0, tiled=True)  31.9 us
    reduce_scatter x1, waiting for transfers between devices, shards(): lax.psum_scatter(total.transpose(1, 0, 2), 'tp', scatter_dimension=0, til...  20.3 us
    all_gather x1, blocking collectives, shards(): hidden_bf = lax.all_gather(hidden_part_bf[None], 'tp', axis=0, tiled=True)  19.6 us
    all_to_all x1, waiting for transfers between devices, shards(): lax.all_to_all(attn_blocks.transpose(1, 0, 2), 'tp', split_axis=0, concat...  15.9 us
    dot_general x2, matrix products, shards(): jnp.einsum('md,dcf->mcf', rows, expert_gate_up[expert], preferred_element...  13.3 us
    all_to_all x2, starting transfers between devices, shards(): lax.all_to_all(outbox, 'req', split_axis=0, concat_axis=0, tiled=True)  9.22 us
    all_to_all x2, starting transfers between devices, shards(): lax.all_to_all(outputs, 'req', split_axis=0, concat_axis=0, tiled=True)  8.75 us
  transfers between devices with their start and end apart: 7, of which 5 were waited for; matrix products, arithmetic and copies ran while one was open for 21% of the time, Pallas kernels for 0%

profile of v14, /device:TPU:0, one launch (start us, length us, event | category | flops | bytes accessed | tf_op | source)
XLA Modules:
  0.0 283.9 jit_solution(15768230704337169327)
XLA Ops:
  6.6 0.8 compare_select_fusion
  7.5 0.9 iota_compare_fusion.6
  8.4 2.9 %gather_fusion = bf16[64,64,128]{2,1,0:T(8,128)(2,1)} fusion(bf16[64,64,128]{2,1,0:T(8,128)(2,1)} %param.21, s32[1024]{0:T(1024)S(1)} %pad_clamp_fusion), kind=kCustom, calls=%fused_computation | custom fusion | bytes 2097408 | tf_op jit(solution)/shard_map/gather | solution.py:94
  11.3 2.9 %gather_fusion.1 = bf16[64,64,128]{2,1,0:T(8,128)(2,1)} fusion(bf16[64,64,128]{2,1,0:T(8,128)(2,1)} %param.20, s32[1024]{0:T(1024)S(1)} %pad_clamp_fusion), kind=kCustom, calls=%fused_computation.1 | custom fusion | bytes 2097408 | tf_op jit(solution)/shard_map/gather | solution.py:93
  14.2 1.0 reshape.224
  16.8 2.1 bitcast_reduce_fusion
  19.0 0.4 fusion.69
  19.4 1.0 fusion.7
  20.5 1.3 fusion.13
  21.8 0.3 fusion.29
  22.2 0.9 convolution_convert_fusion.4
  23.2 1.0 copy.165
  24.2 6.3 %all-to-all-start = ((bf16[4,192,640]{2,1,0:T(8,128)(2,1)}), bf16[4,192,640]{2,1,0:T(8,128)(2,1)S(1)}, u32[]{:S(2)}, u32[]{:S(2)}) async-start(bf16[4,192,640]{2,1,0:T(8,128)(2,1)} %bitcast.214), calls=%async_computation | async-start | bytes 1966080 | tf_op jit(solution)/shard_map/all_to_all | solution.py:125
  31.0 4.5 %reduce-window.6 = s32[16,9,128]{2,1,0:T(8,128)S(1)} reduce-window(s32[16,9,128]{2,1,0:T(8,128)S(1)} %fusion.54, s32[]{:T(128)} %constant.17.clone.1), window={size=1x1x128 pad=0_0x0_0x127_0}, to_apply=%region_6.7 | reduce-window | flops 2340864 | bytes 147460 | tf_op jit(solution)/shard_map/reduce-window
  35.5 0.4 slice_reduce_fusion
  36.5 1.2 fusion
  37.7 1.2 copy.111
  38.9 15.9 %all-to-all-done = bf16[4,192,640]{2,1,0:T(8,128)(2,1)S(1)} async-done(((bf16[4,192,640]{2,1,0:T(8,128)(2,1)}), bf16[4,192,640]{2,1,0:T(8,128)(2,1)S(1)}, u32[]{:S(2)}, u32[]{:S(2)}) %all-to-all-start) | async-done | bytes 983072 | tf_op jit(solution)/shard_map/all_to_all | solution.py:125
  55.0 1.0 add_convert_fusion
  56.0 19.6 %all-gather = bf16[768,640]{1,0:T(8,128)(2,1)S(1)} all-gather(bf16[192,640]{1,0:T(8,128)(2,1)S(1)} %add_convert_fusion), channel_id=2, replica_groups=mesh['req'=8,'tp'=4] {'tp'}, dimensions={0}, use_global_device_ids=true | all-gather | bytes 1228800 | tf_op jit(solution)/shard_map/all_gather | solution.py:131
  75.8 0.3 fusion.33
  76.1 0.8 copy.113
  76.9 0.4 reshape.270
  77.3 4.0 %convolution_convert_fusion = bf16[8,96,2560]{2,1,0:T(8,128)(2,1)} fusion(bf16[192,2560,1]{1,0,2:T(8,128)(2,1)S(1)} %reshape.270, pred[192,8,2,96]{0,3,2,1:T(32,128)(4,1)} %bitcast.228), kind=kOutput, calls=%fused_computation.5 | convolution fusion | flops 756940800 | bytes 5111808 | tf_op jit(solution)/shard_map/tgc,td->gcd/dot_general | solution.py:143
  81.3 4.7 %all-to-all-start.3 = ((bf16[8,96,2560]{2,1,0:T(8,128)(2,1)}), bf16[8,96,2560]{2,1,0:T(8,128)(2,1)}, u32[]{:S(2)}, u32[]{:S(2)}) async-start(bf16[8,96,2560]{2,1,0:T(8,128)(2,1)} %convolution_convert_fusion), calls=%async_computation.4 | async-start | bytes 7864320 | tf_op jit(solution)/shard_map/all_to_all | solution.py:146
  86.0 8.2 %fusion.67 = (bf16[1,2560,2,384]{3,2,1,0:T(2,128)(2,1)}, bf16[1,2560,2,384]{3,2,1,0:T(2,128)(2,1)}) fusion(bf16[2,2560,2,384]{3,2,1,0:T(2,128)(2,1)} %param.30), kind=kLoop, calls=%fused_computation.124 | loop fusion | bytes 15728640 | tf_op jit(solution)/shard_map/slice | solution.py:149
  94.2 3.1 %convolution_convert_fusion.1 = bf16[8,96,2560]{2,1,0:T(8,128)(2,1)} fusion(bf16[192,2560,1]{1,0,2:T(8,128)(2,1)S(1)} %reshape.270, pred[192,8,2,96]{0,3,2,1:T(32,128)(4,1)S(1)} %bitcast.229), kind=kOutput, calls=%fused_computation.6 | convolution fusion | flops 756940800 | bytes 5111808 | tf_op jit(solution)/shard_map/tgc,td->gcd/dot_general | solution.py:143
  97.3 34.9 %all-to-all-done.3 = bf16[8,96,2560]{2,1,0:T(8,128)(2,1)} async-done(((bf16[8,96,2560]{2,1,0:T(8,128)(2,1)}), bf16[8,96,2560]{2,1,0:T(8,128)(2,1)}, u32[]{:S(2)}, u32[]{:S(2)}) %all-to-all-start.3) | async-done | bytes 3932192 | tf_op jit(solution)/shard_map/all_to_all | solution.py:146
  132.2 4.5 %all-to-all-start.1 = ((bf16[8,96,2560]{2,1,0:T(8,128)(2,1)}), bf16[8,96,2560]{2,1,0:T(8,128)(2,1)}, u32[]{:S(2)}, u32[]{:S(2)}) async-start(bf16[8,96,2560]{2,1,0:T(8,128)(2,1)} %convolution_convert_fusion.1), calls=%async_computation.1 | async-start | bytes 7864320 | tf_op jit(solution)/shard_map/all_to_all | solution.py:146
  136.8 6.7 %fusion.1 = f32[768,2,384]{2,0,1:T(8,128)S(1)} fusion(bf16[768,2560,1]{1,0,2:T(8,128)(2,1)} %bitcast.45, bf16[1,2560,2,384]{3,2,1,0:T(2,128)(2,1)} %get-tuple-element.6), kind=kOutput, calls=%fused_computation.12 | convolution fusion | flops 3019898880 | bytes 10223616 | tf_op jit(solution)/shard_map/md,dcf->mcf/dot_general | solution.py:148
  143.4 2.2 convolution_convert_fusion.2
  145.7 2.2 copy.163
  147.9 35.1 %all-to-all-done.1 = bf16[8,96,2560]{2,1,0:T(8,128)(2,1)} async-done(((bf16[8,96,2560]{2,1,0:T(8,128)(2,1)}), bf16[8,96,2560]{2,1,0:T(8,128)(2,1)}, u32[]{:S(2)}, u32[]{:S(2)}) %all-to-all-start.1) | async-done | bytes 3932192 | tf_op jit(solution)/shard_map/all_to_all | solution.py:146
  183.0 6.7 %fusion.2 = f32[768,2,384]{2,0,1:T(8,128)S(1)} fusion(bf16[768,2560,1]{1,0,2:T(8,128)(2,1)} %bitcast.34, bf16[1,2560,2,384]{3,2,1,0:T(2,128)(2,1)} %get-tuple-element.5), kind=kOutput, calls=%fused_computation.14 | convolution fusion | flops 3019898880 | bytes 10223616 | tf_op jit(solution)/shard_map/md,dcf->mcf/dot_general | solution.py:148
  189.7 4.2 %convolution_convert_fusion.3 = bf16[768,2560]{1,0:T(8,128)(2,1)} fusion(bf16[2,384,2560]{2,1,0:T(8,128)(2,1)S(1)} %copy-done.14, f32[768,2,384]{2,0,1:T(8,128)S(1)} %fusion.2), kind=kOutput, calls=%fused_computation.8 | convolution fusion | flops 1513684992 | bytes 8257536 | tf_op jit(solution)/shard_map/dot_general | solution.py:152
  193.9 4.5 %all-to-all-start.2 = ((bf16[8,96,2560]{2,1,0:T(8,128)(2,1)}), bf16[8,96,2560]{2,1,0:T(8,128)(2,1)}, u32[]{:S(2)}, u32[]{:S(2)}) async-start(bf16[8,96,2560]{2,1,0:T(8,128)(2,1)} %bitcast.224), calls=%async_computation.2 | async-start | bytes 7864320 | tf_op jit(solution)/shard_map/all_to_all | solution.py:161
  199.4 1.7 fusion.18
  201.2 2.1 select_reduce_fusion
  203.2 3.3 %convert_element_type.125 = bf16[192,8,2,96]{3,2,1,0:T(2,128)(2,1)S(1)} reshape(bf16[192,1536]{1,0:T(8,128)(2,1)} %select_reduce_fusion) | data formatting | bytes 1179648 | tf_op jit(solution)/shard_map/convert_element_type | solution.py:170
  206.5 2.3 fusion.68
  208.8 4.0 %fusion.4 = f32[192,2,384]{2,0,1:T(8,128)} fusion(bf16[2560,2,384]{2,1,0:T(2,128)(2,1)} %param.32, f32[192,2560]{1,0:T(8,128)S(1)} %bitcast.221, f32[2560]{0:T(1024)S(1)} %copy-done.11, f32[192]{0:T(256)S(1)} %add_rsqrt_fusion), kind=kOutput, calls=%fused_computation.19 | convolution fusion | flops 756449280 | bytes 6499072 | tf_op jit(solution)/shard_map/td,dcf->tcf/dot_general | solution.py:182
  212.8 31.9 %all-to-all-done.2 = bf16[8,96,2560]{2,1,0:T(8,128)(2,1)} async-done(((bf16[8,96,2560]{2,1,0:T(8,128)(2,1)}), bf16[8,96,2560]{2,1,0:T(8,128)(2,1)}, u32[]{:S(2)}, u32[]{:S(2)}) %all-to-all-start.2) | async-done | bytes 3932192 | tf_op jit(solution)/shard_map/all_to_all | solution.py:161
  244.8 3.3 %convolution_bitcast_fusion = f32[192,2560]{1,0:T(8,128)S(1)} fusion(bf16[8,96,2560]{2,1,0:T(8,128)(2,1)} %all-to-all-done.2, bf16[192,8,1,96]{3,2,1,0:T(2,128)(2,1)S(1)} %copy-done.6), kind=kOutput, calls=%fused_computation.22 | convolution fusion | flops 754974720 | bytes 6193152 | tf_op jit(solution)/shard_map/tgc,gcd->td/dot_general | solution.py:173
  248.1 0.7 fusion.6
  248.8 1.0 copy.164
  249.9 4.2 %all-to-all-start.4 = ((bf16[8,96,640]{2,1,0:T(8,128)(2,1)}), bf16[8,96,640]{2,1,0:T(8,128)(2,1)}, u32[]{:S(2)}, u32[]{:S(2)}) async-start(bf16[8,96,640]{2,1,0:T(8,128)(2,1)} %bitcast.232), calls=%async_computation.6 | async-start | bytes 1966080 | tf_op jit(solution)/shard_map/all_to_all | solution.py:161
  254.1 20.3 %reduce-scatter.3.cloned.1.call-done = bf16[1,192,640]{2,1,0:T(8,128)(2,1)} async-done(((bf16[4,192,640]{2,1,0:T(8,128)(2,1)}), bf16[1,192,640]{2,1,0:T(8,128)(2,1)}) %reduce-scatter.3.cloned.1.call-update) | async-done | bytes 245776 | tf_op jit(solution)/shard_map/reduce_scatter | solution.py:188
  274.4 2.6 fusion.24
  (73 shorter events, 4.3 us)
Async XLA Ops:
  6.5 15.7 %copy-start = (bf16[640,2560]{1,0:T(8,128)(2,1)S(1)}, bf16[640,2560]{1,0:T(8,128)(2,1)}, u32[]{:S(2)}) copy-start(bf16[640,2560]{1,0:T(8,128)(2,1)} %param.26) | copy-start | bytes 9830404
  6.5 7.7 %copy-start.7 = (bf16[192,640]{1,0:T(8,128)(2,1)S(1)}, bf16[192,640]{1,0:T(8,128)(2,1)}, u32[]{:S(2)}) copy-start(bf16[192,640]{1,0:T(8,128)(2,1)} %param.17) | copy-start | bytes 737284
  6.5 8.7 %copy-start.16 = (s32[4,48]{1,0:T(4,128)S(1)}, s32[4,48]{1,0:T(4,128)}, u32[]{:S(2)}) copy-start(s32[4,48]{1,0:T(4,128)} %param.24) | copy-start | bytes 2308
  15.3 3.7 %copy-start.12 = (bf16[192,128]{1,0:T(8,128)(2,1)S(1)}, bf16[192,128]{1,0:T(8,128)(2,1)}, u32[]{:S(2)}) copy-start(bf16[192,128]{1,0:T(8,128)(2,1)} %param.18) | copy-start | bytes 147460
  16.8 2.2 copy-start.2
  18.9 1.5 copy-start.5
  20.5 1.3 copy-start.15
  22.2 8.3 %copy-start.10 = (s32[192,6]{0,1:T(8,128)S(1)}, s32[192,6]{0,1:T(8,128)}, u32[]{:S(2)}) copy-start(s32[192,6]{0,1:T(8,128)} %param.29) | copy-start | bytes 13828
  22.2 8.7 %copy-start.11 = (f32[2560]{0:T(1024)S(1)}, f32[2560]{0:T(1024)}, u32[]{:S(2)}) copy-start(f32[2560]{0:T(1024)} %param.27) | copy-start | bytes 30724
  24.2 30.6 %all-to-all-start = ((bf16[4,192,640]{2,1,0:T(8,128)(2,1)}), bf16[4,192,640]{2,1,0:T(8,128)(2,1)S(1)}, u32[]{:S(2)}, u32[]{:S(2)}) async-start(bf16[4,192,640]{2,1,0:T(8,128)(2,1)} %bitcast.214), calls=%async_computation | async-start | bytes 1966080 | tf_op jit(solution)/shard_map/all_to_all | solution.py:125
  81.3 50.8 %all-to-all-start.3 = ((bf16[8,96,2560]{2,1,0:T(8,128)(2,1)}), bf16[8,96,2560]{2,1,0:T(8,128)(2,1)}, u32[]{:S(2)}, u32[]{:S(2)}) async-start(bf16[8,96,2560]{2,1,0:T(8,128)(2,1)} %convolution_convert_fusion), calls=%async_computation.4 | async-start | bytes 7864320 | tf_op jit(solution)/shard_map/all_to_all | solution.py:146
  86.0 8.2 %copy-start.4 = (pred[192,1536]{0,1:T(32,128)(4,1)S(1)}, pred[192,1536]{0,1:T(32,128)(4,1)}, u32[]{:S(2)}) copy-start(pred[192,1536]{0,1:T(32,128)(4,1)} %copy.111) | copy-start | bytes 884740
  132.2 50.9 %all-to-all-start.1 = ((bf16[8,96,2560]{2,1,0:T(8,128)(2,1)}), bf16[8,96,2560]{2,1,0:T(8,128)(2,1)}, u32[]{:S(2)}, u32[]{:S(2)}) async-start(bf16[8,96,2560]{2,1,0:T(8,128)(2,1)} %convolution_convert_fusion.1), calls=%async_computation.1 | async-start | bytes 7864320 | tf_op jit(solution)/shard_map/all_to_all | solution.py:146
  136.7 113.2 %reduce-scatter.5.cloned.1.call-start = ((), (), s32[]{:S(2)}) async-start(), calls=%async_computation.8 | async-start | bytes 4915200 | tf_op jit(solution)/shard_map/reduce_scatter | solution.py:157
  136.8 6.7 %copy-start.13 = (bf16[2,384,2560]{2,1,0:T(8,128)(2,1)S(1)}, bf16[2,384,2560]{2,1,0:T(8,128)(2,1)}, u32[]{:S(2)}) copy-start(bf16[2,384,2560]{2,1,0:T(8,128)(2,1)} %param.31) | copy-start | bytes 11796484
  183.0 6.7 %copy-start.14 = (bf16[2,384,2560]{2,1,0:T(8,128)(2,1)S(1)}, bf16[2,384,2560]{2,1,0:T(8,128)(2,1)}, u32[]{:S(2)}) copy-start(bf16[2,384,2560]{2,1,0:T(8,128)(2,1)} %param.31) | copy-start | bytes 11796484
  193.9 50.8 %all-to-all-start.2 = ((bf16[8,96,2560]{2,1,0:T(8,128)(2,1)}), bf16[8,96,2560]{2,1,0:T(8,128)(2,1)}, u32[]{:S(2)}, u32[]{:S(2)}) async-start(bf16[8,96,2560]{2,1,0:T(8,128)(2,1)} %bitcast.224), calls=%async_computation.2 | async-start | bytes 7864320 | tf_op jit(solution)/shard_map/all_to_all | solution.py:161
  198.4 0.9 copy-start.8
  198.4 76.0 %reduce-scatter.3.cloned.1.call-start = ((), (), s32[]{:S(2)}) async-start(), calls=%async_computation.7 | async-start | bytes 1228800 | tf_op jit(solution)/shard_map/reduce_scatter | solution.py:188
  208.8 36.0 %copy-start.6 = (bf16[192,8,1,96]{3,2,1,0:T(2,128)(2,1)S(1)}, bf16[192,8,1,96]{3,2,1,0:T(2,128)(2,1)}, u32[]{:S(2)}) copy-start(bf16[192,8,1,96]{3,2,1,0:T(2,128)(2,1)} %get-tuple-element.7) | copy-start | bytes 884740
  244.7 3.3 %copy-start.3 = (bf16[384,2560]{1,0:T(8,128)(2,1)S(1)}, bf16[384,2560]{1,0:T(8,128)(2,1)}, u32[]{:S(2)}) copy-start(bf16[384,2560]{1,0:T(8,128)(2,1)} %param.33) | copy-start | bytes 5898244
  244.8 3.3 %copy-start.9 = (f32[192,2,384]{2,0,1:T(8,128)S(1)}, f32[192,2,384]{2,0,1:T(8,128)}, u32[]{:S(2)}) copy-start(f32[192,2,384]{2,0,1:T(8,128)} %fusion.4) | copy-start | bytes 1769476
  248.1 29.0 %copy-start.1 = (bf16[640,2560]{1,0:T(8,128)(2,1)S(1)}, bf16[640,2560]{1,0:T(8,128)(2,1)}, u32[]{:S(2)}) copy-start(bf16[640,2560]{1,0:T(8,128)(2,1)} %param.26) | copy-start | bytes 9830404
  249.9 24.5 %all-to-all-start.4 = ((bf16[8,96,640]{2,1,0:T(8,128)(2,1)}), bf16[8,96,640]{2,1,0:T(8,128)(2,1)}, u32[]{:S(2)}, u32[]{:S(2)}) async-start(bf16[8,96,640]{2,1,0:T(8,128)(2,1)} %bitcast.232), calls=%async_computation.6 | async-start | bytes 1966080 | tf_op jit(solution)/shard_map/all_to_all | solution.py:161
Sparse Core Ops, SparseCore 0:
  148.0 73.1 reduce-scatter.4
  250.0 24.3 reduce-scatter.2

commit v15 on v14

--- a/solution.py
+++ b/solution.py
@@ -128,8 +128,7 @@
     attn_part = jnp.sum(attn_blocks.astype(jnp.float32), axis=0)
     residual_part = lax.dynamic_slice_in_dim(residual, column, part_width, 1)
     hidden_part_bf = (residual_part.astype(jnp.float32) + attn_part).astype(jnp.bfloat16)
-    hidden_bf = lax.all_gather(hidden_part_bf[None], "tp", axis=0, tiled=True)
-    hidden = hidden_bf.transpose(1, 0, 2).reshape(row_count, model_width).astype(jnp.float32)
+    hidden = lax.all_gather(hidden_part_bf, "tp", axis=1, tiled=True).astype(jnp.float32)
     rstd = lax.rsqrt(jnp.mean(hidden * hidden, axis=1, keepdims=True) + EPSILON)
     normed = hidden * rstd * norm_gain
     logits = jnp.dot(normed, router_weight, precision=lax.Precision.HIGHEST)

time: 285 us -> 288 us (1.011)
  waiting for transfers between devices: 138 us -> 143 us
  local copies, waits for them, and re-layouts: 29.1 us -> 26.1 us
    all_to_all x2, waiting for transfers between devices: 31.9 us -> 36.2 us  [shards(): lax.all_to_all(outputs, 'req', split_axis=0, concat_axis=0, tiled=True)]
  transfers between devices with their start and end apart: 7 -> 7, of which waited for: 5 -> 5; matrix products, arithmetic and copies ran while one was open for 21% -> 19% of each run, Pallas kernels for 0% -> 0%
where the time goes in v15:
time: 288 us; the launch traced here: 287 us
  waiting for transfers between devices  143 us (50%)
  matrix products  48 us (17%)
  local copies, waits for them, and re-layouts  26.1 us (9%)
  starting transfers between devices  24.7 us (9%)
  blocking collectives  19.7 us (7%)
  between operations  13.9 us (5%)
  other arithmetic  11.5 us (4%)
    all_to_all x2, waiting for transfers between devices, shards(): lax.all_to_all(outbox, 'req', split_axis=0, concat_axis=0, tiled=True)  69.9 us
    all_to_all x2, waiting for transfers between devices, shards(): lax.all_to_all(outputs, 'req', split_axis=0, concat_axis=0, tiled=True)  36.2 us
    reduce_scatter x1, waiting for transfers between devices, shards(): lax.psum_scatter(total.transpose(1, 0, 2), 'tp', scatter_dimension=0, til...  20.3 us
    all_gather x1, blocking collectives, shards(): lax.all_gather(hidden_part_bf, 'tp', axis=1, tiled=True).astype(jnp.float32)  19.7 us
    all_to_all x1, waiting for transfers between devices, shards(): lax.all_to_all(attn_blocks.transpose(1, 0, 2), 'tp', split_axis=0, concat...  16.7 us
    dot_general x2, matrix products, shards(): jnp.einsum('md,dcf->mcf', rows, expert_gate_up[expert], preferred_element...  13.3 us
    all_to_all x2, starting transfers between devices, shards(): lax.all_to_all(outbox, 'req', split_axis=0, concat_axis=0, tiled=True)  9.22 us
    all_to_all x2, starting transfers between devices, shards(): lax.all_to_all(outputs, 'req', split_axis=0, concat_axis=0, tiled=True)  8.88 us
  transfers between devices with their start and end apart: 7, of which 5 were waited for; matrix products, arithmetic and copies ran while one was open for 19% of the time, Pallas kernels for 0%

profile of v15, /device:TPU:0, one launch (start us, length us, event | category | flops | bytes accessed | tf_op | source)
XLA Modules:
  0.0 287.1 jit_solution(8017054268751026715)
XLA Ops:
  6.6 0.8 compare_select_fusion
  7.5 0.8 iota_compare_fusion.6
  8.3 2.0 reshape.201
  10.2 1.0 convolution_minimum_fusion.5
  12.5 2.9 %gather_fusion.1 = bf16[64,64,128]{2,1,0:T(8,128)(2,1)} fusion(bf16[64,64,128]{2,1,0:T(8,128)(2,1)} %param.20, s32[1024]{0:T(1024)S(1)} %pad_clamp_fusion), kind=kCustom, calls=%fused_computation.1 | custom fusion | bytes 2097408 | tf_op jit(solution)/shard_map/gather | solution.py:93
  15.4 2.1 bitcast_reduce_fusion
  17.6 0.4 fusion.68
  18.0 1.4 copy-done.2
  19.4 1.0 fusion.7
  20.5 2.9 %gather_fusion = bf16[64,64,128]{2,1,0:T(8,128)(2,1)} fusion(bf16[64,64,128]{2,1,0:T(8,128)(2,1)} %param.21, s32[1024]{0:T(1024)S(1)} %pad_clamp_fusion), kind=kCustom, calls=%fused_computation | custom fusion | bytes 2097408 | tf_op jit(solution)/shard_map/gather | solution.py:94
  23.4 3.5 %fusion.15 = f32[4,128,5,48]{1,3,2,0:T(8,128)S(1)} fusion(bf16[4,1024,128,1]{2,1,3,0:T(8,128)(2,1)} %bitcast.217, f32[4,1024,48,5]{1,2,3,0:T(8,128)} %copy-done.2, f32[4,5,48]{2,1,0:T(8,128)S(1)} %add.75, f32[4,5,48]{2,1,0:T(8,128)S(1)} %max.9, pred[4,1024]{1,0:T(4,128)(4,1)S(1)} %iota_compare_fusion.6), kind=kOutput, calls=%fused_computation.34 | convolution fusion | flops 256573440 | bytes 5484032 | tf_op jit(solution)/shard_map/rkgtc,rckd->rtkgd/dot_general | solution.py:54
  26.9 0.3 fusion.29
  27.4 0.9 convolution_convert_fusion.4
  28.3 1.0 copy.154
  29.3 6.3 %all-to-all-start = ((bf16[4,192,640]{2,1,0:T(8,128)(2,1)}), bf16[4,192,640]{2,1,0:T(8,128)(2,1)S(1)}, u32[]{:S(2)}, u32[]{:S(2)}) async-start(bf16[4,192,640]{2,1,0:T(8,128)(2,1)} %bitcast.206), calls=%async_computation | async-start | bytes 1966080 | tf_op jit(solution)/shard_map/all_to_all | solution.py:125
  36.1 4.5 %reduce-window.6 = s32[16,9,128]{2,1,0:T(8,128)S(1)} reduce-window(s32[16,9,128]{2,1,0:T(8,128)S(1)} %fusion.50, s32[]{:T(128)} %constant.17.clone.1), window={size=1x1x128 pad=0_0x0_0x127_0}, to_apply=%region_6.7 | reduce-window | flops 2340864 | bytes 147460 | tf_op jit(solution)/shard_map/reduce-window
  40.6 0.4 slice_reduce_fusion
  41.6 1.2 fusion
  42.8 0.5 copy.102
  43.3 16.7 %all-to-all-done = bf16[4,192,640]{2,1,0:T(8,128)(2,1)S(1)} async-done(((bf16[4,192,640]{2,1,0:T(8,128)(2,1)}), bf16[4,192,640]{2,1,0:T(8,128)(2,1)S(1)}, u32[]{:S(2)}, u32[]{:S(2)}) %all-to-all-start) | async-done | bytes 983072 | tf_op jit(solution)/shard_map/all_to_all | solution.py:125
  60.1 1.0 add_convert_fusion
  61.1 19.7 %all_gather.3 = bf16[192,2560]{1,0:T(8,128)(2,1)S(1)} all-gather(bf16[192,640]{1,0:T(8,128)(2,1)S(1)} %add_convert_fusion), channel_id=1, replica_groups=mesh['req'=8,'tp'=4] {'tp'}, dimensions={1}, use_global_device_ids=true | all-gather | bytes 1228800 | tf_op jit(solution)/shard_map/all_gather | solution.py:131
  80.8 0.3 fusion.8
  81.1 3.3 %convolution_convert_fusion = bf16[8,96,2560]{2,1,0:T(8,128)(2,1)} fusion(pred[192,8,2,96]{0,3,2,1:T(32,128)(4,1)S(1)} %bitcast.215, bf16[192,2560]{1,0:T(8,128)(2,1)S(1)} %all_gather.3, f32[2560]{0:T(1024)S(1)} %copy-done.9, f32[192]{0:T(256)S(1)} %add_rsqrt_fusion), kind=kOutput, calls=%fused_computation.5 | convolution fusion | flops 758906880 | bytes 5125120 | tf_op jit(solution)/shard_map/tgc,td->gcd/dot_general | solution.py:142
  84.4 4.7 %all-to-all-start.3 = ((bf16[8,96,2560]{2,1,0:T(8,128)(2,1)}), bf16[8,96,2560]{2,1,0:T(8,128)(2,1)}, u32[]{:S(2)}, u32[]{:S(2)}) async-start(bf16[8,96,2560]{2,1,0:T(8,128)(2,1)} %convolution_convert_fusion), calls=%async_computation.4 | async-start | bytes 7864320 | tf_op jit(solution)/shard_map/all_to_all | solution.py:145
  89.1 8.1 %fusion.66 = (bf16[1,2560,2,384]{3,2,1,0:T(2,128)(2,1)}, bf16[1,2560,2,384]{3,2,1,0:T(2,128)(2,1)}) fusion(bf16[2,2560,2,384]{3,2,1,0:T(2,128)(2,1)} %param.30), kind=kLoop, calls=%fused_computation.118 | loop fusion | bytes 15728640 | tf_op jit(solution)/shard_map/slice | solution.py:148
  97.2 3.2 %convolution_convert_fusion.1 = bf16[8,96,2560]{2,1,0:T(8,128)(2,1)} fusion(pred[192,8,2,96]{0,3,2,1:T(32,128)(4,1)S(1)} %bitcast.216, bf16[192,2560]{1,0:T(8,128)(2,1)S(1)} %all_gather.3, f32[2560]{0:T(1024)S(1)} %copy-done.9, f32[192]{0:T(256)S(1)} %add_rsqrt_fusion), kind=kOutput, calls=%fused_computation.6 | convolution fusion | flops 758906880 | bytes 5125120 | tf_op jit(solution)/shard_map/tgc,td->gcd/dot_general | solution.py:142
  100.5 34.8 %all-to-all-done.3 = bf16[8,96,2560]{2,1,0:T(8,128)(2,1)} async-done(((bf16[8,96,2560]{2,1,0:T(8,128)(2,1)}), bf16[8,96,2560]{2,1,0:T(8,128)(2,1)}, u32[]{:S(2)}, u32[]{:S(2)}) %all-to-all-start.3) | async-done | bytes 3932192 | tf_op jit(solution)/shard_map/all_to_all | solution.py:145
  135.2 4.5 %all-to-all-start.1 = ((bf16[8,96,2560]{2,1,0:T(8,128)(2,1)}), bf16[8,96,2560]{2,1,0:T(8,128)(2,1)}, u32[]{:S(2)}, u32[]{:S(2)}) async-start(bf16[8,96,2560]{2,1,0:T(8,128)(2,1)} %convolution_convert_fusion.1), calls=%async_computation.1 | async-start | bytes 7864320 | tf_op jit(solution)/shard_map/all_to_all | solution.py:145
  139.8 6.7 %fusion.1 = f32[768,2,384]{2,0,1:T(8,128)S(1)} fusion(bf16[768,2560,1]{1,0,2:T(8,128)(2,1)} %bitcast.41, bf16[1,2560,2,384]{3,2,1,0:T(2,128)(2,1)} %get-tuple-element.6), kind=kOutput, calls=%fused_computation.12 | convolution fusion | flops 3019898880 | bytes 10223616 | tf_op jit(solution)/shard_map/md,dcf->mcf/dot_general | solution.py:147
  146.5 2.2 convolution_convert_fusion.2
  148.7 2.2 copy.152
  150.9 35.1 %all-to-all-done.1 = bf16[8,96,2560]{2,1,0:T(8,128)(2,1)} async-done(((bf16[8,96,2560]{2,1,0:T(8,128)(2,1)}), bf16[8,96,2560]{2,1,0:T(8,128)(2,1)}, u32[]{:S(2)}, u32[]{:S(2)}) %all-to-all-start.1) | async-done | bytes 3932192 | tf_op jit(solution)/shard_map/all_to_all | solution.py:145
  186.1 6.7 %fusion.2 = f32[768,2,384]{2,0,1:T(8,128)S(1)} fusion(bf16[768,2560,1]{1,0,2:T(8,128)(2,1)} %bitcast.30, bf16[1,2560,2,384]{3,2,1,0:T(2,128)(2,1)} %get-tuple-element.5), kind=kOutput, calls=%fused_computation.14 | convolution fusion | flops 3019898880 | bytes 10223616 | tf_op jit(solution)/shard_map/md,dcf->mcf/dot_general | solution.py:147
  192.7 4.2 %convolution_convert_fusion.3 = bf16[768,2560]{1,0:T(8,128)(2,1)} fusion(bf16[2,384,2560]{2,1,0:T(8,128)(2,1)S(1)} %copy-done.12, f32[768,2,384]{2,0,1:T(8,128)S(1)} %fusion.2), kind=kOutput, calls=%fused_computation.8 | convolution fusion | flops 1513684992 | bytes 8257536 | tf_op jit(solution)/shard_map/dot_general | solution.py:151
  196.9 4.6 %all-to-all-start.2 = ((bf16[8,96,2560]{2,1,0:T(8,128)(2,1)}), bf16[8,96,2560]{2,1,0:T(8,128)(2,1)}, u32[]{:S(2)}, u32[]{:S(2)}) async-start(bf16[8,96,2560]{2,1,0:T(8,128)(2,1)} %bitcast.211), calls=%async_computation.2 | async-start | bytes 7864320 | tf_op jit(solution)/shard_map/all_to_all | solution.py:160
  201.9 1.8 fusion.10
  203.7 1.2 select_reduce_fusion
  205.0 0.7 convert_element_type.106
  205.6 2.0 fusion.67
  207.6 4.1 %fusion.4 = f32[192,2,384]{2,0,1:T(8,128)} fusion(bf16[2560,2,384]{2,1,0:T(2,128)(2,1)} %param.32, bf16[192,2560]{1,0:T(8,128)(2,1)S(1)} %all_gather.3, f32[2560]{0:T(1024)S(1)} %copy-done.9, f32[192]{0:T(256)S(1)} %add_rsqrt_fusion), kind=kOutput, calls=%fused_computation.19 | convolution fusion | flops 756940800 | bytes 5516032 | tf_op jit(solution)/shard_map/td,dcf->tcf/dot_general | solution.py:181
  211.7 36.2 %all-to-all-done.2 = bf16[8,96,2560]{2,1,0:T(8,128)(2,1)} async-done(((bf16[8,96,2560]{2,1,0:T(8,128)(2,1)}), bf16[8,96,2560]{2,1,0:T(8,128)(2,1)}, u32[]{:S(2)}, u32[]{:S(2)}) %all-to-all-start.2) | async-done | bytes 3932192 | tf_op jit(solution)/shard_map/all_to_all | solution.py:160
  247.9 3.3 %convolution_bitcast_fusion = f32[192,2560]{1,0:T(8,128)S(1)} fusion(bf16[8,96,2560]{2,1,0:T(8,128)(2,1)} %all-to-all-done.2, bf16[192,8,1,96]{3,2,1,0:T(2,128)(2,1)S(1)} %get-tuple-element.7), kind=kOutput, calls=%fused_computation.22 | convolution fusion | flops 754974720 | bytes 6193152 | tf_op jit(solution)/shard_map/tgc,gcd->td/dot_general | solution.py:172
  251.2 0.7 fusion.6
  251.9 1.0 copy.153
  253.0 4.2 %all-to-all-start.4 = ((bf16[8,96,640]{2,1,0:T(8,128)(2,1)}), bf16[8,96,640]{2,1,0:T(8,128)(2,1)}, u32[]{:S(2)}, u32[]{:S(2)}) async-start(bf16[8,96,640]{2,1,0:T(8,128)(2,1)} %bitcast.219), calls=%async_computation.6 | async-start | bytes 1966080 | tf_op jit(solution)/shard_map/all_to_all | solution.py:160
  257.3 20.3 %reduce-scatter.3.cloned.1.call-done = bf16[1,192,640]{2,1,0:T(8,128)(2,1)} async-done(((bf16[4,192,640]{2,1,0:T(8,128)(2,1)}), bf16[1,192,640]{2,1,0:T(8,128)(2,1)}) %reduce-scatter.3.cloned.1.call-update) | async-done | bytes 245776 | tf_op jit(solution)/shard_map/reduce_scatter | solution.py:187
  277.6 2.6 fusion.24
  (63 shorter events, 3.1 us)
Async XLA Ops:
  6.5 20.8 %copy-start = (bf16[640,2560]{1,0:T(8,128)(2,1)S(1)}, bf16[640,2560]{1,0:T(8,128)(2,1)}, u32[]{:S(2)}) copy-start(bf16[640,2560]{1,0:T(8,128)(2,1)} %param.26) | copy-start | bytes 9830404
  11.9 5.6 %copy-start.10 = (bf16[192,128]{1,0:T(8,128)(2,1)S(1)}, bf16[192,128]{1,0:T(8,128)(2,1)}, u32[]{:S(2)}) copy-start(bf16[192,128]{1,0:T(8,128)(2,1)} %param.18) | copy-start | bytes 147460
  15.4 2.2 copy-start.3
  17.6 1.9 copy-start.2
  18.0 2.4 copy-start.4
  23.4 3.5 %copy-start.5 = (f32[4,1,5,48,48]{3,4,2,0,1:T(8,128)S(1)}, f32[4,1,5,48,48]{3,4,2,0,1:T(8,128)}, u32[]{:S(2)}) copy-start(f32[4,1,5,48,48]{3,4,2,0,1:T(8,128)} %copy-done.4) | copy-start | bytes 552964
  23.4 3.5 %copy-start.14 = (bf16[192,128]{1,0:T(8,128)(2,1)S(1)}, bf16[192,128]{1,0:T(8,128)(2,1)}, u32[]{:S(2)}) copy-start(bf16[192,128]{1,0:T(8,128)(2,1)} %param.19) | copy-start | bytes 147460
  27.3 8.3 %copy-start.8 = (s32[192,6]{0,1:T(8,128)S(1)}, s32[192,6]{0,1:T(8,128)}, u32[]{:S(2)}) copy-start(s32[192,6]{0,1:T(8,128)} %param.29) | copy-start | bytes 13828
  29.3 30.6 %all-to-all-start = ((bf16[4,192,640]{2,1,0:T(8,128)(2,1)}), bf16[4,192,640]{2,1,0:T(8,128)(2,1)S(1)}, u32[]{:S(2)}, u32[]{:S(2)}) async-start(bf16[4,192,640]{2,1,0:T(8,128)(2,1)} %bitcast.206), calls=%async_computation | async-start | bytes 1966080 | tf_op jit(solution)/shard_map/all_to_all | solution.py:125
  35.7 45.4 %copy-start.9 = (f32[2560]{0:T(1024)S(1)}, f32[2560]{0:T(1024)}, u32[]{:S(2)}) copy-start(f32[2560]{0:T(1024)} %param.27) | copy-start | bytes 30724
  84.4 50.8 %all-to-all-start.3 = ((bf16[8,96,2560]{2,1,0:T(8,128)(2,1)}), bf16[8,96,2560]{2,1,0:T(8,128)(2,1)}, u32[]{:S(2)}, u32[]{:S(2)}) async-start(bf16[8,96,2560]{2,1,0:T(8,128)(2,1)} %convolution_convert_fusion), calls=%async_computation.4 | async-start | bytes 7864320 | tf_op jit(solution)/shard_map/all_to_all | solution.py:145
  135.2 50.9 %all-to-all-start.1 = ((bf16[8,96,2560]{2,1,0:T(8,128)(2,1)}), bf16[8,96,2560]{2,1,0:T(8,128)(2,1)}, u32[]{:S(2)}, u32[]{:S(2)}) async-start(bf16[8,96,2560]{2,1,0:T(8,128)(2,1)} %convolution_convert_fusion.1), calls=%async_computation.1 | async-start | bytes 7864320 | tf_op jit(solution)/shard_map/all_to_all | solution.py:145
  139.7 113.3 %reduce-scatter.5.cloned.1.call-start = ((), (), s32[]{:S(2)}) async-start(), calls=%async_computation.8 | async-start | bytes 4915200 | tf_op jit(solution)/shard_map/reduce_scatter | solution.py:156
  139.8 6.7 %copy-start.11 = (bf16[2,384,2560]{2,1,0:T(8,128)(2,1)S(1)}, bf16[2,384,2560]{2,1,0:T(8,128)(2,1)}, u32[]{:S(2)}) copy-start(bf16[2,384,2560]{2,1,0:T(8,128)(2,1)} %param.31) | copy-start | bytes 11796484
  186.1 6.7 %copy-start.12 = (bf16[2,384,2560]{2,1,0:T(8,128)(2,1)S(1)}, bf16[2,384,2560]{2,1,0:T(8,128)(2,1)}, u32[]{:S(2)}) copy-start(bf16[2,384,2560]{2,1,0:T(8,128)(2,1)} %param.31) | copy-start | bytes 11796484
  196.9 4.9 %copy-start.13 = (f32[2560,16]{0,1:T(8,128)S(1)}, f32[2560,16]{0,1:T(8,128)}, u32[]{:S(2)}) copy-start(f32[2560,16]{0,1:T(8,128)} %param.28) | copy-start | bytes 491524
  196.9 51.0 %all-to-all-start.2 = ((bf16[8,96,2560]{2,1,0:T(8,128)(2,1)}), bf16[8,96,2560]{2,1,0:T(8,128)(2,1)}, u32[]{:S(2)}, u32[]{:S(2)}) async-start(bf16[8,96,2560]{2,1,0:T(8,128)(2,1)} %bitcast.211), calls=%async_computation.2 | async-start | bytes 7864320 | tf_op jit(solution)/shard_map/all_to_all | solution.py:160
  201.6 76.0 %reduce-scatter.3.cloned.1.call-start = ((), (), s32[]{:S(2)}) async-start(), calls=%async_computation.7 | async-start | bytes 1228800 | tf_op jit(solution)/shard_map/reduce_scatter | solution.py:187
  247.9 3.3 %copy-start.6 = (bf16[384,2560]{1,0:T(8,128)(2,1)S(1)}, bf16[384,2560]{1,0:T(8,128)(2,1)}, u32[]{:S(2)}) copy-start(bf16[384,2560]{1,0:T(8,128)(2,1)} %param.33) | copy-start | bytes 5898244
  247.9 3.3 %copy-start.7 = (f32[192,2,384]{2,0,1:T(8,128)S(1)}, f32[192,2,384]{2,0,1:T(8,128)}, u32[]{:S(2)}) copy-start(f32[192,2,384]{2,0,1:T(8,128)} %fusion.4) | copy-start | bytes 1769476
  251.2 29.0 %copy-start.1 = (bf16[640,2560]{1,0:T(8,128)(2,1)S(1)}, bf16[640,2560]{1,0:T(8,128)(2,1)}, u32[]{:S(2)}) copy-start(bf16[640,2560]{1,0:T(8,128)(2,1)} %param.26) | copy-start | bytes 9830404
  253.0 24.5 %all-to-all-start.4 = ((bf16[8,96,640]{2,1,0:T(8,128)(2,1)}), bf16[8,96,640]{2,1,0:T(8,128)(2,1)}, u32[]{:S(2)}, u32[]{:S(2)}) async-start(bf16[8,96,640]{2,1,0:T(8,128)(2,1)} %bitcast.219), calls=%async_computation.6 | async-start | bytes 1966080 | tf_op jit(solution)/shard_map/all_to_all | solution.py:160
Sparse Core Ops, SparseCore 0:
  151.1 73.1 reduce-scatter.4
  253.1 24.3 reduce-scatter.2

commit v16 on v8

--- a/solution.py
+++ b/solution.py
@@ -122,10 +122,9 @@
     hit = slot[:, :, None] == slot_ids[None, None, :]
 
     attn_blocks = attn_terms.astype(jnp.bfloat16).reshape(row_count, tp_count, part_width)
-    attn_blocks = lax.all_to_all(
-        attn_blocks.transpose(1, 0, 2), "tp", split_axis=0, concat_axis=0, tiled=True
-    )
-    attn_part = jnp.sum(attn_blocks.astype(jnp.float32), axis=0)
+    attn_part = lax.psum_scatter(
+        attn_blocks.transpose(1, 0, 2), "tp", scatter_dimension=0, tiled=True
+    )[0].astype(jnp.float32)
     residual_part = lax.dynamic_slice_in_dim(residual, column, part_width, 1)
     hidden_part_bf = (residual_part.astype(jnp.float32) + attn_part).astype(jnp.bfloat16)
     hidden_bf = lax.all_gather(hidden_part_bf[None], "tp", axis=0, tiled=True)

time: 285 us -> 283 us (level)
  starting transfers between devices: 20.4 us -> 14 us
  waiting for transfers between devices: 124 us -> 128 us
    reduce_scatter x0 -> x1, waiting for transfers between devices: none -> 20.6 us  [shards(): lax.psum_scatter(attn_blocks.transpose(1, 0, 2), 'tp', scatter_dimension=...]
    all_to_all x1 -> x0, waiting for transfers between devices: 15.9 us -> none  [shards(): lax.all_to_all(attn_blocks.transpose(1, 0, 2), 'tp', split_axis=0, concat...]
    all_to_all x1 -> x0, starting transfers between devices: 6.31 us -> none  [shards(): lax.all_to_all(attn_blocks.transpose(1, 0, 2), 'tp', split_axis=0, concat...]
where the time goes in v16:
time: 283 us; the launch traced here: 282 us
  waiting for transfers between devices  128 us (45%)
  matrix products  46 us (16%)
  blocking collectives  38.6 us (14%)
  local copies, waits for them, and re-layouts  27.1 us (10%)
  other arithmetic  14.5 us (5%)
  starting transfers between devices  14 us (5%)
  between operations  13.7 us (5%)
    all_to_all x2, waiting for transfers between devices, shards(): lax.all_to_all(outbox, 'req', split_axis=0, concat_axis=0, tiled=True)  70 us
    all_to_all x1, waiting for transfers between devices, shards(): lax.all_to_all(outputs, 'req', split_axis=0, concat_axis=0, tiled=True)  34.9 us
    reduce_scatter x1, waiting for transfers between devices, shards(): lax.psum_scatter(attn_blocks.transpose(1, 0, 2), 'tp', scatter_dimension=...  20.6 us
    all_gather x1, blocking collectives, shards(): hidden_bf = lax.all_gather(hidden_part_bf[None], 'tp', axis=0, tiled=True)  20.2 us
    all_to_all x1, blocking collectives, shards(): lax.all_to_all(outputs, 'req', split_axis=0, concat_axis=0, tiled=True)  18.4 us
    dot_general x2, matrix products, shards(): jnp.einsum('md,dcf->mcf', rows, expert_gate_up[expert], preferred_element...  13.3 us
    all_to_all x2, starting transfers between devices, shards(): lax.all_to_all(outbox, 'req', split_axis=0, concat_axis=0, tiled=True)  9.22 us
    slice x1, local copies, waits for them, and re-layouts, shards(): expert_gate_up[expert]  8.16 us
  transfers between devices with their start and end apart: 6, of which 5 were waited for; matrix products, arithmetic and copies ran while one was open for 21% of the time, Pallas kernels for 0%

profile of v16, /device:TPU:0, one launch (start us, length us, event | category | flops | bytes accessed | tf_op | source)
XLA Modules:
  0.0 282.1 jit_solution(17091085564202939300)
XLA Ops:
  6.6 0.8 compare_select_fusion
  7.5 0.9 iota_compare_fusion.6
  8.4 2.9 %gather_fusion = bf16[64,64,128]{2,1,0:T(8,128)(2,1)} fusion(bf16[64,64,128]{2,1,0:T(8,128)(2,1)} %param.21, s32[1024]{0:T(1024)S(1)} %pad_clamp_fusion), kind=kCustom, calls=%fused_computation | custom fusion | bytes 2097408 | tf_op jit(solution)/shard_map/gather | solution.py:94
  11.3 2.9 %gather_fusion.1 = bf16[64,64,128]{2,1,0:T(8,128)(2,1)} fusion(bf16[64,64,128]{2,1,0:T(8,128)(2,1)} %param.20, s32[1024]{0:T(1024)S(1)} %pad_clamp_fusion), kind=kCustom, calls=%fused_computation.1 | custom fusion | bytes 2097408 | tf_op jit(solution)/shard_map/gather | solution.py:93
  14.2 1.0 reshape.260
  16.8 2.1 bitcast_reduce_fusion
  19.0 0.4 fusion.81
  19.4 1.0 fusion.8
  20.5 1.3 fusion.15
  22.2 0.9 convolution_convert_fusion.4
  23.2 1.0 copy.145
  24.7 4.5 %reduce-window.6 = s32[16,9,128]{2,1,0:T(8,128)S(1)} reduce-window(s32[16,9,128]{2,1,0:T(8,128)S(1)} %fusion.65, s32[]{:T(128)} %constant.17.clone.1), window={size=1x1x128 pad=0_0x0_0x127_0}, to_apply=%region_6.7 | reduce-window | flops 2340864 | bytes 147460 | tf_op jit(solution)/shard_map/reduce-window
  29.2 0.4 slice_reduce_fusion
  30.2 1.2 fusion
  31.4 1.2 copy.91
  32.6 20.6 %reduce-scatter.4.cloned.1.call-done = bf16[1,192,640]{2,1,0:T(8,128)(2,1)} async-done(((bf16[4,192,640]{2,1,0:T(8,128)(2,1)}), bf16[1,192,640]{2,1,0:T(8,128)(2,1)}) %reduce-scatter.4.cloned.1.call-update) | async-done | bytes 245776 | tf_op jit(solution)/shard_map/reduce_scatter | solution.py:125
  53.2 1.1 fusion.52
  54.3 20.2 %all-gather = bf16[768,640]{1,0:T(8,128)(2,1)S(1)} all-gather(bf16[192,640]{1,0:T(8,128)(2,1)S(1)} %fusion.52), channel_id=2, replica_groups=mesh['req'=8,'tp'=4] {'tp'}, dimensions={0}, use_global_device_ids=true | all-gather | bytes 1228800 | tf_op jit(solution)/shard_map/all_gather | solution.py:130
  75.1 0.8 copy.93
  75.9 0.4 reshape.307
  76.3 4.0 %convolution_convert_fusion = bf16[8,96,2560]{2,1,0:T(8,128)(2,1)} fusion(bf16[192,2560,1]{1,0,2:T(8,128)(2,1)S(1)} %reshape.307, pred[192,8,2,96]{0,3,2,1:T(32,128)(4,1)} %bitcast.238), kind=kOutput, calls=%fused_computation.5 | convolution fusion | flops 756940800 | bytes 5111808 | tf_op jit(solution)/shard_map/tgc,td->gcd/dot_general | solution.py:142
  80.3 4.7 %all-to-all-start.2 = ((bf16[8,96,2560]{2,1,0:T(8,128)(2,1)}), bf16[8,96,2560]{2,1,0:T(8,128)(2,1)}, u32[]{:S(2)}, u32[]{:S(2)}) async-start(bf16[8,96,2560]{2,1,0:T(8,128)(2,1)} %convolution_convert_fusion), calls=%async_computation.4 | async-start | bytes 7864320 | tf_op jit(solution)/shard_map/all_to_all | solution.py:145
  85.0 8.2 %fusion.80 = (bf16[1,2560,2,384]{3,2,1,0:T(2,128)(2,1)}, bf16[1,2560,2,384]{3,2,1,0:T(2,128)(2,1)}) fusion(bf16[2,2560,2,384]{3,2,1,0:T(2,128)(2,1)} %param.30), kind=kLoop, calls=%fused_computation.139 | loop fusion | bytes 15728640 | tf_op jit(solution)/shard_map/slice | solution.py:148
  93.2 3.1 %convolution_convert_fusion.1 = bf16[8,96,2560]{2,1,0:T(8,128)(2,1)} fusion(bf16[192,2560,1]{1,0,2:T(8,128)(2,1)S(1)} %reshape.307, pred[192,8,2,96]{0,3,2,1:T(32,128)(4,1)S(1)} %bitcast.239), kind=kOutput, calls=%fused_computation.6 | convolution fusion | flops 756940800 | bytes 5111808 | tf_op jit(solution)/shard_map/tgc,td->gcd/dot_general | solution.py:142
  96.3 34.9 %all-to-all-done.2 = bf16[8,96,2560]{2,1,0:T(8,128)(2,1)} async-done(((bf16[8,96,2560]{2,1,0:T(8,128)(2,1)}), bf16[8,96,2560]{2,1,0:T(8,128)(2,1)}, u32[]{:S(2)}, u32[]{:S(2)}) %all-to-all-start.2) | async-done | bytes 3932192 | tf_op jit(solution)/shard_map/all_to_all | solution.py:145
  131.1 4.5 %all-to-all-start = ((bf16[8,96,2560]{2,1,0:T(8,128)(2,1)}), bf16[8,96,2560]{2,1,0:T(8,128)(2,1)}, u32[]{:S(2)}, u32[]{:S(2)}) async-start(bf16[8,96,2560]{2,1,0:T(8,128)(2,1)} %convolution_convert_fusion.1), calls=%async_computation.1 | async-start | bytes 7864320 | tf_op jit(solution)/shard_map/all_to_all | solution.py:145
  135.7 6.7 %fusion.1 = f32[768,2,384]{2,0,1:T(8,128)S(1)} fusion(bf16[768,2560,1]{1,0,2:T(8,128)(2,1)} %bitcast.48, bf16[1,2560,2,384]{3,2,1,0:T(2,128)(2,1)} %get-tuple-element.6), kind=kOutput, calls=%fused_computation.13 | convolution fusion | flops 3019898880 | bytes 10223616 | tf_op jit(solution)/shard_map/md,dcf->mcf/dot_general | solution.py:147
  142.4 2.2 convolution_convert_fusion.2
  144.6 2.2 copy.143
  146.9 35.1 %all-to-all-done = bf16[8,96,2560]{2,1,0:T(8,128)(2,1)} async-done(((bf16[8,96,2560]{2,1,0:T(8,128)(2,1)}), bf16[8,96,2560]{2,1,0:T(8,128)(2,1)}, u32[]{:S(2)}, u32[]{:S(2)}) %all-to-all-start) | async-done | bytes 3932192 | tf_op jit(solution)/shard_map/all_to_all | solution.py:145
  182.0 6.7 %fusion.2 = f32[768,2,384]{2,0,1:T(8,128)S(1)} fusion(bf16[768,2560,1]{1,0,2:T(8,128)(2,1)} %bitcast.35, bf16[1,2560,2,384]{3,2,1,0:T(2,128)(2,1)} %get-tuple-element.5), kind=kOutput, calls=%fused_computation.15 | convolution fusion | flops 3019898880 | bytes 10223616 | tf_op jit(solution)/shard_map/md,dcf->mcf/dot_general | solution.py:147
  188.7 4.2 %convolution_convert_fusion.3 = bf16[768,2560]{1,0:T(8,128)(2,1)} fusion(bf16[2,384,2560]{2,1,0:T(8,128)(2,1)S(1)} %copy-done.15, f32[768,2,384]{2,0,1:T(8,128)S(1)} %fusion.2), kind=kOutput, calls=%fused_computation.8 | convolution fusion | flops 1513684992 | bytes 8257536 | tf_op jit(solution)/shard_map/dot_general | solution.py:151
  192.9 4.5 %all-to-all-start.1 = ((bf16[8,96,2560]{2,1,0:T(8,128)(2,1)}), bf16[8,96,2560]{2,1,0:T(8,128)(2,1)}, u32[]{:S(2)}, u32[]{:S(2)}) async-start(bf16[8,96,2560]{2,1,0:T(8,128)(2,1)} %bitcast.233), calls=%async_computation.2 | async-start | bytes 7864320 | tf_op jit(solution)/shard_map/all_to_all | solution.py:160
  198.3 1.7 fusion.20
  200.2 1.2 select_reduce_fusion
  201.3 2.4 reshape.267
  203.7 0.5 copy.138
  204.2 0.5 subtract_convert_fusion
  204.8 0.6 copy-done.3
  205.4 3.4 %fusion.5 = f32[192,2,384]{2,0,1:T(8,128)S(1)} fusion(bf16[2560,2,384]{2,1,0:T(2,128)(2,1)} %param.32, f32[192,2560]{1,0:T(8,128)S(1)} %bitcast.231, f32[2560]{0:T(1024)S(1)} %copy-done.12, f32[192]{0:T(256)S(1)} %add_rsqrt_fusion), kind=kOutput, calls=%fused_computation.21 | convolution fusion | flops 756449280 | bytes 6499072 | tf_op jit(solution)/shard_map/td,dcf->tcf/dot_general | solution.py:183
  208.8 34.9 %all-to-all-done.1 = bf16[8,96,2560]{2,1,0:T(8,128)(2,1)} async-done(((bf16[8,96,2560]{2,1,0:T(8,128)(2,1)}), bf16[8,96,2560]{2,1,0:T(8,128)(2,1)}, u32[]{:S(2)}, u32[]{:S(2)}) %all-to-all-start.1) | async-done | bytes 3932192 | tf_op jit(solution)/shard_map/all_to_all | solution.py:160
  243.7 4.1 %convolution_bitcast_fusion = f32[2,192,2560]{2,1,0:T(8,128)S(1)} fusion(bf16[8,96,2560]{2,1,0:T(8,128)(2,1)} %all-to-all-done.1, bf16[1,192,8,2,96]{4,1,2,0,3:T(8,128)(2,1)S(1)} %copy.138, bf16[1,192,8,2,96]{4,1,2,0,3:T(8,128)(2,1)S(1)} %subtract_convert_fusion), kind=kOutput, calls=%fused_computation.9 | convolution fusion | flops 1510244352 | bytes 9043968 | tf_op jit(solution)/shard_map/stgc,gcd->std/dot_general | solution.py:174
  247.8 0.7 fusion.7
  248.5 1.0 copy.144
  249.6 18.4 %all_to_all.20 = bf16[8,96,640]{2,1,0:T(8,128)(2,1)S(1)} all-to-all(bf16[8,96,640]{2,1,0:T(8,128)(2,1)} %bitcast.242), channel_id=1, replica_groups=mesh['req'=8,'tp'=4] {'req'}, dimensions={0} | all-to-all | bytes 1966080 | tf_op jit(solution)/shard_map/all_to_all | solution.py:160
  268.0 2.8 %convolution_bitcast_fusion.1 = f32[2,192,640]{2,1,0:T(8,128)} fusion(bf16[8,96,640]{2,1,0:T(8,128)(2,1)S(1)} %all_to_all.20, bf16[1,192,8,2,96]{4,1,2,0,3:T(8,128)(2,1)} %copy-done.5, bf16[1,192,8,2,96]{4,1,2,0,3:T(8,128)(2,1)} %copy-done.4), kind=kOutput, calls=%fused_computation.49 | convolution fusion | flops 377782272 | bytes 3145728 | tf_op jit(solution)/shard_map/stgc,gcd->std/dot_general | solution.py:174
  270.9 2.7 reduce-scatter.6.cloned.1.call-done
  273.5 2.0 fusion.51
  (78 shorter events, 4.7 us)
Async XLA Ops:
  6.5 15.7 %copy-start = (bf16[640,2560]{1,0:T(8,128)(2,1)S(1)}, bf16[640,2560]{1,0:T(8,128)(2,1)}, u32[]{:S(2)}) copy-start(bf16[640,2560]{1,0:T(8,128)(2,1)} %param.26) | copy-start | bytes 9830404
  6.5 7.7 %copy-start.9 = (bf16[192,640]{1,0:T(8,128)(2,1)S(1)}, bf16[192,640]{1,0:T(8,128)(2,1)}, u32[]{:S(2)}) copy-start(bf16[192,640]{1,0:T(8,128)(2,1)} %param.17) | copy-start | bytes 737284
  6.5 8.7 %copy-start.18 = (s32[4,48]{1,0:T(4,128)S(1)}, s32[4,48]{1,0:T(4,128)}, u32[]{:S(2)}) copy-start(s32[4,48]{1,0:T(4,128)} %param.24) | copy-start | bytes 2308
  6.5 46.7 %reduce-scatter.4.cloned.1.call-start = ((), (), s32[]{:S(2)}) async-start(), calls=%async_computation.7 | async-start | bytes 1228800 | tf_op jit(solution)/shard_map/reduce_scatter | solution.py:125
  15.3 3.7 %copy-start.13 = (bf16[192,128]{1,0:T(8,128)(2,1)S(1)}, bf16[192,128]{1,0:T(8,128)(2,1)}, u32[]{:S(2)}) copy-start(bf16[192,128]{1,0:T(8,128)(2,1)} %param.18) | copy-start | bytes 147460
  16.8 2.2 copy-start.6
  18.9 1.5 copy-start.8
  20.5 1.3 copy-start.17
  22.1 2.2 copy-start.11
  22.2 2.5 copy-start.12
  80.3 50.8 %all-to-all-start.2 = ((bf16[8,96,2560]{2,1,0:T(8,128)(2,1)}), bf16[8,96,2560]{2,1,0:T(8,128)(2,1)}, u32[]{:S(2)}, u32[]{:S(2)}) async-start(bf16[8,96,2560]{2,1,0:T(8,128)(2,1)} %convolution_convert_fusion), calls=%async_computation.4 | async-start | bytes 7864320 | tf_op jit(solution)/shard_map/all_to_all | solution.py:145
  85.0 8.2 %copy-start.7 = (pred[192,1536]{0,1:T(32,128)(4,1)S(1)}, pred[192,1536]{0,1:T(32,128)(4,1)}, u32[]{:S(2)}) copy-start(pred[192,1536]{0,1:T(32,128)(4,1)} %copy.91) | copy-start | bytes 884740
  131.1 50.9 %all-to-all-start = ((bf16[8,96,2560]{2,1,0:T(8,128)(2,1)}), bf16[8,96,2560]{2,1,0:T(8,128)(2,1)}, u32[]{:S(2)}, u32[]{:S(2)}) async-start(bf16[8,96,2560]{2,1,0:T(8,128)(2,1)} %convolution_convert_fusion.1), calls=%async_computation.1 | async-start | bytes 7864320 | tf_op jit(solution)/shard_map/all_to_all | solution.py:145
  135.7 113.9 %reduce-scatter.8.cloned.1.call-start = ((), (), s32[]{:S(2)}) async-start(), calls=%async_computation.9 | async-start | bytes 4915200 | tf_op jit(solution)/shard_map/reduce_scatter | solution.py:156
  135.7 6.7 %copy-start.14 = (bf16[2,384,2560]{2,1,0:T(8,128)(2,1)S(1)}, bf16[2,384,2560]{2,1,0:T(8,128)(2,1)}, u32[]{:S(2)}) copy-start(bf16[2,384,2560]{2,1,0:T(8,128)(2,1)} %param.31) | copy-start | bytes 11796484
  182.0 6.7 %copy-start.15 = (bf16[2,384,2560]{2,1,0:T(8,128)(2,1)S(1)}, bf16[2,384,2560]{2,1,0:T(8,128)(2,1)}, u32[]{:S(2)}) copy-start(bf16[2,384,2560]{2,1,0:T(8,128)(2,1)} %param.31) | copy-start | bytes 11796484
  192.9 50.8 %all-to-all-start.1 = ((bf16[8,96,2560]{2,1,0:T(8,128)(2,1)}), bf16[8,96,2560]{2,1,0:T(8,128)(2,1)}, u32[]{:S(2)}, u32[]{:S(2)}) async-start(bf16[8,96,2560]{2,1,0:T(8,128)(2,1)} %bitcast.233), calls=%async_computation.2 | async-start | bytes 7864320 | tf_op jit(solution)/shard_map/all_to_all | solution.py:160
  197.4 0.9 copy-start.10
  197.4 76.1 %reduce-scatter.6.cloned.1.call-start = ((), (), s32[]{:S(2)}) async-start(), calls=%async_computation.8 | async-start | bytes 1228800 | tf_op jit(solution)/shard_map/reduce_scatter | solution.py:189
  198.1 2.1 copy-start.2
  203.7 1.7 copy-start.3
  204.2 39.5 %copy-start.4 = (bf16[1,192,8,2,96]{4,1,2,0,3:T(8,128)(2,1)}, bf16[1,192,8,2,96]{4,1,2,0,3:T(8,128)(2,1)S(1)}, u32[]{:S(2)}) copy-start(bf16[1,192,8,2,96]{4,1,2,0,3:T(8,128)(2,1)S(1)} %copy.138) | copy-start | bytes 1769476
  205.4 42.4 %copy-start.5 = (bf16[1,192,8,2,96]{4,1,2,0,3:T(8,128)(2,1)}, bf16[1,192,8,2,96]{4,1,2,0,3:T(8,128)(2,1)S(1)}, u32[]{:S(2)}) copy-start(bf16[1,192,8,2,96]{4,1,2,0,3:T(8,128)(2,1)S(1)} %subtract_convert_fusion) | copy-start | bytes 1769476
  243.7 4.1 %copy-start.16 = (bf16[384,2560]{1,0:T(8,128)(2,1)S(1)}, bf16[384,2560]{1,0:T(8,128)(2,1)}, u32[]{:S(2)}) copy-start(bf16[384,2560]{1,0:T(8,128)(2,1)} %param.33) | copy-start | bytes 5898244
  249.6 26.0 %copy-start.1 = (bf16[640,2560]{1,0:T(8,128)(2,1)S(1)}, bf16[640,2560]{1,0:T(8,128)(2,1)}, u32[]{:S(2)}) copy-start(bf16[640,2560]{1,0:T(8,128)(2,1)} %param.26) | copy-start | bytes 9830404
Sparse Core Ops, SparseCore 0:
  24.4 28.8 reduce-scatter.3
  147.0 72.5 reduce-scatter.7
  249.7 23.7 reduce-scatter.5

commit v17 on v16

--- a/solution.py
+++ b/solution.py
@@ -122,9 +122,16 @@
     hit = slot[:, :, None] == slot_ids[None, None, :]
 
     attn_blocks = attn_terms.astype(jnp.bfloat16).reshape(row_count, tp_count, part_width)
-    attn_part = lax.psum_scatter(
-        attn_blocks.transpose(1, 0, 2), "tp", scatter_dimension=0, tiled=True
+    attn_blocks = attn_blocks.transpose(1, 0, 2)
+    split_rows = row_count // 2
+    attn_first = lax.psum_scatter(
+        attn_blocks[:, :split_rows], "tp", scatter_dimension=0, tiled=True
     )[0].astype(jnp.float32)
+    attn_second = lax.all_to_all(
+        attn_blocks[:, split_rows:], "tp", split_axis=0, concat_axis=0, tiled=True
+    )
+    attn_second = jnp.sum(attn_second.astype(jnp.float32), axis=0)
+    attn_part = jnp.concatenate([attn_first, attn_second], axis=0)
     residual_part = lax.dynamic_slice_in_dim(residual, column, part_width, 1)
     hidden_part_bf = (residual_part.astype(jnp.float32) + attn_part).astype(jnp.bfloat16)
     hidden_bf = lax.all_gather(hidden_part_bf[None], "tp", axis=0, tiled=True)

time: 283 us -> 286 us (1.011)
  starting transfers between devices: 14 us -> 20.4 us
  waiting for transfers between devices: 128 us -> 125 us
    reduce_scatter x1, waiting for transfers between devices: 20.6 us -> 11.3 us  [shards(): lax.psum_scatter(attn_blocks[:, :split_rows], 'tp', scatter_dimension=0,...]
    all_to_all x0 -> x1, starting transfers between devices: none -> 6.31 us  [shards(): lax.all_to_all(attn_blocks[:, split_rows:], 'tp', split_axis=0, concat_ax...]
    all_to_all x0 -> x1, waiting for transfers between devices: none -> 5.08 us  [shards(): lax.all_to_all(attn_blocks[:, split_rows:], 'tp', split_axis=0, concat_ax...]
  transfers between devices with their start and end apart: 6 -> 7, of which waited for: 5 -> 6; matrix products, arithmetic and copies ran while one was open for 21% -> 21% of each run, Pallas kernels for 0% -> 0%
where the time goes in v17:
time: 286 us
  waiting for transfers between devices  125 us (44%)
  matrix products  46 us (16%)
  blocking collectives  38.1 us (13%)
  local copies, waits for them, and re-layouts  27.2 us (10%)
  starting transfers between devices  20.4 us (7%)
  other arithmetic  15.4 us (5%)
  between operations  13.7 us (5%)
    all_to_all x2, waiting for transfers between devices, shards(): lax.all_to_all(outbox, 'req', split_axis=0, concat_axis=0, tiled=True)  70 us
    all_to_all x1, waiting for transfers between devices, shards(): lax.all_to_all(outputs, 'req', split_axis=0, concat_axis=0, tiled=True)  34.9 us
    all_gather x1, blocking collectives, shards(): hidden_bf = lax.all_gather(hidden_part_bf[None], 'tp', axis=0, tiled=True)  19.7 us
    all_to_all x1, blocking collectives, shards(): lax.all_to_all(outputs, 'req', split_axis=0, concat_axis=0, tiled=True)  18.4 us
    dot_general x2, matrix products, shards(): jnp.einsum('md,dcf->mcf', rows, expert_gate_up[expert], preferred_element...  13.3 us
    reduce_scatter x1, waiting for transfers between devices, shards(): lax.psum_scatter(attn_blocks[:, :split_rows], 'tp', scatter_dimension=0,...  11.3 us
    all_to_all x2, starting transfers between devices, shards(): lax.all_to_all(outbox, 'req', split_axis=0, concat_axis=0, tiled=True)  9.22 us
    slice x1, local copies, waits for them, and re-layouts, shards(): expert_gate_up[expert]  8.16 us
  transfers between devices with their start and end apart: 7, of which 6 were waited for; matrix products, arithmetic and copies ran while one was open for 21% of the time, Pallas kernels for 0%

profile of v17, /device:TPU:0, one launch (start us, length us, event | category | flops | bytes accessed | tf_op | source)
XLA Modules:
  0.0 285.5 jit_solution(12252515845098473383)
XLA Ops:
  6.6 0.8 compare_select_fusion
  7.5 0.9 iota_compare_fusion.6
  8.4 2.9 %gather_fusion = bf16[64,64,128]{2,1,0:T(8,128)(2,1)} fusion(bf16[64,64,128]{2,1,0:T(8,128)(2,1)} %param.21, s32[1024]{0:T(1024)S(1)} %pad_clamp_fusion), kind=kCustom, calls=%fused_computation | custom fusion | bytes 2097408 | tf_op jit(solution)/shard_map/gather | solution.py:94
  11.3 2.9 %gather_fusion.1 = bf16[64,64,128]{2,1,0:T(8,128)(2,1)} fusion(bf16[64,64,128]{2,1,0:T(8,128)(2,1)} %param.20, s32[1024]{0:T(1024)S(1)} %pad_clamp_fusion), kind=kCustom, calls=%fused_computation.1 | custom fusion | bytes 2097408 | tf_op jit(solution)/shard_map/gather | solution.py:93
  14.2 1.0 reshape.260
  16.8 2.1 bitcast_reduce_fusion
  19.4 1.0 fusion.8
  20.5 1.3 fusion.15
  22.2 0.9 convolution_convert_fusion.4
  23.3 1.0 fusion.81
  24.3 6.3 %all-to-all-start = ((bf16[4,96,640]{2,1,0:T(8,128)(2,1)}), bf16[4,96,640]{2,1,0:T(8,128)(2,1)S(1)}, u32[]{:S(2)}, u32[]{:S(2)}) async-start(bf16[4,96,640]{2,1,0:T(8,128)(2,1)} %get-tuple-element.8), calls=%async_computation.1 | async-start | bytes 983040 | tf_op jit(solution)/shard_map/all_to_all | solution.py:130
  30.6 0.7 reduce-scatter.4.cloned.1.call-update
  31.8 4.5 %reduce-window.6 = s32[16,9,128]{2,1,0:T(8,128)S(1)} reduce-window(s32[16,9,128]{2,1,0:T(8,128)S(1)} %fusion.65, s32[]{:T(128)} %constant.17.clone.1), window={size=1x1x128 pad=0_0x0_0x127_0}, to_apply=%region_7.8 | reduce-window | flops 2340864 | bytes 147460 | tf_op jit(solution)/shard_map/reduce-window
  37.3 1.2 fusion
  38.5 1.2 copy.91
  39.7 5.1 %all-to-all-done = bf16[4,96,640]{2,1,0:T(8,128)(2,1)S(1)} async-done(((bf16[4,96,640]{2,1,0:T(8,128)(2,1)}), bf16[4,96,640]{2,1,0:T(8,128)(2,1)S(1)}, u32[]{:S(2)}, u32[]{:S(2)}) %all-to-all-start) | async-done | bytes 491552 | tf_op jit(solution)/shard_map/all_to_all | solution.py:130
  44.9 11.3 %reduce-scatter.4.cloned.1.call-done = bf16[1,96,640]{2,1,0:T(8,128)(2,1)} async-done(((bf16[4,96,640]{2,1,0:T(8,128)(2,1)}), bf16[1,96,640]{2,1,0:T(8,128)(2,1)}) %reduce-scatter.4.cloned.1.call-update) | async-done | bytes 122896 | tf_op jit(solution)/shard_map/reduce_scatter | solution.py:127
  56.2 0.9 bitcast_convert_fusion
  57.2 1.0 fusion.52
  58.1 19.7 %all-gather = bf16[768,640]{1,0:T(8,128)(2,1)S(1)} all-gather(bf16[192,640]{1,0:T(8,128)(2,1)S(1)} %fusion.52), channel_id=2, replica_groups=mesh['req'=8,'tp'=4] {'tp'}, dimensions={0}, use_global_device_ids=true | all-gather | bytes 1228800 | tf_op jit(solution)/shard_map/all_gather | solution.py:137
  78.5 0.8 copy.93
  79.6 4.0 %convolution_convert_fusion = bf16[8,96,2560]{2,1,0:T(8,128)(2,1)} fusion(bf16[192,2560,1]{1,0,2:T(8,128)(2,1)S(1)} %reshape.307, pred[192,8,2,96]{0,3,2,1:T(32,128)(4,1)} %bitcast.238), kind=kOutput, calls=%fused_computation.5 | convolution fusion | flops 756940800 | bytes 5111808 | tf_op jit(solution)/shard_map/tgc,td->gcd/dot_general | solution.py:149
  83.7 4.7 %all-to-all-start.3 = ((bf16[8,96,2560]{2,1,0:T(8,128)(2,1)}), bf16[8,96,2560]{2,1,0:T(8,128)(2,1)}, u32[]{:S(2)}, u32[]{:S(2)}) async-start(bf16[8,96,2560]{2,1,0:T(8,128)(2,1)} %convolution_convert_fusion), calls=%async_computation.5 | async-start | bytes 7864320 | tf_op jit(solution)/shard_map/all_to_all | solution.py:152
  88.4 8.2 %fusion.80 = (bf16[1,2560,2,384]{3,2,1,0:T(2,128)(2,1)}, bf16[1,2560,2,384]{3,2,1,0:T(2,128)(2,1)}) fusion(bf16[2,2560,2,384]{3,2,1,0:T(2,128)(2,1)} %param.30), kind=kLoop, calls=%fused_computation.141 | loop fusion | bytes 15728640 | tf_op jit(solution)/shard_map/slice | solution.py:155
  96.5 3.1 %convolution_convert_fusion.1 = bf16[8,96,2560]{2,1,0:T(8,128)(2,1)} fusion(bf16[192,2560,1]{1,0,2:T(8,128)(2,1)S(1)} %reshape.307, pred[192,8,2,96]{0,3,2,1:T(32,128)(4,1)S(1)} %bitcast.239), kind=kOutput, calls=%fused_computation.6 | convolution fusion | flops 756940800 | bytes 5111808 | tf_op jit(solution)/shard_map/tgc,td->gcd/dot_general | solution.py:149
  99.6 34.9 %all-to-all-done.3 = bf16[8,96,2560]{2,1,0:T(8,128)(2,1)} async-done(((bf16[8,96,2560]{2,1,0:T(8,128)(2,1)}), bf16[8,96,2560]{2,1,0:T(8,128)(2,1)}, u32[]{:S(2)}, u32[]{:S(2)}) %all-to-all-start.3) | async-done | bytes 3932192 | tf_op jit(solution)/shard_map/all_to_all | solution.py:152
  134.5 4.5 %all-to-all-start.1 = ((bf16[8,96,2560]{2,1,0:T(8,128)(2,1)}), bf16[8,96,2560]{2,1,0:T(8,128)(2,1)}, u32[]{:S(2)}, u32[]{:S(2)}) async-start(bf16[8,96,2560]{2,1,0:T(8,128)(2,1)} %convolution_convert_fusion.1), calls=%async_computation.2 | async-start | bytes 7864320 | tf_op jit(solution)/shard_map/all_to_all | solution.py:152
  139.1 6.7 %fusion.1 = f32[768,2,384]{2,0,1:T(8,128)S(1)} fusion(bf16[768,2560,1]{1,0,2:T(8,128)(2,1)} %bitcast.48, bf16[1,2560,2,384]{3,2,1,0:T(2,128)(2,1)} %get-tuple-element.6), kind=kOutput, calls=%fused_computation.13 | convolution fusion | flops 3019898880 | bytes 10223616 | tf_op jit(solution)/shard_map/md,dcf->mcf/dot_general | solution.py:154
  145.8 2.2 convolution_convert_fusion.2
  148.0 2.2 copy.143
  150.2 35.1 %all-to-all-done.1 = bf16[8,96,2560]{2,1,0:T(8,128)(2,1)} async-done(((bf16[8,96,2560]{2,1,0:T(8,128)(2,1)}), bf16[8,96,2560]{2,1,0:T(8,128)(2,1)}, u32[]{:S(2)}, u32[]{:S(2)}) %all-to-all-start.1) | async-done | bytes 3932192 | tf_op jit(solution)/shard_map/all_to_all | solution.py:152
  185.3 6.7 %fusion.2 = f32[768,2,384]{2,0,1:T(8,128)S(1)} fusion(bf16[768,2560,1]{1,0,2:T(8,128)(2,1)} %bitcast.35, bf16[1,2560,2,384]{3,2,1,0:T(2,128)(2,1)} %get-tuple-element.5), kind=kOutput, calls=%fused_computation.15 | convolution fusion | flops 3019898880 | bytes 10223616 | tf_op jit(solution)/shard_map/md,dcf->mcf/dot_general | solution.py:154
  192.0 4.2 %convolution_convert_fusion.3 = bf16[768,2560]{1,0:T(8,128)(2,1)} fusion(bf16[2,384,2560]{2,1,0:T(8,128)(2,1)S(1)} %copy-done.15, f32[768,2,384]{2,0,1:T(8,128)S(1)} %fusion.2), kind=kOutput, calls=%fused_computation.8 | convolution fusion | flops 1513684992 | bytes 8257536 | tf_op jit(solution)/shard_map/dot_general | solution.py:158
  196.2 4.5 %all-to-all-start.2 = ((bf16[8,96,2560]{2,1,0:T(8,128)(2,1)}), bf16[8,96,2560]{2,1,0:T(8,128)(2,1)}, u32[]{:S(2)}, u32[]{:S(2)}) async-start(bf16[8,96,2560]{2,1,0:T(8,128)(2,1)} %bitcast.233), calls=%async_computation.3 | async-start | bytes 7864320 | tf_op jit(solution)/shard_map/all_to_all | solution.py:167
  201.7 1.7 fusion.20
  203.5 1.2 select_reduce_fusion
  204.7 2.4 reshape.267
  207.6 0.5 subtract_convert_fusion
  208.1 0.6 copy-done.3
  208.7 3.4 %fusion.5 = f32[192,2,384]{2,0,1:T(8,128)S(1)} fusion(bf16[2560,2,384]{2,1,0:T(2,128)(2,1)} %param.32, f32[192,2560]{1,0:T(8,128)S(1)} %bitcast.231, f32[2560]{0:T(1024)S(1)} %copy-done.12, f32[192]{0:T(256)S(1)} %add_rsqrt_fusion), kind=kOutput, calls=%fused_computation.21 | convolution fusion | flops 756449280 | bytes 6499072 | tf_op jit(solution)/shard_map/td,dcf->tcf/dot_general | solution.py:190
  212.2 34.9 %all-to-all-done.2 = bf16[8,96,2560]{2,1,0:T(8,128)(2,1)} async-done(((bf16[8,96,2560]{2,1,0:T(8,128)(2,1)}), bf16[8,96,2560]{2,1,0:T(8,128)(2,1)}, u32[]{:S(2)}, u32[]{:S(2)}) %all-to-all-start.2) | async-done | bytes 3932192 | tf_op jit(solution)/shard_map/all_to_all | solution.py:167
  247.1 4.1 %convolution_bitcast_fusion = f32[2,192,2560]{2,1,0:T(8,128)S(1)} fusion(bf16[8,96,2560]{2,1,0:T(8,128)(2,1)} %all-to-all-done.2, bf16[1,192,8,2,96]{4,1,2,0,3:T(8,128)(2,1)S(1)} %copy.138, bf16[1,192,8,2,96]{4,1,2,0,3:T(8,128)(2,1)S(1)} %subtract_convert_fusion), kind=kOutput, calls=%fused_computation.9 | convolution fusion | flops 1510244352 | bytes 9043968 | tf_op jit(solution)/shard_map/stgc,gcd->std/dot_general | solution.py:181
  251.2 0.7 fusion.7
  251.9 1.0 copy.144
  253.0 18.4 %all_to_all.25 = bf16[8,96,640]{2,1,0:T(8,128)(2,1)S(1)} all-to-all(bf16[8,96,640]{2,1,0:T(8,128)(2,1)} %bitcast.242), channel_id=1, replica_groups=mesh['req'=8,'tp'=4] {'req'}, dimensions={0} | all-to-all | bytes 1966080 | tf_op jit(solution)/shard_map/all_to_all | solution.py:167
  271.4 2.8 convolution_bitcast_fusion.1
  274.2 2.8 reduce-scatter.6.cloned.1.call-done
  277.0 2.0 fusion.51
  (83 shorter events, 6.6 us)
Async XLA Ops:
  6.5 15.7 %copy-start = (bf16[640,2560]{1,0:T(8,128)(2,1)S(1)}, bf16[640,2560]{1,0:T(8,128)(2,1)}, u32[]{:S(2)}) copy-start(bf16[640,2560]{1,0:T(8,128)(2,1)} %param.26) | copy-start | bytes 9830404
  6.5 7.7 %copy-start.9 = (bf16[192,640]{1,0:T(8,128)(2,1)S(1)}, bf16[192,640]{1,0:T(8,128)(2,1)}, u32[]{:S(2)}) copy-start(bf16[192,640]{1,0:T(8,128)(2,1)} %param.17) | copy-start | bytes 737284
  6.5 8.7 %copy-start.18 = (s32[4,48]{1,0:T(4,128)S(1)}, s32[4,48]{1,0:T(4,128)}, u32[]{:S(2)}) copy-start(s32[4,48]{1,0:T(4,128)} %param.24) | copy-start | bytes 2308
  15.3 3.7 %copy-start.13 = (bf16[192,128]{1,0:T(8,128)(2,1)S(1)}, bf16[192,128]{1,0:T(8,128)(2,1)}, u32[]{:S(2)}) copy-start(bf16[192,128]{1,0:T(8,128)(2,1)} %param.18) | copy-start | bytes 147460
  16.8 2.2 copy-start.6
  18.9 1.5 copy-start.8
  20.5 1.3 copy-start.17
  22.2 9.1 %copy-start.11 = (s32[192,6]{0,1:T(8,128)S(1)}, s32[192,6]{0,1:T(8,128)}, u32[]{:S(2)}) copy-start(s32[192,6]{0,1:T(8,128)} %param.29) | copy-start | bytes 13828
  23.1 8.6 %copy-start.12 = (f32[2560]{0:T(1024)S(1)}, f32[2560]{0:T(1024)}, u32[]{:S(2)}) copy-start(f32[2560]{0:T(1024)} %param.27) | copy-start | bytes 30724
  24.3 20.5 %all-to-all-start = ((bf16[4,96,640]{2,1,0:T(8,128)(2,1)}), bf16[4,96,640]{2,1,0:T(8,128)(2,1)S(1)}, u32[]{:S(2)}, u32[]{:S(2)}) async-start(bf16[4,96,640]{2,1,0:T(8,128)(2,1)} %get-tuple-element.8), calls=%async_computation.1 | async-start | bytes 983040 | tf_op jit(solution)/shard_map/all_to_all | solution.py:130
  30.6 25.6 %reduce-scatter.4.cloned.1.call-start = ((), (), s32[]{:S(2)}) async-start(), calls=%async_computation.8 | async-start | bytes 614400 | tf_op jit(solution)/shard_map/reduce_scatter | solution.py:127
  83.7 50.8 %all-to-all-start.3 = ((bf16[8,96,2560]{2,1,0:T(8,128)(2,1)}), bf16[8,96,2560]{2,1,0:T(8,128)(2,1)}, u32[]{:S(2)}, u32[]{:S(2)}) async-start(bf16[8,96,2560]{2,1,0:T(8,128)(2,1)} %convolution_convert_fusion), calls=%async_computation.5 | async-start | bytes 7864320 | tf_op jit(solution)/shard_map/all_to_all | solution.py:152
  88.4 8.2 %copy-start.7 = (pred[192,1536]{0,1:T(32,128)(4,1)S(1)}, pred[192,1536]{0,1:T(32,128)(4,1)}, u32[]{:S(2)}) copy-start(pred[192,1536]{0,1:T(32,128)(4,1)} %copy.91) | copy-start | bytes 884740
  134.5 50.9 %all-to-all-start.1 = ((bf16[8,96,2560]{2,1,0:T(8,128)(2,1)}), bf16[8,96,2560]{2,1,0:T(8,128)(2,1)}, u32[]{:S(2)}, u32[]{:S(2)}) async-start(bf16[8,96,2560]{2,1,0:T(8,128)(2,1)} %convolution_convert_fusion.1), calls=%async_computation.2 | async-start | bytes 7864320 | tf_op jit(solution)/shard_map/all_to_all | solution.py:152
  139.0 113.9 %reduce-scatter.8.cloned.1.call-start = ((), (), s32[]{:S(2)}) async-start(), calls=%async_computation.10 | async-start | bytes 4915200 | tf_op jit(solution)/shard_map/reduce_scatter | solution.py:163
  139.1 6.7 %copy-start.14 = (bf16[2,384,2560]{2,1,0:T(8,128)(2,1)S(1)}, bf16[2,384,2560]{2,1,0:T(8,128)(2,1)}, u32[]{:S(2)}) copy-start(bf16[2,384,2560]{2,1,0:T(8,128)(2,1)} %param.31) | copy-start | bytes 11796484
  185.3 6.7 %copy-start.15 = (bf16[2,384,2560]{2,1,0:T(8,128)(2,1)S(1)}, bf16[2,384,2560]{2,1,0:T(8,128)(2,1)}, u32[]{:S(2)}) copy-start(bf16[2,384,2560]{2,1,0:T(8,128)(2,1)} %param.31) | copy-start | bytes 11796484
  196.2 50.8 %all-to-all-start.2 = ((bf16[8,96,2560]{2,1,0:T(8,128)(2,1)}), bf16[8,96,2560]{2,1,0:T(8,128)(2,1)}, u32[]{:S(2)}, u32[]{:S(2)}) async-start(bf16[8,96,2560]{2,1,0:T(8,128)(2,1)} %bitcast.233), calls=%async_computation.3 | async-start | bytes 7864320 | tf_op jit(solution)/shard_map/all_to_all | solution.py:167
  200.8 0.9 copy-start.10
  200.8 76.2 %reduce-scatter.6.cloned.1.call-start = ((), (), s32[]{:S(2)}) async-start(), calls=%async_computation.9 | async-start | bytes 1228800 | tf_op jit(solution)/shard_map/reduce_scatter | solution.py:196
  201.4 2.1 copy-start.2
  207.0 1.7 copy-start.3
  207.6 39.5 %copy-start.4 = (bf16[1,192,8,2,96]{4,1,2,0,3:T(8,128)(2,1)}, bf16[1,192,8,2,96]{4,1,2,0,3:T(8,128)(2,1)S(1)}, u32[]{:S(2)}) copy-start(bf16[1,192,8,2,96]{4,1,2,0,3:T(8,128)(2,1)S(1)} %copy.138) | copy-start | bytes 1769476
  208.7 42.4 %copy-start.5 = (bf16[1,192,8,2,96]{4,1,2,0,3:T(8,128)(2,1)}, bf16[1,192,8,2,96]{4,1,2,0,3:T(8,128)(2,1)S(1)}, u32[]{:S(2)}) copy-start(bf16[1,192,8,2,96]{4,1,2,0,3:T(8,128)(2,1)S(1)} %subtract_convert_fusion) | copy-start | bytes 1769476
  247.1 4.1 %copy-start.16 = (bf16[384,2560]{1,0:T(8,128)(2,1)S(1)}, bf16[384,2560]{1,0:T(8,128)(2,1)}, u32[]{:S(2)}) copy-start(bf16[384,2560]{1,0:T(8,128)(2,1)} %param.33) | copy-start | bytes 5898244
  252.9 26.1 %copy-start.1 = (bf16[640,2560]{1,0:T(8,128)(2,1)S(1)}, bf16[640,2560]{1,0:T(8,128)(2,1)}, u32[]{:S(2)}) copy-start(bf16[640,2560]{1,0:T(8,128)(2,1)} %param.26) | copy-start | bytes 9830404
Sparse Core Ops, SparseCore 0:
  33.7 22.4 reduce-scatter.3
  150.4 72.6 reduce-scatter.7
  253.1 23.8 reduce-scatter.5

commit v18 on v16

--- a/solution.py
+++ b/solution.py
@@ -135,12 +135,12 @@
     normed_bf = normed.astype(jnp.bfloat16)
     hidden_part = hidden_part_bf.astype(jnp.float32)
 
-    dispatch = jnp.any(hit, axis=1).astype(jnp.bfloat16)
-    dispatch = dispatch.reshape(row_count, groups, experts_local, capacity)
+    dispatch = jnp.any(slot_ids[:, None, None] == slot[None, :, :], axis=2).astype(jnp.bfloat16)
+    dispatch = dispatch.reshape(groups, experts_local, capacity, row_count)
     returns = []
     for expert in range(experts_local):
         outbox = jnp.einsum(
-            "tgc,td->gcd", dispatch[:, :, expert], normed_bf, preferred_element_type=jnp.float32
+            "gct,td->gcd", dispatch[:, expert], normed_bf, preferred_element_type=jnp.float32
         ).astype(jnp.bfloat16)
         arrived = lax.all_to_all(outbox, "req", split_axis=0, concat_axis=0, tiled=True)
         rows = arrived.reshape(groups * capacity, model_width)

time: 283 us -> 283 us (level)
  no operation moved by 1% of the time
where the time goes in v18:
time: 283 us; the launch traced here: 282 us
  waiting for transfers between devices  128 us (45%)
  matrix products  46 us (16%)
  blocking collectives  38.6 us (14%)
  local copies, waits for them, and re-layouts  27.1 us (10%)
  other arithmetic  14.5 us (5%)
  starting transfers between devices  14 us (5%)
  between operations  13.7 us (5%)
    all_to_all x2, waiting for transfers between devices, shards(): lax.all_to_all(outbox, 'req', split_axis=0, concat_axis=0, tiled=True)  70 us
    all_to_all x1, waiting for transfers between devices, shards(): lax.all_to_all(outputs, 'req', split_axis=0, concat_axis=0, tiled=True)  34.9 us
    reduce_scatter x1, waiting for transfers between devices, shards(): lax.psum_scatter(attn_blocks.transpose(1, 0, 2), 'tp', scatter_dimension=...  20.6 us
    all_gather x1, blocking collectives, shards(): hidden_bf = lax.all_gather(hidden_part_bf[None], 'tp', axis=0, tiled=True)  20.2 us
    all_to_all x1, blocking collectives, shards(): lax.all_to_all(outputs, 'req', split_axis=0, concat_axis=0, tiled=True)  18.4 us
    dot_general x2, matrix products, shards(): jnp.einsum('md,dcf->mcf', rows, expert_gate_up[expert], preferred_element...  13.3 us
    all_to_all x2, starting transfers between devices, shards(): lax.all_to_all(outbox, 'req', split_axis=0, concat_axis=0, tiled=True)  9.22 us
    slice x1, local copies, waits for them, and re-layouts, shards(): expert_gate_up[expert]  8.16 us
  transfers between devices with their start and end apart: 6, of which 5 were waited for; matrix products, arithmetic and copies ran while one was open for 21% of the time, Pallas kernels for 0%

profile of v18, /device:TPU:0, one launch (start us, length us, event | category | flops | bytes accessed | tf_op | source)
XLA Modules:
  0.0 282.1 jit_solution(14873253255540877749)
XLA Ops:
  6.6 0.8 compare_select_fusion
  7.5 0.9 iota_compare_fusion.7
  8.4 2.9 %gather_fusion = bf16[64,64,128]{2,1,0:T(8,128)(2,1)} fusion(bf16[64,64,128]{2,1,0:T(8,128)(2,1)} %param.21, s32[1024]{0:T(1024)S(1)} %pad_clamp_fusion), kind=kCustom, calls=%fused_computation | custom fusion | bytes 2097408 | tf_op jit(solution)/shard_map/gather | solution.py:94
  11.3 2.9 %gather_fusion.1 = bf16[64,64,128]{2,1,0:T(8,128)(2,1)} fusion(bf16[64,64,128]{2,1,0:T(8,128)(2,1)} %param.20, s32[1024]{0:T(1024)S(1)} %pad_clamp_fusion), kind=kCustom, calls=%fused_computation.1 | custom fusion | bytes 2097408 | tf_op jit(solution)/shard_map/gather | solution.py:93
  14.2 1.0 reshape.266
  16.8 2.1 bitcast_reduce_fusion
  19.0 0.4 fusion.81
  19.4 1.0 fusion.8
  20.5 1.3 fusion.15
  22.2 0.9 convolution_convert_fusion.4
  23.2 1.0 copy.147
  24.7 4.5 %reduce-window.6 = s32[16,9,128]{2,1,0:T(8,128)S(1)} reduce-window(s32[16,9,128]{2,1,0:T(8,128)S(1)} %fusion.65, s32[]{:T(128)} %constant.17.clone.1), window={size=1x1x128 pad=0_0x0_0x127_0}, to_apply=%region_6.7 | reduce-window | flops 2340864 | bytes 147460 | tf_op jit(solution)/shard_map/reduce-window
  29.2 0.4 slice_reduce_fusion
  30.2 1.2 fusion
  31.4 1.2 copy.93
  32.6 20.6 %reduce-scatter.4.cloned.1.call-done = bf16[1,192,640]{2,1,0:T(8,128)(2,1)} async-done(((bf16[4,192,640]{2,1,0:T(8,128)(2,1)}), bf16[1,192,640]{2,1,0:T(8,128)(2,1)}) %reduce-scatter.4.cloned.1.call-update) | async-done | bytes 245776 | tf_op jit(solution)/shard_map/reduce_scatter | solution.py:125
  53.2 1.1 fusion.52
  54.3 20.2 %all-gather = bf16[768,640]{1,0:T(8,128)(2,1)S(1)} all-gather(bf16[192,640]{1,0:T(8,128)(2,1)S(1)} %fusion.52), channel_id=2, replica_groups=mesh['req'=8,'tp'=4] {'tp'}, dimensions={0}, use_global_device_ids=true | all-gather | bytes 1228800 | tf_op jit(solution)/shard_map/all_gather | solution.py:130
  75.1 0.8 copy.95
  75.9 0.4 reshape.313
  76.3 4.0 %convolution_convert_fusion = bf16[8,96,2560]{2,1,0:T(8,128)(2,1)} fusion(bf16[192,2560,1]{1,0,2:T(8,128)(2,1)S(1)} %reshape.313, pred[8,2,96,192]{3,2,1,0:T(32,128)(4,1)} %bitcast.238), kind=kOutput, calls=%fused_computation.6 | convolution fusion | flops 756940800 | bytes 5111808 | tf_op jit(solution)/shard_map/gct,td->gcd/dot_general | solution.py:142
  80.3 4.7 %all-to-all-start.2 = ((bf16[8,96,2560]{2,1,0:T(8,128)(2,1)}), bf16[8,96,2560]{2,1,0:T(8,128)(2,1)}, u32[]{:S(2)}, u32[]{:S(2)}) async-start(bf16[8,96,2560]{2,1,0:T(8,128)(2,1)} %convolution_convert_fusion), calls=%async_computation.4 | async-start | bytes 7864320 | tf_op jit(solution)/shard_map/all_to_all | solution.py:145
  85.0 8.2 %fusion.80 = (bf16[1,2560,2,384]{3,2,1,0:T(2,128)(2,1)}, bf16[1,2560,2,384]{3,2,1,0:T(2,128)(2,1)}) fusion(bf16[2,2560,2,384]{3,2,1,0:T(2,128)(2,1)} %param.30), kind=kLoop, calls=%fused_computation.140 | loop fusion | bytes 15728640 | tf_op jit(solution)/shard_map/slice | solution.py:148
  93.2 3.1 %convolution_convert_fusion.1 = bf16[8,96,2560]{2,1,0:T(8,128)(2,1)} fusion(bf16[192,2560,1]{1,0,2:T(8,128)(2,1)S(1)} %reshape.313, pred[8,2,96,192]{3,2,1,0:T(32,128)(4,1)S(1)} %bitcast.239), kind=kOutput, calls=%fused_computation.7 | convolution fusion | flops 756940800 | bytes 5111808 | tf_op jit(solution)/shard_map/gct,td->gcd/dot_general | solution.py:142
  96.3 34.9 %all-to-all-done.2 = bf16[8,96,2560]{2,1,0:T(8,128)(2,1)} async-done(((bf16[8,96,2560]{2,1,0:T(8,128)(2,1)}), bf16[8,96,2560]{2,1,0:T(8,128)(2,1)}, u32[]{:S(2)}, u32[]{:S(2)}) %all-to-all-start.2) | async-done | bytes 3932192 | tf_op jit(solution)/shard_map/all_to_all | solution.py:145
  131.1 4.5 %all-to-all-start = ((bf16[8,96,2560]{2,1,0:T(8,128)(2,1)}), bf16[8,96,2560]{2,1,0:T(8,128)(2,1)}, u32[]{:S(2)}, u32[]{:S(2)}) async-start(bf16[8,96,2560]{2,1,0:T(8,128)(2,1)} %convolution_convert_fusion.1), calls=%async_computation.1 | async-start | bytes 7864320 | tf_op jit(solution)/shard_map/all_to_all | solution.py:145
  135.7 6.7 %fusion.1 = f32[768,2,384]{2,0,1:T(8,128)S(1)} fusion(bf16[768,2560,1]{1,0,2:T(8,128)(2,1)} %bitcast.48, bf16[1,2560,2,384]{3,2,1,0:T(2,128)(2,1)} %get-tuple-element.6), kind=kOutput, calls=%fused_computation.14 | convolution fusion | flops 3019898880 | bytes 10223616 | tf_op jit(solution)/shard_map/md,dcf->mcf/dot_general | solution.py:147
  142.4 2.2 convolution_convert_fusion.2
  144.6 2.2 copy.145
  146.9 35.1 %all-to-all-done = bf16[8,96,2560]{2,1,0:T(8,128)(2,1)} async-done(((bf16[8,96,2560]{2,1,0:T(8,128)(2,1)}), bf16[8,96,2560]{2,1,0:T(8,128)(2,1)}, u32[]{:S(2)}, u32[]{:S(2)}) %all-to-all-start) | async-done | bytes 3932192 | tf_op jit(solution)/shard_map/all_to_all | solution.py:145
  182.0 6.7 %fusion.2 = f32[768,2,384]{2,0,1:T(8,128)S(1)} fusion(bf16[768,2560,1]{1,0,2:T(8,128)(2,1)} %bitcast.35, bf16[1,2560,2,384]{3,2,1,0:T(2,128)(2,1)} %get-tuple-element.5), kind=kOutput, calls=%fused_computation.16 | convolution fusion | flops 3019898880 | bytes 10223616 | tf_op jit(solution)/shard_map/md,dcf->mcf/dot_general | solution.py:147
  188.7 4.2 %convolution_convert_fusion.3 = bf16[768,2560]{1,0:T(8,128)(2,1)} fusion(bf16[2,384,2560]{2,1,0:T(8,128)(2,1)S(1)} %copy-done.15, f32[768,2,384]{2,0,1:T(8,128)S(1)} %fusion.2), kind=kOutput, calls=%fused_computation.9 | convolution fusion | flops 1513684992 | bytes 8257536 | tf_op jit(solution)/shard_map/dot_general | solution.py:151
  192.9 4.5 %all-to-all-start.1 = ((bf16[8,96,2560]{2,1,0:T(8,128)(2,1)}), bf16[8,96,2560]{2,1,0:T(8,128)(2,1)}, u32[]{:S(2)}, u32[]{:S(2)}) async-start(bf16[8,96,2560]{2,1,0:T(8,128)(2,1)} %bitcast.233), calls=%async_computation.2 | async-start | bytes 7864320 | tf_op jit(solution)/shard_map/all_to_all | solution.py:160
  198.3 1.7 fusion.20
  200.2 1.2 select_reduce_fusion
  201.3 2.4 reshape.273
  203.7 0.5 copy.140
  204.2 0.5 subtract_convert_fusion
  204.8 0.6 copy-done.3
  205.4 3.4 %fusion.5 = f32[192,2,384]{2,0,1:T(8,128)S(1)} fusion(bf16[2560,2,384]{2,1,0:T(2,128)(2,1)} %param.32, f32[192,2560]{1,0:T(8,128)S(1)} %bitcast.231, f32[2560]{0:T(1024)S(1)} %copy-done.12, f32[192]{0:T(256)S(1)} %add_rsqrt_fusion), kind=kOutput, calls=%fused_computation.22 | convolution fusion | flops 756449280 | bytes 6499072 | tf_op jit(solution)/shard_map/td,dcf->tcf/dot_general | solution.py:183
  208.8 34.9 %all-to-all-done.1 = bf16[8,96,2560]{2,1,0:T(8,128)(2,1)} async-done(((bf16[8,96,2560]{2,1,0:T(8,128)(2,1)}), bf16[8,96,2560]{2,1,0:T(8,128)(2,1)}, u32[]{:S(2)}, u32[]{:S(2)}) %all-to-all-start.1) | async-done | bytes 3932192 | tf_op jit(solution)/shard_map/all_to_all | solution.py:160
  243.7 4.1 %convolution_bitcast_fusion = f32[2,192,2560]{2,1,0:T(8,128)S(1)} fusion(bf16[8,96,2560]{2,1,0:T(8,128)(2,1)} %all-to-all-done.1, bf16[1,192,8,2,96]{4,1,2,0,3:T(8,128)(2,1)S(1)} %copy.140, bf16[1,192,8,2,96]{4,1,2,0,3:T(8,128)(2,1)S(1)} %subtract_convert_fusion), kind=kOutput, calls=%fused_computation.10 | convolution fusion | flops 1510244352 | bytes 9043968 | tf_op jit(solution)/shard_map/stgc,gcd->std/dot_general | solution.py:174
  247.8 0.7 fusion.7
  248.5 1.0 copy.146
  249.6 18.4 %all_to_all.20 = bf16[8,96,640]{2,1,0:T(8,128)(2,1)S(1)} all-to-all(bf16[8,96,640]{2,1,0:T(8,128)(2,1)} %bitcast.242), channel_id=1, replica_groups=mesh['req'=8,'tp'=4] {'req'}, dimensions={0} | all-to-all | bytes 1966080 | tf_op jit(solution)/shard_map/all_to_all | solution.py:160
  268.0 2.8 %convolution_bitcast_fusion.1 = f32[2,192,640]{2,1,0:T(8,128)} fusion(bf16[8,96,640]{2,1,0:T(8,128)(2,1)S(1)} %all_to_all.20, bf16[1,192,8,2,96]{4,1,2,0,3:T(8,128)(2,1)} %copy-done.5, bf16[1,192,8,2,96]{4,1,2,0,3:T(8,128)(2,1)} %copy-done.4), kind=kOutput, calls=%fused_computation.50 | convolution fusion | flops 377782272 | bytes 3145728 | tf_op jit(solution)/shard_map/stgc,gcd->std/dot_general | solution.py:174
  270.9 2.7 reduce-scatter.6.cloned.1.call-done
  273.5 2.0 fusion.51
  (78 shorter events, 4.7 us)
Async XLA Ops:
  6.5 15.7 %copy-start = (bf16[640,2560]{1,0:T(8,128)(2,1)S(1)}, bf16[640,2560]{1,0:T(8,128)(2,1)}, u32[]{:S(2)}) copy-start(bf16[640,2560]{1,0:T(8,128)(2,1)} %param.26) | copy-start | bytes 9830404
  6.5 7.7 %copy-start.9 = (bf16[192,640]{1,0:T(8,128)(2,1)S(1)}, bf16[192,640]{1,0:T(8,128)(2,1)}, u32[]{:S(2)}) copy-start(bf16[192,640]{1,0:T(8,128)(2,1)} %param.17) | copy-start | bytes 737284
  6.5 8.7 %copy-start.18 = (s32[4,48]{1,0:T(4,128)S(1)}, s32[4,48]{1,0:T(4,128)}, u32[]{:S(2)}) copy-start(s32[4,48]{1,0:T(4,128)} %param.24) | copy-start | bytes 2308
  6.5 46.7 %reduce-scatter.4.cloned.1.call-start = ((), (), s32[]{:S(2)}) async-start(), calls=%async_computation.7 | async-start | bytes 1228800 | tf_op jit(solution)/shard_map/reduce_scatter | solution.py:125
  15.3 3.7 %copy-start.13 = (bf16[192,128]{1,0:T(8,128)(2,1)S(1)}, bf16[192,128]{1,0:T(8,128)(2,1)}, u32[]{:S(2)}) copy-start(bf16[192,128]{1,0:T(8,128)(2,1)} %param.18) | copy-start | bytes 147460
  16.8 2.2 copy-start.6
  18.9 1.5 copy-start.8
  20.5 1.3 copy-start.17
  22.1 2.2 copy-start.11
  22.2 2.5 copy-start.12
  80.3 50.8 %all-to-all-start.2 = ((bf16[8,96,2560]{2,1,0:T(8,128)(2,1)}), bf16[8,96,2560]{2,1,0:T(8,128)(2,1)}, u32[]{:S(2)}, u32[]{:S(2)}) async-start(bf16[8,96,2560]{2,1,0:T(8,128)(2,1)} %convolution_convert_fusion), calls=%async_computation.4 | async-start | bytes 7864320 | tf_op jit(solution)/shard_map/all_to_all | solution.py:145
  85.0 8.2 %copy-start.7 = (pred[1536,192]{1,0:T(32,128)(4,1)S(1)}, pred[1536,192]{1,0:T(32,128)(4,1)}, u32[]{:S(2)}) copy-start(pred[1536,192]{1,0:T(32,128)(4,1)} %copy.93) | copy-start | bytes 884740
  131.1 50.9 %all-to-all-start = ((bf16[8,96,2560]{2,1,0:T(8,128)(2,1)}), bf16[8,96,2560]{2,1,0:T(8,128)(2,1)}, u32[]{:S(2)}, u32[]{:S(2)}) async-start(bf16[8,96,2560]{2,1,0:T(8,128)(2,1)} %convolution_convert_fusion.1), calls=%async_computation.1 | async-start | bytes 7864320 | tf_op jit(solution)/shard_map/all_to_all | solution.py:145
  135.7 113.9 %reduce-scatter.8.cloned.1.call-start = ((), (), s32[]{:S(2)}) async-start(), calls=%async_computation.9 | async-start | bytes 4915200 | tf_op jit(solution)/shard_map/reduce_scatter | solution.py:156
  135.7 6.7 %copy-start.14 = (bf16[2,384,2560]{2,1,0:T(8,128)(2,1)S(1)}, bf16[2,384,2560]{2,1,0:T(8,128)(2,1)}, u32[]{:S(2)}) copy-start(bf16[2,384,2560]{2,1,0:T(8,128)(2,1)} %param.31) | copy-start | bytes 11796484
  182.0 6.7 %copy-start.15 = (bf16[2,384,2560]{2,1,0:T(8,128)(2,1)S(1)}, bf16[2,384,2560]{2,1,0:T(8,128)(2,1)}, u32[]{:S(2)}) copy-start(bf16[2,384,2560]{2,1,0:T(8,128)(2,1)} %param.31) | copy-start | bytes 11796484
  192.9 50.8 %all-to-all-start.1 = ((bf16[8,96,2560]{2,1,0:T(8,128)(2,1)}), bf16[8,96,2560]{2,1,0:T(8,128)(2,1)}, u32[]{:S(2)}, u32[]{:S(2)}) async-start(bf16[8,96,2560]{2,1,0:T(8,128)(2,1)} %bitcast.233), calls=%async_computation.2 | async-start | bytes 7864320 | tf_op jit(solution)/shard_map/all_to_all | solution.py:160
  197.4 0.9 copy-start.10
  197.4 76.1 %reduce-scatter.6.cloned.1.call-start = ((), (), s32[]{:S(2)}) async-start(), calls=%async_computation.8 | async-start | bytes 1228800 | tf_op jit(solution)/shard_map/reduce_scatter | solution.py:189
  198.1 2.1 copy-start.2
  203.7 1.7 copy-start.3
  204.2 39.5 %copy-start.4 = (bf16[1,192,8,2,96]{4,1,2,0,3:T(8,128)(2,1)}, bf16[1,192,8,2,96]{4,1,2,0,3:T(8,128)(2,1)S(1)}, u32[]{:S(2)}) copy-start(bf16[1,192,8,2,96]{4,1,2,0,3:T(8,128)(2,1)S(1)} %copy.140) | copy-start | bytes 1769476
  205.4 42.4 %copy-start.5 = (bf16[1,192,8,2,96]{4,1,2,0,3:T(8,128)(2,1)}, bf16[1,192,8,2,96]{4,1,2,0,3:T(8,128)(2,1)S(1)}, u32[]{:S(2)}) copy-start(bf16[1,192,8,2,96]{4,1,2,0,3:T(8,128)(2,1)S(1)} %subtract_convert_fusion) | copy-start | bytes 1769476
  243.7 4.1 %copy-start.16 = (bf16[384,2560]{1,0:T(8,128)(2,1)S(1)}, bf16[384,2560]{1,0:T(8,128)(2,1)}, u32[]{:S(2)}) copy-start(bf16[384,2560]{1,0:T(8,128)(2,1)} %param.33) | copy-start | bytes 5898244
  249.6 26.0 %copy-start.1 = (bf16[640,2560]{1,0:T(8,128)(2,1)S(1)}, bf16[640,2560]{1,0:T(8,128)(2,1)}, u32[]{:S(2)}) copy-start(bf16[640,2560]{1,0:T(8,128)(2,1)} %param.26) | copy-start | bytes 9830404
Sparse Core Ops, SparseCore 0:
  24.4 28.8 reduce-scatter.3
  147.0 72.5 reduce-scatter.7
  249.7 23.7 reduce-scatter.5

commit v19 on v16

--- a/solution.py
+++ b/solution.py
@@ -101,8 +101,9 @@
         cache_lengths,
         ancestors(parents),
     )
-    attn_terms = jnp.dot(
-        head_outputs.reshape(row_count, -1), out_weight, preferred_element_type=jnp.float32
+    attn_terms = jnp.einsum(
+        "tk,kzd->ztd", head_outputs.reshape(row_count, -1),
+        out_weight.reshape(out_weight.shape[0], tp_count, -1), preferred_element_type=jnp.float32,
     )
     column = lax.axis_index("tp") * part_width
     experts_local = expert_gate_up.shape[0]
@@ -121,9 +122,9 @@
     slot_ids = jnp.arange(slot_count, dtype=jnp.int32)
     hit = slot[:, :, None] == slot_ids[None, None, :]
 
-    attn_blocks = attn_terms.astype(jnp.bfloat16).reshape(row_count, tp_count, part_width)
+    attn_blocks = attn_terms.astype(jnp.bfloat16)
     attn_part = lax.psum_scatter(
-        attn_blocks.transpose(1, 0, 2), "tp", scatter_dimension=0, tiled=True
+        attn_blocks, "tp", scatter_dimension=0, tiled=True
     )[0].astype(jnp.float32)
     residual_part = lax.dynamic_slice_in_dim(residual, column, part_width, 1)
     hidden_part_bf = (residual_part.astype(jnp.float32) + attn_part).astype(jnp.bfloat16)

time: 283 us -> 287 us (1.014)
  local copies, waits for them, and re-layouts: 27.1 us -> 30 us
    all_to_all x1, waiting for transfers between devices: 34.9 us -> 31.1 us  [shards(): lax.all_to_all(outputs, 'req', split_axis=0, concat_axis=0, tiled=True)]
    dot_general x1, matrix products: 0.93 us -> 3.82 us  [shards(): jnp.einsum('tk,kzd->ztd', head_outputs.reshape(row_count, -1), out_weight...]
  transfers between devices with their start and end apart: 6 -> 6, of which waited for: 5 -> 5; matrix products, arithmetic and copies ran while one was open for 21% -> 22% of each run, Pallas kernels for 0% -> 0%
where the time goes in v19:
time: 287 us; the launch traced here: 286 us
  waiting for transfers between devices  126 us (44%)
  matrix products  47.6 us (17%)
  blocking collectives  38.3 us (13%)
  local copies, waits for them, and re-layouts  30 us (10%)
  other arithmetic  15.9 us (6%)
  starting transfers between devices  14 us (5%)
  between operations  13.6 us (5%)
    all_to_all x2, waiting for transfers between devices, shards(): lax.all_to_all(outbox, 'req', split_axis=0, concat_axis=0, tiled=True)  69.9 us
    all_to_all x1, waiting for transfers between devices, shards(): lax.all_to_all(outputs, 'req', split_axis=0, concat_axis=0, tiled=True)  31.1 us
    reduce_scatter x1, waiting for transfers between devices, shards(): lax.psum_scatter(attn_blocks, 'tp', scatter_dimension=0, tiled=True)[0]  21.3 us
    all_gather x1, blocking collectives, shards(): hidden_bf = lax.all_gather(hidden_part_bf[None], 'tp', axis=0, tiled=True)  20.2 us
    all_to_all x1, blocking collectives, shards(): lax.all_to_all(outputs, 'req', split_axis=0, concat_axis=0, tiled=True)  18.1 us
    dot_general x2, matrix products, shards(): jnp.einsum('md,dcf->mcf', rows, expert_gate_up[expert], preferred_element...  13.3 us
    all_to_all x2, starting transfers between devices, shards(): lax.all_to_all(outbox, 'req', split_axis=0, concat_axis=0, tiled=True)  9.22 us
    slice x1, local copies, waits for them, and re-layouts, shards(): expert_gate_up[expert]  8.19 us
  transfers between devices with their start and end apart: 6, of which 5 were waited for; matrix products, arithmetic and copies ran while one was open for 22% of the time, Pallas kernels for 0%

profile of v19, /device:TPU:0, one launch (start us, length us, event | category | flops | bytes accessed | tf_op | source)
XLA Modules:
  0.0 285.8 jit_solution(6277893371137129010)
XLA Ops:
  6.6 0.8 compare_select_fusion
  7.5 0.7 iota_compare_fusion.6
  8.2 2.9 %gather_fusion = bf16[64,64,128]{2,1,0:T(8,128)(2,1)} fusion(bf16[64,64,128]{2,1,0:T(8,128)(2,1)} %param.21, s32[1024]{0:T(1024)S(1)} %pad_clamp_fusion), kind=kCustom, calls=%fused_computation | custom fusion | bytes 2097408 | tf_op jit(solution)/shard_map/gather | solution.py:94
  11.1 2.0 gather_fusion.1
  13.1 1.2 reshape.260
  15.9 0.8 bitcast_reduce_fusion
  16.7 0.4 fusion.88
  17.1 1.0 fusion.11
  18.2 1.3 fusion.18
  20.2 3.8 %fusion.28 = bf16[4,192,640]{2,1,0:T(8,128)(2,1)} fusion(bf16[192,640,1]{1,0,2:T(8,128)(2,1)S(1)} %reshape.306, bf16[80,4,8,640]{3,2,1,0:T(8,128)(2,1)} %bitcast.243), kind=kOutput, calls=%fused_computation.53 | convolution fusion | flops 629637120 | bytes 4505600 | tf_op jit(solution)/shard_map/tk,kzd->ztd/dot_general | solution.py:104
  24.5 4.5 %reduce-window.6 = s32[16,9,128]{2,1,0:T(8,128)S(1)} reduce-window(s32[16,9,128]{2,1,0:T(8,128)S(1)} %fusion.72, s32[]{:T(128)} %constant.17.clone.1), window={size=1x1x128 pad=0_0x0_0x127_0}, to_apply=%region_6.7 | reduce-window | flops 2340864 | bytes 147460 | tf_op jit(solution)/shard_map/reduce-window
  29.1 0.4 slice_reduce_fusion
  30.1 1.2 fusion
  31.2 0.5 copy.90
  31.7 21.3 %reduce-scatter.4.cloned.1.call-done = bf16[1,192,640]{2,1,0:T(8,128)(2,1)} async-done(((bf16[4,192,640]{2,1,0:T(8,128)(2,1)}), bf16[1,192,640]{2,1,0:T(8,128)(2,1)}) %reduce-scatter.4.cloned.1.call-update) | async-done | bytes 245776 | tf_op jit(solution)/shard_map/reduce_scatter | solution.py:126
  53.0 1.1 fusion.61
  54.2 0.7 copy-done.6
  54.9 20.2 %all-gather = bf16[768,640]{1,0:T(8,128)(2,1)S(1)} all-gather(bf16[192,640]{1,0:T(8,128)(2,1)S(1)} %fusion.61), channel_id=2, replica_groups=mesh['req'=8,'tp'=4] {'tp'}, dimensions={0}, use_global_device_ids=true | all-gather | bytes 1228800 | tf_op jit(solution)/shard_map/all_gather | solution.py:131
  75.3 0.3 fusion.41
  75.6 1.7 copy.92
  77.3 2.6 reshape.308
  79.9 4.4 %convolution_convert_fusion = bf16[8,96,2560]{2,1,0:T(8,128)(2,1)} fusion(bf16[192,2560,1]{1,0,2:T(8,128)(2,1)} %reshape.308, pred[192,8,2,96]{0,3,2,1:T(32,128)(4,1)S(1)} %bitcast.235), kind=kOutput, calls=%fused_computation.5 | convolution fusion | flops 756940800 | bytes 5111808 | tf_op jit(solution)/shard_map/tgc,td->gcd/dot_general | solution.py:143
  84.3 4.7 %all-to-all-start.2 = ((bf16[8,96,2560]{2,1,0:T(8,128)(2,1)}), bf16[8,96,2560]{2,1,0:T(8,128)(2,1)}, u32[]{:S(2)}, u32[]{:S(2)}) async-start(bf16[8,96,2560]{2,1,0:T(8,128)(2,1)} %convolution_convert_fusion), calls=%async_computation.4 | async-start | bytes 7864320 | tf_op jit(solution)/shard_map/all_to_all | solution.py:146
  89.0 8.2 %fusion.87 = (bf16[1,2560,2,384]{3,2,1,0:T(2,128)(2,1)}, bf16[1,2560,2,384]{3,2,1,0:T(2,128)(2,1)}) fusion(bf16[2,2560,2,384]{3,2,1,0:T(2,128)(2,1)} %param.30), kind=kLoop, calls=%fused_computation.140 | loop fusion | bytes 15728640 | tf_op jit(solution)/shard_map/slice | solution.py:149
  97.2 3.1 %convolution_convert_fusion.1 = bf16[8,96,2560]{2,1,0:T(8,128)(2,1)} fusion(bf16[192,2560,1]{1,0,2:T(8,128)(2,1)S(1)} %copy-done.1, pred[192,8,2,96]{0,3,2,1:T(32,128)(4,1)S(1)} %bitcast.236), kind=kOutput, calls=%fused_computation.6 | convolution fusion | flops 756940800 | bytes 5111808 | tf_op jit(solution)/shard_map/tgc,td->gcd/dot_general | solution.py:143
  100.3 34.8 %all-to-all-done.2 = bf16[8,96,2560]{2,1,0:T(8,128)(2,1)} async-done(((bf16[8,96,2560]{2,1,0:T(8,128)(2,1)}), bf16[8,96,2560]{2,1,0:T(8,128)(2,1)}, u32[]{:S(2)}, u32[]{:S(2)}) %all-to-all-start.2) | async-done | bytes 3932192 | tf_op jit(solution)/shard_map/all_to_all | solution.py:146
  135.2 4.5 %all-to-all-start = ((bf16[8,96,2560]{2,1,0:T(8,128)(2,1)}), bf16[8,96,2560]{2,1,0:T(8,128)(2,1)}, u32[]{:S(2)}, u32[]{:S(2)}) async-start(bf16[8,96,2560]{2,1,0:T(8,128)(2,1)} %convolution_convert_fusion.1), calls=%async_computation.1 | async-start | bytes 7864320 | tf_op jit(solution)/shard_map/all_to_all | solution.py:146
  139.8 6.7 %fusion.1 = f32[768,2,384]{2,0,1:T(8,128)S(1)} fusion(bf16[768,2560,1]{1,0,2:T(8,128)(2,1)} %bitcast.48, bf16[1,2560,2,384]{3,2,1,0:T(2,128)(2,1)} %get-tuple-element.6), kind=kOutput, calls=%fused_computation.13 | convolution fusion | flops 3019898880 | bytes 10223616 | tf_op jit(solution)/shard_map/md,dcf->mcf/dot_general | solution.py:148
  146.4 2.2 convolution_convert_fusion.2
  148.7 2.2 copy.144
  150.9 35.1 %all-to-all-done = bf16[8,96,2560]{2,1,0:T(8,128)(2,1)} async-done(((bf16[8,96,2560]{2,1,0:T(8,128)(2,1)}), bf16[8,96,2560]{2,1,0:T(8,128)(2,1)}, u32[]{:S(2)}, u32[]{:S(2)}) %all-to-all-start) | async-done | bytes 3932192 | tf_op jit(solution)/shard_map/all_to_all | solution.py:146
  186.0 6.7 %fusion.2 = f32[768,2,384]{2,0,1:T(8,128)S(1)} fusion(bf16[768,2560,1]{1,0,2:T(8,128)(2,1)} %bitcast.35, bf16[1,2560,2,384]{3,2,1,0:T(2,128)(2,1)} %get-tuple-element.5), kind=kOutput, calls=%fused_computation.15 | convolution fusion | flops 3019898880 | bytes 10223616 | tf_op jit(solution)/shard_map/md,dcf->mcf/dot_general | solution.py:148
  192.7 4.2 %convolution_convert_fusion.3 = bf16[768,2560]{1,0:T(8,128)(2,1)} fusion(bf16[2,384,2560]{2,1,0:T(8,128)(2,1)S(1)} %copy-done.14, f32[768,2,384]{2,0,1:T(8,128)S(1)} %fusion.2), kind=kOutput, calls=%fused_computation.8 | convolution fusion | flops 1513684992 | bytes 8257536 | tf_op jit(solution)/shard_map/dot_general | solution.py:152
  196.9 4.5 %all-to-all-start.1 = ((bf16[8,96,2560]{2,1,0:T(8,128)(2,1)}), bf16[8,96,2560]{2,1,0:T(8,128)(2,1)}, u32[]{:S(2)}, u32[]{:S(2)}) async-start(bf16[8,96,2560]{2,1,0:T(8,128)(2,1)} %bitcast.232), calls=%async_computation.2 | async-start | bytes 7864320 | tf_op jit(solution)/shard_map/all_to_all | solution.py:161
  202.3 1.7 fusion.23
  204.2 2.2 select_reduce_fusion
  206.3 3.3 %reshape.267 = f32[1,192,8,2,96]{4,3,2,1,0:T(2,128)S(1)} reshape(f32[192,1536]{1,0:T(8,128)} %select_reduce_fusion) | data formatting | bytes 2359296 | tf_op jit(solution)/shard_map/reshape | solution.py:169
  209.7 1.4 copy.139
  211.1 1.4 subtract_convert_fusion
  212.5 4.1 %fusion.5 = f32[192,2,384]{2,0,1:T(8,128)} fusion(bf16[2560,2,384]{2,1,0:T(2,128)(2,1)} %param.32, f32[192,2560]{1,0:T(8,128)S(1)} %bitcast.230, f32[2560]{0:T(1024)S(1)} %copy-done.11, f32[192]{0:T(256)S(1)} %add_rsqrt_fusion), kind=kOutput, calls=%fused_computation.21 | convolution fusion | flops 756449280 | bytes 6499072 | tf_op jit(solution)/shard_map/td,dcf->tcf/dot_general | solution.py:184
  216.7 31.1 %all-to-all-done.1 = bf16[8,96,2560]{2,1,0:T(8,128)(2,1)} async-done(((bf16[8,96,2560]{2,1,0:T(8,128)(2,1)}), bf16[8,96,2560]{2,1,0:T(8,128)(2,1)}, u32[]{:S(2)}, u32[]{:S(2)}) %all-to-all-start.1) | async-done | bytes 3932192 | tf_op jit(solution)/shard_map/all_to_all | solution.py:161
  247.8 4.0 %convolution_bitcast_fusion = f32[2,192,2560]{2,1,0:T(8,128)S(1)} fusion(bf16[8,96,2560]{2,1,0:T(8,128)(2,1)} %all-to-all-done.1, bf16[1,192,8,2,96]{4,1,2,0,3:T(8,128)(2,1)S(1)} %copy-done.4, bf16[1,192,8,2,96]{4,1,2,0,3:T(8,128)(2,1)S(1)} %copy-done.5), kind=kOutput, calls=%fused_computation.9 | convolution fusion | flops 1510244352 | bytes 9043968 | tf_op jit(solution)/shard_map/stgc,gcd->std/dot_general | solution.py:175
  251.8 0.7 fusion.7
  252.5 1.0 copy.145
  253.6 18.1 %all_to_all.20 = bf16[8,96,640]{2,1,0:T(8,128)(2,1)S(1)} all-to-all(bf16[8,96,640]{2,1,0:T(8,128)(2,1)} %bitcast.238), channel_id=1, replica_groups=mesh['req'=8,'tp'=4] {'req'}, dimensions={0} | all-to-all | bytes 1966080 | tf_op jit(solution)/shard_map/all_to_all | solution.py:161
  271.7 1.9 convolution_bitcast_fusion.1
  273.6 3.9 %reduce-scatter.6.cloned.1.call-done = bf16[1,192,640]{2,1,0:T(8,128)(2,1)} async-done(((bf16[4,192,640]{2,1,0:T(8,128)(2,1)}), bf16[1,192,640]{2,1,0:T(8,128)(2,1)}) %reduce-scatter.6.cloned.1.call-update) | async-done | bytes 245776 | tf_op jit(solution)/shard_map/reduce_scatter | solution.py:190
  277.5 1.7 fusion.60
  (76 shorter events, 4.7 us)
Async XLA Ops:
  6.5 245.2 %copy-start = (bf16[384,2560]{1,0:T(8,128)(2,1)S(1)}, bf16[384,2560]{1,0:T(8,128)(2,1)}, u32[]{:S(2)}) copy-start(bf16[384,2560]{1,0:T(8,128)(2,1)} %param.33) | copy-start | bytes 5898244
  6.5 7.8 %copy-start.16 = (s32[4,48]{1,0:T(4,128)S(1)}, s32[4,48]{1,0:T(4,128)}, u32[]{:S(2)}) copy-start(s32[4,48]{1,0:T(4,128)} %param.24) | copy-start | bytes 2308
  6.5 46.5 %reduce-scatter.4.cloned.1.call-start = ((), (), s32[]{:S(2)}) async-start(), calls=%async_computation.7 | async-start | bytes 1228800 | tf_op jit(solution)/shard_map/reduce_scatter | solution.py:126
  13.1 3.6 %copy-start.12 = (bf16[192,128]{1,0:T(8,128)(2,1)S(1)}, bf16[192,128]{1,0:T(8,128)(2,1)}, u32[]{:S(2)}) copy-start(bf16[192,128]{1,0:T(8,128)(2,1)} %param.18) | copy-start | bytes 147460
  16.6 1.5 copy-start.8
  18.2 1.3 copy-start.15
  19.8 4.3 %copy-start.10 = (s32[192,6]{0,1:T(8,128)S(1)}, s32[192,6]{0,1:T(8,128)}, u32[]{:S(2)}) copy-start(s32[192,6]{0,1:T(8,128)} %param.29) | copy-start | bytes 13828
  19.8 4.7 %copy-start.11 = (f32[2560]{0:T(1024)S(1)}, f32[2560]{0:T(1024)}, u32[]{:S(2)}) copy-start(f32[2560]{0:T(1024)} %param.27) | copy-start | bytes 30724
  54.2 0.7 copy-start.6
  84.3 50.8 %all-to-all-start.2 = ((bf16[8,96,2560]{2,1,0:T(8,128)(2,1)}), bf16[8,96,2560]{2,1,0:T(8,128)(2,1)}, u32[]{:S(2)}, u32[]{:S(2)}) async-start(bf16[8,96,2560]{2,1,0:T(8,128)(2,1)} %convolution_convert_fusion), calls=%async_computation.4 | async-start | bytes 7864320 | tf_op jit(solution)/shard_map/all_to_all | solution.py:146
  89.0 8.2 %copy-start.1 = (bf16[192,2560,1]{1,0,2:T(8,128)(2,1)S(1)}, bf16[192,2560,1]{1,0,2:T(8,128)(2,1)}, u32[]{:S(2)}) copy-start(bf16[192,2560,1]{1,0,2:T(8,128)(2,1)} %reshape.308) | copy-start | bytes 2949124
  135.2 50.9 %all-to-all-start = ((bf16[8,96,2560]{2,1,0:T(8,128)(2,1)}), bf16[8,96,2560]{2,1,0:T(8,128)(2,1)}, u32[]{:S(2)}, u32[]{:S(2)}) async-start(bf16[8,96,2560]{2,1,0:T(8,128)(2,1)} %convolution_convert_fusion.1), calls=%async_computation.1 | async-start | bytes 7864320 | tf_op jit(solution)/shard_map/all_to_all | solution.py:146
  139.7 113.9 %reduce-scatter.8.cloned.1.call-start = ((), (), s32[]{:S(2)}) async-start(), calls=%async_computation.9 | async-start | bytes 4915200 | tf_op jit(solution)/shard_map/reduce_scatter | solution.py:157
  139.8 6.7 %copy-start.13 = (bf16[2,384,2560]{2,1,0:T(8,128)(2,1)S(1)}, bf16[2,384,2560]{2,1,0:T(8,128)(2,1)}, u32[]{:S(2)}) copy-start(bf16[2,384,2560]{2,1,0:T(8,128)(2,1)} %param.31) | copy-start | bytes 11796484
  186.0 6.7 %copy-start.14 = (bf16[2,384,2560]{2,1,0:T(8,128)(2,1)S(1)}, bf16[2,384,2560]{2,1,0:T(8,128)(2,1)}, u32[]{:S(2)}) copy-start(bf16[2,384,2560]{2,1,0:T(8,128)(2,1)} %param.31) | copy-start | bytes 11796484
  196.9 50.8 %all-to-all-start.1 = ((bf16[8,96,2560]{2,1,0:T(8,128)(2,1)}), bf16[8,96,2560]{2,1,0:T(8,128)(2,1)}, u32[]{:S(2)}, u32[]{:S(2)}) async-start(bf16[8,96,2560]{2,1,0:T(8,128)(2,1)} %bitcast.232), calls=%async_computation.2 | async-start | bytes 7864320 | tf_op jit(solution)/shard_map/all_to_all | solution.py:161
  201.4 0.9 copy-start.9
  201.4 76.1 %reduce-scatter.6.cloned.1.call-start = ((), (), s32[]{:S(2)}) async-start(), calls=%async_computation.8 | async-start | bytes 1228800 | tf_op jit(solution)/shard_map/reduce_scatter | solution.py:190
  202.1 2.1 copy-start.2
  209.7 2.8 copy-start.3
  212.5 35.2 %copy-start.4 = (bf16[1,192,8,2,96]{4,1,2,0,3:T(8,128)(2,1)S(1)}, bf16[1,192,8,2,96]{4,1,2,0,3:T(8,128)(2,1)}, u32[]{:S(2)}) copy-start(bf16[1,192,8,2,96]{4,1,2,0,3:T(8,128)(2,1)} %copy.139) | copy-start | bytes 1769476
  212.5 35.2 %copy-start.5 = (bf16[1,192,8,2,96]{4,1,2,0,3:T(8,128)(2,1)S(1)}, bf16[1,192,8,2,96]{4,1,2,0,3:T(8,128)(2,1)}, u32[]{:S(2)}) copy-start(bf16[1,192,8,2,96]{4,1,2,0,3:T(8,128)(2,1)} %subtract_convert_fusion) | copy-start | bytes 1769476
  247.7 4.0 %copy-start.17 = (f32[192,2,384]{2,0,1:T(8,128)S(1)}, f32[192,2,384]{2,0,1:T(8,128)}, u32[]{:S(2)}) copy-start(f32[192,2,384]{2,0,1:T(8,128)} %fusion.5) | copy-start | bytes 1769476
  252.5 25.0 %copy-start.7 = (bf16[192,640]{1,0:T(8,128)(2,1)S(1)}, bf16[192,640]{1,0:T(8,128)(2,1)}, u32[]{:S(2)}) copy-start(bf16[192,640]{1,0:T(8,128)(2,1)} %copy-done.6) | copy-start | bytes 737284
Sparse Core Ops, SparseCore 0:
  24.2 28.8 reduce-scatter.3
  151.0 72.4 reduce-scatter.7
  253.7 23.7 reduce-scatter.5
